TPU v7x, 32 devices: a whole 2x2x4 slice. The times are simulated.
32 devices in a mesh: table: 4 (over y, x), batch: 4 (over z), ctx: 2 (over core).
Axes of the slice: x: 2, y: 2, z: 4, core: 2. Of those that a mesh axis runs over, the one named last changes fastest.
Arguments:
- item_table: bfloat16 [65536, 256], P('table')
- context_table: bfloat16 [4096, 256], replicated
- user_table: bfloat16 [16384, 256], P(('table', 'batch')), may hold values from -3 to 3
- item_owner: int32 [1024, 64, 1], P(('table', 'batch', 'ctx')), may hold values from 0 to 3; in each aligned block of 2048 rows (0 to 2047, 2048 to 4095, ..., all dimensions but the last counted through in order) at most 1024 rows name the same one
- item_row: int32 [1024, 64], P(('table', 'batch', 'ctx')), may hold values from 0 to 16383
- context_id: int32 [1024, 64], P(('table', 'batch', 'ctx')), may hold values from 0 to 4095
- bucket: int32 [1024, 64], P(('table', 'batch', 'ctx')), may hold values from 0 to 3
- user_ids: int32 [1024], P(('table', 'batch', 'ctx')), may hold values from 0 to 16383, as said below
Outputs:
- updated_users: bfloat16 [16384, 256], P(('table', 'batch'))
Inputs may be any that keep to these rules, and one draw needn't show every extreme that they name: `item_owner`: among the 2048 slots of one device no table shard is named more than 1024 times. `bucket`: 0 marks an empty slot. `user_ids`: all ids are distinct. User u is owned by index u // 1024 of table+batch at row u % 1024. At most 2 of the users of one device share an owner, and on every device some owner has exactly 2.
All inputs are finite; a program needn't handle non-finite values.
Results may differ from a plain program's by a relative error of at most 0.001.
Values may be sent and summed in bfloat16 or wider, within the bound.
No kernel may reach another device: no remote copies, remote signals or barrier semaphores. Data moves between devices by JAX's collectives and lax.ppermute only.
A program may use at most 64 MiB of HBM per device.

v0:
```python
import jax
import jax.numpy as jnp
from jax import lax
from jax.sharding import PartitionSpec as P

CG_STEPS = 3


REG_LAMBDA = 0.1
CONF_SCALE = 2.0
EPSILON = 1e-06


def gram_of(table_rows):
    return lax.dot_general(
        table_rows, table_rows, (((0,), (0,)), ((), ())), preferred_element_type=jnp.float32
    )


def owner_slots(owners, groups, capacity):
    one_hot = (jnp.arange(groups, dtype=jnp.int32)[:, None] == owners[None, :]).astype(jnp.int32)
    earlier = jnp.cumsum(one_hot, axis=1) - one_hot
    position = jnp.sum(earlier * one_hot, axis=0)
    return owners * capacity + position


def place_integers(values, placing):
    upper = (values // 128).astype(jnp.bfloat16)
    lower = (values % 128).astype(jnp.bfloat16)
    stacked = jnp.stack([upper, lower], axis=0)
    placed = lax.dot_general(
        stacked, placing, (((1,), (0,)), ((), ())), preferred_element_type=jnp.float32
    )
    return placed[0].astype(jnp.int32) * 128 + placed[1].astype(jnp.int32)


def conjugate_solve(slot_rows, confidence, weights, gram_matrix):
    highest = lax.Precision.HIGHEST
    rank_width = slot_rows.shape[-1]
    right_side = jnp.einsum(
        "usk,us->uk", slot_rows, weights, precision=highest, preferred_element_type=jnp.float32
    ) * rank_width ** (-0.5)
    solution = jnp.zeros_like(right_side)
    residual = right_side
    direction = right_side
    norm_now = jnp.sum(residual * residual, axis=1, keepdims=True)
    for iteration in range(CG_STEPS):
        projected = jnp.einsum(
            "usk,uk->us",
            slot_rows,
            direction,
            precision=highest,
            preferred_element_type=jnp.float32,
        )
        image_vec = (
            jnp.dot(direction, gram_matrix, precision=highest)
            + REG_LAMBDA * direction
            + jnp.einsum(
                "us,usk->uk",
                confidence * projected,
                slot_rows,
                precision=highest,
                preferred_element_type=jnp.float32,
            )
            / rank_width
        )
        step_size = norm_now / (jnp.sum(direction * image_vec, axis=1, keepdims=True) + EPSILON)
        solution = solution + step_size * direction
        residual = residual - step_size * image_vec
        norm_next = jnp.sum(residual * residual, axis=1, keepdims=True)
        direction = residual + norm_next / (norm_now + EPSILON) * direction
        norm_now = norm_next
    return solution


def per_device(
    item_table, context_table, user_table, item_owner, item_row, context_id, bucket, user_ids
):
    n_table = lax.axis_size("table")
    n_batch = lax.axis_size("batch")
    item_gram = lax.psum(gram_of(item_table).astype(jnp.bfloat16), "table").astype(jnp.float32)
    context_gram = gram_of(context_table)
    pair_count = item_table.shape[0] * n_table * context_table.shape[0]
    gram_matrix = item_gram * context_gram / pair_count
    user_count, slot_count = bucket.shape
    rank_width = item_table.shape[1]
    flat_count = user_count * slot_count
    capacity = 2 * flat_count // n_table
    owners = item_owner.reshape(flat_count)
    target = owner_slots(owners, n_table, capacity)
    placing = (target[:, None] == jnp.arange(n_table * capacity, dtype=jnp.int32)[None, :]).astype(
        jnp.bfloat16
    )
    row_requests = place_integers(item_row.reshape(flat_count), placing).reshape(n_table, capacity)
    context_flat = context_id.reshape(flat_count)
    fetched = lax.all_to_all(
        item_table[lax.all_to_all(row_requests, "table", split_axis=0, concat_axis=0, tiled=True)],
        "table",
        split_axis=0,
        concat_axis=0,
        tiled=True,
    )
    picked = jnp.dot(
        placing, fetched.reshape(n_table * capacity, rank_width), preferred_element_type=jnp.float32
    )
    slot_rows = (picked * context_table[context_flat].astype(jnp.float32)).astype(jnp.bfloat16)
    slot_rows = slot_rows.reshape(user_count, slot_count, rank_width)
    confidence = CONF_SCALE * bucket.astype(jnp.float32)
    weights = jnp.where(bucket > 0, 1.0 + confidence, 0.0)
    solved = conjugate_solve(slot_rows, confidence, weights, gram_matrix).astype(jnp.bfloat16)
    user_rows = user_table.shape[0]
    owner_count = n_table * n_batch
    user_capacity = (user_count + owner_count - 1) // owner_count
    user_owner = user_ids // user_rows
    local_rows = user_ids % user_rows
    user_target = owner_slots(user_owner, owner_count, user_capacity)
    user_placing = (
        user_target[:, None] == jnp.arange(owner_count * user_capacity, dtype=jnp.int32)[None, :]
    ).astype(jnp.bfloat16)
    send_rows = lax.dot_general(
        user_placing, solved, (((0,), (0,)), ((), ())), preferred_element_type=jnp.float32
    ).astype(jnp.bfloat16)
    filled = jnp.sum(user_placing.astype(jnp.float32), axis=0)
    placed_ids = place_integers(local_rows, user_placing)
    send_ids = jnp.where(filled > 0.5, placed_ids, user_rows)
    got_rows, got_ids = (
        lax.all_to_all(send_rows, ("table", "batch"), split_axis=0, concat_axis=0, tiled=True),
        lax.all_to_all(send_ids, ("table", "batch"), split_axis=0, concat_axis=0, tiled=True),
    )
    all_rows, all_ids = (
        lax.all_gather(got_rows, "ctx", axis=0, tiled=True),
        lax.all_gather(got_ids, "ctx", axis=0, tiled=True),
    )
    hitting = (jnp.arange(user_rows, dtype=jnp.int32)[:, None] == all_ids[None, :]).astype(
        jnp.bfloat16
    )
    landed = jnp.dot(hitting, all_rows, preferred_element_type=jnp.float32).astype(jnp.bfloat16)
    covered = jnp.sum(hitting.astype(jnp.float32), axis=1, keepdims=True) > 0.5
    return jnp.where(covered, landed, user_table)


def solution(mesh):
    in_specs = (
        P("table", None),
        P(),
        P(("table", "batch"), None),
        P(("table", "batch", "ctx"), None, None),
        P(("table", "batch", "ctx"), None),
        P(("table", "batch", "ctx"), None),
        P(("table", "batch", "ctx"), None),
        P(("table", "batch", "ctx")),
    )
    out_specs = P(("table", "batch"), None)
    return jax.shard_map(
        per_device, mesh=mesh, in_specs=in_specs, out_specs=out_specs, check_vma=False
    )
```

profile of v0, /device:TPU:0, one launch (start us, length us, event | category | flops | bytes accessed | tf_op | source)
XLA Modules:
  0.0 154.9 jit_solution(15914122811694390057)
XLA Ops:
  6.5 0.5 broadcast.313
  7.1 1.5 fusion.54
  8.6 0.1 eq.84
  8.7 1.1 reduce-window.6
  9.8 0.2 slice_reduce_fusion
  10.0 0.2 reduce-window.9
  10.2 0.1 select_reduce_fusion
  10.3 0.1 mul.174
  10.4 0.8 reshape.350
  11.3 0.0 copy-start.4
  11.3 6.0 %fusion.1 = f32[2,4096]{1,0:T(2,128)S(1)} fusion(s32[2048]{0:T(1024)S(1)} %bitcast_add_fusion, bf16[1,2048]{1,0:T(2,128)(2,1)S(1)} %fusion.39, bf16[1,2048]{1,0:T(2,128)(2,1)S(1)} %get-tuple-element.16), kind=kOutput, calls=%fused_computation.4 | convolution fusion | flops 41959424 | bytes 49152 | tf_op jit(solution)/shard_map/dot_general | solution.py:31
  17.3 0.6 fusion.28
  17.9 5.2 %all-to-all-start.1 = ((s32[4,1,1024]{2,1,0:T(1,128)}), s32[4,1,1024]{2,1,0:T(1,128)S(1)}, u32[]{:S(2)}, u32[]{:S(2)}) async-start(s32[4,1,1024]{2,1,0:T(1,128)} %bitcast.5), calls=%async_computation.1 | async-start | bytes 32768 | tf_op jit(solution)/shard_map/all_to_all | solution.py:97
  23.1 0.0 copy-done.4
  23.1 0.2 reduce_window_sum.24
  23.3 0.1 convert_reduce_fusion.1
  23.4 0.2 fusion.34
  23.7 0.1 add.178
  23.8 0.1 gt.35
  23.8 0.6 broadcast_select_fusion
  24.5 3.3 %all-to-all-done.1 = s32[4,1,1024]{2,1,0:T(1,128)S(1)} async-done(((s32[4,1,1024]{2,1,0:T(1,128)}), s32[4,1,1024]{2,1,0:T(1,128)S(1)}, u32[]{:S(2)}, u32[]{:S(2)}) %all-to-all-start.1) | async-done | bytes 16416 | tf_op jit(solution)/shard_map/all_to_all | solution.py:97
  27.8 5.0 %all-to-all-start = ((s32[16,2,1]{1,2,0:T(1,128)}), s32[16,2,1]{1,2,0:T(1,128)S(1)}, u32[]{:S(2)}, u32[]{:S(2)}) async-start(s32[16,2,1]{1,2,0:T(1,128)} %bitcast.2), calls=%async_computation | async-start | bytes 16384 | tf_op jit(solution)/shard_map/all_to_all | solution.py:128
  32.9 20.3 %gather_fusion = bf16[4096,256]{1,0:T(8,128)(2,1)} fusion(bf16[16384,256]{1,0:T(8,128)(2,1)} %param.8, s32[4096]{0:T(1024)S(1)} %broadcast_clamp_fusion), kind=kCustom, calls=%fused_computation | custom fusion | bytes 4210688 | tf_op jit(solution)/shard_map/gather | solution.py:97
  53.1 0.0 all-to-all-done
  53.1 4.4 %all-to-all-start.2 = ((bf16[4,1024,256]{2,1,0:T(8,128)(2,1)}), bf16[4,1024,256]{2,1,0:T(8,128)(2,1)}, u32[]{:S(2)}, u32[]{:S(2)}) async-start(bf16[4,1024,256]{2,1,0:T(8,128)(2,1)} %bitcast.110), calls=%async_computation.2 | async-start | bytes 4194304 | tf_op jit(solution)/shard_map/all_to_all | solution.py:96
  57.6 0.0 copy-start.3
  57.6 0.0 copy-start.2
  57.6 0.2 all-reduce.3.cloned.1.call-start
  57.9 8.8 %convolution_convert_fusion.1 = bf16[256,256]{1,0:T(8,128)(2,1)} fusion(bf16[16384,256]{1,0:T(8,128)(2,1)} %param.8), kind=kOutput, calls=%fused_computation.13 | convolution fusion | flops 2147549184 | bytes 8519680 | tf_op jit(solution)/shard_map/dot_general | solution.py:15
  66.7 0.0 all-reduce.3.cloned.1.call-update
  66.7 0.1 reshape.352
  66.8 0.0 copy-start.5
  66.9 7.5 %gather_fusion.1 = bf16[2048,256]{1,0:T(8,128)(2,1)S(1)} fusion(bf16[4096,256]{1,0:T(8,128)(2,1)S(1)} %copy-done, s32[2048]{0:T(1024)S(1)} %broadcast_clamp_fusion.1), kind=kCustom, calls=%fused_computation.1 | custom fusion | bytes 2105344 | tf_op jit(solution)/shard_map/gather | solution.py:106
  74.4 0.6 dynamic-slice
  75.6 0.6 reduce.18
  76.2 0.1 reshape.371
  76.3 0.2 dynamic-update-slice
  76.6 1.8 %all-reduce = s32[64]{0:T(128)S(1)} all-reduce(s32[64]{0:T(128)S(1)} %dynamic-update-slice), channel_id=1, replica_groups=mesh['table'=4,'batch'=4,'ctx'=2] {'ctx'}, use_global_device_ids=true, to_apply=%add | all-reduce | flops 64 | bytes 512
  78.4 0.1 convert_reduce_fusion
  78.5 36.9 %all-reduce.3.cloned.1.call-done = bf16[256,256]{1,0:T(8,128)(2,1)} async-done(((bf16[256,256]{1,0:T(8,128)(2,1)}), bf16[256,256]{1,0:T(8,128)(2,1)}) %all-reduce.3.cloned.1.call-update) | async-done | bytes 131088 | tf_op jit(solution)/shard_map/psum | solution.py:81
  115.4 1.6 %fusion.7 = f32[256,256]{1,0:T(8,128)S(1)} fusion(bf16[4096,256]{1,0:T(8,128)(2,1)S(1)} %copy-done, bf16[256,256]{1,0:T(8,128)(2,1)} %all-reduce.3.cloned.1.call-done), kind=kOutput, calls=%fused_computation.12 | convolution fusion | flops 537067520 | bytes 2490368 | tf_op jit(solution)/shard_map/dot_general | solution.py:15
  117.1 0.0 all-to-all-done.2
  117.1 7.4 %fusion.5 = bf16[2048,256]{1,0:T(8,128)(2,1)S(1)} fusion(bf16[4096,256]{1,0:T(8,128)(2,1)} %bitcast.9, s32[2048]{0:T(1024)S(1)} %bitcast_add_fusion, bf16[2048,256]{1,0:T(8,128)(2,1)S(1)} %gather_fusion.1), kind=kOutput, calls=%fused_computation.8 | convolution fusion | flops 4304928768 | bytes 4202496 | tf_op jit(solution)/shard_map/dot_general | solution.py:103
  124.5 0.5 fusion.55
  125.0 0.9 fusion.23
  126.0 0.5 fusion.56
  126.5 0.3 multiply_reduce_fusion.3
  126.9 0.2 multiply_reduce_fusion.2
  127.1 0.1 fusion.18
  127.1 0.9 fusion.21
  128.1 0.0 copy-start.1
  128.1 0.5 fusion.57
  128.6 0.3 multiply_reduce_fusion.1
  129.0 0.2 multiply_reduce_fusion
  129.2 0.1 multiply_add_fusion
  129.3 0.9 fusion.19
  130.2 0.5 fusion.58
  130.7 0.3 fusion.12
  131.1 0.3 convolution_convert_fusion.2
  131.4 0.6 all_to_all.28
  132.0 5.6 %all-to-all-start.3 = ((bf16[16,2,256]{2,1,0:T(2,128)(2,1)}), bf16[16,2,256]{2,1,0:T(2,128)(2,1)S(1)}, u32[]{:S(2)}, u32[]{:S(2)}) async-start(bf16[16,2,256]{2,1,0:T(2,128)(2,1)} %all_to_all.28), calls=%async_computation.3 | async-start | bytes 32768 | tf_op jit(solution)/shard_map/all_to_all | solution.py:127
  137.6 7.3 %all-to-all-done.3 = bf16[16,2,256]{2,1,0:T(2,128)(2,1)S(1)} async-done(((bf16[16,2,256]{2,1,0:T(2,128)(2,1)}), bf16[16,2,256]{2,1,0:T(2,128)(2,1)S(1)}, u32[]{:S(2)}, u32[]{:S(2)}) %all-to-all-start.3) | async-done | bytes 16416 | tf_op jit(solution)/shard_map/all_to_all | solution.py:127
  144.9 1.8 %all_gather.7 = bf16[64,256]{1,0:T(8,128)(2,1)S(1)} all-gather(bf16[32,256]{1,0:T(8,128)(2,1)S(1)} %all_to_all.30), channel_id=1, replica_groups=mesh['table'=4,'batch'=4,'ctx'=2] {'ctx'}, dimensions={0}, use_global_device_ids=true | all-gather | bytes 49152 | tf_op jit(solution)/shard_map/all_gather | solution.py:131
  146.8 1.3 fusion.6
  (35 shorter events, 0.3 us)
Async XLA Ops:
  6.5 60.3 %copy-start = (bf16[4096,256]{1,0:T(8,128)(2,1)S(1)}, bf16[4096,256]{1,0:T(8,128)(2,1)}, u32[]{:S(2)}) copy-start(bf16[4096,256]{1,0:T(8,128)(2,1)} %param.9) | copy-start | bytes 6291460
  11.3 11.8 %copy-start.4 = (s32[32]{0:T(128)S(1)}, s32[32]{0:T(128)}, u32[]{:S(2)}) copy-start(s32[32]{0:T(128)} %param.15) | copy-start | bytes 388
  17.9 9.9 %all-to-all-start.1 = ((s32[4,1,1024]{2,1,0:T(1,128)}), s32[4,1,1024]{2,1,0:T(1,128)S(1)}, u32[]{:S(2)}, u32[]{:S(2)}) async-start(s32[4,1,1024]{2,1,0:T(1,128)} %bitcast.5), calls=%async_computation.1 | async-start | bytes 32768 | tf_op jit(solution)/shard_map/all_to_all | solution.py:97
  27.8 25.4 %all-to-all-start = ((s32[16,2,1]{1,2,0:T(1,128)}), s32[16,2,1]{1,2,0:T(1,128)S(1)}, u32[]{:S(2)}, u32[]{:S(2)}) async-start(s32[16,2,1]{1,2,0:T(1,128)} %bitcast.2), calls=%async_computation | async-start | bytes 16384 | tf_op jit(solution)/shard_map/all_to_all | solution.py:128
  53.1 63.9 %all-to-all-start.2 = ((bf16[4,1024,256]{2,1,0:T(8,128)(2,1)}), bf16[4,1024,256]{2,1,0:T(8,128)(2,1)}, u32[]{:S(2)}, u32[]{:S(2)}) async-start(bf16[4,1024,256]{2,1,0:T(8,128)(2,1)} %bitcast.110), calls=%async_computation.2 | async-start | bytes 4194304 | tf_op jit(solution)/shard_map/all_to_all | solution.py:96
  57.6 9.1 %copy-start.3 = (s32[32,64]{1,0:T(8,128)S(1)}, s32[32,64]{1,0:T(8,128)}, u32[]{:S(2)}) copy-start(s32[32,64]{1,0:T(8,128)} %param.13) | copy-start | bytes 24580
  57.6 9.2 %copy-start.2 = (s32[32,64]{1,0:T(8,128)S(1)}, s32[32,64]{1,0:T(8,128)}, u32[]{:S(2)}) copy-start(s32[32,64]{1,0:T(8,128)} %param.14) | copy-start | bytes 24580
  57.6 57.8 %all-reduce.3.cloned.1.call-start = ((), (), s32[]{:S(2)}) async-start(), calls=%async_computation.4 | async-start | bytes 262144 | tf_op jit(solution)/shard_map/psum | solution.py:81
  66.8 7.5 %copy-start.5 = (u32[32]{0:T(128)S(1)}, u32[32]{0:T(128)}, u32[]{:S(2)}) copy-start(u32[32]{0:T(128)} %constant.113) | copy-start | bytes 388
  128.1 18.7 %copy-start.1 = (bf16[1024,256]{1,0:T(8,128)(2,1)S(1)}, bf16[1024,256]{1,0:T(8,128)(2,1)}, u32[]{:S(2)}) copy-start(bf16[1024,256]{1,0:T(8,128)(2,1)} %param.10) | copy-start | bytes 1572868
  132.0 12.9 %all-to-all-start.3 = ((bf16[16,2,256]{2,1,0:T(2,128)(2,1)}), bf16[16,2,256]{2,1,0:T(2,128)(2,1)S(1)}, u32[]{:S(2)}, u32[]{:S(2)}) async-start(bf16[16,2,256]{2,1,0:T(2,128)(2,1)} %all_to_all.28), calls=%async_computation.3 | async-start | bytes 32768 | tf_op jit(solution)/shard_map/all_to_all | solution.py:127
Sparse Core Ops, SparseCore 0:
  66.8 48.5 all-reduce.2
where the time goes:
time: 155 us
  waiting for transfers between devices  47.6 us (31%)
  matrix products  31.5 us (20%)
  local copies, waits for them, and re-layouts  31.4 us (20%)
  starting transfers between devices  20.5 us (13%)
  between operations  14.3 us (9%)
  other arithmetic  6.01 us (4%)
  blocking collectives  3.64 us (2%)
    psum x1, waiting for transfers between devices, per_device(): lax.psum(gram_of(item_table).astype(jnp.bfloat16), 'table')  36.9 us
    gather x1, local copies, waits for them, and re-layouts, per_device(): item_table[lax.all_to_all(row_requests, 'table', split_axis=0, concat_axi...  20.3 us
    dot_general x2, matrix products, gram_of(): lax.dot_general(table_rows, table_rows, (((0,), (0,)), ((), ())), preferr...  10.5 us
    gather x1, local copies, waits for them, and re-layouts, per_device(): context_table[context_flat].astype(jnp.float32)  7.5 us
    dot_general x1, matrix products, per_device(): jnp.dot(placing, fetched.reshape(n_table * capacity, rank_width), preferr...  7.39 us
    all_to_all x1, waiting for transfers between devices, per_device(): lax.all_to_all(send_rows, ('table', 'batch'), split_axis=0, concat_axis=0...  7.3 us
    dot_general x2, matrix products, place_integers(): lax.dot_general(stacked, placing, (((1,), (0,)), ((), ())), preferred_ele...  6.17 us
    all_to_all x1, starting transfers between devices, per_device(): lax.all_to_all(send_rows, ('table', 'batch'), split_axis=0, concat_axis=0...  5.61 us
  transfers between devices with their start and end apart: 5, of which 3 were waited for; matrix products, arithmetic and copies ran while one was open for 27% of the time, Pallas kernels for 0%

commit v1 on v0

--- a/solution.py
+++ b/solution.py
@@ -15,6 +15,16 @@
     return lax.dot_general(
         table_rows, table_rows, (((0,), (0,)), ((), ())), preferred_element_type=jnp.float32
     )
+
+
+def butterfly_sum(value, axes):
+    for name, size in axes:
+        step = 1
+        while step < size:
+            pairs = [(i, i ^ step) for i in range(size)]
+            value = value + lax.ppermute(value, name, pairs)
+            step *= 2
+    return value
 
 
 def owner_slots(owners, groups, capacity):
@@ -78,7 +88,11 @@
 ):
     n_table = lax.axis_size("table")
     n_batch = lax.axis_size("batch")
-    item_gram = lax.psum(gram_of(item_table).astype(jnp.bfloat16), "table").astype(jnp.float32)
+    n_ctx = lax.axis_size("ctx")
+    share = item_table.shape[0] // (n_batch * n_ctx)
+    part = lax.axis_index("batch") * n_ctx + lax.axis_index("ctx")
+    own_rows = lax.dynamic_slice_in_dim(item_table, part * share, share, axis=0)
+    item_gram = butterfly_sum(gram_of(own_rows), (("ctx", n_ctx), ("table", n_table), ("batch", n_batch)))
     context_gram = gram_of(context_table)
     pair_count = item_table.shape[0] * n_table * context_table.shape[0]
     gram_matrix = item_gram * context_gram / pair_count

time: 155 us -> 119 us (0.77)
  waiting for transfers between devices: 47.6 us -> 19.5 us
  between operations: 14.3 us -> 0.95 us
  starting transfers between devices: 20.5 us -> 31.2 us
  matrix products: 31.5 us -> 24 us
    psum x1 -> x0, waiting for transfers between devices: 36.9 us -> none  [per_device(): lax.psum(gram_of(item_table).astype(jnp.bfloat16), 'table')]
    ppermute x0 -> x5, waiting for transfers between devices: none -> 12.2 us  [butterfly_sum(): value = value + lax.ppermute(value, name, pairs)]
    ppermute x0 -> x5, starting transfers between devices: none -> 8.1 us  [butterfly_sum(): value = value + lax.ppermute(value, name, pairs)]
    dot_general x2, matrix products: 10.5 us -> 2.79 us  [gram_of(): lax.dot_general(table_rows, table_rows, (((0,), (0,)), ((), ())), preferr...]
    all_to_all x1, waiting for transfers between devices: 3.32 us -> 0.01 us  [per_device(): lax.all_to_all(row_requests, 'table', split_axis=0, concat_axis=0, tiled=...]
    all_to_all x1, starting transfers between devices: 5.61 us -> 7.51 us  [per_device(): lax.all_to_all(send_rows, ('table', 'batch'), split_axis=0, concat_axis=0...]
  transfers between devices with their start and end apart: 5 -> 9, of which waited for: 3 -> 4; matrix products, arithmetic and copies ran while one was open for 27% -> 30% of each run, Pallas kernels for 0% -> 0%
where the time goes in v1:
time: 119 us; the launch traced here: 118 us
  local copies, waits for them, and re-layouts  32.8 us (28%)
  starting transfers between devices  31.2 us (26%)
  matrix products  24 us (20%)
  waiting for transfers between devices  19.5 us (16%)
  other arithmetic  6.26 us (5%)
  blocking collectives  3.64 us (3%)
    gather x1, local copies, waits for them, and re-layouts, per_device(): item_table[lax.all_to_all(row_requests, 'table', split_axis=0, concat_axi...  20.3 us
    ppermute x5, waiting for transfers between devices, butterfly_sum(): value = value + lax.ppermute(value, name, pairs)  12.2 us
    gather x1, local copies, waits for them, and re-layouts, per_device(): context_table[context_flat].astype(jnp.float32)  9 us
    ppermute x5, starting transfers between devices, butterfly_sum(): value = value + lax.ppermute(value, name, pairs)  8.1 us
    dot_general x1, matrix products, per_device(): jnp.dot(placing, fetched.reshape(n_table * capacity, rank_width), preferr...  7.57 us
    all_to_all x1, starting transfers between devices, per_device(): lax.all_to_all(send_rows, ('table', 'batch'), split_axis=0, concat_axis=0...  7.51 us
    all_to_all x1, waiting for transfers between devices, per_device(): lax.all_to_all(send_rows, ('table', 'batch'), split_axis=0, concat_axis=0...  7.3 us
    dot_general x2, matrix products, place_integers(): lax.dot_general(stacked, placing, (((1,), (0,)), ((), ())), preferred_ele...  6.17 us
  transfers between devices with their start and end apart: 9, of which 4 were waited for; matrix products, arithmetic and copies ran while one was open for 30% of the time, Pallas kernels for 0%

profile of v1, /device:TPU:0, one launch (start us, length us, event | category | flops | bytes accessed | tf_op | source)
XLA Modules:
  0.0 118.4 jit_solution(11829603243904387996)
XLA Ops:
  0.0 0.5 broadcast.313
  0.5 1.5 %fusion.56 = (s32[32,64]{1,0:T(8,128)S(1)}, s32[32,64]{1,0:T(8,128)S(1)}) fusion(s32[32,64,1]{1,2,0:T(1,128)} %param.11, s32[]{:T(128)} %broadcast.313), kind=kLoop, calls=%fused_computation.126 | loop fusion | flops 2048 | bytes 24580 | tf_op args[3]
  2.1 0.1 mul.180
  2.1 0.1 eq.84
  2.2 1.1 reduce-window.6
  3.4 0.2 slice_reduce_fusion
  3.6 0.2 reduce-window.9
  3.8 0.1 select_reduce_fusion
  3.8 0.8 reshape.350
  4.7 6.0 %fusion.1 = f32[2,4096]{1,0:T(2,128)S(1)} fusion(s32[2048]{0:T(1024)S(1)} %bitcast_add_fusion, bf16[1,2048]{1,0:T(2,128)(2,1)S(1)} %fusion.40, bf16[1,2048]{1,0:T(2,128)(2,1)S(1)} %get-tuple-element.16), kind=kOutput, calls=%fused_computation.4 | convolution fusion | flops 41959424 | bytes 49152 | tf_op jit(solution)/shard_map/dot_general | solution.py:41
  10.7 0.6 fusion.29
  11.4 5.2 %all-to-all-start.1 = ((s32[4,1,1024]{2,1,0:T(1,128)}), s32[4,1,1024]{2,1,0:T(1,128)S(1)}, u32[]{:S(2)}, u32[]{:S(2)}) async-start(s32[4,1,1024]{2,1,0:T(1,128)} %bitcast.5), calls=%async_computation.1 | async-start | bytes 32768 | tf_op jit(solution)/shard_map/all_to_all | solution.py:111
  16.5 2.0 %fusion.12 = f32[256,256]{1,0:T(8,128)S(1)} fusion(bf16[16384,256]{1,0:T(8,128)(2,1)} %param.8, s32[]{:T(128)S(6)} %select_n.96), kind=kOutput, calls=%fused_computation.20 | convolution fusion | flops 268435456 | bytes 1310724 | tf_op jit(solution)/shard_map/dot_general | solution.py:15
  18.6 0.1 collective-permute-start
  18.7 0.2 reduce_window_sum.24
  19.0 0.1 convert_reduce_fusion.1
  19.1 0.2 fusion.35
  19.3 0.1 gt.35
  19.4 0.1 add.197
  19.5 0.6 broadcast_select_fusion
  20.1 0.1 reshape.352
  20.2 0.0 collective-permute-done
  20.2 2.1 %collective-permute-start.1 = (f32[256,256]{1,0:T(8,128)S(1)}, f32[256,256]{1,0:T(8,128)S(1)}, u32[]{:S(2)}, u32[]{:S(2)}) collective-permute-start(f32[256,256]{1,0:T(8,128)S(1)} %add.210), channel_id=1, source_target_pairs={{0,8},{8,0},{16,24},{24,16},{1,9},{9,1},{17,25},{25,17},{2,10},{10... | collective-permute-start | bytes 786440 | tf_op jit(solution)/shard_map/ppermute | solution.py:25
  22.3 5.9 %all-to-all-start = ((s32[16,2,1]{1,2,0:T(1,128)}), s32[16,2,1]{1,2,0:T(1,128)S(1)}, u32[]{:S(2)}, u32[]{:S(2)}) async-start(s32[16,2,1]{1,2,0:T(1,128)} %bitcast.2), calls=%async_computation | async-start | bytes 16384 | tf_op jit(solution)/shard_map/all_to_all | solution.py:142
  28.3 20.3 %gather_fusion = bf16[4096,256]{1,0:T(8,128)(2,1)} fusion(bf16[16384,256]{1,0:T(8,128)(2,1)} %param.8, s32[4096]{0:T(1024)S(1)} %broadcast_clamp_fusion), kind=kCustom, calls=%fused_computation | custom fusion | bytes 4210688 | tf_op jit(solution)/shard_map/gather | solution.py:111
  48.7 2.0 %collective-permute-start.2 = (f32[256,256]{1,0:T(8,128)S(1)}, f32[256,256]{1,0:T(8,128)S(1)}, u32[]{:S(2)}, u32[]{:S(2)}) collective-permute-start(f32[256,256]{1,0:T(8,128)S(1)} %add.211), channel_id=1, source_target_pairs={{0,16},{8,24},{16,0},{24,8},{1,17},{9,25},{17,1},{25,9},{2,18},{10... | collective-permute-start | bytes 786440 | tf_op jit(solution)/shard_map/ppermute | solution.py:25
  50.6 4.4 %all-to-all-start.2 = ((bf16[4,1024,256]{2,1,0:T(8,128)(2,1)}), bf16[4,1024,256]{2,1,0:T(8,128)(2,1)}, u32[]{:S(2)}, u32[]{:S(2)}) async-start(bf16[4,1024,256]{2,1,0:T(8,128)(2,1)} %bitcast.108), calls=%async_computation.2 | async-start | bytes 4194304 | tf_op jit(solution)/shard_map/all_to_all | solution.py:110
  55.1 0.0 copy-start.5
  55.2 9.0 %gather_fusion.1 = bf16[2048,256]{1,0:T(8,128)(2,1)} fusion(bf16[4096,256]{1,0:T(8,128)(2,1)S(1)} %copy-done, s32[2048]{0:T(1024)S(1)} %broadcast_clamp_fusion.1), kind=kCustom, calls=%fused_computation.1 | custom fusion | bytes 2105344 | tf_op jit(solution)/shard_map/gather | solution.py:120
  64.2 0.6 dynamic-slice
  65.4 1.2 %collective-permute-done.2 = f32[256,256]{1,0:T(8,128)S(1)} collective-permute-done((f32[256,256]{1,0:T(8,128)S(1)}, f32[256,256]{1,0:T(8,128)S(1)}, u32[]{:S(2)}, u32[]{:S(2)}) %collective-permute-start.2) | collective-permute-done | bytes 262176 | tf_op jit(solution)/shard_map/ppermute | solution.py:25
  66.7 1.5 %collective-permute-start.3 = (f32[256,256]{1,0:T(8,128)S(1)}, f32[256,256]{1,0:T(8,128)S(1)}, u32[]{:S(2)}, u32[]{:S(2)}) collective-permute-start(f32[256,256]{1,0:T(8,128)S(1)} %add.212), channel_id=1, source_target_pairs={{0,2},{2,0},{4,6},{6,4},{1,3},{3,1},{5,7},{7,5},{8,10},{10,8},{12,... | collective-permute-start | bytes 786440 | tf_op jit(solution)/shard_map/ppermute | solution.py:25
  68.2 0.7 fusion.58
  68.9 4.2 %collective-permute-done.3 = f32[256,256]{1,0:T(8,128)S(1)} collective-permute-done((f32[256,256]{1,0:T(8,128)S(1)}, f32[256,256]{1,0:T(8,128)S(1)}, u32[]{:S(2)}, u32[]{:S(2)}) %collective-permute-start.3) | collective-permute-done | bytes 262176 | tf_op jit(solution)/shard_map/ppermute | solution.py:25
  73.1 2.4 %collective-permute-start.4 = (f32[256,256]{1,0:T(8,128)S(1)}, f32[256,256]{1,0:T(8,128)S(1)}, u32[]{:S(2)}, u32[]{:S(2)}) collective-permute-start(f32[256,256]{1,0:T(8,128)S(1)} %add.213), channel_id=1, source_target_pairs={{0,4},{2,6},{4,0},{6,2},{1,5},{3,7},{5,1},{7,3},{8,12},{10,14},{12... | collective-permute-start | bytes 786440 | tf_op jit(solution)/shard_map/ppermute | solution.py:25
  75.6 0.7 reduce.18
  76.2 0.1 reshape.371
  76.3 0.2 dynamic-update-slice
  76.6 1.8 %all-reduce = s32[64]{0:T(128)S(1)} all-reduce(s32[64]{0:T(128)S(1)} %dynamic-update-slice), channel_id=1, replica_groups=mesh['table'=4,'batch'=4,'ctx'=2] {'ctx'}, use_global_device_ids=true, to_apply=%add | all-reduce | flops 64 | bytes 512
  78.4 0.1 convert_reduce_fusion
  78.5 6.8 %collective-permute-done.4 = f32[256,256]{1,0:T(8,128)S(1)} collective-permute-done((f32[256,256]{1,0:T(8,128)S(1)}, f32[256,256]{1,0:T(8,128)S(1)}, u32[]{:S(2)}, u32[]{:S(2)}) %collective-permute-start.4) | collective-permute-done | bytes 262176 | tf_op jit(solution)/shard_map/ppermute | solution.py:25
  85.3 0.1 multiply_multiply_fusion
  85.4 7.6 %fusion.5 = bf16[2048,256]{1,0:T(8,128)(2,1)S(1)} fusion(bf16[4096,256]{1,0:T(8,128)(2,1)} %bitcast.9, s32[2048]{0:T(1024)S(1)} %bitcast_add_fusion, bf16[2048,256]{1,0:T(8,128)(2,1)} %gather_fusion.1), kind=kOutput, calls=%fused_computation.8 | convolution fusion | flops 4304928768 | bytes 4202496 | tf_op jit(solution)/shard_map/dot_general | solution.py:117
  93.0 0.5 fusion.57
  93.5 0.9 fusion.24
  94.4 0.5 fusion.59
  95.0 0.3 multiply_reduce_fusion.3
  95.3 0.2 multiply_reduce_fusion.2
  95.5 0.1 fusion.19
  95.6 0.9 fusion.22
  96.6 0.0 copy-start.1
  96.6 0.5 fusion.60
  97.1 0.3 multiply_reduce_fusion.1
  97.5 0.2 multiply_reduce_fusion
  97.7 0.1 multiply_add_fusion
  97.7 0.9 fusion.20
  98.7 0.5 fusion.61
  99.2 0.3 fusion.11
  99.6 0.3 convolution_convert_fusion.1
  99.8 0.6 all_to_all.28
  100.5 7.5 %all-to-all-start.3 = ((bf16[16,2,256]{2,1,0:T(2,128)(2,1)}), bf16[16,2,256]{2,1,0:T(2,128)(2,1)S(1)}, u32[]{:S(2)}, u32[]{:S(2)}) async-start(bf16[16,2,256]{2,1,0:T(2,128)(2,1)} %all_to_all.28), calls=%async_computation.3 | async-start | bytes 32768 | tf_op jit(solution)/shard_map/all_to_all | solution.py:141
  108.0 7.3 %all-to-all-done.3 = bf16[16,2,256]{2,1,0:T(2,128)(2,1)S(1)} async-done(((bf16[16,2,256]{2,1,0:T(2,128)(2,1)}), bf16[16,2,256]{2,1,0:T(2,128)(2,1)S(1)}, u32[]{:S(2)}, u32[]{:S(2)}) %all-to-all-start.3) | async-done | bytes 16416 | tf_op jit(solution)/shard_map/all_to_all | solution.py:141
  115.3 1.8 %all_gather.7 = bf16[64,256]{1,0:T(8,128)(2,1)S(1)} all-gather(bf16[32,256]{1,0:T(8,128)(2,1)S(1)} %all_to_all.30), channel_id=1, replica_groups=mesh['table'=4,'batch'=4,'ctx'=2] {'ctx'}, dimensions={0}, use_global_device_ids=true | all-gather | bytes 49152 | tf_op jit(solution)/shard_map/all_gather | solution.py:145
  117.1 1.3 %fusion.6 = bf16[1024,256]{1,0:T(8,128)(2,1)} fusion(bf16[1024,256]{1,0:T(8,128)(2,1)S(1)} %copy-done.1, bf16[64,256]{1,0:T(8,128)(2,1)S(1)} %all_gather.7, pred[1024]{0:T(1024)(128)(4,1)S(1)} %broadcast_compare_fusion, s32[64]{0:T(128)S(1)} %all-reduce), kind=kOutput, calls=%fused_computation.10 | convolution fusion | flops 34144256 | bytes 1082624 | tf_op jit(solution)/shard_map/dot_general | solution.py:151
  (47 shorter events, 0.5 us)
Async XLA Ops:
  0.0 55.1 %copy-start = (bf16[4096,256]{1,0:T(8,128)(2,1)S(1)}, bf16[4096,256]{1,0:T(8,128)(2,1)}, u32[]{:S(2)}) copy-start(bf16[4096,256]{1,0:T(8,128)(2,1)} %param.9) | copy-start | bytes 6291460
  10.7 8.0 %copy-start.4 = (s32[32]{0:T(128)S(1)}, s32[32]{0:T(128)}, u32[]{:S(2)}) copy-start(s32[32]{0:T(128)} %param.15) | copy-start | bytes 388
  10.7 9.4 %copy-start.3 = (s32[32,64]{1,0:T(8,128)S(1)}, s32[32,64]{1,0:T(8,128)}, u32[]{:S(2)}) copy-start(s32[32,64]{1,0:T(8,128)} %param.13) | copy-start | bytes 24580
  11.4 10.9 %all-to-all-start.1 = ((s32[4,1,1024]{2,1,0:T(1,128)}), s32[4,1,1024]{2,1,0:T(1,128)S(1)}, u32[]{:S(2)}, u32[]{:S(2)}) async-start(s32[4,1,1024]{2,1,0:T(1,128)} %bitcast.5), calls=%async_computation.1 | async-start | bytes 32768 | tf_op jit(solution)/shard_map/all_to_all | solution.py:111
  18.6 1.6 %collective-permute-start = (f32[256,256]{1,0:T(8,128)S(1)}, f32[256,256]{1,0:T(8,128)S(1)}, u32[]{:S(2)}, u32[]{:S(2)}) collective-permute-start(f32[256,256]{1,0:T(8,128)S(1)} %fusion.12), channel_id=1, source_target_pairs={{0,1},{1,0},{2,3},{3,2},{4,5},{5,4},{6,7},{7,6},{8,9},{9,8},{10,11... | collective-permute-start | bytes 786440 | tf_op jit(solution)/shard_map/ppermute | solution.py:25
  20.2 28.4 %collective-permute-start.1 = (f32[256,256]{1,0:T(8,128)S(1)}, f32[256,256]{1,0:T(8,128)S(1)}, u32[]{:S(2)}, u32[]{:S(2)}) collective-permute-start(f32[256,256]{1,0:T(8,128)S(1)} %add.210), channel_id=1, source_target_pairs={{0,8},{8,0},{16,24},{24,16},{1,9},{9,1},{17,25},{25,17},{2,10},{10... | collective-permute-start | bytes 786440 | tf_op jit(solution)/shard_map/ppermute | solution.py:25
  22.3 28.3 %all-to-all-start = ((s32[16,2,1]{1,2,0:T(1,128)}), s32[16,2,1]{1,2,0:T(1,128)S(1)}, u32[]{:S(2)}, u32[]{:S(2)}) async-start(s32[16,2,1]{1,2,0:T(1,128)} %bitcast.2), calls=%async_computation | async-start | bytes 16384 | tf_op jit(solution)/shard_map/all_to_all | solution.py:142
  48.7 18.0 %collective-permute-start.2 = (f32[256,256]{1,0:T(8,128)S(1)}, f32[256,256]{1,0:T(8,128)S(1)}, u32[]{:S(2)}, u32[]{:S(2)}) collective-permute-start(f32[256,256]{1,0:T(8,128)S(1)} %add.211), channel_id=1, source_target_pairs={{0,16},{8,24},{16,0},{24,8},{1,17},{9,25},{17,1},{25,9},{2,18},{10... | collective-permute-start | bytes 786440 | tf_op jit(solution)/shard_map/ppermute | solution.py:25
  50.6 34.7 %all-to-all-start.2 = ((bf16[4,1024,256]{2,1,0:T(8,128)(2,1)}), bf16[4,1024,256]{2,1,0:T(8,128)(2,1)}, u32[]{:S(2)}, u32[]{:S(2)}) async-start(bf16[4,1024,256]{2,1,0:T(8,128)(2,1)} %bitcast.108), calls=%async_computation.2 | async-start | bytes 4194304 | tf_op jit(solution)/shard_map/all_to_all | solution.py:110
  55.1 9.0 %copy-start.5 = (u32[32]{0:T(128)S(1)}, u32[32]{0:T(128)}, u32[]{:S(2)}) copy-start(u32[32]{0:T(128)} %constant.125) | copy-start | bytes 388
  66.7 8.9 %copy-start.2 = (s32[32,64]{1,0:T(8,128)S(1)}, s32[32,64]{1,0:T(8,128)}, u32[]{:S(2)}) copy-start(s32[32,64]{1,0:T(8,128)} %param.14) | copy-start | bytes 24580
  66.7 6.4 %collective-permute-start.3 = (f32[256,256]{1,0:T(8,128)S(1)}, f32[256,256]{1,0:T(8,128)S(1)}, u32[]{:S(2)}, u32[]{:S(2)}) collective-permute-start(f32[256,256]{1,0:T(8,128)S(1)} %add.212), channel_id=1, source_target_pairs={{0,2},{2,0},{4,6},{6,4},{1,3},{3,1},{5,7},{7,5},{8,10},{10,8},{12,... | collective-permute-start | bytes 786440 | tf_op jit(solution)/shard_map/ppermute | solution.py:25
  73.1 12.2 %collective-permute-start.4 = (f32[256,256]{1,0:T(8,128)S(1)}, f32[256,256]{1,0:T(8,128)S(1)}, u32[]{:S(2)}, u32[]{:S(2)}) collective-permute-start(f32[256,256]{1,0:T(8,128)S(1)} %add.213), channel_id=1, source_target_pairs={{0,4},{2,6},{4,0},{6,2},{1,5},{3,7},{5,1},{7,3},{8,12},{10,14},{12... | collective-permute-start | bytes 786440 | tf_op jit(solution)/shard_map/ppermute | solution.py:25
  96.6 20.6 %copy-start.1 = (bf16[1024,256]{1,0:T(8,128)(2,1)S(1)}, bf16[1024,256]{1,0:T(8,128)(2,1)}, u32[]{:S(2)}) copy-start(bf16[1024,256]{1,0:T(8,128)(2,1)} %param.10) | copy-start | bytes 1572868
  100.5 14.8 %all-to-all-start.3 = ((bf16[16,2,256]{2,1,0:T(2,128)(2,1)}), bf16[16,2,256]{2,1,0:T(2,128)(2,1)S(1)}, u32[]{:S(2)}, u32[]{:S(2)}) async-start(bf16[16,2,256]{2,1,0:T(2,128)(2,1)} %all_to_all.28), calls=%async_computation.3 | async-start | bytes 32768 | tf_op jit(solution)/shard_map/all_to_all | solution.py:141

commit v2 on v1

--- a/solution.py
+++ b/solution.py
@@ -89,10 +89,9 @@
     n_table = lax.axis_size("table")
     n_batch = lax.axis_size("batch")
     n_ctx = lax.axis_size("ctx")
-    share = item_table.shape[0] // (n_batch * n_ctx)
-    part = lax.axis_index("batch") * n_ctx + lax.axis_index("ctx")
-    own_rows = lax.dynamic_slice_in_dim(item_table, part * share, share, axis=0)
-    item_gram = butterfly_sum(gram_of(own_rows), (("ctx", n_ctx), ("table", n_table), ("batch", n_batch)))
+    share = item_table.shape[0] // n_ctx
+    own_rows = lax.dynamic_slice_in_dim(item_table, lax.axis_index("ctx") * share, share, axis=0)
+    item_gram = butterfly_sum(gram_of(own_rows), (("ctx", n_ctx), ("table", n_table)))
     context_gram = gram_of(context_table)
     pair_count = item_table.shape[0] * n_table * context_table.shape[0]
     gram_matrix = item_gram * context_gram / pair_count
@@ -136,15 +135,18 @@
     ).astype(jnp.bfloat16)
     filled = jnp.sum(user_placing.astype(jnp.float32), axis=0)
     placed_ids = place_integers(local_rows, user_placing)
-    send_ids = jnp.where(filled > 0.5, placed_ids, user_rows)
-    got_rows, got_ids = (
-        lax.all_to_all(send_rows, ("table", "batch"), split_axis=0, concat_axis=0, tiled=True),
-        lax.all_to_all(send_ids, ("table", "batch"), split_axis=0, concat_axis=0, tiled=True),
-    )
-    all_rows, all_ids = (
-        lax.all_gather(got_rows, "ctx", axis=0, tiled=True),
-        lax.all_gather(got_ids, "ctx", axis=0, tiled=True),
-    )
+    send_ids = jnp.where(filled > 0.5, placed_ids, user_rows).astype(jnp.float32)
+    id_column = jnp.zeros((owner_count * user_capacity, 128), jnp.float32).at[:, 0].set(send_ids)
+    payload = jnp.concatenate([send_rows.astype(jnp.float32), id_column], axis=1)
+    payload = payload.reshape(owner_count, 1, user_capacity, rank_width + 128)
+    n_ctx = lax.axis_size("ctx")
+    payload = jnp.broadcast_to(
+        payload, (owner_count, n_ctx, user_capacity, rank_width + 128)
+    ).reshape(owner_count * n_ctx, user_capacity, rank_width + 128)
+    got = lax.all_to_all(payload, ("table", "batch", "ctx"), split_axis=0, concat_axis=0, tiled=True)
+    got = got.reshape(owner_count * n_ctx * user_capacity, rank_width + 128)
+    all_rows = got[:, :rank_width].astype(jnp.bfloat16)
+    all_ids = got[:, rank_width].astype(jnp.int32)
     hitting = (jnp.arange(user_rows, dtype=jnp.int32)[:, None] == all_ids[None, :]).astype(
         jnp.bfloat16
     )

time: 119 us -> 120 us (level)
  starting transfers between devices: 31.2 us -> 13.6 us
  waiting for transfers between devices: 19.5 us -> 29.2 us
  blocking collectives: 3.64 us -> 11.5 us
  matrix products: 24 us -> 26.7 us
  local copies, waits for them, and re-layouts: 32.8 us -> 31.4 us
    ppermute x5 -> x3, waiting for transfers between devices: 12.2 us -> 29.2 us  [butterfly_sum(): value = value + lax.ppermute(value, name, pairs)]
    all_to_all x2 -> x0, starting transfers between devices: 13.5 us -> none  [the longest x1 7.51 us: per_device(): lax.all_to_all(send_rows, ('table', 'batch'), split_axis=0, concat_axis=0...]
    all_to_all x0 -> x1, blocking collectives: none -> 11.5 us  [per_device(): lax.all_to_all(payload, ('table', 'batch', 'ctx'), split_axis=0, concat_a...]
    all_to_all x2 -> x0, waiting for transfers between devices: 7.3 us -> none  [the longest x1 7.3 us: per_device(): lax.all_to_all(send_rows, ('table', 'batch'), split_axis=0, concat_axis=0...]
    ppermute x5 -> x3, starting transfers between devices: 8.1 us -> 3.7 us  [butterfly_sum(): value = value + lax.ppermute(value, name, pairs)]
    dot_general x2, matrix products: 2.79 us -> 5.49 us  [gram_of(): lax.dot_general(table_rows, table_rows, (((0,), (0,)), ((), ())), preferr...]
    all_gather x1 -> x0, blocking collectives: 1.83 us -> none  [per_device(): lax.all_gather(got_rows, 'ctx', axis=0, tiled=True)]
    unnamed x1 -> x0, blocking collectives: 1.81 us -> none
  transfers between devices with their start and end apart: 9 -> 5, of which waited for: 4 -> 1; matrix products, arithmetic and copies ran while one was open for 30% -> 31% of each run, Pallas kernels for 0% -> 0%
where the time goes in v2:
time: 120 us; the launch traced here: 119 us
  local copies, waits for them, and re-layouts  31.4 us (26%)
  waiting for transfers between devices  29.2 us (24%)
  matrix products  26.7 us (22%)
  starting transfers between devices  13.6 us (11%)
  blocking collectives  11.5 us (10%)
  other arithmetic  6.35 us (5%)
    ppermute x3, waiting for transfers between devices, butterfly_sum(): value = value + lax.ppermute(value, name, pairs)  29.2 us
    gather x1, local copies, waits for them, and re-layouts, per_device(): item_table[lax.all_to_all(row_requests, 'table', split_axis=0, concat_axi...  20.3 us
    all_to_all x1, blocking collectives, per_device(): lax.all_to_all(payload, ('table', 'batch', 'ctx'), split_axis=0, concat_a...  11.5 us
    gather x1, local copies, waits for them, and re-layouts, per_device(): context_table[context_flat].astype(jnp.float32)  8.99 us
    dot_general x1, matrix products, per_device(): jnp.dot(placing, fetched.reshape(n_table * capacity, rank_width), preferr...  7.57 us
    dot_general x2, matrix products, place_integers(): lax.dot_general(stacked, placing, (((1,), (0,)), ((), ())), preferred_ele...  6.17 us
    dot_general x2, matrix products, gram_of(): lax.dot_general(table_rows, table_rows, (((0,), (0,)), ((), ())), preferr...  5.49 us
    all_to_all x1, starting transfers between devices, per_device(): lax.all_to_all(row_requests, 'table', split_axis=0, concat_axis=0, tiled=...  5.16 us
  transfers between devices with their start and end apart: 5, of which 1 were waited for; matrix products, arithmetic and copies ran while one was open for 31% of the time, Pallas kernels for 0%

profile of v2, /device:TPU:0, one launch (start us, length us, event | category | flops | bytes accessed | tf_op | source)
XLA Modules:
  0.0 119.2 jit_solution(912379103641141961)
XLA Ops:
  0.0 0.0 copy-start
  0.0 0.5 broadcast.351
  0.5 1.6 %fusion.58 = (s32[32,64]{1,0:T(8,128)S(1)}, s32[32,64]{1,0:T(8,128)S(1)}) fusion(s32[32,64,1]{1,2,0:T(1,128)} %param.13, s32[]{:T(128)} %broadcast.351), kind=kLoop, calls=%fused_computation.133 | loop fusion | flops 2048 | bytes 24580 | tf_op args[3]
  2.1 0.1 eq.82
  2.2 1.1 reduce-window.6
  3.3 0.2 slice_reduce_fusion
  3.5 0.2 reduce-window.9
  3.7 0.1 select_reduce_fusion
  3.8 0.1 mul.174
  3.9 0.8 reshape.375
  4.8 6.0 %fusion.1 = f32[2,4096]{1,0:T(2,128)S(1)} fusion(s32[2048]{0:T(1024)S(1)} %bitcast_add_fusion, bf16[1,2048]{1,0:T(2,128)(2,1)S(1)} %fusion.42, bf16[1,2048]{1,0:T(2,128)(2,1)S(1)} %get-tuple-element.25), kind=kOutput, calls=%fused_computation.4 | convolution fusion | flops 41959424 | bytes 49152 | tf_op jit(solution)/shard_map/dot_general | solution.py:41
  10.7 0.6 fusion.31
  11.4 5.2 %all-to-all-start = ((s32[4,1,1024]{2,1,0:T(1,128)}), s32[4,1,1024]{2,1,0:T(1,128)S(1)}, u32[]{:S(2)}, u32[]{:S(2)}) async-start(s32[4,1,1024]{2,1,0:T(1,128)} %bitcast.1), calls=%async_computation | async-start | bytes 32768 | tf_op jit(solution)/shard_map/all_to_all | solution.py:110
  16.6 0.0 copy-start.3
  16.6 4.8 %fusion.4 = f32[256,256]{1,0:T(8,128)S(1)} fusion(bf16[16384,256]{1,0:T(8,128)(2,1)} %param.10, s32[]{:T(128)S(6)} %select_n.90), kind=kOutput, calls=%fused_computation.7 | convolution fusion | flops 1073741824 | bytes 4456452 | tf_op jit(solution)/shard_map/dot_general | solution.py:15
  21.3 0.1 collective-permute-start
  21.4 0.0 copy-done.3
  21.4 0.1 reshape.377
  21.5 0.0 copy-done
  21.5 0.0 copy-start.4
  21.5 0.7 fusion.60
  22.3 0.0 copy-done.4
  22.3 0.2 reduce_window_sum.24
  22.6 0.0 all-to-all-done
  22.6 20.3 %gather_fusion = bf16[4096,256]{1,0:T(8,128)(2,1)} fusion(bf16[16384,256]{1,0:T(8,128)(2,1)} %param.10, s32[4096]{0:T(1024)S(1)} %broadcast_clamp_fusion), kind=kCustom, calls=%fused_computation | custom fusion | bytes 4210688 | tf_op jit(solution)/shard_map/gather | solution.py:110
  42.9 4.8 %all-to-all-start.1 = ((bf16[4,1024,256]{2,1,0:T(8,128)(2,1)}), bf16[4,1024,256]{2,1,0:T(8,128)(2,1)}, u32[]{:S(2)}, u32[]{:S(2)}) async-start(bf16[4,1024,256]{2,1,0:T(8,128)(2,1)} %bitcast.109), calls=%async_computation.1 | async-start | bytes 4194304 | tf_op jit(solution)/shard_map/all_to_all | solution.py:109
  47.7 0.2 fusion.37
  47.9 0.0 collective-permute-done
  47.9 2.1 %collective-permute-start.1 = (f32[256,256]{1,0:T(8,128)S(1)}, f32[256,256]{1,0:T(8,128)S(1)}, u32[]{:S(2)}, u32[]{:S(2)}) collective-permute-start(f32[256,256]{1,0:T(8,128)S(1)} %add.198), channel_id=1, source_target_pairs={{0,8},{8,0},{16,24},{24,16},{1,9},{9,1},{17,25},{25,17},{2,10},{10... | collective-permute-start | bytes 786440 | tf_op jit(solution)/shard_map/ppermute | solution.py:25
  50.0 0.1 convert_reduce_fusion.1
  50.1 0.0 copy-done.2
  50.1 29.2 %collective-permute-done.1 = f32[256,256]{1,0:T(8,128)S(1)} collective-permute-done((f32[256,256]{1,0:T(8,128)S(1)}, f32[256,256]{1,0:T(8,128)S(1)}, u32[]{:S(2)}, u32[]{:S(2)}) %collective-permute-start.1) | collective-permute-done | bytes 262176 | tf_op jit(solution)/shard_map/ppermute | solution.py:25
  79.4 1.5 %collective-permute-start.2 = (f32[256,256]{1,0:T(8,128)S(1)}, f32[256,256]{1,0:T(8,128)S(1)}, u32[]{:S(2)}, u32[]{:S(2)}) collective-permute-start(f32[256,256]{1,0:T(8,128)S(1)} %add.199), channel_id=1, source_target_pairs={{0,16},{8,24},{16,0},{24,8},{1,17},{9,25},{17,1},{25,9},{2,18},{10... | collective-permute-start | bytes 786440 | tf_op jit(solution)/shard_map/ppermute | solution.py:25
  80.9 9.0 %gather_fusion.1 = bf16[2048,256]{1,0:T(8,128)(2,1)} fusion(bf16[4096,256]{1,0:T(8,128)(2,1)S(1)} %copy-done, s32[2048]{0:T(1024)S(1)} %broadcast_clamp_fusion.1), kind=kCustom, calls=%fused_computation.1 | custom fusion | bytes 2105344 | tf_op jit(solution)/shard_map/gather | solution.py:119
  89.9 0.1 copy.21
  90.0 0.1 copy.20
  90.1 0.6 compare_reduce_fusion
  90.7 0.7 convert_select_fusion
  91.4 0.0 collective-permute-done.2
  91.4 0.1 multiply_multiply_fusion
  91.5 0.0 all-to-all-done.1
  91.5 7.6 %fusion.7 = bf16[2048,256]{1,0:T(8,128)(2,1)S(1)} fusion(bf16[4096,256]{1,0:T(8,128)(2,1)} %bitcast.5, s32[2048]{0:T(1024)S(1)} %bitcast_add_fusion, bf16[2048,256]{1,0:T(8,128)(2,1)} %gather_fusion.1), kind=kOutput, calls=%fused_computation.10 | convolution fusion | flops 4304928768 | bytes 4202496 | tf_op jit(solution)/shard_map/dot_general | solution.py:116
  99.1 0.5 fusion.59
  99.6 0.9 fusion.26
  100.5 0.5 fusion.61
  101.1 0.3 multiply_reduce_fusion.3
  101.4 0.2 multiply_reduce_fusion.2
  101.6 0.1 fusion.21
  101.7 0.9 fusion.24
  102.7 0.5 fusion.62
  103.2 0.0 copy-start.1
  103.2 0.3 multiply_reduce_fusion.1
  103.6 0.2 multiply_reduce_fusion
  103.8 0.1 multiply_add_fusion
  103.8 0.9 fusion.22
  104.8 0.5 fusion.63
  105.3 0.3 fusion.14
  105.7 0.3 fusion.13
  106.0 11.5 %all_to_all.19 = f32[32,2,384]{2,1,0:T(2,128)S(1)} all-to-all(f32[32,2,384]{2,1,0:T(2,128)S(1)} %bitcast.110), channel_id=1, replica_groups=mesh['table'=4,'batch'=4,'ctx'=2] {'table','batch','ctx'}, dimensions={0} | all-to-all | bytes 196608 | tf_op jit(solution)/shard_map/all_to_all | solution.py:146
  117.6 0.1 reshape.380
  117.6 0.1 fusion.17
  117.8 0.1 convert_reduce_fusion
  117.9 0.0 copy-done.1
  117.9 1.3 %fusion.8 = bf16[1024,256]{1,0:T(8,128)(2,1)} fusion(bf16[1024,256]{1,0:T(8,128)(2,1)S(1)} %copy-done.1, pred[1024]{0:T(1024)(128)(4,1)S(1)} %broadcast_compare_fusion, s32[64]{0:T(128)S(1)} %fusion.17, f32[64,384]{1,0:T(8,128)S(1)} %reshape.380), kind=kOutput, calls=%fused_computation.12 | convolution fusion | flops 34144256 | bytes 1082880 | tf_op jit(solution)/shard_map/dot_general | solution.py:153
  (33 shorter events, 0.4 us)
Async XLA Ops:
  0.0 21.5 %copy-start = (bf16[4096,256]{1,0:T(8,128)(2,1)S(1)}, bf16[4096,256]{1,0:T(8,128)(2,1)}, u32[]{:S(2)}) copy-start(bf16[4096,256]{1,0:T(8,128)(2,1)} %param.11) | copy-start | bytes 6291460
  11.4 11.2 %all-to-all-start = ((s32[4,1,1024]{2,1,0:T(1,128)}), s32[4,1,1024]{2,1,0:T(1,128)S(1)}, u32[]{:S(2)}, u32[]{:S(2)}) async-start(s32[4,1,1024]{2,1,0:T(1,128)} %bitcast.1), calls=%async_computation | async-start | bytes 32768 | tf_op jit(solution)/shard_map/all_to_all | solution.py:110
  16.6 4.8 %copy-start.3 = (s32[32,64]{1,0:T(8,128)S(1)}, s32[32,64]{1,0:T(8,128)}, u32[]{:S(2)}) copy-start(s32[32,64]{1,0:T(8,128)} %param.15) | copy-start | bytes 24580
  21.3 26.6 %collective-permute-start = (f32[256,256]{1,0:T(8,128)S(1)}, f32[256,256]{1,0:T(8,128)S(1)}, u32[]{:S(2)}, u32[]{:S(2)}) collective-permute-start(f32[256,256]{1,0:T(8,128)S(1)} %fusion.4), channel_id=1, source_target_pairs={{0,1},{1,0},{2,3},{3,2},{4,5},{5,4},{6,7},{7,6},{8,9},{9,8},{10,11... | collective-permute-start | bytes 786440 | tf_op jit(solution)/shard_map/ppermute | solution.py:25
  21.5 0.8 copy-start.4
  42.9 7.2 %copy-start.2 = (s32[32,64]{1,0:T(8,128)S(1)}, s32[32,64]{1,0:T(8,128)}, u32[]{:S(2)}) copy-start(s32[32,64]{1,0:T(8,128)} %param.16) | copy-start | bytes 24580
  42.9 48.6 %all-to-all-start.1 = ((bf16[4,1024,256]{2,1,0:T(8,128)(2,1)}), bf16[4,1024,256]{2,1,0:T(8,128)(2,1)}, u32[]{:S(2)}, u32[]{:S(2)}) async-start(bf16[4,1024,256]{2,1,0:T(8,128)(2,1)} %bitcast.109), calls=%async_computation.1 | async-start | bytes 4194304 | tf_op jit(solution)/shard_map/all_to_all | solution.py:109
  47.9 31.4 %collective-permute-start.1 = (f32[256,256]{1,0:T(8,128)S(1)}, f32[256,256]{1,0:T(8,128)S(1)}, u32[]{:S(2)}, u32[]{:S(2)}) collective-permute-start(f32[256,256]{1,0:T(8,128)S(1)} %add.198), channel_id=1, source_target_pairs={{0,8},{8,0},{16,24},{24,16},{1,9},{9,1},{17,25},{25,17},{2,10},{10... | collective-permute-start | bytes 786440 | tf_op jit(solution)/shard_map/ppermute | solution.py:25
  79.4 12.0 %collective-permute-start.2 = (f32[256,256]{1,0:T(8,128)S(1)}, f32[256,256]{1,0:T(8,128)S(1)}, u32[]{:S(2)}, u32[]{:S(2)}) collective-permute-start(f32[256,256]{1,0:T(8,128)S(1)} %add.199), channel_id=1, source_target_pairs={{0,16},{8,24},{16,0},{24,8},{1,17},{9,25},{17,1},{25,9},{2,18},{10... | collective-permute-start | bytes 786440 | tf_op jit(solution)/shard_map/ppermute | solution.py:25
  103.2 14.7 %copy-start.1 = (bf16[1024,256]{1,0:T(8,128)(2,1)S(1)}, bf16[1024,256]{1,0:T(8,128)(2,1)}, u32[]{:S(2)}) copy-start(bf16[1024,256]{1,0:T(8,128)(2,1)} %param.12) | copy-start | bytes 1572868

commit v3 on v2

--- a/solution.py
+++ b/solution.py
@@ -106,8 +106,10 @@
     )
     row_requests = place_integers(item_row.reshape(flat_count), placing).reshape(n_table, capacity)
     context_flat = context_id.reshape(flat_count)
+    served = item_table[lax.all_to_all(row_requests, "table", split_axis=0, concat_axis=0, tiled=True)]
+    served, gram_matrix = lax.optimization_barrier((served, gram_matrix))
     fetched = lax.all_to_all(
-        item_table[lax.all_to_all(row_requests, "table", split_axis=0, concat_axis=0, tiled=True)],
+        served,
         "table",
         split_axis=0,
         concat_axis=0,

time: 120 us -> 110 us (0.917)
  waiting for transfers between devices: 29.2 us -> 19.3 us
    ppermute x3, waiting for transfers between devices: 29.2 us -> 6.42 us  [butterfly_sum(): value = value + lax.ppermute(value, name, pairs)]
    all_to_all x1, waiting for transfers between devices: 0.01 us -> 12.9 us  [per_device(): lax.all_to_all(served, 'table', split_axis=0, concat_axis=0, tiled=True)]
  transfers between devices with their start and end apart: 5 -> 5, of which waited for: 1 -> 2; matrix products, arithmetic and copies ran while one was open for 31% -> 38% of each run, Pallas kernels for 0% -> 0%
where the time goes in v3:
time: 110 us
  local copies, waits for them, and re-layouts  30.7 us (28%)
  matrix products  27.8 us (25%)
  waiting for transfers between devices  19.3 us (18%)
  starting transfers between devices  13.8 us (13%)
  blocking collectives  12.5 us (11%)
  other arithmetic  5.52 us (5%)
    gather x1, local copies, waits for them, and re-layouts, per_device(): item_table[lax.all_to_all(row_requests, 'table', split_axis=0, concat_axi...  20.3 us
    all_to_all x1, waiting for transfers between devices, per_device(): lax.all_to_all(served, 'table', split_axis=0, concat_axis=0, tiled=True)  12.9 us
    all_to_all x1, blocking collectives, per_device(): lax.all_to_all(payload, ('table', 'batch', 'ctx'), split_axis=0, concat_a...  12.5 us
    gather x1, local copies, waits for them, and re-layouts, per_device(): context_table[context_flat].astype(jnp.float32)  9 us
    dot_general x1, matrix products, per_device(): jnp.dot(placing, fetched.reshape(n_table * capacity, rank_width), preferr...  7.56 us
    ppermute x3, waiting for transfers between devices, butterfly_sum(): value = value + lax.ppermute(value, name, pairs)  6.42 us
    dot_general x2, matrix products, place_integers(): lax.dot_general(stacked, placing, (((1,), (0,)), ((), ())), preferred_ele...  6.18 us
    dot_general x2, matrix products, gram_of(): lax.dot_general(table_rows, table_rows, (((0,), (0,)), ((), ())), preferr...  5.61 us
  transfers between devices with their start and end apart: 5, of which 2 were waited for; matrix products, arithmetic and copies ran while one was open for 38% of the time, Pallas kernels for 0%

profile of v3, /device:TPU:0, one launch (start us, length us, event | category | flops | bytes accessed | tf_op | source)
XLA Modules:
  0.0 109.8 jit_solution(3880164660026762154)
XLA Ops:
  0.0 0.0 copy-start
  0.0 4.9 %fusion.4 = f32[256,256]{1,0:T(8,128)S(1)} fusion(bf16[16384,256]{1,0:T(8,128)(2,1)} %param.10, s32[]{:T(128)S(6)} %select_n.88), kind=kOutput, calls=%fused_computation.7 | convolution fusion | flops 1073741824 | bytes 4456452 | tf_op jit(solution)/shard_map/dot_general | solution.py:15
  4.9 0.5 collective-permute-start
  5.4 0.5 broadcast.351
  5.9 0.0 copy-done.2
  5.9 0.7 fusion.58
  6.7 0.1 eq.82
  6.7 1.1 %reduce-window.6 = s32[4,16,128]{2,1,0:T(8,128)S(1)} reduce-window(s32[4,16,128]{2,1,0:T(8,128)S(1)} %fusion.28, s32[]{:T(128)} %constant.122.clone.1), window={size=1x1x128 pad=0_0x0_0x127_0}, to_apply=%region_2.3 | reduce-window | flops 1040384 | bytes 65540 | tf_op jit(solution)/shard_map/reduce-window
  7.9 0.2 slice_reduce_fusion
  8.1 0.2 reduce-window.9
  8.3 0.1 select_reduce_fusion
  8.4 0.1 mul.174
  8.4 0.0 copy-done.3
  8.4 0.1 reshape.375
  8.5 0.1 fusion.49
  8.6 6.0 %fusion.1 = f32[2,4096]{1,0:T(2,128)S(1)} fusion(s32[2048]{0:T(1024)S(1)} %bitcast_add_fusion, bf16[1,2048]{1,0:T(2,128)(2,1)S(1)} %fusion.42, bf16[1,2048]{1,0:T(2,128)(2,1)S(1)} %get-tuple-element.29), kind=kOutput, calls=%fused_computation.4 | convolution fusion | flops 41959424 | bytes 49152 | tf_op jit(solution)/shard_map/dot_general | solution.py:41
  14.6 0.6 fusion.31
  15.3 4.7 %all-to-all-start = ((s32[4,1,1024]{2,1,0:T(1,128)}), s32[4,1,1024]{2,1,0:T(1,128)S(1)}, u32[]{:S(2)}, u32[]{:S(2)}) async-start(s32[4,1,1024]{2,1,0:T(1,128)} %bitcast.1), calls=%async_computation | async-start | bytes 32768 | tf_op jit(solution)/shard_map/all_to_all | solution.py:109
  20.0 0.0 copy-done
  20.0 0.7 fusion.59
  20.7 0.0 copy-done.4
  20.8 0.1 reshape.377
  20.9 0.0 copy-done.5
  20.9 0.0 collective-permute-done
  21.0 2.1 %collective-permute-start.1 = (f32[256,256]{1,0:T(8,128)S(1)}, f32[256,256]{1,0:T(8,128)S(1)}, u32[]{:S(2)}, u32[]{:S(2)}) collective-permute-start(f32[256,256]{1,0:T(8,128)S(1)} %add.194), channel_id=1, source_target_pairs={{0,8},{8,0},{16,24},{24,16},{1,9},{9,1},{17,25},{25,17},{2,10},{10... | collective-permute-start | bytes 786440 | tf_op jit(solution)/shard_map/ppermute | solution.py:25
  23.1 6.4 %collective-permute-done.1 = f32[256,256]{1,0:T(8,128)S(1)} collective-permute-done((f32[256,256]{1,0:T(8,128)S(1)}, f32[256,256]{1,0:T(8,128)S(1)}, u32[]{:S(2)}, u32[]{:S(2)}) %collective-permute-start.1) | collective-permute-done | bytes 262176 | tf_op jit(solution)/shard_map/ppermute | solution.py:25
  29.5 1.8 %collective-permute-start.2 = (f32[256,256]{1,0:T(8,128)S(1)}, f32[256,256]{1,0:T(8,128)S(1)}, u32[]{:S(2)}, u32[]{:S(2)}) collective-permute-start(f32[256,256]{1,0:T(8,128)S(1)} %add.195), channel_id=1, source_target_pairs={{0,16},{8,24},{16,0},{24,8},{1,17},{9,25},{17,1},{25,9},{2,18},{10... | collective-permute-start | bytes 786440 | tf_op jit(solution)/shard_map/ppermute | solution.py:25
  31.3 0.0 all-to-all-done
  31.3 20.3 %gather_fusion = bf16[4096,256]{1,0:T(8,128)(2,1)} fusion(bf16[16384,256]{1,0:T(8,128)(2,1)} %param.10, s32[4096]{0:T(1024)S(1)} %broadcast_clamp_fusion), kind=kCustom, calls=%fused_computation | custom fusion | bytes 4210688 | tf_op jit(solution)/shard_map/gather | solution.py:109
  51.6 0.0 collective-permute-done.2
  51.6 0.1 multiply_multiply_fusion
  51.7 4.6 %all-to-all-start.1 = ((bf16[4,1024,256]{2,1,0:T(8,128)(2,1)}), bf16[4,1024,256]{2,1,0:T(8,128)(2,1)}, u32[]{:S(2)}, u32[]{:S(2)}) async-start(bf16[4,1024,256]{2,1,0:T(8,128)(2,1)} %bitcast.109), calls=%async_computation.1 | async-start | bytes 4194304 | tf_op jit(solution)/shard_map/all_to_all | solution.py:111
  56.3 0.0 copy-start.1
  56.3 9.0 %gather_fusion.1 = bf16[2048,256]{1,0:T(8,128)(2,1)} fusion(bf16[4096,256]{1,0:T(8,128)(2,1)S(1)} %copy-done, s32[2048]{0:T(1024)S(1)} %broadcast_clamp_fusion.1), kind=kCustom, calls=%fused_computation.1 | custom fusion | bytes 2105344 | tf_op jit(solution)/shard_map/gather | solution.py:121
  65.3 0.2 reduce_window_sum.24
  65.6 0.2 fusion.37
  65.8 0.1 copy.21
  65.9 0.1 convert_reduce_fusion.1
  66.0 0.1 copy.20
  66.1 0.6 compare_reduce_fusion
  66.7 0.0 copy-done.1
  66.7 0.7 convert_select_fusion
  67.4 12.9 %all-to-all-done.1 = bf16[4,1024,256]{2,1,0:T(8,128)(2,1)} async-done(((bf16[4,1024,256]{2,1,0:T(8,128)(2,1)}), bf16[4,1024,256]{2,1,0:T(8,128)(2,1)}, u32[]{:S(2)}, u32[]{:S(2)}) %all-to-all-start.1) | async-done | bytes 2097184 | tf_op jit(solution)/shard_map/all_to_all | solution.py:111
  80.3 7.6 %fusion.7 = bf16[2048,256]{1,0:T(8,128)(2,1)S(1)} fusion(bf16[4096,256]{1,0:T(8,128)(2,1)} %bitcast.5, s32[2048]{0:T(1024)S(1)} %bitcast_add_fusion, bf16[2048,256]{1,0:T(8,128)(2,1)} %gather_fusion.1), kind=kOutput, calls=%fused_computation.10 | convolution fusion | flops 4304928768 | bytes 4202496 | tf_op jit(solution)/shard_map/dot_general | solution.py:118
  87.9 0.5 fusion.60
  88.4 0.9 fusion.26
  89.3 0.5 fusion.61
  89.9 0.3 multiply_reduce_fusion.3
  90.2 0.2 multiply_reduce_fusion.2
  90.4 0.1 fusion.21
  90.5 0.9 fusion.24
  91.4 0.5 fusion.62
  92.0 0.3 multiply_reduce_fusion.1
  92.3 0.2 multiply_reduce_fusion
  92.5 0.1 multiply_add_fusion
  92.6 0.9 fusion.22
  93.5 0.5 fusion.63
  94.1 0.3 fusion.14
  94.4 0.3 fusion.13
  94.8 12.5 %all_to_all.19 = f32[32,2,384]{2,1,0:T(2,128)S(1)} all-to-all(f32[32,2,384]{2,1,0:T(2,128)S(1)} %bitcast.110), channel_id=1, replica_groups=mesh['table'=4,'batch'=4,'ctx'=2] {'table','batch','ctx'}, dimensions={0} | all-to-all | bytes 196608 | tf_op jit(solution)/shard_map/all_to_all | solution.py:148
  107.2 0.1 reshape.380
  107.3 0.1 fusion.17
  107.4 0.1 convert_reduce_fusion
  107.5 2.3 %fusion.8 = bf16[1024,256]{1,0:T(8,128)(2,1)} fusion(bf16[1024,256]{1,0:T(8,128)(2,1)} %param.12, pred[1024]{0:T(1024)(128)(4,1)S(1)} %broadcast_compare_fusion, s32[64]{0:T(128)S(1)} %fusion.17, f32[64,384]{1,0:T(8,128)S(1)} %reshape.380), kind=kOutput, calls=%fused_computation.12 | convolution fusion | flops 34144256 | bytes 1082880 | tf_op jit(solution)/shard_map/dot_general | solution.py:155
  (35 shorter events, 0.4 us)
Async XLA Ops:
  0.0 20.0 %copy-start = (bf16[4096,256]{1,0:T(8,128)(2,1)S(1)}, bf16[4096,256]{1,0:T(8,128)(2,1)}, u32[]{:S(2)}) copy-start(bf16[4096,256]{1,0:T(8,128)(2,1)} %param.11) | copy-start | bytes 6291460
  0.0 5.9 %copy-start.2 = (s32[32,64,1]{1,2,0:T(1,128)S(1)}, s32[32,64,1]{1,2,0:T(1,128)}, u32[]{:S(2)}) copy-start(s32[32,64,1]{1,2,0:T(1,128)} %param.13) | copy-start | bytes 24580
  0.0 8.4 %copy-start.3 = (s32[32,64]{1,0:T(8,128)S(1)}, s32[32,64]{1,0:T(8,128)}, u32[]{:S(2)}) copy-start(s32[32,64]{1,0:T(8,128)} %param.14) | copy-start | bytes 24580
  4.9 16.0 %collective-permute-start = (f32[256,256]{1,0:T(8,128)S(1)}, f32[256,256]{1,0:T(8,128)S(1)}, u32[]{:S(2)}, u32[]{:S(2)}) collective-permute-start(f32[256,256]{1,0:T(8,128)S(1)} %fusion.4), channel_id=1, source_target_pairs={{0,1},{1,0},{2,3},{3,2},{4,5},{5,4},{6,7},{7,6},{8,9},{9,8},{10,11... | collective-permute-start | bytes 786440 | tf_op jit(solution)/shard_map/ppermute | solution.py:25
  15.3 16.0 %all-to-all-start = ((s32[4,1,1024]{2,1,0:T(1,128)}), s32[4,1,1024]{2,1,0:T(1,128)S(1)}, u32[]{:S(2)}, u32[]{:S(2)}) async-start(s32[4,1,1024]{2,1,0:T(1,128)} %bitcast.1), calls=%async_computation | async-start | bytes 32768 | tf_op jit(solution)/shard_map/all_to_all | solution.py:109
  20.0 0.8 copy-start.4
  20.0 0.9 copy-start.5
  21.0 8.5 %collective-permute-start.1 = (f32[256,256]{1,0:T(8,128)S(1)}, f32[256,256]{1,0:T(8,128)S(1)}, u32[]{:S(2)}, u32[]{:S(2)}) collective-permute-start(f32[256,256]{1,0:T(8,128)S(1)} %add.194), channel_id=1, source_target_pairs={{0,8},{8,0},{16,24},{24,16},{1,9},{9,1},{17,25},{25,17},{2,10},{10... | collective-permute-start | bytes 786440 | tf_op jit(solution)/shard_map/ppermute | solution.py:25
  29.5 22.1 %collective-permute-start.2 = (f32[256,256]{1,0:T(8,128)S(1)}, f32[256,256]{1,0:T(8,128)S(1)}, u32[]{:S(2)}, u32[]{:S(2)}) collective-permute-start(f32[256,256]{1,0:T(8,128)S(1)} %add.195), channel_id=1, source_target_pairs={{0,16},{8,24},{16,0},{24,8},{1,17},{9,25},{17,1},{25,9},{2,18},{10... | collective-permute-start | bytes 786440 | tf_op jit(solution)/shard_map/ppermute | solution.py:25
  51.7 28.6 %all-to-all-start.1 = ((bf16[4,1024,256]{2,1,0:T(8,128)(2,1)}), bf16[4,1024,256]{2,1,0:T(8,128)(2,1)}, u32[]{:S(2)}, u32[]{:S(2)}) async-start(bf16[4,1024,256]{2,1,0:T(8,128)(2,1)} %bitcast.109), calls=%async_computation.1 | async-start | bytes 4194304 | tf_op jit(solution)/shard_map/all_to_all | solution.py:111
  56.3 10.4 %copy-start.1 = (s32[32,64]{1,0:T(8,128)S(1)}, s32[32,64]{1,0:T(8,128)}, u32[]{:S(2)}) copy-start(s32[32,64]{1,0:T(8,128)} %param.16) | copy-start | bytes 24580

commit v4 on v2

--- a/solution.py
+++ b/solution.py
@@ -106,16 +106,22 @@
     )
     row_requests = place_integers(item_row.reshape(flat_count), placing).reshape(n_table, capacity)
     context_flat = context_id.reshape(flat_count)
-    fetched = lax.all_to_all(
-        item_table[lax.all_to_all(row_requests, "table", split_axis=0, concat_axis=0, tiled=True)],
-        "table",
-        split_axis=0,
-        concat_axis=0,
-        tiled=True,
-    )
-    picked = jnp.dot(
-        placing, fetched.reshape(n_table * capacity, rank_width), preferred_element_type=jnp.float32
-    )
+    requests_in = lax.all_to_all(row_requests, "table", split_axis=0, concat_axis=0, tiled=True)
+    chunks = 2
+    chunk = capacity // chunks
+    placing_blocks = placing.reshape(flat_count, n_table, capacity)
+    picked = None
+    for c in range(chunks):
+        served = item_table[requests_in[:, c * chunk:(c + 1) * chunk]]
+        if c == 0:
+            served, gram_matrix = lax.optimization_barrier((served, gram_matrix))
+        fetched = lax.all_to_all(served, "table", split_axis=0, concat_axis=0, tiled=True)
+        part_pick = jnp.dot(
+            placing_blocks[:, :, c * chunk:(c + 1) * chunk].reshape(flat_count, n_table * chunk),
+            fetched.reshape(n_table * chunk, rank_width),
+            preferred_element_type=jnp.float32,
+        )
+        picked = part_pick if picked is None else picked + part_pick
     slot_rows = (picked * context_table[context_flat].astype(jnp.float32)).astype(jnp.bfloat16)
     slot_rows = slot_rows.reshape(user_count, slot_count, rank_width)
     confidence = CONF_SCALE * bucket.astype(jnp.float32)

time: 120 us -> 124 us (1.033)
  waiting for transfers between devices: 29.2 us -> 13.2 us
  other arithmetic: 6.35 us -> 12.5 us
  local copies, waits for them, and re-layouts: 31.4 us -> 36.2 us
  matrix products: 26.7 us -> 31.4 us
  starting transfers between devices: 13.6 us -> 17.1 us
    ppermute x3, waiting for transfers between devices: 29.2 us -> 6.3 us  [butterfly_sum(): value = value + lax.ppermute(value, name, pairs)]
    eq x0 -> x2, other arithmetic: none -> 7.03 us  [per_device(): target[:, None] == jnp.arange(n_table * capacity, dtype=jnp.int32)[None, :]]
    all_to_all x1 -> x2, waiting for transfers between devices: 0.01 us -> 6.86 us  [per_device(): lax.all_to_all(served, 'table', split_axis=0, concat_axis=0, tiled=True)]
    gather x1 -> x2, local copies, waits for them, and re-layouts: 20.3 us -> 25.8 us  [per_device(): served = item_table[requests_in[:, c * chunk:(c + 1) * chunk]]]
    dot_general x1 -> x2, matrix products: 7.57 us -> 12.1 us  [per_device(): jnp.dot(placing_blocks[:, :, c * chunk:(c + 1) * chunk].reshape(flat_coun...]
    all_to_all x1 -> x2, starting transfers between devices: 4.75 us -> 7.95 us  [per_device(): lax.all_to_all(served, 'table', split_axis=0, concat_axis=0, tiled=True)]
  transfers between devices with their start and end apart: 5 -> 6, of which waited for: 1 -> 2; matrix products, arithmetic and copies ran while one was open for 31% -> 49% of each run, Pallas kernels for 0% -> 0%
where the time goes in v4:
time: 124 us; the launch traced here: 123 us
  local copies, waits for them, and re-layouts  36.2 us (29%)
  matrix products  31.4 us (25%)
  starting transfers between devices  17.1 us (14%)
  waiting for transfers between devices  13.2 us (11%)
  other arithmetic  12.5 us (10%)
  blocking collectives  12.4 us (10%)
    gather x2, local copies, waits for them, and re-layouts, per_device(): served = item_table[requests_in[:, c * chunk:(c + 1) * chunk]]  25.8 us
    all_to_all x1, blocking collectives, per_device(): lax.all_to_all(payload, ('table', 'batch', 'ctx'), split_axis=0, concat_a...  12.4 us
    dot_general x2, matrix products, per_device(): jnp.dot(placing_blocks[:, :, c * chunk:(c + 1) * chunk].reshape(flat_coun...  12.1 us
    gather x1, local copies, waits for them, and re-layouts, per_device(): context_table[context_flat].astype(jnp.float32)  8.99 us
    all_to_all x2, starting transfers between devices, per_device(): lax.all_to_all(served, 'table', split_axis=0, concat_axis=0, tiled=True)  7.95 us
    eq x2, other arithmetic, per_device(): target[:, None] == jnp.arange(n_table * capacity, dtype=jnp.int32)[None, :]  7.03 us
    all_to_all x2, waiting for transfers between devices, per_device(): lax.all_to_all(served, 'table', split_axis=0, concat_axis=0, tiled=True)  6.86 us
    ppermute x3, waiting for transfers between devices, butterfly_sum(): value = value + lax.ppermute(value, name, pairs)  6.3 us
  transfers between devices with their start and end apart: 6, of which 2 were waited for; matrix products, arithmetic and copies ran while one was open for 49% of the time, Pallas kernels for 0%

profile of v4, /device:TPU:0, one launch (start us, length us, event | category | flops | bytes accessed | tf_op | source)
XLA Modules:
  0.0 123.1 jit_solution(7351779957457470803)
XLA Ops:
  0.0 4.9 %fusion.6 = f32[256,256]{1,0:T(8,128)S(1)} fusion(bf16[16384,256]{1,0:T(8,128)(2,1)} %param.10, s32[]{:T(128)S(6)} %select_n.84), kind=kOutput, calls=%fused_computation.11 | convolution fusion | flops 1073741824 | bytes 4456452 | tf_op jit(solution)/shard_map/dot_general | solution.py:15
  4.9 0.5 collective-permute-start
  5.4 0.5 broadcast.363
  5.9 0.7 fusion.75
  6.7 0.1 eq.95
  6.7 1.1 reduce-window.6
  7.9 0.2 slice_reduce_fusion
  8.1 0.2 reduce-window.9
  8.3 0.1 select_reduce_fusion
  8.4 0.1 mul.174
  8.4 0.1 reshape.363
  8.5 0.1 fusion.66
  8.6 6.0 %fusion = f32[2,4096]{1,0:T(2,128)S(1)} fusion(s32[2048]{0:T(1024)S(1)} %bitcast_add_fusion, bf16[1,2048]{1,0:T(2,128)(2,1)S(1)} %fusion.59, bf16[1,2048]{1,0:T(2,128)(2,1)S(1)} %get-tuple-element.29), kind=kOutput, calls=%fused_computation.4 | convolution fusion | flops 41959424 | bytes 49152 | tf_op jit(solution)/shard_map/dot_general | solution.py:41
  14.6 0.6 fusion.46
  15.3 4.7 %all-to-all-start = ((s32[4,1,1024]{2,1,0:T(1,128)}), s32[4,1,1024]{2,1,0:T(1,128)S(1)}, u32[]{:S(2)}, u32[]{:S(2)}) async-start(s32[4,1,1024]{2,1,0:T(1,128)} %bitcast.1), calls=%async_computation | async-start | bytes 32768 | tf_op jit(solution)/shard_map/all_to_all | solution.py:109
  20.0 0.7 fusion.76
  20.8 0.0 copy-start.5
  20.8 0.0 copy-start.6
  20.8 7.0 %broadcast_compare_fusion = pred[2048,4,1024]{2,0,1:T(32,128)(4,1)} fusion(s32[4,1024]{1,0:T(4,128)S(1)} %multiply_add_fusion.1, s32[2048]{0:T(1024)S(1)} %bitcast_add_fusion), kind=kLoop, calls=%fused_computation.6 | loop fusion | flops 8388608 | bytes 8413184 | tf_op jit(solution)/shard_map/eq | solution.py:104
  27.8 0.1 reshape.364
  28.0 0.2 reduce_window_sum.24
  28.2 0.2 fusion.52
  28.4 0.0 collective-permute-done
  28.4 2.1 %collective-permute-start.1 = (f32[256,256]{1,0:T(8,128)S(1)}, f32[256,256]{1,0:T(8,128)S(1)}, u32[]{:S(2)}, u32[]{:S(2)}) collective-permute-start(f32[256,256]{1,0:T(8,128)S(1)} %add.193), channel_id=1, source_target_pairs={{0,8},{8,0},{16,24},{24,16},{1,9},{9,1},{17,25},{25,17},{2,10},{10... | collective-permute-start | bytes 786440 | tf_op jit(solution)/shard_map/ppermute | solution.py:25
  30.5 0.1 convert_reduce_fusion.1
  30.6 0.0 all-to-all-done
  30.6 6.3 %collective-permute-done.1 = f32[256,256]{1,0:T(8,128)S(1)} collective-permute-done((f32[256,256]{1,0:T(8,128)S(1)}, f32[256,256]{1,0:T(8,128)S(1)}, u32[]{:S(2)}, u32[]{:S(2)}) %collective-permute-start.1) | collective-permute-done | bytes 262176 | tf_op jit(solution)/shard_map/ppermute | solution.py:25
  37.0 1.8 %collective-permute-start.2 = (f32[256,256]{1,0:T(8,128)S(1)}, f32[256,256]{1,0:T(8,128)S(1)}, u32[]{:S(2)}, u32[]{:S(2)}) collective-permute-start(f32[256,256]{1,0:T(8,128)S(1)} %add.194), channel_id=1, source_target_pairs={{0,16},{8,24},{16,0},{24,8},{1,17},{9,25},{17,1},{25,9},{2,18},{10... | collective-permute-start | bytes 786440 | tf_op jit(solution)/shard_map/ppermute | solution.py:25
  38.8 12.9 %gather_fusion = bf16[2048,256]{1,0:T(8,128)(2,1)} fusion(bf16[16384,256]{1,0:T(8,128)(2,1)} %param.10, s32[2048]{0:T(1024)S(1)} %broadcast_clamp_fusion.2), kind=kCustom, calls=%fused_computation | custom fusion | bytes 2105344 | tf_op jit(solution)/shard_map/gather | solution.py:115
  51.7 0.0 collective-permute-done.2
  51.7 0.1 multiply_multiply_fusion
  51.8 3.7 %all-to-all-start.1 = ((bf16[4,512,256]{2,1,0:T(8,128)(2,1)}), bf16[4,512,256]{2,1,0:T(8,128)(2,1)S(1)}, u32[]{:S(2)}, u32[]{:S(2)}) async-start(bf16[4,512,256]{2,1,0:T(8,128)(2,1)} %bitcast.2), calls=%async_computation.1 | async-start | bytes 2097152 | tf_op jit(solution)/shard_map/all_to_all | solution.py:118
  55.5 0.0 copy-start.2
  55.5 9.0 %gather_fusion.2 = bf16[2048,256]{1,0:T(8,128)(2,1)} fusion(bf16[4096,256]{1,0:T(8,128)(2,1)S(1)} %copy-done, s32[2048]{0:T(1024)S(1)} %broadcast_clamp_fusion), kind=kCustom, calls=%fused_computation.2 | custom fusion | bytes 2105344 | tf_op jit(solution)/shard_map/gather | solution.py:125
  64.5 0.1 copy.21
  64.6 0.1 copy.20
  64.7 0.6 compare_reduce_fusion
  65.3 0.7 convert_select_fusion
  66.0 12.9 %gather_fusion.1 = bf16[2048,256]{1,0:T(8,128)(2,1)} fusion(bf16[16384,256]{1,0:T(8,128)(2,1)} %param.10, s32[2048]{0:T(1024)S(1)} %broadcast_clamp_fusion.1), kind=kCustom, calls=%fused_computation.1 | custom fusion | bytes 2105344 | tf_op jit(solution)/shard_map/gather | solution.py:115
  78.9 0.0 all-to-all-done.1
  78.9 4.2 %all-to-all-start.2 = ((bf16[4,512,256]{2,1,0:T(8,128)(2,1)}), bf16[4,512,256]{2,1,0:T(8,128)(2,1)}, u32[]{:S(2)}, u32[]{:S(2)}) async-start(bf16[4,512,256]{2,1,0:T(8,128)(2,1)} %bitcast.4), calls=%async_computation.2 | async-start | bytes 2097152 | tf_op jit(solution)/shard_map/all_to_all | solution.py:118
  83.2 6.1 %fusion.8 = f32[2048,256]{1,0:T(8,128)} fusion(bf16[4,512,256]{2,1,0:T(8,128)(2,1)S(1)} %all-to-all-done.1, pred[2048,4,1024]{2,0,1:T(32,128)(4,1)} %broadcast_compare_fusion), kind=kOutput, calls=%fused_computation.13 | convolution fusion | flops 2147483648 | bytes 7340032 | tf_op jit(solution)/shard_map/dot_general | solution.py:119
  89.3 6.9 %all-to-all-done.2 = bf16[4,512,256]{2,1,0:T(8,128)(2,1)} async-done(((bf16[4,512,256]{2,1,0:T(8,128)(2,1)}), bf16[4,512,256]{2,1,0:T(8,128)(2,1)}, u32[]{:S(2)}, u32[]{:S(2)}) %all-to-all-start.2) | async-done | bytes 1048608 | tf_op jit(solution)/shard_map/all_to_all | solution.py:118
  96.1 6.1 %fusion.20 = bf16[2048,256]{1,0:T(8,128)(2,1)S(1)} fusion(f32[2048,256]{1,0:T(8,128)} %fusion.8, bf16[4,512,256]{2,1,0:T(8,128)(2,1)} %all-to-all-done.2, pred[2048,4,1024]{2,0,1:T(32,128)(4,1)} %broadcast_compare_fusion, bf16[2048,256]{1,0:T(8,128)(2,1)} %gather_fusion.2), kind=kOutput, calls=%fused_computation.17 | convolution fusion | flops 2149580800 | bytes 9437184 | tf_op jit(solution)/shard_map/dot_general | solution.py:119
  102.2 0.5 fusion.77
  102.7 0.9 fusion.41
  103.7 0.5 fusion.78
  104.2 0.3 multiply_reduce_fusion.3
  104.5 0.2 multiply_reduce_fusion.2
  104.7 0.1 fusion.36
  104.8 0.9 fusion.39
  105.8 0.5 fusion.79
  106.3 0.3 multiply_reduce_fusion.1
  106.6 0.2 multiply_reduce_fusion
  106.9 0.1 multiply_add_fusion
  106.9 0.9 fusion.37
  107.9 0.5 fusion.80
  108.4 0.3 fusion.29
  108.8 0.3 fusion.28
  109.1 12.4 %all_to_all.24 = f32[32,2,384]{2,1,0:T(2,128)S(1)} all-to-all(f32[32,2,384]{2,1,0:T(2,128)S(1)} %bitcast.126), channel_id=1, replica_groups=mesh['table'=4,'batch'=4,'ctx'=2] {'table','batch','ctx'}, dimensions={0} | all-to-all | bytes 196608 | tf_op jit(solution)/shard_map/all_to_all | solution.py:152
  121.6 0.1 reshape.367
  121.6 0.1 fusion.32
  121.7 0.1 convert_reduce_fusion
  121.9 1.3 %fusion.23 = bf16[1024,256]{1,0:T(8,128)(2,1)} fusion(bf16[1024,256]{1,0:T(8,128)(2,1)S(1)} %copy-done.1, pred[1024]{0:T(1024)(128)(4,1)S(1)} %broadcast_compare_fusion.1, s32[64]{0:T(128)S(1)} %fusion.32, f32[64,384]{1,0:T(8,128)S(1)} %reshape.367), kind=kOutput, calls=%fused_computation.19 | convolution fusion | flops 34144256 | bytes 1082880 | tf_op jit(solution)/shard_map/dot_general | solution.py:159
  (47 shorter events, 0.4 us)
Async XLA Ops:
  0.0 20.0 %copy-start = (bf16[4096,256]{1,0:T(8,128)(2,1)S(1)}, bf16[4096,256]{1,0:T(8,128)(2,1)}, u32[]{:S(2)}) copy-start(bf16[4096,256]{1,0:T(8,128)(2,1)} %param.11) | copy-start | bytes 6291460
  0.0 5.9 %copy-start.3 = (s32[32,64,1]{1,2,0:T(1,128)S(1)}, s32[32,64,1]{1,2,0:T(1,128)}, u32[]{:S(2)}) copy-start(s32[32,64,1]{1,2,0:T(1,128)} %param.13) | copy-start | bytes 24580
  0.0 8.4 %copy-start.4 = (s32[32,64]{1,0:T(8,128)S(1)}, s32[32,64]{1,0:T(8,128)}, u32[]{:S(2)}) copy-start(s32[32,64]{1,0:T(8,128)} %param.14) | copy-start | bytes 24580
  4.9 23.5 %collective-permute-start = (f32[256,256]{1,0:T(8,128)S(1)}, f32[256,256]{1,0:T(8,128)S(1)}, u32[]{:S(2)}, u32[]{:S(2)}) collective-permute-start(f32[256,256]{1,0:T(8,128)S(1)} %fusion.6), channel_id=1, source_target_pairs={{0,1},{1,0},{2,3},{3,2},{4,5},{5,4},{6,7},{7,6},{8,9},{9,8},{10,11... | collective-permute-start | bytes 786440 | tf_op jit(solution)/shard_map/ppermute | solution.py:25
  15.3 15.4 %all-to-all-start = ((s32[4,1,1024]{2,1,0:T(1,128)}), s32[4,1,1024]{2,1,0:T(1,128)S(1)}, u32[]{:S(2)}, u32[]{:S(2)}) async-start(s32[4,1,1024]{2,1,0:T(1,128)} %bitcast.1), calls=%async_computation | async-start | bytes 32768 | tf_op jit(solution)/shard_map/all_to_all | solution.py:109
  20.8 7.1 %copy-start.5 = (s32[32,64]{1,0:T(8,128)S(1)}, s32[32,64]{1,0:T(8,128)}, u32[]{:S(2)}) copy-start(s32[32,64]{1,0:T(8,128)} %param.15) | copy-start | bytes 24580
  20.8 7.1 %copy-start.6 = (s32[32]{0:T(128)S(1)}, s32[32]{0:T(128)}, u32[]{:S(2)}) copy-start(s32[32]{0:T(128)} %param.17) | copy-start | bytes 388
  28.4 8.5 %collective-permute-start.1 = (f32[256,256]{1,0:T(8,128)S(1)}, f32[256,256]{1,0:T(8,128)S(1)}, u32[]{:S(2)}, u32[]{:S(2)}) collective-permute-start(f32[256,256]{1,0:T(8,128)S(1)} %add.193), channel_id=1, source_target_pairs={{0,8},{8,0},{16,24},{24,16},{1,9},{9,1},{17,25},{25,17},{2,10},{10... | collective-permute-start | bytes 786440 | tf_op jit(solution)/shard_map/ppermute | solution.py:25
  37.0 14.7 %collective-permute-start.2 = (f32[256,256]{1,0:T(8,128)S(1)}, f32[256,256]{1,0:T(8,128)S(1)}, u32[]{:S(2)}, u32[]{:S(2)}) collective-permute-start(f32[256,256]{1,0:T(8,128)S(1)} %add.194), channel_id=1, source_target_pairs={{0,16},{8,24},{16,0},{24,8},{1,17},{9,25},{17,1},{25,9},{2,18},{10... | collective-permute-start | bytes 786440 | tf_op jit(solution)/shard_map/ppermute | solution.py:25
  51.8 27.2 %all-to-all-start.1 = ((bf16[4,512,256]{2,1,0:T(8,128)(2,1)}), bf16[4,512,256]{2,1,0:T(8,128)(2,1)S(1)}, u32[]{:S(2)}, u32[]{:S(2)}) async-start(bf16[4,512,256]{2,1,0:T(8,128)(2,1)} %bitcast.2), calls=%async_computation.1 | async-start | bytes 2097152 | tf_op jit(solution)/shard_map/all_to_all | solution.py:118
  55.5 9.8 %copy-start.2 = (s32[32,64]{1,0:T(8,128)S(1)}, s32[32,64]{1,0:T(8,128)}, u32[]{:S(2)}) copy-start(s32[32,64]{1,0:T(8,128)} %param.16) | copy-start | bytes 24580
  78.9 17.2 %all-to-all-start.2 = ((bf16[4,512,256]{2,1,0:T(8,128)(2,1)}), bf16[4,512,256]{2,1,0:T(8,128)(2,1)}, u32[]{:S(2)}, u32[]{:S(2)}) async-start(bf16[4,512,256]{2,1,0:T(8,128)(2,1)} %bitcast.4), calls=%async_computation.2 | async-start | bytes 2097152 | tf_op jit(solution)/shard_map/all_to_all | solution.py:118
  103.6 18.2 %copy-start.1 = (bf16[1024,256]{1,0:T(8,128)(2,1)S(1)}, bf16[1024,256]{1,0:T(8,128)(2,1)}, u32[]{:S(2)}) copy-start(bf16[1024,256]{1,0:T(8,128)(2,1)} %param.12) | copy-start | bytes 1572868

commit v5 on v3

--- a/solution.py
+++ b/solution.py
@@ -89,9 +89,15 @@
     n_table = lax.axis_size("table")
     n_batch = lax.axis_size("batch")
     n_ctx = lax.axis_size("ctx")
-    share = item_table.shape[0] // n_ctx
-    own_rows = lax.dynamic_slice_in_dim(item_table, lax.axis_index("ctx") * share, share, axis=0)
-    item_gram = butterfly_sum(gram_of(own_rows), (("ctx", n_ctx), ("table", n_table)))
+    rank_width = item_table.shape[1]
+    ctx_index = lax.axis_index("ctx")
+    width = rank_width // n_ctx
+    own_columns = lax.dynamic_slice_in_dim(item_table, ctx_index * width, width, axis=1)
+    column_gram = lax.dot_general(
+        item_table, own_columns, (((0,), (0,)), ((), ())), preferred_element_type=jnp.float32
+    )
+    column_gram = butterfly_sum(column_gram, (("table", n_table),))
+    item_gram = lax.all_gather(column_gram, "ctx", axis=1, tiled=True)
     context_gram = gram_of(context_table)
     pair_count = item_table.shape[0] * n_table * context_table.shape[0]
     gram_matrix = item_gram * context_gram / pair_count
@@ -104,7 +110,19 @@
     placing = (target[:, None] == jnp.arange(n_table * capacity, dtype=jnp.int32)[None, :]).astype(
         jnp.bfloat16
     )
-    row_requests = place_integers(item_row.reshape(flat_count), placing).reshape(n_table, capacity)
+    position = target % capacity
+    by_position = (position[:, None] == jnp.arange(capacity, dtype=jnp.int32)[None, :]).astype(
+        jnp.bfloat16
+    )
+    owner_mask = jnp.arange(n_table, dtype=jnp.int32)[:, None] == owners[None, :]
+    rows_flat = item_row.reshape(flat_count)
+    digits = jnp.stack([rows_flat // 128, rows_flat % 128], axis=0)
+    masked = jnp.where(owner_mask[:, None, :], digits[None, :, :], 0).astype(jnp.bfloat16)
+    placed = lax.dot_general(
+        masked.reshape(n_table * 2, flat_count), by_position, (((1,), (0,)), ((), ())),
+        preferred_element_type=jnp.float32,
+    ).reshape(n_table, 2, capacity)
+    row_requests = placed[:, 0].astype(jnp.int32) * 128 + placed[:, 1].astype(jnp.int32)
     context_flat = context_id.reshape(flat_count)
     served = item_table[lax.all_to_all(row_requests, "table", split_axis=0, concat_axis=0, tiled=True)]
     served, gram_matrix = lax.optimization_barrier((served, gram_matrix))

time: 110 us -> 106 us (0.964)
  matrix products: 27.8 us -> 25.5 us
  starting transfers between devices: 13.8 us -> 11.6 us
  blocking collectives: 12.5 us -> 14.5 us
  waiting for transfers between devices: 19.3 us -> 17.8 us
    dot_general x0 -> x2, matrix products: none -> 8.03 us  [the longest x1 6.31 us: per_device(): lax.dot_general(item_table, own_columns, (((0,), (0,)), ((), ())), prefer...]
    ppermute x3 -> x2, waiting for transfers between devices: 6.42 us -> 0.01 us  [butterfly_sum(): value = value + lax.ppermute(value, name, pairs)]
    dot_general x2 -> x1, matrix products: 6.18 us -> 0.19 us  [place_integers(): lax.dot_general(stacked, placing, (((1,), (0,)), ((), ())), preferred_ele...]
    dot_general x2 -> x1, matrix products: 5.61 us -> 0.93 us  [gram_of(): lax.dot_general(table_rows, table_rows, (((0,), (0,)), ((), ())), preferr...]
    all_to_all x1, waiting for transfers between devices: 0.01 us -> 3.53 us  [per_device(): lax.all_to_all(row_requests, 'table', split_axis=0, concat_axis=0, tiled=...]
    all_gather x0 -> x1, blocking collectives: none -> 1.99 us  [per_device(): item_gram = lax.all_gather(column_gram, 'ctx', axis=1, tiled=True)]
    all_to_all x1, starting transfers between devices: 4.73 us -> 3.25 us  [per_device(): lax.all_to_all(row_requests, 'table', split_axis=0, concat_axis=0, tiled=...]
    all_to_all x1, waiting for transfers between devices: 12.9 us -> 14.3 us  [per_device(): lax.all_to_all(served, 'table', split_axis=0, concat_axis=0, tiled=True)]
  transfers between devices with their start and end apart: 5 -> 4, of which waited for: 2 -> 2; matrix products, arithmetic and copies ran while one was open for 38% -> 36% of each run, Pallas kernels for 0% -> 0%
where the time goes in v5:
time: 106 us
  local copies, waits for them, and re-layouts  31.3 us (30%)
  matrix products  25.5 us (24%)
  waiting for transfers between devices  17.8 us (17%)
  blocking collectives  14.5 us (14%)
  starting transfers between devices  11.6 us (11%)
  other arithmetic  4.81 us (5%)
    gather x1, local copies, waits for them, and re-layouts, per_device(): item_table[lax.all_to_all(row_requests, 'table', split_axis=0, concat_axi...  20.3 us
    all_to_all x1, waiting for transfers between devices, per_device(): lax.all_to_all(served, 'table', split_axis=0, concat_axis=0, tiled=True)  14.3 us
    all_to_all x1, blocking collectives, per_device(): lax.all_to_all(payload, ('table', 'batch', 'ctx'), split_axis=0, concat_a...  12.5 us
    gather x1, local copies, waits for them, and re-layouts, per_device(): context_table[context_flat].astype(jnp.float32)  9 us
    dot_general x1, matrix products, per_device(): jnp.dot(placing, fetched.reshape(n_table * capacity, rank_width), preferr...  7.56 us
    dot_general x1, matrix products, per_device(): lax.dot_general(item_table, own_columns, (((0,), (0,)), ((), ())), prefer...  6.31 us
    all_to_all x1, starting transfers between devices, per_device(): lax.all_to_all(served, 'table', split_axis=0, concat_axis=0, tiled=True)  4.63 us
    ppermute x2, starting transfers between devices, butterfly_sum(): value = value + lax.ppermute(value, name, pairs)  3.68 us
  transfers between devices with their start and end apart: 4, of which 2 were waited for; matrix products, arithmetic and copies ran while one was open for 36% of the time, Pallas kernels for 0%

profile of v5, /device:TPU:0, one launch (start us, length us, event | category | flops | bytes accessed | tf_op | source)
XLA Modules:
  0.0 105.8 jit_solution(10678940638916464869)
XLA Ops:
  0.0 0.0 copy-start
  0.0 0.0 copy-start.2
  0.0 6.3 %fusion.11 = f32[256,128]{0,1:T(8,128)S(1)} fusion(bf16[16384,256]{1,0:T(8,128)(2,1)} %param.10, s32[]{:T(128)S(6)} %select_n.104), kind=kOutput, calls=%fused_computation.15 | convolution fusion | flops 1073741824 | bytes 12713988 | tf_op jit(solution)/shard_map/dot_general | solution.py:96
  6.3 3.0 %collective-permute-start = (f32[256,128]{0,1:T(8,128)S(1)}, f32[256,128]{0,1:T(8,128)S(1)}, u32[]{:S(2)}, u32[]{:S(2)}) collective-permute-start(f32[256,128]{0,1:T(8,128)S(1)} %fusion.11), channel_id=1, source_target_pairs={{0,8},{8,0},{16,24},{24,16},{1,9},{9,1},{17,25},{25,17},{2,10},{10... | collective-permute-start | bytes 393224 | tf_op jit(solution)/shard_map/ppermute | solution.py:25
  9.3 0.0 copy-done.2
  9.3 0.1 eq.113
  9.4 1.1 %reduce-window.6 = s32[4,16,128]{2,1,0:T(8,128)S(1)} reduce-window(s32[4,16,128]{2,1,0:T(8,128)S(1)} %fusion.35, s32[]{:T(128)} %constant.126.clone.1), window={size=1x1x128 pad=0_0x0_0x127_0}, to_apply=%region_2.3 | reduce-window | flops 1040384 | bytes 65540 | tf_op jit(solution)/shard_map/reduce-window
  10.6 0.2 slice_reduce_fusion
  10.8 0.2 reduce-window.9
  11.0 0.1 select_reduce_fusion
  11.0 0.5 broadcast.381
  11.6 0.7 reduce.18
  12.3 0.1 reshape.377
  12.4 0.0 copy-done.3
  12.4 0.1 reshape.379
  12.6 1.7 %fusion.3 = f32[4,2,1024]{2,0,1:T(4,128)S(1)} fusion(s32[2048]{0:T(1024)S(1)} %get-tuple-element.29, s32[2,2048]{1,0:T(2,128)S(1)} %pad_add_fusion, pred[4,2048]{1,0:T(4,128)(4,1)S(1)} %iota_compare_fusion.10), kind=kOutput, calls=%fused_computation.7 | convolution fusion | flops 35684352 | bytes 65536 | tf_op jit(solution)/shard_map/dot_general | solution.py:121
  14.3 0.6 copy.23
  14.9 3.3 %all-to-all-start = ((s32[4,1,1024]{2,1,0:T(1,128)}), s32[4,1,1024]{2,1,0:T(1,128)S(1)}, u32[]{:S(2)}, u32[]{:S(2)}) async-start(s32[4,1,1024]{2,1,0:T(1,128)} %copy.23), calls=%async_computation | async-start | bytes 32768 | tf_op jit(solution)/shard_map/all_to_all | solution.py:127
  18.2 0.0 copy-done
  18.2 0.0 copy-start.4
  18.2 0.0 copy-start.5
  18.2 0.9 fusion.62
  19.1 0.0 copy-done.4
  19.2 0.1 reshape.381
  19.3 0.0 copy-done.5
  19.3 3.5 %all-to-all-done = s32[4,1,1024]{2,1,0:T(1,128)S(1)} async-done(((s32[4,1,1024]{2,1,0:T(1,128)}), s32[4,1,1024]{2,1,0:T(1,128)S(1)}, u32[]{:S(2)}, u32[]{:S(2)}) %all-to-all-start) | async-done | bytes 16416 | tf_op jit(solution)/shard_map/all_to_all | solution.py:127
  22.9 0.0 collective-permute-done
  22.9 0.7 collective-permute-start.1
  23.6 20.3 %gather_fusion = bf16[4096,256]{1,0:T(8,128)(2,1)} fusion(bf16[16384,256]{1,0:T(8,128)(2,1)} %param.10, s32[4096]{0:T(1024)S(1)} %broadcast_clamp_fusion), kind=kCustom, calls=%fused_computation | custom fusion | bytes 4210688 | tf_op jit(solution)/shard_map/gather | solution.py:127
  43.9 0.0 collective-permute-done.1
  43.9 2.0 %all_gather.3 = f32[256,256]{0,1:T(8,128)S(1)} all-gather(f32[256,128]{0,1:T(8,128)S(1)} %add.193), channel_id=1, replica_groups=mesh['table'=4,'batch'=4,'ctx'=2] {'ctx'}, dimensions={1}, use_global_device_ids=true | all-gather | bytes 393216 | tf_op jit(solution)/shard_map/all_gather | solution.py:100
  45.9 4.6 %all-to-all-start.1 = ((bf16[4,1024,256]{2,1,0:T(8,128)(2,1)}), bf16[4,1024,256]{2,1,0:T(8,128)(2,1)}, u32[]{:S(2)}, u32[]{:S(2)}) async-start(bf16[4,1024,256]{2,1,0:T(8,128)(2,1)} %bitcast.116), calls=%async_computation.1 | async-start | bytes 4194304 | tf_op jit(solution)/shard_map/all_to_all | solution.py:129
  50.6 0.0 copy-start.1
  50.6 9.0 %gather_fusion.1 = bf16[2048,256]{1,0:T(8,128)(2,1)} fusion(bf16[4096,256]{1,0:T(8,128)(2,1)S(1)} %copy-done, s32[2048]{0:T(1024)S(1)} %broadcast_clamp_fusion.1), kind=kCustom, calls=%fused_computation.1 | custom fusion | bytes 2105344 | tf_op jit(solution)/shard_map/gather | solution.py:139
  59.6 0.2 reduce_window_sum.24
  59.8 0.2 fusion.45
  60.0 0.1 copy.26
  60.1 0.1 convert_reduce_fusion.1
  60.2 0.1 copy.25
  60.3 0.6 compare_reduce_fusion
  61.0 0.0 copy-done.1
  61.0 0.7 convert_select_fusion
  61.6 14.3 %all-to-all-done.1 = bf16[4,1024,256]{2,1,0:T(8,128)(2,1)} async-done(((bf16[4,1024,256]{2,1,0:T(8,128)(2,1)}), bf16[4,1024,256]{2,1,0:T(8,128)(2,1)}, u32[]{:S(2)}, u32[]{:S(2)}) %all-to-all-start.1) | async-done | bytes 2097184 | tf_op jit(solution)/shard_map/all_to_all | solution.py:129
  75.9 7.6 %fusion.9 = bf16[2048,256]{1,0:T(8,128)(2,1)S(1)} fusion(bf16[4096,256]{1,0:T(8,128)(2,1)} %bitcast.6, s32[2048]{0:T(1024)S(1)} %get-tuple-element.30, bf16[2048,256]{1,0:T(8,128)(2,1)} %gather_fusion.1), kind=kOutput, calls=%fused_computation.12 | convolution fusion | flops 4304928768 | bytes 4202496 | tf_op jit(solution)/shard_map/dot_general | solution.py:136
  83.5 0.5 fusion.63
  84.0 0.9 fusion.31
  84.9 0.5 fusion.64
  85.5 0.5 multiply_reduce_fusion.3
  85.9 0.2 multiply_reduce_fusion.2
  86.2 0.1 fusion.26
  86.2 0.9 fusion.29
  87.2 0.5 fusion.65
  87.7 0.5 multiply_reduce_fusion.1
  88.2 0.2 multiply_reduce_fusion
  88.4 0.1 multiply_add_fusion
  88.4 0.9 fusion.27
  89.4 0.5 fusion.66
  89.9 0.5 fusion.19
  90.4 0.3 fusion.18
  90.7 12.5 %all_to_all.19 = f32[32,2,384]{2,1,0:T(2,128)S(1)} all-to-all(f32[32,2,384]{2,1,0:T(2,128)S(1)} %bitcast.117), channel_id=1, replica_groups=mesh['table'=4,'batch'=4,'ctx'=2] {'table','batch','ctx'}, dimensions={0} | all-to-all | bytes 196608 | tf_op jit(solution)/shard_map/all_to_all | solution.py:166
  103.2 0.1 reshape.384
  103.3 0.1 fusion.22
  103.4 0.1 convert_reduce_fusion
  103.5 2.3 %fusion.10 = bf16[1024,256]{1,0:T(8,128)(2,1)} fusion(bf16[1024,256]{1,0:T(8,128)(2,1)} %param.12, pred[1024]{0:T(1024)(128)(4,1)S(1)} %broadcast_compare_fusion, s32[64]{0:T(128)S(1)} %fusion.22, f32[64,384]{1,0:T(8,128)S(1)} %reshape.384), kind=kOutput, calls=%fused_computation.14 | convolution fusion | flops 34144256 | bytes 1082880 | tf_op jit(solution)/shard_map/dot_general | solution.py:173
  (37 shorter events, 0.5 us)
Async XLA Ops:
  0.0 18.2 %copy-start = (bf16[4096,256]{1,0:T(8,128)(2,1)S(1)}, bf16[4096,256]{1,0:T(8,128)(2,1)}, u32[]{:S(2)}) copy-start(bf16[4096,256]{1,0:T(8,128)(2,1)} %param.11) | copy-start | bytes 6291460
  0.0 9.3 %copy-start.2 = (s32[32,64,1]{1,2,0:T(1,128)S(1)}, s32[32,64,1]{1,2,0:T(1,128)}, u32[]{:S(2)}) copy-start(s32[32,64,1]{1,2,0:T(1,128)} %param.13) | copy-start | bytes 24580
  0.0 12.4 %copy-start.3 = (s32[32,64]{1,0:T(8,128)S(1)}, s32[32,64]{1,0:T(8,128)}, u32[]{:S(2)}) copy-start(s32[32,64]{1,0:T(8,128)} %param.14) | copy-start | bytes 24580
  6.3 16.6 %collective-permute-start = (f32[256,128]{0,1:T(8,128)S(1)}, f32[256,128]{0,1:T(8,128)S(1)}, u32[]{:S(2)}, u32[]{:S(2)}) collective-permute-start(f32[256,128]{0,1:T(8,128)S(1)} %fusion.11), channel_id=1, source_target_pairs={{0,8},{8,0},{16,24},{24,16},{1,9},{9,1},{17,25},{25,17},{2,10},{10... | collective-permute-start | bytes 393224 | tf_op jit(solution)/shard_map/ppermute | solution.py:25
  14.9 7.9 %all-to-all-start = ((s32[4,1,1024]{2,1,0:T(1,128)}), s32[4,1,1024]{2,1,0:T(1,128)S(1)}, u32[]{:S(2)}, u32[]{:S(2)}) async-start(s32[4,1,1024]{2,1,0:T(1,128)} %copy.23), calls=%async_computation | async-start | bytes 32768 | tf_op jit(solution)/shard_map/all_to_all | solution.py:127
  18.2 1.0 copy-start.4
  18.2 1.1 %copy-start.5 = (s32[32]{0:T(128)S(1)}, s32[32]{0:T(128)}, u32[]{:S(2)}) copy-start(s32[32]{0:T(128)} %param.17) | copy-start | bytes 388
  22.9 21.0 %collective-permute-start.1 = (f32[256,128]{0,1:T(8,128)S(1)}, f32[256,128]{0,1:T(8,128)S(1)}, u32[]{:S(2)}, u32[]{:S(2)}) collective-permute-start(f32[256,128]{0,1:T(8,128)S(1)} %add.192), channel_id=1, source_target_pairs={{0,16},{8,24},{16,0},{24,8},{1,17},{9,25},{17,1},{25,9},{2,18},{10... | collective-permute-start | bytes 393224 | tf_op jit(solution)/shard_map/ppermute | solution.py:25
  45.9 30.0 %all-to-all-start.1 = ((bf16[4,1024,256]{2,1,0:T(8,128)(2,1)}), bf16[4,1024,256]{2,1,0:T(8,128)(2,1)}, u32[]{:S(2)}, u32[]{:S(2)}) async-start(bf16[4,1024,256]{2,1,0:T(8,128)(2,1)} %bitcast.116), calls=%async_computation.1 | async-start | bytes 4194304 | tf_op jit(solution)/shard_map/all_to_all | solution.py:129
  50.6 10.4 %copy-start.1 = (s32[32,64]{1,0:T(8,128)S(1)}, s32[32,64]{1,0:T(8,128)}, u32[]{:S(2)}) copy-start(s32[32,64]{1,0:T(8,128)} %param.16) | copy-start | bytes 24580

commit v6 on v5

--- a/solution.py
+++ b/solution.py
@@ -89,18 +89,6 @@
     n_table = lax.axis_size("table")
     n_batch = lax.axis_size("batch")
     n_ctx = lax.axis_size("ctx")
-    rank_width = item_table.shape[1]
-    ctx_index = lax.axis_index("ctx")
-    width = rank_width // n_ctx
-    own_columns = lax.dynamic_slice_in_dim(item_table, ctx_index * width, width, axis=1)
-    column_gram = lax.dot_general(
-        item_table, own_columns, (((0,), (0,)), ((), ())), preferred_element_type=jnp.float32
-    )
-    column_gram = butterfly_sum(column_gram, (("table", n_table),))
-    item_gram = lax.all_gather(column_gram, "ctx", axis=1, tiled=True)
-    context_gram = gram_of(context_table)
-    pair_count = item_table.shape[0] * n_table * context_table.shape[0]
-    gram_matrix = item_gram * context_gram / pair_count
     user_count, slot_count = bucket.shape
     rank_width = item_table.shape[1]
     flat_count = user_count * slot_count
@@ -125,7 +113,19 @@
     row_requests = placed[:, 0].astype(jnp.int32) * 128 + placed[:, 1].astype(jnp.int32)
     context_flat = context_id.reshape(flat_count)
     served = item_table[lax.all_to_all(row_requests, "table", split_axis=0, concat_axis=0, tiled=True)]
-    served, gram_matrix = lax.optimization_barrier((served, gram_matrix))
+    gram_source, served = lax.optimization_barrier((item_table, served))
+    rank_width = item_table.shape[1]
+    ctx_index = lax.axis_index("ctx")
+    width = rank_width // n_ctx
+    own_columns = lax.dynamic_slice_in_dim(gram_source, ctx_index * width, width, axis=1)
+    column_gram = lax.dot_general(
+        gram_source, own_columns, (((0,), (0,)), ((), ())), preferred_element_type=jnp.float32
+    )
+    column_gram = butterfly_sum(column_gram, (("table", n_table),))
+    item_gram = lax.all_gather(column_gram, "ctx", axis=1, tiled=True)
+    context_gram = gram_of(context_table)
+    pair_count = item_table.shape[0] * n_table * context_table.shape[0]
+    gram_matrix = item_gram * context_gram / pair_count
     fetched = lax.all_to_all(
         served,
         "table",

time: 106 us -> 105 us (level)
  waiting for transfers between devices: 17.8 us -> 13.7 us
  starting transfers between devices: 11.6 us -> 13.2 us
  local copies, waits for them, and re-layouts: 31.3 us -> 32.9 us
    all_to_all x1, waiting for transfers between devices: 14.3 us -> 0.01 us  [per_device(): lax.all_to_all(served, 'table', split_axis=0, concat_axis=0, tiled=True)]
    ppermute x2, waiting for transfers between devices: 0.01 us -> 9.71 us  [butterfly_sum(): value = value + lax.ppermute(value, name, pairs)]
    all_to_all x1, starting transfers between devices: 3.25 us -> 5.17 us  [per_device(): lax.all_to_all(row_requests, 'table', split_axis=0, concat_axis=0, tiled=...]
  transfers between devices with their start and end apart: 4 -> 4, of which waited for: 2 -> 3; matrix products, arithmetic and copies ran while one was open for 36% -> 18% of each run, Pallas kernels for 0% -> 0%
where the time goes in v6:
time: 105 us
  local copies, waits for them, and re-layouts  32.9 us (31%)
  matrix products  24.7 us (24%)
  blocking collectives  14.6 us (14%)
  waiting for transfers between devices  13.7 us (13%)
  starting transfers between devices  13.2 us (13%)
  other arithmetic  5.48 us (5%)
    gather x1, local copies, waits for them, and re-layouts, per_device(): item_table[lax.all_to_all(row_requests, 'table', split_axis=0, concat_axi...  20.3 us
    all_to_all x1, blocking collectives, per_device(): lax.all_to_all(payload, ('table', 'batch', 'ctx'), split_axis=0, concat_a...  12.5 us
    ppermute x2, waiting for transfers between devices, butterfly_sum(): value = value + lax.ppermute(value, name, pairs)  9.71 us
    gather x1, local copies, waits for them, and re-layouts, per_device(): context_table[context_flat].astype(jnp.float32)  8.99 us
    dot_general x1, matrix products, per_device(): jnp.dot(placing, fetched.reshape(n_table * capacity, rank_width), preferr...  7.56 us
    dot_general x1, matrix products, per_device(): lax.dot_general(gram_source, own_columns, (((0,), (0,)), ((), ())), prefe...  6.97 us
    all_to_all x1, starting transfers between devices, per_device(): lax.all_to_all(row_requests, 'table', split_axis=0, concat_axis=0, tiled=...  5.17 us
    all_to_all x1, starting transfers between devices, per_device(): lax.all_to_all(served, 'table', split_axis=0, concat_axis=0, tiled=True)  4.44 us
  transfers between devices with their start and end apart: 4, of which 3 were waited for; matrix products, arithmetic and copies ran while one was open for 18% of the time, Pallas kernels for 0%

profile of v6, /device:TPU:0, one launch (start us, length us, event | category | flops | bytes accessed | tf_op | source)
XLA Modules:
  0.0 104.9 jit_solution(15904749096914788632)
XLA Ops:
  0.0 0.0 copy-start
  0.0 0.0 copy-start.4
  0.0 0.0 copy-start.3
  0.0 0.9 eq.113
  1.0 1.1 %reduce-window.6 = s32[4,16,128]{2,1,0:T(8,128)S(1)} reduce-window(s32[4,16,128]{2,1,0:T(8,128)S(1)} %fusion.32, s32[]{:T(128)} %constant.126.clone.1), window={size=1x1x128 pad=0_0x0_0x127_0}, to_apply=%region_2.3 | reduce-window | flops 1040384 | bytes 65540 | tf_op jit(solution)/shard_map/reduce-window
  2.1 0.2 slice_reduce_fusion
  2.3 0.2 reduce-window.9
  2.5 0.1 select_reduce_fusion
  2.6 0.5 broadcast.381
  3.1 1.4 %reduce.18 = s32[32,64]{1,0:T(8,128)S(1)} reduce(s32[32,64,1]{1,2,0:T(1,128)} %param.13, s32[]{:T(128)} %broadcast.381), dimensions={2}, to_apply=%param.13.reduce_sub_computation.5 | reduce | bytes 16388 | tf_op args[3]
  4.5 0.1 reshape.377
  4.6 0.8 reshape.379
  5.5 1.7 %fusion.3 = f32[4,2,1024]{2,0,1:T(4,128)S(1)} fusion(s32[2048]{0:T(1024)S(1)} %get-tuple-element.29, s32[2,2048]{1,0:T(2,128)S(1)} %pad_add_fusion, pred[4,2048]{1,0:T(4,128)(4,1)S(1)} %iota_compare_fusion.10), kind=kOutput, calls=%fused_computation.7 | convolution fusion | flops 35684352 | bytes 65536 | tf_op jit(solution)/shard_map/dot_general | solution.py:109
  7.3 0.6 copy.19
  7.9 5.2 %all-to-all-start = ((s32[4,1,1024]{2,1,0:T(1,128)}), s32[4,1,1024]{2,1,0:T(1,128)S(1)}, u32[]{:S(2)}, u32[]{:S(2)}) async-start(s32[4,1,1024]{2,1,0:T(1,128)} %copy.19), calls=%async_computation | async-start | bytes 32768 | tf_op jit(solution)/shard_map/all_to_all | solution.py:115
  13.0 0.0 copy-done.4
  13.1 0.2 reduce_window_sum.24
  13.3 0.2 fusion.42
  13.5 0.0 copy-done.3
  13.5 0.1 reshape.381
  13.6 0.1 convert_reduce_fusion.1
  13.7 4.0 %all-to-all-done = s32[4,1,1024]{2,1,0:T(1,128)S(1)} async-done(((s32[4,1,1024]{2,1,0:T(1,128)}), s32[4,1,1024]{2,1,0:T(1,128)S(1)}, u32[]{:S(2)}, u32[]{:S(2)}) %all-to-all-start) | async-done | bytes 16416 | tf_op jit(solution)/shard_map/all_to_all | solution.py:115
  17.8 20.3 %gather_fusion = bf16[4096,256]{1,0:T(8,128)(2,1)} fusion(bf16[16384,256]{1,0:T(8,128)(2,1)} %param.10, s32[4096]{0:T(1024)S(1)} %broadcast_clamp_fusion), kind=kCustom, calls=%fused_computation | custom fusion | bytes 4210688 | tf_op jit(solution)/shard_map/gather | solution.py:115
  38.1 4.4 %all-to-all-start.1 = ((bf16[4,1024,256]{2,1,0:T(8,128)(2,1)}), bf16[4,1024,256]{2,1,0:T(8,128)(2,1)}, u32[]{:S(2)}, u32[]{:S(2)}) async-start(bf16[4,1024,256]{2,1,0:T(8,128)(2,1)} %bitcast.111), calls=%async_computation.1 | async-start | bytes 4194304 | tf_op jit(solution)/shard_map/all_to_all | solution.py:129
  42.5 0.1 copy.20
  42.7 0.1 copy.21
  42.7 0.0 copy-done
  42.7 9.0 %gather_fusion.1 = bf16[2048,256]{1,0:T(8,128)(2,1)} fusion(bf16[4096,256]{1,0:T(8,128)(2,1)S(1)} %copy-done, s32[2048]{0:T(1024)S(1)} %broadcast_clamp_fusion.1), kind=kCustom, calls=%fused_computation.1 | custom fusion | bytes 2105344 | tf_op jit(solution)/shard_map/gather | solution.py:139
  51.7 0.6 compare_reduce_fusion
  52.4 0.7 fusion.60
  53.1 0.0 copy-start.2
  53.1 7.0 %fusion.5 = f32[256,128]{1,0:T(8,128)S(1)} fusion(bf16[16384,256]{1,0:T(8,128)(2,1)} %param.10, s32[]{:T(128)S(6)} %select_n.106), kind=kOutput, calls=%fused_computation.8 | convolution fusion | flops 1073741824 | bytes 12713988 | tf_op jit(solution)/shard_map/dot_general | solution.py:121
  60.1 2.0 %collective-permute-start = (f32[256,128]{1,0:T(8,128)S(1)}, f32[256,128]{1,0:T(8,128)S(1)}, u32[]{:S(2)}, u32[]{:S(2)}) collective-permute-start(f32[256,128]{1,0:T(8,128)S(1)} %fusion.5), channel_id=1, source_target_pairs={{0,8},{8,0},{16,24},{24,16},{1,9},{9,1},{17,25},{25,17},{2,10},{10... | collective-permute-start | bytes 393224 | tf_op jit(solution)/shard_map/ppermute | solution.py:25
  62.1 0.7 convert_select_fusion
  62.8 6.2 %collective-permute-done = f32[256,128]{1,0:T(8,128)S(1)} collective-permute-done((f32[256,128]{1,0:T(8,128)S(1)}, f32[256,128]{1,0:T(8,128)S(1)}, u32[]{:S(2)}, u32[]{:S(2)}) %collective-permute-start) | collective-permute-done | bytes 131104 | tf_op jit(solution)/shard_map/ppermute | solution.py:25
  69.0 1.5 %collective-permute-start.1 = (f32[256,128]{1,0:T(8,128)S(1)}, f32[256,128]{1,0:T(8,128)S(1)}, u32[]{:S(2)}, u32[]{:S(2)}) collective-permute-start(f32[256,128]{1,0:T(8,128)S(1)} %add.196), channel_id=1, source_target_pairs={{0,16},{8,24},{16,0},{24,8},{1,17},{9,25},{17,1},{25,9},{2,18},{10... | collective-permute-start | bytes 393224 | tf_op jit(solution)/shard_map/ppermute | solution.py:25
  70.6 0.0 copy-done.2
  70.6 3.5 %collective-permute-done.1 = f32[256,128]{1,0:T(8,128)S(1)} collective-permute-done((f32[256,128]{1,0:T(8,128)S(1)}, f32[256,128]{1,0:T(8,128)S(1)}, u32[]{:S(2)}, u32[]{:S(2)}) %collective-permute-start.1) | collective-permute-done | bytes 131104 | tf_op jit(solution)/shard_map/ppermute | solution.py:25
  74.1 2.2 %all_gather.3 = f32[256,256]{1,0:T(8,128)S(1)} all-gather(f32[256,128]{1,0:T(8,128)S(1)} %add.197), channel_id=1, replica_groups=mesh['table'=4,'batch'=4,'ctx'=2] {'ctx'}, dimensions={1}, use_global_device_ids=true | all-gather | bytes 393216 | tf_op jit(solution)/shard_map/all_gather | solution.py:125
  76.3 0.0 all-to-all-done.1
  76.3 7.6 %fusion.9 = bf16[2048,256]{1,0:T(8,128)(2,1)S(1)} fusion(bf16[4096,256]{1,0:T(8,128)(2,1)} %bitcast.5, s32[2048]{0:T(1024)S(1)} %get-tuple-element.30, bf16[2048,256]{1,0:T(8,128)(2,1)} %gather_fusion.1), kind=kOutput, calls=%fused_computation.12 | convolution fusion | flops 4304928768 | bytes 4202496 | tf_op jit(solution)/shard_map/dot_general | solution.py:136
  83.8 0.5 fusion.59
  84.4 0.9 fusion.28
  85.3 0.5 fusion.61
  85.8 0.4 multiply_reduce_fusion.3
  86.2 0.2 multiply_reduce_fusion.2
  86.4 0.1 fusion.23
  86.5 0.9 fusion.26
  87.4 0.5 fusion.62
  88.0 0.4 multiply_reduce_fusion.1
  88.3 0.0 copy-start.1
  88.4 0.2 multiply_reduce_fusion
  88.5 0.1 multiply_add_fusion
  88.6 0.9 fusion.24
  89.6 0.5 fusion.63
  90.1 0.4 fusion.16
  90.5 0.3 fusion.15
  90.8 12.5 %all_to_all.19 = f32[32,2,384]{2,1,0:T(2,128)S(1)} all-to-all(f32[32,2,384]{2,1,0:T(2,128)S(1)} %bitcast.112), channel_id=1, replica_groups=mesh['table'=4,'batch'=4,'ctx'=2] {'table','batch','ctx'}, dimensions={0} | all-to-all | bytes 196608 | tf_op jit(solution)/shard_map/all_to_all | solution.py:166
  103.3 0.1 reshape.384
  103.4 0.1 fusion.19
  103.5 0.1 convert_reduce_fusion
  103.6 0.0 copy-done.1
  103.6 1.3 %fusion.10 = bf16[1024,256]{1,0:T(8,128)(2,1)} fusion(bf16[1024,256]{1,0:T(8,128)(2,1)S(1)} %copy-done.1, pred[1024]{0:T(1024)(128)(4,1)S(1)} %broadcast_compare_fusion, s32[64]{0:T(128)S(1)} %fusion.19, f32[64,384]{1,0:T(8,128)S(1)} %reshape.384), kind=kOutput, calls=%fused_computation.14 | convolution fusion | flops 34144256 | bytes 1082880 | tf_op jit(solution)/shard_map/dot_general | solution.py:173
  (35 shorter events, 0.4 us)
Async XLA Ops:
  0.0 42.7 %copy-start = (bf16[4096,256]{1,0:T(8,128)(2,1)S(1)}, bf16[4096,256]{1,0:T(8,128)(2,1)}, u32[]{:S(2)}) copy-start(bf16[4096,256]{1,0:T(8,128)(2,1)} %param.11) | copy-start | bytes 6291460
  0.0 13.0 %copy-start.4 = (s32[32]{0:T(128)S(1)}, s32[32]{0:T(128)}, u32[]{:S(2)}) copy-start(s32[32]{0:T(128)} %param.17) | copy-start | bytes 388
  0.0 13.5 %copy-start.3 = (s32[32,64]{1,0:T(8,128)S(1)}, s32[32,64]{1,0:T(8,128)}, u32[]{:S(2)}) copy-start(s32[32,64]{1,0:T(8,128)} %param.15) | copy-start | bytes 24580
  7.9 9.9 %all-to-all-start = ((s32[4,1,1024]{2,1,0:T(1,128)}), s32[4,1,1024]{2,1,0:T(1,128)S(1)}, u32[]{:S(2)}, u32[]{:S(2)}) async-start(s32[4,1,1024]{2,1,0:T(1,128)} %copy.19), calls=%async_computation | async-start | bytes 32768 | tf_op jit(solution)/shard_map/all_to_all | solution.py:115
  38.1 38.2 %all-to-all-start.1 = ((bf16[4,1024,256]{2,1,0:T(8,128)(2,1)}), bf16[4,1024,256]{2,1,0:T(8,128)(2,1)}, u32[]{:S(2)}, u32[]{:S(2)}) async-start(bf16[4,1024,256]{2,1,0:T(8,128)(2,1)} %bitcast.111), calls=%async_computation.1 | async-start | bytes 4194304 | tf_op jit(solution)/shard_map/all_to_all | solution.py:129
  53.1 17.4 %copy-start.2 = (s32[32,64]{1,0:T(8,128)S(1)}, s32[32,64]{1,0:T(8,128)}, u32[]{:S(2)}) copy-start(s32[32,64]{1,0:T(8,128)} %param.16) | copy-start | bytes 24580
  60.1 8.9 %collective-permute-start = (f32[256,128]{1,0:T(8,128)S(1)}, f32[256,128]{1,0:T(8,128)S(1)}, u32[]{:S(2)}, u32[]{:S(2)}) collective-permute-start(f32[256,128]{1,0:T(8,128)S(1)} %fusion.5), channel_id=1, source_target_pairs={{0,8},{8,0},{16,24},{24,16},{1,9},{9,1},{17,25},{25,17},{2,10},{10... | collective-permute-start | bytes 393224 | tf_op jit(solution)/shard_map/ppermute | solution.py:25
  69.0 5.0 %collective-permute-start.1 = (f32[256,128]{1,0:T(8,128)S(1)}, f32[256,128]{1,0:T(8,128)S(1)}, u32[]{:S(2)}, u32[]{:S(2)}) collective-permute-start(f32[256,128]{1,0:T(8,128)S(1)} %add.196), channel_id=1, source_target_pairs={{0,16},{8,24},{16,0},{24,8},{1,17},{9,25},{17,1},{25,9},{2,18},{10... | collective-permute-start | bytes 393224 | tf_op jit(solution)/shard_map/ppermute | solution.py:25
  88.3 15.3 %copy-start.1 = (bf16[1024,256]{1,0:T(8,128)(2,1)S(1)}, bf16[1024,256]{1,0:T(8,128)(2,1)}, u32[]{:S(2)}) copy-start(bf16[1024,256]{1,0:T(8,128)(2,1)} %param.12) | copy-start | bytes 1572868

commit v7 on v6

--- a/solution.py
+++ b/solution.py
@@ -95,9 +95,6 @@
     capacity = 2 * flat_count // n_table
     owners = item_owner.reshape(flat_count)
     target = owner_slots(owners, n_table, capacity)
-    placing = (target[:, None] == jnp.arange(n_table * capacity, dtype=jnp.int32)[None, :]).astype(
-        jnp.bfloat16
-    )
     position = target % capacity
     by_position = (position[:, None] == jnp.arange(capacity, dtype=jnp.int32)[None, :]).astype(
         jnp.bfloat16
@@ -112,8 +109,16 @@
     ).reshape(n_table, 2, capacity)
     row_requests = placed[:, 0].astype(jnp.int32) * 128 + placed[:, 1].astype(jnp.int32)
     context_flat = context_id.reshape(flat_count)
-    served = item_table[lax.all_to_all(row_requests, "table", split_axis=0, concat_axis=0, tiled=True)]
-    gram_source, served = lax.optimization_barrier((item_table, served))
+    requests_in = lax.all_to_all(row_requests, "table", split_axis=0, concat_axis=0, tiled=True)
+    table_index = lax.axis_index("table")
+    got = [item_table[lax.dynamic_index_in_dim(requests_in, table_index, keepdims=False)]]
+    for k in range(1, n_table):
+        partner = table_index ^ k
+        served = item_table[lax.dynamic_index_in_dim(requests_in, partner, keepdims=False)]
+        if k == n_table - 1:
+            gram_source, served = lax.optimization_barrier((item_table, served))
+        pairs = [(i, i ^ k) for i in range(n_table)]
+        got.append(lax.ppermute(served, "table", pairs))
     rank_width = item_table.shape[1]
     ctx_index = lax.axis_index("ctx")
     width = rank_width // n_ctx
@@ -126,12 +131,10 @@
     context_gram = gram_of(context_table)
     pair_count = item_table.shape[0] * n_table * context_table.shape[0]
     gram_matrix = item_gram * context_gram / pair_count
-    fetched = lax.all_to_all(
-        served,
-        "table",
-        split_axis=0,
-        concat_axis=0,
-        tiled=True,
+    fetched = jnp.stack(got, axis=0)
+    relative = (owners ^ table_index) * capacity + target % capacity
+    placing = (relative[:, None] == jnp.arange(n_table * capacity, dtype=jnp.int32)[None, :]).astype(
+        jnp.bfloat16
     )
     picked = jnp.dot(
         placing, fetched.reshape(n_table * capacity, rank_width), preferred_element_type=jnp.float32

time: 105 us -> 115 us (1.095)
  local copies, waits for them, and re-layouts: 32.9 us -> 48.4 us
  waiting for transfers between devices: 13.7 us -> 5.84 us
  other arithmetic: 5.48 us -> 10.3 us
  matrix products: 24.7 us -> 23.1 us
    gather x1 -> x4, local copies, waits for them, and re-layouts: 20.3 us -> 35.5 us  [the longest x3 27.1 us: per_device(): item_table[lax.dynamic_index_in_dim(requests_in, partner, keepdims=False)]]
    all_to_all x1 -> x0, starting transfers between devices: 4.44 us -> none  [per_device(): lax.all_to_all(served, 'table', split_axis=0, concat_axis=0, tiled=True)]
    all_to_all x1, waiting for transfers between devices: 4.03 us -> 0.01 us  [per_device(): lax.all_to_all(row_requests, 'table', split_axis=0, concat_axis=0, tiled=...]
    ppermute x2, waiting for transfers between devices: 9.71 us -> 5.82 us  [butterfly_sum(): value = value + lax.ppermute(value, name, pairs)]
    ppermute x0 -> x3, starting transfers between devices: none -> 3.5 us  [per_device(): got.append(lax.ppermute(served, 'table', pairs))]
    another operation x4 -> x5, other arithmetic: 2.62 us -> 4.78 us
    dot_general x1, matrix products: 7.56 us -> 5.86 us  [per_device(): jnp.dot(placing, fetched.reshape(n_table * capacity, rank_width), preferr...]
  transfers between devices with their start and end apart: 4 -> 6, of which waited for: 3 -> 1; matrix products, arithmetic and copies ran while one was open for 18% -> 42% of each run, Pallas kernels for 0% -> 0%
where the time goes in v7:
time: 115 us; the launch traced here: 114 us
  local copies, waits for them, and re-layouts  48.4 us (42%)
  matrix products  23.1 us (20%)
  blocking collectives  13.8 us (12%)
  starting transfers between devices  12.3 us (11%)
  other arithmetic  10.3 us (9%)
  waiting for transfers between devices  5.84 us (5%)
    gather x3, local copies, waits for them, and re-layouts, per_device(): item_table[lax.dynamic_index_in_dim(requests_in, partner, keepdims=False)]  27.1 us
    all_to_all x1, blocking collectives, per_device(): lax.all_to_all(payload, ('table', 'batch', 'ctx'), split_axis=0, concat_a...  11.6 us
    gather x1, local copies, waits for them, and re-layouts, per_device(): context_table[context_flat].astype(jnp.float32)  8.99 us
    gather x1, local copies, waits for them, and re-layouts, per_device(): item_table[lax.dynamic_index_in_dim(requests_in, table_index, keepdims=Fa...  8.41 us
    dot_general x1, matrix products, per_device(): lax.dot_general(gram_source, own_columns, (((0,), (0,)), ((), ())), prefe...  7.04 us
    dot_general x1, matrix products, per_device(): jnp.dot(placing, fetched.reshape(n_table * capacity, rank_width), preferr...  5.86 us
    ppermute x2, waiting for transfers between devices, butterfly_sum(): value = value + lax.ppermute(value, name, pairs)  5.82 us
    all_to_all x1, starting transfers between devices, per_device(): lax.all_to_all(row_requests, 'table', split_axis=0, concat_axis=0, tiled=...  5.16 us
  transfers between devices with their start and end apart: 6, of which 1 were waited for; matrix products, arithmetic and copies ran while one was open for 42% of the time, Pallas kernels for 0%

profile of v7, /device:TPU:0, one launch (start us, length us, event | category | flops | bytes accessed | tf_op | source)
XLA Modules:
  0.0 114.1 jit_solution(6421292730324448236)
XLA Ops:
  0.0 0.9 eq.114
  1.0 1.1 reduce-window.6
  2.1 0.2 slice_reduce_fusion
  2.3 0.2 reduce-window.9
  2.5 0.1 select_reduce_fusion
  2.6 0.5 broadcast.493
  3.1 1.4 %reduce.18 = s32[32,64]{1,0:T(8,128)S(1)} reduce(s32[32,64,1]{1,2,0:T(1,128)} %param.13, s32[]{:T(128)} %broadcast.493), dimensions={2}, to_apply=%param.13.reduce_sub_computation.5 | reduce | bytes 16388 | tf_op args[3]
  4.5 0.1 reshape.475
  4.6 0.8 reshape.477
  5.5 0.6 multiply_add_fusion.1
  6.1 1.7 %fusion.3 = f32[4,2,1024]{2,0,1:T(4,128)S(1)} fusion(s32[2048]{0:T(1024)S(1)} %get-tuple-element.33, s32[2,2048]{1,0:T(2,128)S(1)} %pad_add_fusion, pred[4,2048]{1,0:T(4,128)(4,1)S(1)} %iota_compare_fusion.10), kind=kOutput, calls=%fused_computation.10 | convolution fusion | flops 35684352 | bytes 65536 | tf_op jit(solution)/shard_map/dot_general | solution.py:106
  7.9 0.6 copy.19
  8.5 5.2 %all-to-all-start = ((s32[4,1,1024]{2,1,0:T(1,128)}), s32[4,1,1024]{2,1,0:T(1,128)S(1)}, u32[]{:S(2)}, u32[]{:S(2)}) async-start(s32[4,1,1024]{2,1,0:T(1,128)} %copy.19), calls=%async_computation | async-start | bytes 32768 | tf_op jit(solution)/shard_map/all_to_all | solution.py:112
  13.6 0.7 compare_reduce_fusion
  14.3 0.1 reshape.479
  14.4 0.0 copy-start.8
  14.4 0.7 fusion.60
  15.2 0.2 reduce_window_sum.24
  15.5 0.1 convert_reduce_fusion.1
  15.6 0.2 fusion.42
  15.8 0.3 copy-done.9
  16.0 0.1 copy.21
  16.1 0.1 copy.20
  16.2 1.2 %convert_select_fusion = f32[32,1]{1,0:T(8,128)} fusion(pred[32,1]{1,0:T(8,128)(4,1)S(1)} %copy.20, s32[32,1]{1,0:T(8,128)S(1)} %copy.21, pred[]{:T(512)} %compare_reduce_fusion), kind=kLoop, calls=%fused_computation.89 | loop fusion | flops 96 | bytes 289 | tf_op jit(solution)/shard_map/select.70
  17.5 9.0 %gather_fusion.4 = bf16[2048,256]{1,0:T(8,128)(2,1)} fusion(bf16[4096,256]{1,0:T(8,128)(2,1)S(1)} %copy-done, s32[2048]{0:T(1024)S(1)} %broadcast_clamp_fusion), kind=kCustom, calls=%fused_computation.4 | custom fusion | bytes 2105344 | tf_op jit(solution)/shard_map/gather | solution.py:142
  26.5 9.1 %gather_fusion.3 = bf16[1024,256]{1,0:T(8,128)(2,1)} fusion(bf16[16384,256]{1,0:T(8,128)(2,1)} %param.10, s32[1024]{0:T(1024)S(1)} %broadcast_clamp_fusion.1), kind=kCustom, calls=%fused_computation.3 | custom fusion | bytes 1052672 | tf_op jit(solution)/shard_map/gather | solution.py:117
  35.6 2.9 %collective-permute-start.2 = (bf16[1024,256]{1,0:T(8,128)(2,1)}, bf16[1024,256]{1,0:T(8,128)(2,1)S(1)}, u32[]{:S(2)}, u32[]{:S(2)}) collective-permute-start(bf16[1024,256]{1,0:T(8,128)(2,1)} %gather_fusion.3), channel_id=1, source_target_pairs={{0,24},{8,16},{16,8},{24,0},{1,25},{9,17},{17,9},{25,1},{2,26},{10... | collective-permute-start | bytes 1572872 | tf_op jit(solution)/shard_map/ppermute | solution.py:121
  38.5 9.0 %gather_fusion.2 = bf16[1024,256]{1,0:T(8,128)(2,1)} fusion(bf16[16384,256]{1,0:T(8,128)(2,1)} %param.10, s32[1024]{0:T(1024)S(1)} %broadcast_clamp_fusion.2), kind=kCustom, calls=%fused_computation.2 | custom fusion | bytes 1052672 | tf_op jit(solution)/shard_map/gather | solution.py:117
  47.5 0.6 collective-permute-start.1
  48.1 9.0 %gather_fusion.1 = bf16[1024,256]{1,0:T(8,128)(2,1)} fusion(bf16[16384,256]{1,0:T(8,128)(2,1)} %param.10, s32[1024]{0:T(1024)S(1)} %broadcast_clamp_fusion.3), kind=kCustom, calls=%fused_computation.1 | custom fusion | bytes 1052672 | tf_op jit(solution)/shard_map/gather | solution.py:117
  57.1 0.0 collective-permute-start
  57.2 7.0 %fusion.5 = f32[256,128]{1,0:T(8,128)S(1)} fusion(bf16[16384,256]{1,0:T(8,128)(2,1)} %param.10, s32[]{:T(128)S(6)} %select_n.161), kind=kOutput, calls=%fused_computation.11 | convolution fusion | flops 1073741824 | bytes 12713988 | tf_op jit(solution)/shard_map/dot_general | solution.py:126
  64.2 2.1 %collective-permute-start.3 = (f32[256,128]{1,0:T(8,128)S(1)}, f32[256,128]{1,0:T(8,128)S(1)}, u32[]{:S(2)}, u32[]{:S(2)}) collective-permute-start(f32[256,128]{1,0:T(8,128)S(1)} %fusion.5), channel_id=1, source_target_pairs={{0,8},{8,0},{16,24},{24,16},{1,9},{9,1},{17,25},{25,17},{2,10},{10... | collective-permute-start | bytes 393224 | tf_op jit(solution)/shard_map/ppermute | solution.py:25
  66.3 0.6 add_select_fusion
  66.9 5.8 %collective-permute-done.3 = f32[256,128]{1,0:T(8,128)S(1)} collective-permute-done((f32[256,128]{1,0:T(8,128)S(1)}, f32[256,128]{1,0:T(8,128)S(1)}, u32[]{:S(2)}, u32[]{:S(2)}) %collective-permute-start.3) | collective-permute-done | bytes 131104 | tf_op jit(solution)/shard_map/ppermute | solution.py:25
  72.7 1.5 %collective-permute-start.4 = (f32[256,128]{1,0:T(8,128)S(1)}, f32[256,128]{1,0:T(8,128)}, u32[]{:S(2)}, u32[]{:S(2)}) collective-permute-start(f32[256,128]{1,0:T(8,128)S(1)} %add.255), channel_id=1, source_target_pairs={{0,16},{8,24},{16,0},{24,8},{1,17},{9,25},{17,1},{25,9},{2,18},{10... | collective-permute-start | bytes 393224 | tf_op jit(solution)/shard_map/ppermute | solution.py:25
  74.3 0.6 broadcast_clamp_fusion.4
  74.9 8.4 %gather_fusion = bf16[1024,256]{1,0:T(8,128)(2,1)S(1)} fusion(bf16[16384,256]{1,0:T(8,128)(2,1)} %param.10, s32[1024]{0:T(1024)} %broadcast_clamp_fusion.4), kind=kCustom, calls=%fused_computation | custom fusion | bytes 1052672 | tf_op jit(solution)/shard_map/gather | solution.py:114
  83.3 0.9 add.256
  84.2 2.2 %all_gather.3 = f32[256,256]{1,0:T(8,128)S(1)} all-gather(f32[256,128]{1,0:T(8,128)S(1)} %add.256), channel_id=1, replica_groups=mesh['table'=4,'batch'=4,'ctx'=2] {'ctx'}, dimensions={1}, use_global_device_ids=true | all-gather | bytes 393216 | tf_op jit(solution)/shard_map/all_gather | solution.py:130
  86.4 0.0 collective-permute-done.2
  86.4 0.0 collective-permute-done.1
  86.5 1.5 %pad_maximum_fusion = bf16[4,1024,256]{2,1,0:T(8,128)(2,1)S(1)} fusion(bf16[1,1024,256]{2,1,0:T(8,128)(2,1)S(1)} %bitcast.130, bf16[1,1024,256]{2,1,0:T(8,128)(2,1)} %bitcast.10, bf16[1,1024,256]{2,1,0:T(8,128)(2,1)} %bitcast.7, bf16[1,1024,256]{2,1,0:T(8,128)(2,1)S(1)} %bitcast.129), kind=kLoop, calls=%fused_computation.16 | loop fusion | flops 3145728 | bytes 4194304 | tf_op jit(solution)/shard_map/stack | solution.py:134
  88.0 5.9 %fusion.9 = bf16[2048,256]{1,0:T(8,128)(2,1)S(1)} fusion(bf16[4096,256]{1,0:T(8,128)(2,1)S(1)} %bitcast.128, s32[2048]{0:T(1024)S(1)} %copy-done.7, bf16[2048,256]{1,0:T(8,128)(2,1)S(1)} %copy-done.1), kind=kOutput, calls=%fused_computation.15 | convolution fusion | flops 4304928768 | bytes 4202496 | tf_op jit(solution)/shard_map/dot_general | solution.py:139
  93.9 0.5 fusion.59
  94.5 0.9 fusion.28
  95.4 0.5 fusion.61
  95.9 0.4 multiply_reduce_fusion.3
  96.3 0.2 multiply_reduce_fusion.2
  96.5 0.1 fusion.23
  96.6 0.9 fusion.26
  97.5 0.5 fusion.62
  98.1 0.4 multiply_reduce_fusion.1
  98.5 0.2 multiply_reduce_fusion
  98.7 0.1 multiply_add_fusion
  98.7 0.9 fusion.24
  99.7 0.5 fusion.63
  100.2 0.4 fusion.16
  100.6 0.3 fusion.15
  100.9 11.6 %all_to_all.11 = f32[32,2,384]{2,1,0:T(2,128)S(1)} all-to-all(f32[32,2,384]{2,1,0:T(2,128)S(1)} %bitcast.131), channel_id=1, replica_groups=mesh['table'=4,'batch'=4,'ctx'=2] {'table','batch','ctx'}, dimensions={0} | all-to-all | bytes 196608 | tf_op jit(solution)/shard_map/all_to_all | solution.py:169
  112.5 0.1 reshape.482
  112.6 0.1 fusion.19
  112.7 0.1 convert_reduce_fusion
  112.8 1.3 %fusion.10 = bf16[1024,256]{1,0:T(8,128)(2,1)} fusion(bf16[1024,256]{1,0:T(8,128)(2,1)S(1)} %copy-done.2, pred[1024]{0:T(1024)(128)(4,1)S(1)} %broadcast_compare_fusion, s32[64]{0:T(128)S(1)} %fusion.19, f32[64,384]{1,0:T(8,128)S(1)} %reshape.482), kind=kOutput, calls=%fused_computation.18 | convolution fusion | flops 34144256 | bytes 1082880 | tf_op jit(solution)/shard_map/dot_general | solution.py:176
  (57 shorter events, 0.4 us)
Async XLA Ops:
  0.0 14.4 %copy-start = (bf16[4096,256]{1,0:T(8,128)(2,1)S(1)}, bf16[4096,256]{1,0:T(8,128)(2,1)}, u32[]{:S(2)}) copy-start(bf16[4096,256]{1,0:T(8,128)(2,1)} %param.11) | copy-start | bytes 6291460
  0.0 14.3 %copy-start.6 = (s32[32,64]{1,0:T(8,128)S(1)}, s32[32,64]{1,0:T(8,128)}, u32[]{:S(2)}) copy-start(s32[32,64]{1,0:T(8,128)} %param.15) | copy-start | bytes 24580
  8.5 18.0 %all-to-all-start = ((s32[4,1,1024]{2,1,0:T(1,128)}), s32[4,1,1024]{2,1,0:T(1,128)S(1)}, u32[]{:S(2)}, u32[]{:S(2)}) async-start(s32[4,1,1024]{2,1,0:T(1,128)} %copy.19), calls=%async_computation | async-start | bytes 32768 | tf_op jit(solution)/shard_map/all_to_all | solution.py:112
  14.4 0.8 copy-start.8
  15.5 0.6 copy-start.9
  35.6 50.8 %collective-permute-start.2 = (bf16[1024,256]{1,0:T(8,128)(2,1)}, bf16[1024,256]{1,0:T(8,128)(2,1)S(1)}, u32[]{:S(2)}, u32[]{:S(2)}) collective-permute-start(bf16[1024,256]{1,0:T(8,128)(2,1)} %gather_fusion.3), channel_id=1, source_target_pairs={{0,24},{8,16},{16,8},{24,0},{1,25},{9,17},{17,9},{25,1},{2,26},{10... | collective-permute-start | bytes 1572872 | tf_op jit(solution)/shard_map/ppermute | solution.py:121
  47.5 38.9 %collective-permute-start.1 = (bf16[1024,256]{1,0:T(8,128)(2,1)}, bf16[1024,256]{1,0:T(8,128)(2,1)}, u32[]{:S(2)}, u32[]{:S(2)}) collective-permute-start(bf16[1024,256]{1,0:T(8,128)(2,1)} %gather_fusion.2), channel_id=1, source_target_pairs={{0,16},{8,24},{16,0},{24,8},{1,17},{9,25},{17,1},{25,9},{2,18},{10... | collective-permute-start | bytes 1572872 | tf_op jit(solution)/shard_map/ppermute | solution.py:121
  57.1 9.1 %copy-start.3 = (s32[32,64]{1,0:T(8,128)S(1)}, s32[32,64]{1,0:T(8,128)}, u32[]{:S(2)}) copy-start(s32[32,64]{1,0:T(8,128)} %param.16) | copy-start | bytes 24580
  57.1 29.3 %collective-permute-start = (bf16[1024,256]{1,0:T(8,128)(2,1)}, bf16[1024,256]{1,0:T(8,128)(2,1)}, u32[]{:S(2)}, u32[]{:S(2)}) collective-permute-start(bf16[1024,256]{1,0:T(8,128)(2,1)} %gather_fusion.1), channel_id=1, source_target_pairs={{0,8},{8,0},{16,24},{24,16},{1,9},{9,1},{17,25},{25,17},{2,10},{10... | collective-permute-start | bytes 1572872 | tf_op jit(solution)/shard_map/ppermute | solution.py:121
  64.2 8.5 %collective-permute-start.3 = (f32[256,128]{1,0:T(8,128)S(1)}, f32[256,128]{1,0:T(8,128)S(1)}, u32[]{:S(2)}, u32[]{:S(2)}) collective-permute-start(f32[256,128]{1,0:T(8,128)S(1)} %fusion.5), channel_id=1, source_target_pairs={{0,8},{8,0},{16,24},{24,16},{1,9},{9,1},{17,25},{25,17},{2,10},{10... | collective-permute-start | bytes 393224 | tf_op jit(solution)/shard_map/ppermute | solution.py:25
  72.7 10.5 %collective-permute-start.4 = (f32[256,128]{1,0:T(8,128)S(1)}, f32[256,128]{1,0:T(8,128)}, u32[]{:S(2)}, u32[]{:S(2)}) collective-permute-start(f32[256,128]{1,0:T(8,128)S(1)} %add.255), channel_id=1, source_target_pairs={{0,16},{8,24},{16,0},{24,8},{1,17},{9,25},{17,1},{25,9},{2,18},{10... | collective-permute-start | bytes 393224 | tf_op jit(solution)/shard_map/ppermute | solution.py:25
  86.4 1.6 %copy-start.1 = (bf16[2048,256]{1,0:T(8,128)(2,1)S(1)}, bf16[2048,256]{1,0:T(8,128)(2,1)}, u32[]{:S(2)}) copy-start(bf16[2048,256]{1,0:T(8,128)(2,1)} %gather_fusion.4) | copy-start | bytes 3145732
  86.4 1.6 %copy-start.7 = (s32[2048]{0:T(1024)S(1)}, s32[2048]{0:T(1024)}, u32[]{:S(2)}) copy-start(s32[2048]{0:T(1024)} %get-tuple-element.32) | copy-start | bytes 24580
  88.0 5.9 %copy-start.4 = (f32[32,64]{1,0:T(8,128)S(1)}, f32[32,64]{1,0:T(8,128)}, u32[]{:S(2)}) copy-start(f32[32,64]{1,0:T(8,128)} %add_select_fusion) | copy-start | bytes 24580
  98.1 2.5 %copy-start.10 = (s32[32]{0:T(128)S(1)}, s32[32]{0:T(128)}, u32[]{:S(2)}) copy-start(s32[32]{0:T(128)} %copy-done.9) | copy-start | bytes 388
  98.1 2.8 %copy-start.5 = (f32[32,1]{1,0:T(8,128)S(1)}, f32[32,1]{1,0:T(8,128)}, u32[]{:S(2)}) copy-start(f32[32,1]{1,0:T(8,128)} %convert_select_fusion) | copy-start | bytes 388
  98.4 14.4 %copy-start.2 = (bf16[1024,256]{1,0:T(8,128)(2,1)S(1)}, bf16[1024,256]{1,0:T(8,128)(2,1)}, u32[]{:S(2)}) copy-start(bf16[1024,256]{1,0:T(8,128)(2,1)} %param.12) | copy-start | bytes 1572868

commit v8 on v6

--- a/solution.py
+++ b/solution.py
@@ -112,7 +112,9 @@
     ).reshape(n_table, 2, capacity)
     row_requests = placed[:, 0].astype(jnp.int32) * 128 + placed[:, 1].astype(jnp.int32)
     context_flat = context_id.reshape(flat_count)
-    served = item_table[lax.all_to_all(row_requests, "table", split_axis=0, concat_axis=0, tiled=True)]
+    every_request = lax.all_gather(row_requests, "table", axis=0, tiled=False)
+    requests_in = lax.dynamic_index_in_dim(every_request, lax.axis_index("table"), axis=1, keepdims=False)
+    served = item_table[requests_in]
     gram_source, served = lax.optimization_barrier((item_table, served))
     rank_width = item_table.shape[1]
     ctx_index = lax.axis_index("ctx")

time: 105 us -> 104 us (level)
  blocking collectives: 14.6 us -> 24.3 us
  waiting for transfers between devices: 13.7 us -> 8.44 us
  starting transfers between devices: 13.2 us -> 8 us
    all_gather x0 -> x1, blocking collectives: none -> 9.69 us  [per_device(): every_request = lax.all_gather(row_requests, 'table', axis=0, tiled=False)]
    all_to_all x1 -> x0, starting transfers between devices: 5.17 us -> none  [per_device(): lax.all_to_all(row_requests, 'table', split_axis=0, concat_axis=0, tiled=...]
    all_to_all x1 -> x0, waiting for transfers between devices: 4.03 us -> none  [per_device(): lax.all_to_all(row_requests, 'table', split_axis=0, concat_axis=0, tiled=...]
    ppermute x2, waiting for transfers between devices: 9.71 us -> 8.44 us  [butterfly_sum(): value = value + lax.ppermute(value, name, pairs)]
  transfers between devices with their start and end apart: 4 -> 3, of which waited for: 3 -> 2; matrix products, arithmetic and copies ran while one was open for 18% -> 18% of each run, Pallas kernels for 0% -> 0%
where the time goes in v8:
time: 104 us
  local copies, waits for them, and re-layouts  32.3 us (31%)
  matrix products  24.7 us (24%)
  blocking collectives  24.3 us (23%)
  waiting for transfers between devices  8.44 us (8%)
  starting transfers between devices  8 us (8%)
  other arithmetic  5.65 us (5%)
    gather x1, local copies, waits for them, and re-layouts, per_device(): served = item_table[requests_in]  20.3 us
    all_to_all x1, blocking collectives, per_device(): lax.all_to_all(payload, ('table', 'batch', 'ctx'), split_axis=0, concat_a...  12.5 us
    all_gather x1, blocking collectives, per_device(): every_request = lax.all_gather(row_requests, 'table', axis=0, tiled=False)  9.69 us
    gather x1, local copies, waits for them, and re-layouts, per_device(): context_table[context_flat].astype(jnp.float32)  9 us
    ppermute x2, waiting for transfers between devices, butterfly_sum(): value = value + lax.ppermute(value, name, pairs)  8.44 us
    dot_general x1, matrix products, per_device(): jnp.dot(placing, fetched.reshape(n_table * capacity, rank_width), preferr...  7.56 us
    dot_general x1, matrix products, per_device(): lax.dot_general(gram_source, own_columns, (((0,), (0,)), ((), ())), prefe...  6.97 us
    all_to_all x1, starting transfers between devices, per_device(): lax.all_to_all(served, 'table', split_axis=0, concat_axis=0, tiled=True)  4.44 us
  transfers between devices with their start and end apart: 3, of which 2 were waited for; matrix products, arithmetic and copies ran while one was open for 18% of the time, Pallas kernels for 0%

profile of v8, /device:TPU:0, one launch (start us, length us, event | category | flops | bytes accessed | tf_op | source)
XLA Modules:
  0.0 103.7 jit_solution(15343930783688488885)
XLA Ops:
  0.0 0.0 copy-start
  0.0 0.9 eq.113
  0.9 1.1 %reduce-window.6 = s32[4,16,128]{2,1,0:T(8,128)S(1)} reduce-window(s32[4,16,128]{2,1,0:T(8,128)S(1)} %fusion.32, s32[]{:T(128)} %constant.134.clone.1), window={size=1x1x128 pad=0_0x0_0x127_0}, to_apply=%region_2.3 | reduce-window | flops 1040384 | bytes 65540 | tf_op jit(solution)/shard_map/reduce-window
  2.1 0.2 slice_reduce_fusion
  2.3 0.2 reduce-window.9
  2.5 0.1 select_reduce_fusion
  2.6 0.5 broadcast.390
  3.1 1.4 %reduce.19 = s32[32,64]{1,0:T(8,128)S(1)} reduce(s32[32,64,1]{1,2,0:T(1,128)} %param.13, s32[]{:T(128)} %broadcast.390), dimensions={2}, to_apply=%param.13.reduce_sub_computation.5 | reduce | bytes 16388 | tf_op args[3]
  4.5 0.1 reshape.406
  4.6 0.8 reshape.408
  5.5 1.7 %fusion.3 = f32[4,2,1024]{2,0,1:T(4,128)S(1)} fusion(s32[2048]{0:T(1024)S(1)} %get-tuple-element.29, s32[2,2048]{1,0:T(2,128)S(1)} %pad_add_fusion, pred[4,2048]{1,0:T(4,128)(4,1)S(1)} %iota_compare_fusion.10), kind=kOutput, calls=%fused_computation.7 | convolution fusion | flops 35684352 | bytes 65536 | tf_op jit(solution)/shard_map/dot_general | solution.py:109
  7.3 9.7 %all-gather = s32[16,1,1024]{2,1,0:T(1,128)S(1)} all-gather(s32[4,1,1024]{2,1,0:T(1,128)S(1)} %copy.19), channel_id=2, replica_groups=mesh['table'=4,'batch'=4,'ctx'=2] {'table'}, dimensions={0}, use_global_device_ids=true | all-gather | bytes 81920 | tf_op jit(solution)/shard_map/all_gather | solution.py:115
  17.0 0.2 reduce.11
  17.2 20.3 %gather_fusion = bf16[4096,256]{1,0:T(8,128)(2,1)} fusion(bf16[16384,256]{1,0:T(8,128)(2,1)} %param.10, s32[4096]{0:T(1024)S(1)} %broadcast_clamp_fusion), kind=kCustom, calls=%fused_computation | custom fusion | bytes 4210688 | tf_op jit(solution)/shard_map/gather | solution.py:117
  37.5 4.4 %all-to-all-start = ((bf16[4,1024,256]{2,1,0:T(8,128)(2,1)}), bf16[4,1024,256]{2,1,0:T(8,128)(2,1)}, u32[]{:S(2)}, u32[]{:S(2)}) async-start(bf16[4,1024,256]{2,1,0:T(8,128)(2,1)} %bitcast.111), calls=%async_computation | async-start | bytes 4194304 | tf_op jit(solution)/shard_map/all_to_all | solution.py:131
  42.0 0.0 copy-start.4
  42.0 0.0 copy-start.3
  42.0 7.0 %fusion.5 = f32[256,128]{1,0:T(8,128)S(1)} fusion(bf16[16384,256]{1,0:T(8,128)(2,1)} %param.10, s32[]{:T(128)S(6)} %select_n.111), kind=kOutput, calls=%fused_computation.8 | convolution fusion | flops 1073741824 | bytes 12713988 | tf_op jit(solution)/shard_map/dot_general | solution.py:123
  49.0 2.0 %collective-permute-start = (f32[256,128]{1,0:T(8,128)S(1)}, f32[256,128]{1,0:T(8,128)S(1)}, u32[]{:S(2)}, u32[]{:S(2)}) collective-permute-start(f32[256,128]{1,0:T(8,128)S(1)} %fusion.5), channel_id=1, source_target_pairs={{0,8},{8,0},{16,24},{24,16},{1,9},{9,1},{17,25},{25,17},{2,10},{10... | collective-permute-start | bytes 393224 | tf_op jit(solution)/shard_map/ppermute | solution.py:25
  51.0 0.0 copy-done.4
  51.0 0.2 reduce_window_sum.24
  51.3 0.1 convert_reduce_fusion.1
  51.4 0.2 fusion.42
  51.6 0.1 copy.20
  51.7 0.1 copy.21
  51.8 0.0 copy-done.3
  51.8 0.1 reshape.410
  51.9 0.0 copy-done
  51.9 9.0 %gather_fusion.1 = bf16[2048,256]{1,0:T(8,128)(2,1)} fusion(bf16[4096,256]{1,0:T(8,128)(2,1)S(1)} %copy-done, s32[2048]{0:T(1024)S(1)} %broadcast_clamp_fusion.1), kind=kCustom, calls=%fused_computation.1 | custom fusion | bytes 2105344 | tf_op jit(solution)/shard_map/gather | solution.py:141
  60.9 0.6 compare_reduce_fusion
  61.5 0.0 copy-start.2
  61.5 0.7 fusion.60
  62.3 0.7 convert_select_fusion
  62.9 4.9 %collective-permute-done = f32[256,128]{1,0:T(8,128)S(1)} collective-permute-done((f32[256,128]{1,0:T(8,128)S(1)}, f32[256,128]{1,0:T(8,128)S(1)}, u32[]{:S(2)}, u32[]{:S(2)}) %collective-permute-start) | collective-permute-done | bytes 131104 | tf_op jit(solution)/shard_map/ppermute | solution.py:25
  67.9 1.5 %collective-permute-start.1 = (f32[256,128]{1,0:T(8,128)S(1)}, f32[256,128]{1,0:T(8,128)S(1)}, u32[]{:S(2)}, u32[]{:S(2)}) collective-permute-start(f32[256,128]{1,0:T(8,128)S(1)} %add.211), channel_id=1, source_target_pairs={{0,16},{8,24},{16,0},{24,8},{1,17},{9,25},{17,1},{25,9},{2,18},{10... | collective-permute-start | bytes 393224 | tf_op jit(solution)/shard_map/ppermute | solution.py:25
  69.4 0.0 copy-done.2
  69.4 3.5 %collective-permute-done.1 = f32[256,128]{1,0:T(8,128)S(1)} collective-permute-done((f32[256,128]{1,0:T(8,128)S(1)}, f32[256,128]{1,0:T(8,128)S(1)}, u32[]{:S(2)}, u32[]{:S(2)}) %collective-permute-start.1) | collective-permute-done | bytes 131104 | tf_op jit(solution)/shard_map/ppermute | solution.py:25
  72.9 2.2 %all_gather.8 = f32[256,256]{1,0:T(8,128)S(1)} all-gather(f32[256,128]{1,0:T(8,128)S(1)} %add.212), channel_id=1, replica_groups=mesh['table'=4,'batch'=4,'ctx'=2] {'ctx'}, dimensions={1}, use_global_device_ids=true | all-gather | bytes 393216 | tf_op jit(solution)/shard_map/all_gather | solution.py:127
  75.1 0.0 all-to-all-done
  75.1 7.6 %fusion.9 = bf16[2048,256]{1,0:T(8,128)(2,1)S(1)} fusion(bf16[4096,256]{1,0:T(8,128)(2,1)} %bitcast.5, s32[2048]{0:T(1024)S(1)} %get-tuple-element.30, bf16[2048,256]{1,0:T(8,128)(2,1)} %gather_fusion.1), kind=kOutput, calls=%fused_computation.12 | convolution fusion | flops 4304928768 | bytes 4202496 | tf_op jit(solution)/shard_map/dot_general | solution.py:138
  82.7 0.5 fusion.59
  83.2 0.9 fusion.28
  84.2 0.5 fusion.61
  84.7 0.4 multiply_reduce_fusion.3
  85.1 0.2 multiply_reduce_fusion.2
  85.3 0.1 fusion.23
  85.4 0.9 fusion.26
  86.3 0.5 fusion.62
  86.8 0.4 multiply_reduce_fusion.1
  87.2 0.0 copy-start.1
  87.2 0.2 multiply_reduce_fusion
  87.4 0.1 multiply_add_fusion
  87.5 0.9 fusion.24
  88.4 0.5 fusion.63
  89.0 0.4 fusion.16
  89.3 0.3 fusion.15
  89.7 12.5 %all_to_all.10 = f32[32,2,384]{2,1,0:T(2,128)S(1)} all-to-all(f32[32,2,384]{2,1,0:T(2,128)S(1)} %bitcast.112), channel_id=1, replica_groups=mesh['table'=4,'batch'=4,'ctx'=2] {'table','batch','ctx'}, dimensions={0} | all-to-all | bytes 196608 | tf_op jit(solution)/shard_map/all_to_all | solution.py:168
  102.1 0.1 reshape.413
  102.2 0.1 fusion.19
  102.3 0.1 convert_reduce_fusion
  102.5 0.0 copy-done.1
  102.5 1.3 %fusion.10 = bf16[1024,256]{1,0:T(8,128)(2,1)} fusion(bf16[1024,256]{1,0:T(8,128)(2,1)S(1)} %copy-done.1, pred[1024]{0:T(1024)(128)(4,1)S(1)} %broadcast_compare_fusion, s32[64]{0:T(128)S(1)} %fusion.19, f32[64,384]{1,0:T(8,128)S(1)} %reshape.413), kind=kOutput, calls=%fused_computation.14 | convolution fusion | flops 34144256 | bytes 1082880 | tf_op jit(solution)/shard_map/dot_general | solution.py:175
  (37 shorter events, 0.5 us)
Async XLA Ops:
  0.0 51.9 %copy-start = (bf16[4096,256]{1,0:T(8,128)(2,1)S(1)}, bf16[4096,256]{1,0:T(8,128)(2,1)}, u32[]{:S(2)}) copy-start(bf16[4096,256]{1,0:T(8,128)(2,1)} %param.11) | copy-start | bytes 6291460
  37.5 37.6 %all-to-all-start = ((bf16[4,1024,256]{2,1,0:T(8,128)(2,1)}), bf16[4,1024,256]{2,1,0:T(8,128)(2,1)}, u32[]{:S(2)}, u32[]{:S(2)}) async-start(bf16[4,1024,256]{2,1,0:T(8,128)(2,1)} %bitcast.111), calls=%async_computation | async-start | bytes 4194304 | tf_op jit(solution)/shard_map/all_to_all | solution.py:131
  42.0 9.0 %copy-start.4 = (s32[32]{0:T(128)S(1)}, s32[32]{0:T(128)}, u32[]{:S(2)}) copy-start(s32[32]{0:T(128)} %param.17) | copy-start | bytes 388
  42.0 9.8 %copy-start.3 = (s32[32,64]{1,0:T(8,128)S(1)}, s32[32,64]{1,0:T(8,128)}, u32[]{:S(2)}) copy-start(s32[32,64]{1,0:T(8,128)} %param.15) | copy-start | bytes 24580
  49.0 18.9 %collective-permute-start = (f32[256,128]{1,0:T(8,128)S(1)}, f32[256,128]{1,0:T(8,128)S(1)}, u32[]{:S(2)}, u32[]{:S(2)}) collective-permute-start(f32[256,128]{1,0:T(8,128)S(1)} %fusion.5), channel_id=1, source_target_pairs={{0,8},{8,0},{16,24},{24,16},{1,9},{9,1},{17,25},{25,17},{2,10},{10... | collective-permute-start | bytes 393224 | tf_op jit(solution)/shard_map/ppermute | solution.py:25
  61.5 7.9 %copy-start.2 = (s32[32,64]{1,0:T(8,128)S(1)}, s32[32,64]{1,0:T(8,128)}, u32[]{:S(2)}) copy-start(s32[32,64]{1,0:T(8,128)} %param.16) | copy-start | bytes 24580
  67.9 5.0 %collective-permute-start.1 = (f32[256,128]{1,0:T(8,128)S(1)}, f32[256,128]{1,0:T(8,128)S(1)}, u32[]{:S(2)}, u32[]{:S(2)}) collective-permute-start(f32[256,128]{1,0:T(8,128)S(1)} %add.211), channel_id=1, source_target_pairs={{0,16},{8,24},{16,0},{24,8},{1,17},{9,25},{17,1},{25,9},{2,18},{10... | collective-permute-start | bytes 393224 | tf_op jit(solution)/shard_map/ppermute | solution.py:25
  87.2 15.3 %copy-start.1 = (bf16[1024,256]{1,0:T(8,128)(2,1)S(1)}, bf16[1024,256]{1,0:T(8,128)(2,1)}, u32[]{:S(2)}) copy-start(bf16[1024,256]{1,0:T(8,128)(2,1)} %param.12) | copy-start | bytes 1572868

commit v9 on v8

--- a/solution.py
+++ b/solution.py
@@ -17,12 +17,13 @@
     )
 
 
-def butterfly_sum(value, axes):
+def butterfly_sum(value, axes, sent_type=None):
     for name, size in axes:
         step = 1
         while step < size:
             pairs = [(i, i ^ step) for i in range(size)]
-            value = value + lax.ppermute(value, name, pairs)
+            sent = value if sent_type is None else value.astype(sent_type)
+            value = value + lax.ppermute(sent, name, pairs).astype(value.dtype)
             step *= 2
     return value
 
@@ -116,15 +117,10 @@
     requests_in = lax.dynamic_index_in_dim(every_request, lax.axis_index("table"), axis=1, keepdims=False)
     served = item_table[requests_in]
     gram_source, served = lax.optimization_barrier((item_table, served))
-    rank_width = item_table.shape[1]
-    ctx_index = lax.axis_index("ctx")
-    width = rank_width // n_ctx
-    own_columns = lax.dynamic_slice_in_dim(gram_source, ctx_index * width, width, axis=1)
-    column_gram = lax.dot_general(
-        gram_source, own_columns, (((0,), (0,)), ((), ())), preferred_element_type=jnp.float32
-    )
-    column_gram = butterfly_sum(column_gram, (("table", n_table),))
-    item_gram = lax.all_gather(column_gram, "ctx", axis=1, tiled=True)
+    share = gram_source.shape[0] // n_ctx
+    own_rows = lax.dynamic_slice_in_dim(gram_source, lax.axis_index("ctx") * share, share, axis=0)
+    item_gram = butterfly_sum(gram_of(own_rows), (("ctx", n_ctx),))
+    item_gram = butterfly_sum(item_gram, (("table", n_table),), jnp.bfloat16)
     context_gram = gram_of(context_table)
     pair_count = item_table.shape[0] * n_table * context_table.shape[0]
     gram_matrix = item_gram * context_gram / pair_count

time: 104 us -> 102 us (0.981)
  waiting for transfers between devices: 8.44 us -> 11.1 us
  matrix products: 24.7 us -> 22.3 us
  blocking collectives: 24.3 us -> 22.2 us
  local copies, waits for them, and re-layouts: 32.3 us -> 30.8 us
  other arithmetic: 5.65 us -> 6.7 us
    dot_general x1 -> x0, matrix products: 6.97 us -> none  [per_device(): lax.dot_general(gram_source, own_columns, (((0,), (0,)), ((), ())), prefe...]
    dot_general x1 -> x2, matrix products: 0.74 us -> 5.49 us  [gram_of(): lax.dot_general(table_rows, table_rows, (((0,), (0,)), ((), ())), preferr...]
    ppermute x2 -> x3, waiting for transfers between devices: 8.44 us -> 11.1 us  [butterfly_sum(): value = value + lax.ppermute(sent, name, pairs).astype(value.dtype)]
    all_gather x1 -> x0, blocking collectives: 2.17 us -> none  [per_device(): item_gram = lax.all_gather(column_gram, 'ctx', axis=1, tiled=True)]
    gather x1, local copies, waits for them, and re-layouts: 9 us -> 7.49 us  [per_device(): context_table[context_flat].astype(jnp.float32)]
    ppermute x2 -> x3, starting transfers between devices: 3.56 us -> 3.45 us  [butterfly_sum(): value = value + lax.ppermute(sent, name, pairs).astype(value.dtype)]
  transfers between devices with their start and end apart: 3 -> 4, of which waited for: 2 -> 2; matrix products, arithmetic and copies ran while one was open for 18% -> 16% of each run, Pallas kernels for 0% -> 0%
where the time goes in v9:
time: 102 us; the launch traced here: 101 us
  local copies, waits for them, and re-layouts  30.8 us (30%)
  matrix products  22.3 us (22%)
  blocking collectives  22.2 us (22%)
  waiting for transfers between devices  11.1 us (11%)
  starting transfers between devices  8.07 us (8%)
  other arithmetic  6.7 us (7%)
    gather x1, local copies, waits for them, and re-layouts, per_device(): served = item_table[requests_in]  20.3 us
    all_to_all x1, blocking collectives, per_device(): lax.all_to_all(payload, ('table', 'batch', 'ctx'), split_axis=0, concat_a...  12.5 us
    ppermute x3, waiting for transfers between devices, butterfly_sum(): value = value + lax.ppermute(sent, name, pairs).astype(value.dtype)  11.1 us
    all_gather x1, blocking collectives, per_device(): every_request = lax.all_gather(row_requests, 'table', axis=0, tiled=False)  9.69 us
    gather x1, local copies, waits for them, and re-layouts, per_device(): context_table[context_flat].astype(jnp.float32)  7.49 us
    dot_general x1, matrix products, per_device(): jnp.dot(placing, fetched.reshape(n_table * capacity, rank_width), preferr...  7.39 us
    dot_general x2, matrix products, gram_of(): lax.dot_general(table_rows, table_rows, (((0,), (0,)), ((), ())), preferr...  5.49 us
    all_to_all x1, starting transfers between devices, per_device(): lax.all_to_all(served, 'table', split_axis=0, concat_axis=0, tiled=True)  4.62 us
  transfers between devices with their start and end apart: 4, of which 2 were waited for; matrix products, arithmetic and copies ran while one was open for 16% of the time, Pallas kernels for 0%

profile of v9, /device:TPU:0, one launch (start us, length us, event | category | flops | bytes accessed | tf_op | source)
XLA Modules:
  0.0 101.4 jit_solution(3218163709440946115)
XLA Ops:
  0.0 0.0 copy-start
  0.0 0.9 eq.113
  0.9 1.1 %reduce-window.6 = s32[4,16,128]{2,1,0:T(8,128)S(1)} reduce-window(s32[4,16,128]{2,1,0:T(8,128)S(1)} %fusion.33, s32[]{:T(128)} %constant.135.clone.1), window={size=1x1x128 pad=0_0x0_0x127_0}, to_apply=%region_2.3 | reduce-window | flops 1040384 | bytes 65540 | tf_op jit(solution)/shard_map/reduce-window
  2.1 0.2 slice_reduce_fusion
  2.3 0.2 reduce-window.9
  2.5 0.1 select_reduce_fusion
  2.6 0.5 broadcast.390
  3.1 1.4 %reduce.19 = s32[32,64]{1,0:T(8,128)S(1)} reduce(s32[32,64,1]{1,2,0:T(1,128)} %param.13, s32[]{:T(128)} %broadcast.390), dimensions={2}, to_apply=%param.13.reduce_sub_computation.5 | reduce | bytes 16388 | tf_op args[3]
  4.5 0.1 reshape.406
  4.6 0.8 reshape.408
  5.5 1.7 %fusion.3 = f32[4,2,1024]{2,0,1:T(4,128)S(1)} fusion(s32[2048]{0:T(1024)S(1)} %get-tuple-element.31, s32[2,2048]{1,0:T(2,128)S(1)} %pad_add_fusion, pred[4,2048]{1,0:T(4,128)(4,1)S(1)} %iota_compare_fusion.10), kind=kOutput, calls=%fused_computation.7 | convolution fusion | flops 35684352 | bytes 65536 | tf_op jit(solution)/shard_map/dot_general | solution.py:110
  7.3 9.7 %all-gather = s32[16,1,1024]{2,1,0:T(1,128)S(1)} all-gather(s32[4,1,1024]{2,1,0:T(1,128)S(1)} %copy.19), channel_id=2, replica_groups=mesh['table'=4,'batch'=4,'ctx'=2] {'table'}, dimensions={0}, use_global_device_ids=true | all-gather | bytes 81920 | tf_op jit(solution)/shard_map/all_gather | solution.py:116
  17.0 0.2 reduce.11
  17.2 20.3 %gather_fusion = bf16[4096,256]{1,0:T(8,128)(2,1)} fusion(bf16[16384,256]{1,0:T(8,128)(2,1)} %param.10, s32[4096]{0:T(1024)S(1)} %broadcast_clamp_fusion), kind=kCustom, calls=%fused_computation | custom fusion | bytes 4210688 | tf_op jit(solution)/shard_map/gather | solution.py:118
  37.5 4.6 %all-to-all-start = ((bf16[4,1024,256]{2,1,0:T(8,128)(2,1)}), bf16[4,1024,256]{2,1,0:T(8,128)(2,1)}, u32[]{:S(2)}, u32[]{:S(2)}) async-start(bf16[4,1024,256]{2,1,0:T(8,128)(2,1)} %bitcast.113), calls=%async_computation | async-start | bytes 4194304 | tf_op jit(solution)/shard_map/all_to_all | solution.py:127
  42.1 0.0 copy-start.4
  42.1 0.0 copy-start.3
  42.2 4.8 %fusion.5 = f32[256,256]{1,0:T(8,128)S(1)} fusion(bf16[16384,256]{1,0:T(8,128)(2,1)} %param.10, s32[]{:T(128)S(6)} %select_n.111), kind=kOutput, calls=%fused_computation.8 | convolution fusion | flops 1073741824 | bytes 4456452 | tf_op jit(solution)/shard_map/dot_general | solution.py:15
  46.9 0.1 collective-permute-start
  47.0 0.0 copy-done.4
  47.1 0.2 reduce_window_sum.24
  47.3 0.1 convert_reduce_fusion.1
  47.4 0.2 fusion.43
  47.6 0.0 copy-done.3
  47.6 0.1 reshape.410
  47.7 0.1 copy.20
  47.8 0.1 copy.21
  47.9 0.0 copy-done
  47.9 7.5 %gather_fusion.1 = bf16[2048,256]{1,0:T(8,128)(2,1)S(1)} fusion(bf16[4096,256]{1,0:T(8,128)(2,1)S(1)} %copy-done, s32[2048]{0:T(1024)S(1)} %broadcast_clamp_fusion.1), kind=kCustom, calls=%fused_computation.1 | custom fusion | bytes 2105344 | tf_op jit(solution)/shard_map/gather | solution.py:137
  55.4 0.6 compare_reduce_fusion
  56.0 0.0 copy-start.2
  56.0 0.7 fusion.62
  56.8 0.0 collective-permute-done
  56.8 1.0 fusion.60
  57.8 1.8 %collective-permute-start.1 = (bf16[256,256]{1,0:T(8,128)(2,1)S(1)}, bf16[256,256]{1,0:T(8,128)(2,1)S(1)}, u32[]{:S(2)}, u32[]{:S(2)}) collective-permute-start(bf16[256,256]{1,0:T(8,128)(2,1)S(1)} %get-tuple-element.27), channel_id=1, source_target_pairs={{0,8},{8,0},{16,24},{24,16},{1,9},{9,1},{17,25},{25,17},{2,10},{10... | collective-permute-start | bytes 393224 | tf_op jit(solution)/shard_map/ppermute | solution.py:26
  59.6 0.7 convert_select_fusion
  60.3 7.6 %collective-permute-done.1 = bf16[256,256]{1,0:T(8,128)(2,1)S(1)} collective-permute-done((bf16[256,256]{1,0:T(8,128)(2,1)S(1)}, bf16[256,256]{1,0:T(8,128)(2,1)S(1)}, u32[]{:S(2)}, u32[]{:S(2)}) %collective-permute-start.1) | collective-permute-done | bytes 131104 | tf_op jit(solution)/shard_map/ppermute | solution.py:26
  67.9 1.5 %collective-permute-start.2 = (bf16[256,256]{1,0:T(8,128)(2,1)S(1)}, bf16[256,256]{1,0:T(8,128)(2,1)S(1)}, u32[]{:S(2)}, u32[]{:S(2)}) collective-permute-start(bf16[256,256]{1,0:T(8,128)(2,1)S(1)} %fusion.18), channel_id=1, source_target_pairs={{0,16},{8,24},{16,0},{24,8},{1,17},{9,25},{17,1},{25,9},{2,18},{10... | collective-permute-start | bytes 393224 | tf_op jit(solution)/shard_map/ppermute | solution.py:26
  69.4 0.0 copy-done.2
  69.5 3.5 %collective-permute-done.2 = bf16[256,256]{1,0:T(8,128)(2,1)S(1)} collective-permute-done((bf16[256,256]{1,0:T(8,128)(2,1)S(1)}, bf16[256,256]{1,0:T(8,128)(2,1)S(1)}, u32[]{:S(2)}, u32[]{:S(2)}) %collective-permute-start.2) | collective-permute-done | bytes 131104 | tf_op jit(solution)/shard_map/ppermute | solution.py:26
  72.9 0.1 multiply_multiply_fusion
  73.0 0.0 all-to-all-done
  73.0 7.4 %fusion.9 = bf16[2048,256]{1,0:T(8,128)(2,1)S(1)} fusion(bf16[4096,256]{1,0:T(8,128)(2,1)} %bitcast.5, s32[2048]{0:T(1024)S(1)} %get-tuple-element.32, bf16[2048,256]{1,0:T(8,128)(2,1)S(1)} %gather_fusion.1), kind=kOutput, calls=%fused_computation.12 | convolution fusion | flops 4304928768 | bytes 4202496 | tf_op jit(solution)/shard_map/dot_general | solution.py:134
  80.4 0.5 fusion.61
  80.9 0.9 fusion.29
  81.9 0.5 fusion.63
  82.4 0.3 multiply_reduce_fusion.3
  82.8 0.2 multiply_reduce_fusion.2
  83.0 0.1 fusion.24
  83.1 0.9 fusion.27
  84.0 0.5 fusion.64
  84.5 0.3 multiply_reduce_fusion.1
  84.9 0.2 multiply_reduce_fusion
  85.1 0.1 multiply_add_fusion
  85.2 0.9 fusion.25
  86.1 0.5 fusion.65
  86.7 0.3 fusion.16
  87.0 0.3 fusion.15
  87.4 12.5 %all_to_all.10 = f32[32,2,384]{2,1,0:T(2,128)S(1)} all-to-all(f32[32,2,384]{2,1,0:T(2,128)S(1)} %bitcast.114), channel_id=1, replica_groups=mesh['table'=4,'batch'=4,'ctx'=2] {'table','batch','ctx'}, dimensions={0} | all-to-all | bytes 196608 | tf_op jit(solution)/shard_map/all_to_all | solution.py:164
  99.8 0.1 reshape.413
  99.9 0.1 fusion.20
  100.0 0.1 convert_reduce_fusion
  100.1 0.0 copy-done.1
  100.2 1.3 %fusion.10 = bf16[1024,256]{1,0:T(8,128)(2,1)} fusion(bf16[1024,256]{1,0:T(8,128)(2,1)S(1)} %copy-done.1, pred[1024]{0:T(1024)(128)(4,1)S(1)} %broadcast_compare_fusion, s32[64]{0:T(128)S(1)} %fusion.20, f32[64,384]{1,0:T(8,128)S(1)} %reshape.413), kind=kOutput, calls=%fused_computation.14 | convolution fusion | flops 34144256 | bytes 1082880 | tf_op jit(solution)/shard_map/dot_general | solution.py:171
  (37 shorter events, 0.5 us)
Async XLA Ops:
  0.0 47.9 %copy-start = (bf16[4096,256]{1,0:T(8,128)(2,1)S(1)}, bf16[4096,256]{1,0:T(8,128)(2,1)}, u32[]{:S(2)}) copy-start(bf16[4096,256]{1,0:T(8,128)(2,1)} %param.11) | copy-start | bytes 6291460
  37.5 35.5 %all-to-all-start = ((bf16[4,1024,256]{2,1,0:T(8,128)(2,1)}), bf16[4,1024,256]{2,1,0:T(8,128)(2,1)}, u32[]{:S(2)}, u32[]{:S(2)}) async-start(bf16[4,1024,256]{2,1,0:T(8,128)(2,1)} %bitcast.113), calls=%async_computation | async-start | bytes 4194304 | tf_op jit(solution)/shard_map/all_to_all | solution.py:127
  42.1 4.9 %copy-start.4 = (s32[32]{0:T(128)S(1)}, s32[32]{0:T(128)}, u32[]{:S(2)}) copy-start(s32[32]{0:T(128)} %param.17) | copy-start | bytes 388
  42.1 5.4 %copy-start.3 = (s32[32,64]{1,0:T(8,128)S(1)}, s32[32,64]{1,0:T(8,128)}, u32[]{:S(2)}) copy-start(s32[32,64]{1,0:T(8,128)} %param.15) | copy-start | bytes 24580
  46.9 9.9 %collective-permute-start = (f32[256,256]{1,0:T(8,128)S(1)}, f32[256,256]{1,0:T(8,128)}, u32[]{:S(2)}, u32[]{:S(2)}) collective-permute-start(f32[256,256]{1,0:T(8,128)S(1)} %fusion.5), channel_id=1, source_target_pairs={{0,1},{1,0},{2,3},{3,2},{4,5},{5,4},{6,7},{7,6},{8,9},{9,8},{10,11... | collective-permute-start | bytes 786440 | tf_op jit(solution)/shard_map/ppermute | solution.py:26
  56.0 13.4 %copy-start.2 = (s32[32,64]{1,0:T(8,128)S(1)}, s32[32,64]{1,0:T(8,128)}, u32[]{:S(2)}) copy-start(s32[32,64]{1,0:T(8,128)} %param.16) | copy-start | bytes 24580
  57.8 10.1 %collective-permute-start.1 = (bf16[256,256]{1,0:T(8,128)(2,1)S(1)}, bf16[256,256]{1,0:T(8,128)(2,1)S(1)}, u32[]{:S(2)}, u32[]{:S(2)}) collective-permute-start(bf16[256,256]{1,0:T(8,128)(2,1)S(1)} %get-tuple-element.27), channel_id=1, source_target_pairs={{0,8},{8,0},{16,24},{24,16},{1,9},{9,1},{17,25},{25,17},{2,10},{10... | collective-permute-start | bytes 393224 | tf_op jit(solution)/shard_map/ppermute | solution.py:26
  67.9 5.0 %collective-permute-start.2 = (bf16[256,256]{1,0:T(8,128)(2,1)S(1)}, bf16[256,256]{1,0:T(8,128)(2,1)S(1)}, u32[]{:S(2)}, u32[]{:S(2)}) collective-permute-start(bf16[256,256]{1,0:T(8,128)(2,1)S(1)} %fusion.18), channel_id=1, source_target_pairs={{0,16},{8,24},{16,0},{24,8},{1,17},{9,25},{17,1},{25,9},{2,18},{10... | collective-permute-start | bytes 393224 | tf_op jit(solution)/shard_map/ppermute | solution.py:26
  84.5 15.6 %copy-start.1 = (bf16[1024,256]{1,0:T(8,128)(2,1)S(1)}, bf16[1024,256]{1,0:T(8,128)(2,1)}, u32[]{:S(2)}) copy-start(bf16[1024,256]{1,0:T(8,128)(2,1)} %param.12) | copy-start | bytes 1572868

commit v10 on v9

--- a/solution.py
+++ b/solution.py
@@ -26,6 +26,15 @@
             value = value + lax.ppermute(sent, name, pairs).astype(value.dtype)
             step *= 2
     return value
+
+
+def exchange_sum(value, name, size, sent_type):
+    sent = value.astype(sent_type)
+    total = value
+    for k in range(1, size):
+        pairs = [(i, i ^ k) for i in range(size)]
+        total = total + lax.ppermute(sent, name, pairs).astype(value.dtype)
+    return total
 
 
 def owner_slots(owners, groups, capacity):
@@ -113,17 +122,24 @@
     ).reshape(n_table, 2, capacity)
     row_requests = placed[:, 0].astype(jnp.int32) * 128 + placed[:, 1].astype(jnp.int32)
     context_flat = context_id.reshape(flat_count)
-    every_request = lax.all_gather(row_requests, "table", axis=0, tiled=False)
-    requests_in = lax.dynamic_index_in_dim(every_request, lax.axis_index("table"), axis=1, keepdims=False)
-    served = item_table[requests_in]
-    gram_source, served = lax.optimization_barrier((item_table, served))
+    table_index = lax.axis_index("table")
+    by_offset = [lax.dynamic_index_in_dim(row_requests, table_index, keepdims=False)]
+    for k in range(1, n_table):
+        pairs = [(i, i ^ k) for i in range(n_table)]
+        outgoing = lax.dynamic_index_in_dim(row_requests, table_index ^ k, keepdims=False)
+        by_offset.append(lax.ppermute(outgoing, "table", pairs))
+    by_offset = jnp.stack(by_offset, axis=0)
+    requests_in = by_offset[jnp.arange(n_table, dtype=jnp.int32) ^ table_index]
+    gram_source = item_table
     share = gram_source.shape[0] // n_ctx
     own_rows = lax.dynamic_slice_in_dim(gram_source, lax.axis_index("ctx") * share, share, axis=0)
     item_gram = butterfly_sum(gram_of(own_rows), (("ctx", n_ctx),))
-    item_gram = butterfly_sum(item_gram, (("table", n_table),), jnp.bfloat16)
+    item_gram = exchange_sum(item_gram, "table", n_table, jnp.bfloat16)
     context_gram = gram_of(context_table)
     pair_count = item_table.shape[0] * n_table * context_table.shape[0]
     gram_matrix = item_gram * context_gram / pair_count
+    served = item_table[requests_in]
+    served, gram_matrix = lax.optimization_barrier((served, gram_matrix))
     fetched = lax.all_to_all(
         served,
         "table",

time: 102 us -> 101 us (level)
  blocking collectives: 22.2 us -> 12.5 us
  starting transfers between devices: 8.07 us -> 12.8 us
  waiting for transfers between devices: 11.1 us -> 15.7 us
  other arithmetic: 6.7 us -> 5.61 us
    all_to_all x1, waiting for transfers between devices: 0.01 us -> 15.7 us  [per_device(): lax.all_to_all(served, 'table', split_axis=0, concat_axis=0, tiled=True)]
    ppermute x3 -> x1, waiting for transfers between devices: 11.1 us -> 0.01 us  [butterfly_sum(): value = value + lax.ppermute(sent, name, pairs).astype(value.dtype)]
    all_gather x1 -> x0, blocking collectives: 9.69 us -> none  [per_device(): every_request = lax.all_gather(row_requests, 'table', axis=0, tiled=False)]
    ppermute x0 -> x6, starting transfers between devices: none -> 8.1 us  [the longest x3 4.54 us: per_device(): by_offset.append(lax.ppermute(outgoing, 'table', pairs))]
    ppermute x3 -> x1, starting transfers between devices: 3.45 us -> 0.07 us  [butterfly_sum(): value = value + lax.ppermute(sent, name, pairs).astype(value.dtype)]
    another operation x4 -> x5, other arithmetic: 2.62 us -> 2.65 us
  transfers between devices with their start and end apart: 4 -> 8, of which waited for: 2 -> 1; matrix products, arithmetic and copies ran while one was open for 16% -> 36% of each run, Pallas kernels for 0% -> 0%
where the time goes in v10:
time: 101 us
  local copies, waits for them, and re-layouts  31.4 us (31%)
  matrix products  22.3 us (22%)
  waiting for transfers between devices  15.7 us (16%)
  starting transfers between devices  12.8 us (13%)
  blocking collectives  12.5 us (12%)
  other arithmetic  5.61 us (6%)
    gather x1, local copies, waits for them, and re-layouts, per_device(): served = item_table[requests_in]  20.3 us
    all_to_all x1, waiting for transfers between devices, per_device(): lax.all_to_all(served, 'table', split_axis=0, concat_axis=0, tiled=True)  15.7 us
    all_to_all x1, blocking collectives, per_device(): lax.all_to_all(payload, ('table', 'batch', 'ctx'), split_axis=0, concat_a...  12.5 us
    gather x1, local copies, waits for them, and re-layouts, per_device(): context_table[context_flat].astype(jnp.float32)  7.5 us
    dot_general x1, matrix products, per_device(): jnp.dot(placing, fetched.reshape(n_table * capacity, rank_width), preferr...  7.37 us
    dot_general x2, matrix products, gram_of(): lax.dot_general(table_rows, table_rows, (((0,), (0,)), ((), ())), preferr...  5.48 us
    all_to_all x1, starting transfers between devices, per_device(): lax.all_to_all(served, 'table', split_axis=0, concat_axis=0, tiled=True)  4.63 us
    ppermute x3, starting transfers between devices, per_device(): by_offset.append(lax.ppermute(outgoing, 'table', pairs))  4.54 us
  transfers between devices with their start and end apart: 8, of which 1 were waited for; matrix products, arithmetic and copies ran while one was open for 36% of the time, Pallas kernels for 0%

profile of v10, /device:TPU:0, one launch (start us, length us, event | category | flops | bytes accessed | tf_op | source)
XLA Modules:
  0.0 100.6 jit_solution(14841239889566068542)
XLA Ops:
  0.0 0.9 eq.113
  0.9 1.1 %reduce-window.6 = s32[4,16,128]{2,1,0:T(8,128)S(1)} reduce-window(s32[4,16,128]{2,1,0:T(8,128)S(1)} %fusion.32, s32[]{:T(128)} %constant.150.clone.1), window={size=1x1x128 pad=0_0x0_0x127_0}, to_apply=%region_2.3 | reduce-window | flops 1040384 | bytes 65540 | tf_op jit(solution)/shard_map/reduce-window
  2.1 0.2 slice_reduce_fusion
  2.3 0.2 reduce-window.9
  2.5 0.1 select_reduce_fusion
  2.6 0.5 broadcast.426
  3.1 1.4 %reduce.18 = s32[32,64]{1,0:T(8,128)S(1)} reduce(s32[32,64,1]{1,2,0:T(1,128)} %param.13, s32[]{:T(128)} %broadcast.426), dimensions={2}, to_apply=%param.13.reduce_sub_computation.5 | reduce | bytes 16388 | tf_op args[3]
  4.5 0.1 reshape.388
  4.6 0.8 reshape.390
  5.5 1.7 %fusion.3 = f32[4,2,1024]{2,0,1:T(4,128)S(1)} fusion(s32[2048]{0:T(1024)S(1)} %get-tuple-element.31, s32[2,2048]{1,0:T(2,128)S(1)} %pad_add_fusion, pred[4,2048]{1,0:T(4,128)(4,1)S(1)} %iota_compare_fusion.10), kind=kOutput, calls=%fused_computation.8 | convolution fusion | flops 35684352 | bytes 65536 | tf_op jit(solution)/shard_map/dot_general | solution.py:119
  7.3 3.0 %collective-permute-start = (s32[1024]{0:T(1024)S(1)}, s32[1024]{0:T(1024)S(1)}, u32[]{:S(2)}, u32[]{:S(2)}) collective-permute-start(s32[1024]{0:T(1024)S(1)} %bitcast.143), channel_id=1, source_target_pairs={{0,8},{8,0},{16,24},{24,16},{1,9},{9,1},{17,25},{25,17},{2,10},{10... | collective-permute-start | bytes 12296 | tf_op jit(solution)/shard_map/ppermute | solution.py:130
  10.3 1.5 %collective-permute-start.1 = (s32[1024]{0:T(1024)S(1)}, s32[1024]{0:T(1024)S(1)}, u32[]{:S(2)}, u32[]{:S(2)}) collective-permute-start(s32[1024]{0:T(1024)S(1)} %bitcast.142), channel_id=1, source_target_pairs={{0,16},{8,24},{16,0},{24,8},{1,17},{9,25},{17,1},{25,9},{2,18},{10... | collective-permute-start | bytes 12296 | tf_op jit(solution)/shard_map/ppermute | solution.py:130
  11.8 0.0 collective-permute-start.2
  11.8 4.7 %fusion.5 = f32[256,256]{1,0:T(8,128)S(1)} fusion(bf16[16384,256]{1,0:T(8,128)(2,1)} %param.10, s32[]{:T(128)S(6)} %select_n.132), kind=kOutput, calls=%fused_computation.9 | convolution fusion | flops 1073741824 | bytes 4456452 | tf_op jit(solution)/shard_map/dot_general | solution.py:15
  16.6 0.1 collective-permute-start.3
  16.7 0.0 copy-start.3
  16.7 0.0 copy-start.4
  16.7 0.7 fusion.62
  17.5 0.1 reshape.392
  17.7 0.0 collective-permute-done
  17.7 0.0 collective-permute-done.1
  17.7 0.0 collective-permute-done.2
  17.7 0.6 gather_fusion
  18.3 0.0 collective-permute-done.3
  18.3 2.0 %collective-permute-start.4 = (bf16[256,256]{1,0:T(8,128)(2,1)S(1)}, bf16[256,256]{1,0:T(8,128)(2,1)S(1)}, u32[]{:S(2)}, u32[]{:S(2)}) collective-permute-start(bf16[256,256]{1,0:T(8,128)(2,1)S(1)} %get-tuple-element.27), channel_id=1, source_target_pairs={{0,8},{8,0},{16,24},{24,16},{1,9},{9,1},{17,25},{25,17},{2,10},{10... | collective-permute-start | bytes 393224 | tf_op jit(solution)/shard_map/ppermute | solution.py:36
  20.4 1.5 %collective-permute-start.5 = (bf16[256,256]{1,0:T(8,128)(2,1)S(1)}, bf16[256,256]{1,0:T(8,128)(2,1)S(1)}, u32[]{:S(2)}, u32[]{:S(2)}) collective-permute-start(bf16[256,256]{1,0:T(8,128)(2,1)S(1)} %get-tuple-element.27), channel_id=1, source_target_pairs={{0,16},{8,24},{16,0},{24,8},{1,17},{9,25},{17,1},{25,9},{2,18},{10... | collective-permute-start | bytes 393224 | tf_op jit(solution)/shard_map/ppermute | solution.py:36
  21.9 0.0 collective-permute-start.6
  21.9 20.3 %gather_fusion.1 = bf16[4096,256]{1,0:T(8,128)(2,1)} fusion(bf16[16384,256]{1,0:T(8,128)(2,1)} %param.10, s32[4096]{0:T(1024)S(1)} %bitcast_clamp_fusion), kind=kCustom, calls=%fused_computation.1 | custom fusion | bytes 4210688 | tf_op jit(solution)/shard_map/gather | solution.py:141
  42.2 0.0 collective-permute-done.4
  42.2 0.0 collective-permute-done.5
  42.2 0.0 collective-permute-done.6
  42.2 0.1 multiply_multiply_fusion
  42.3 4.6 %all-to-all-start = ((bf16[4,1024,256]{2,1,0:T(8,128)(2,1)}), bf16[4,1024,256]{2,1,0:T(8,128)(2,1)}, u32[]{:S(2)}, u32[]{:S(2)}) async-start(bf16[4,1024,256]{2,1,0:T(8,128)(2,1)} %bitcast.127), calls=%async_computation | async-start | bytes 4194304 | tf_op jit(solution)/shard_map/all_to_all | solution.py:143
  47.0 0.0 copy-start.2
  47.0 7.5 %gather_fusion.2 = bf16[2048,256]{1,0:T(8,128)(2,1)S(1)} fusion(bf16[4096,256]{1,0:T(8,128)(2,1)S(1)} %copy-done, s32[2048]{0:T(1024)S(1)} %broadcast_clamp_fusion), kind=kCustom, calls=%fused_computation.2 | custom fusion | bytes 2105344 | tf_op jit(solution)/shard_map/gather | solution.py:153
  54.5 0.2 reduce_window_sum.24
  54.7 0.2 fusion.43
  54.9 0.1 copy.17
  55.0 0.1 convert_reduce_fusion.1
  55.1 0.1 copy.16
  55.2 0.6 compare_reduce_fusion
  55.8 0.7 convert_select_fusion
  56.5 15.7 %all-to-all-done = bf16[4,1024,256]{2,1,0:T(8,128)(2,1)} async-done(((bf16[4,1024,256]{2,1,0:T(8,128)(2,1)}), bf16[4,1024,256]{2,1,0:T(8,128)(2,1)}, u32[]{:S(2)}, u32[]{:S(2)}) %all-to-all-start) | async-done | bytes 2097184 | tf_op jit(solution)/shard_map/all_to_all | solution.py:143
  72.2 7.4 %fusion.9 = bf16[2048,256]{1,0:T(8,128)(2,1)S(1)} fusion(bf16[4096,256]{1,0:T(8,128)(2,1)} %bitcast.12, s32[2048]{0:T(1024)S(1)} %get-tuple-element.32, bf16[2048,256]{1,0:T(8,128)(2,1)S(1)} %gather_fusion.2), kind=kOutput, calls=%fused_computation.13 | convolution fusion | flops 4304928768 | bytes 4202496 | tf_op jit(solution)/shard_map/dot_general | solution.py:150
  79.6 0.5 fusion.63
  80.1 0.9 fusion.28
  81.0 0.5 fusion.64
  81.6 0.3 multiply_reduce_fusion.3
  81.9 0.2 multiply_reduce_fusion.2
  82.1 0.1 fusion.23
  82.2 0.9 fusion.26
  83.2 0.5 fusion.65
  83.7 0.3 multiply_reduce_fusion.1
  84.1 0.2 multiply_reduce_fusion
  84.3 0.1 multiply_add_fusion
  84.3 0.9 fusion.24
  85.3 0.5 fusion.66
  85.8 0.3 fusion.16
  86.2 0.3 fusion.15
  86.5 12.5 %all_to_all.10 = f32[32,2,384]{2,1,0:T(2,128)S(1)} all-to-all(f32[32,2,384]{2,1,0:T(2,128)S(1)} %bitcast.128), channel_id=1, replica_groups=mesh['table'=4,'batch'=4,'ctx'=2] {'table','batch','ctx'}, dimensions={0} | all-to-all | bytes 196608 | tf_op jit(solution)/shard_map/all_to_all | solution.py:180
  99.0 0.1 reshape.395
  99.1 0.1 fusion.19
  99.2 0.1 convert_reduce_fusion
  99.4 1.3 %fusion.10 = bf16[1024,256]{1,0:T(8,128)(2,1)} fusion(bf16[1024,256]{1,0:T(8,128)(2,1)S(1)} %copy-done.1, pred[1024]{0:T(1024)(128)(4,1)S(1)} %broadcast_compare_fusion, s32[64]{0:T(128)S(1)} %fusion.19, f32[64,384]{1,0:T(8,128)S(1)} %reshape.395), kind=kOutput, calls=%fused_computation.15 | convolution fusion | flops 34144256 | bytes 1082880 | tf_op jit(solution)/shard_map/dot_general | solution.py:187
  (45 shorter events, 0.5 us)
Async XLA Ops:
  0.0 16.7 %copy-start = (bf16[4096,256]{1,0:T(8,128)(2,1)S(1)}, bf16[4096,256]{1,0:T(8,128)(2,1)}, u32[]{:S(2)}) copy-start(bf16[4096,256]{1,0:T(8,128)(2,1)} %param.11) | copy-start | bytes 6291460
  7.3 10.4 %collective-permute-start = (s32[1024]{0:T(1024)S(1)}, s32[1024]{0:T(1024)S(1)}, u32[]{:S(2)}, u32[]{:S(2)}) collective-permute-start(s32[1024]{0:T(1024)S(1)} %bitcast.143), channel_id=1, source_target_pairs={{0,8},{8,0},{16,24},{24,16},{1,9},{9,1},{17,25},{25,17},{2,10},{10... | collective-permute-start | bytes 12296 | tf_op jit(solution)/shard_map/ppermute | solution.py:130
  10.3 7.4 %collective-permute-start.1 = (s32[1024]{0:T(1024)S(1)}, s32[1024]{0:T(1024)S(1)}, u32[]{:S(2)}, u32[]{:S(2)}) collective-permute-start(s32[1024]{0:T(1024)S(1)} %bitcast.142), channel_id=1, source_target_pairs={{0,16},{8,24},{16,0},{24,8},{1,17},{9,25},{17,1},{25,9},{2,18},{10... | collective-permute-start | bytes 12296 | tf_op jit(solution)/shard_map/ppermute | solution.py:130
  11.8 5.9 %collective-permute-start.2 = (s32[1024]{0:T(1024)S(1)}, s32[1024]{0:T(1024)S(1)}, u32[]{:S(2)}, u32[]{:S(2)}) collective-permute-start(s32[1024]{0:T(1024)S(1)} %bitcast.141), channel_id=1, source_target_pairs={{0,24},{8,16},{16,8},{24,0},{1,25},{9,17},{17,9},{25,1},{2,26},{10... | collective-permute-start | bytes 12296 | tf_op jit(solution)/shard_map/ppermute | solution.py:130
  16.6 1.7 %collective-permute-start.3 = (f32[256,256]{1,0:T(8,128)S(1)}, f32[256,256]{1,0:T(8,128)S(1)}, u32[]{:S(2)}, u32[]{:S(2)}) collective-permute-start(f32[256,256]{1,0:T(8,128)S(1)} %fusion.5), channel_id=1, source_target_pairs={{0,1},{1,0},{2,3},{3,2},{4,5},{5,4},{6,7},{7,6},{8,9},{9,8},{10,11... | collective-permute-start | bytes 786440 | tf_op jit(solution)/shard_map/ppermute | solution.py:26
  16.7 0.8 copy-start.3
  16.7 0.9 copy-start.4
  18.3 23.9 %collective-permute-start.4 = (bf16[256,256]{1,0:T(8,128)(2,1)S(1)}, bf16[256,256]{1,0:T(8,128)(2,1)S(1)}, u32[]{:S(2)}, u32[]{:S(2)}) collective-permute-start(bf16[256,256]{1,0:T(8,128)(2,1)S(1)} %get-tuple-element.27), channel_id=1, source_target_pairs={{0,8},{8,0},{16,24},{24,16},{1,9},{9,1},{17,25},{25,17},{2,10},{10... | collective-permute-start | bytes 393224 | tf_op jit(solution)/shard_map/ppermute | solution.py:36
  20.4 21.8 %collective-permute-start.5 = (bf16[256,256]{1,0:T(8,128)(2,1)S(1)}, bf16[256,256]{1,0:T(8,128)(2,1)S(1)}, u32[]{:S(2)}, u32[]{:S(2)}) collective-permute-start(bf16[256,256]{1,0:T(8,128)(2,1)S(1)} %get-tuple-element.27), channel_id=1, source_target_pairs={{0,16},{8,24},{16,0},{24,8},{1,17},{9,25},{17,1},{25,9},{2,18},{10... | collective-permute-start | bytes 393224 | tf_op jit(solution)/shard_map/ppermute | solution.py:36
  21.9 20.3 %collective-permute-start.6 = (bf16[256,256]{1,0:T(8,128)(2,1)S(1)}, bf16[256,256]{1,0:T(8,128)(2,1)S(1)}, u32[]{:S(2)}, u32[]{:S(2)}) collective-permute-start(bf16[256,256]{1,0:T(8,128)(2,1)S(1)} %get-tuple-element.27), channel_id=1, source_target_pairs={{0,24},{8,16},{16,8},{24,0},{1,25},{9,17},{17,9},{25,1},{2,26},{10... | collective-permute-start | bytes 393224 | tf_op jit(solution)/shard_map/ppermute | solution.py:36
  42.3 29.9 %all-to-all-start = ((bf16[4,1024,256]{2,1,0:T(8,128)(2,1)}), bf16[4,1024,256]{2,1,0:T(8,128)(2,1)}, u32[]{:S(2)}, u32[]{:S(2)}) async-start(bf16[4,1024,256]{2,1,0:T(8,128)(2,1)} %bitcast.127), calls=%async_computation | async-start | bytes 4194304 | tf_op jit(solution)/shard_map/all_to_all | solution.py:143
  47.0 8.9 %copy-start.2 = (s32[32,64]{1,0:T(8,128)S(1)}, s32[32,64]{1,0:T(8,128)}, u32[]{:S(2)}) copy-start(s32[32,64]{1,0:T(8,128)} %param.16) | copy-start | bytes 24580
  83.7 15.6 %copy-start.1 = (bf16[1024,256]{1,0:T(8,128)(2,1)S(1)}, bf16[1024,256]{1,0:T(8,128)(2,1)}, u32[]{:S(2)}) copy-start(bf16[1024,256]{1,0:T(8,128)(2,1)} %param.12) | copy-start | bytes 1572868

commit v11 on v10

--- a/solution.py
+++ b/solution.py
@@ -128,8 +128,6 @@
         pairs = [(i, i ^ k) for i in range(n_table)]
         outgoing = lax.dynamic_index_in_dim(row_requests, table_index ^ k, keepdims=False)
         by_offset.append(lax.ppermute(outgoing, "table", pairs))
-    by_offset = jnp.stack(by_offset, axis=0)
-    requests_in = by_offset[jnp.arange(n_table, dtype=jnp.int32) ^ table_index]
     gram_source = item_table
     share = gram_source.shape[0] // n_ctx
     own_rows = lax.dynamic_slice_in_dim(gram_source, lax.axis_index("ctx") * share, share, axis=0)
@@ -138,14 +136,16 @@
     context_gram = gram_of(context_table)
     pair_count = item_table.shape[0] * n_table * context_table.shape[0]
     gram_matrix = item_gram * context_gram / pair_count
-    served = item_table[requests_in]
-    served, gram_matrix = lax.optimization_barrier((served, gram_matrix))
-    fetched = lax.all_to_all(
-        served,
-        "table",
-        split_axis=0,
-        concat_axis=0,
-        tiled=True,
+    remote = item_table[jnp.stack(by_offset[1:], axis=0)]
+    remote, gram_matrix = lax.optimization_barrier((remote, gram_matrix))
+    got = [item_table[by_offset[0]]]
+    for k in range(1, n_table):
+        pairs = [(i, i ^ k) for i in range(n_table)]
+        got.append(lax.ppermute(remote[k - 1], "table", pairs))
+    fetched = jnp.stack(got, axis=0)
+    relative = (owners ^ table_index) * capacity + target % capacity
+    placing = (relative[:, None] == jnp.arange(n_table * capacity, dtype=jnp.int32)[None, :]).astype(
+        jnp.bfloat16
     )
     picked = jnp.dot(
         placing, fetched.reshape(n_table * capacity, rank_width), preferred_element_type=jnp.float32

time: 101 us -> 97 us (0.960)
  waiting for transfers between devices: 15.7 us -> 4.83 us
  local copies, waits for them, and re-layouts: 31.4 us -> 38.9 us
  other arithmetic: 5.61 us -> 7.16 us
  matrix products: 22.3 us -> 20.9 us
  starting transfers between devices: 12.8 us -> 11.7 us
    all_to_all x1 -> x0, waiting for transfers between devices: 15.7 us -> none  [per_device(): lax.all_to_all(served, 'table', split_axis=0, concat_axis=0, tiled=True)]
    ppermute x0 -> x3, waiting for transfers between devices: none -> 4.81 us  [per_device(): got.append(lax.ppermute(remote[k - 1], 'table', pairs))]
    all_to_all x1 -> x0, starting transfers between devices: 4.63 us -> none  [per_device(): lax.all_to_all(served, 'table', split_axis=0, concat_axis=0, tiled=True)]
    gather x2, local copies, waits for them, and re-layouts: 20.9 us -> 24.5 us  [the longest x1 16.6 us: per_device(): remote = item_table[jnp.stack(by_offset[1:], axis=0)]]
    ppermute x0 -> x3, starting transfers between devices: none -> 3.49 us  [per_device(): got.append(lax.ppermute(remote[k - 1], 'table', pairs))]
    squeeze x0 -> x1, local copies, waits for them, and re-layouts: none -> 2.44 us  [per_device(): got.append(lax.ppermute(remote[k - 1], 'table', pairs))]
    another operation x5, other arithmetic: 2.65 us -> 4.19 us
    gather x1, local copies, waits for them, and re-layouts: 7.5 us -> 9 us  [per_device(): context_table[context_flat].astype(jnp.float32)]
  transfers between devices with their start and end apart: 8 -> 10, of which waited for: 1 -> 1; matrix products, arithmetic and copies ran while one was open for 36% -> 43% of each run, Pallas kernels for 0% -> 0%
where the time goes in v11:
time: 97 us; the launch traced here: 96.5 us
  local copies, waits for them, and re-layouts  38.9 us (40%)
  matrix products  20.9 us (22%)
  blocking collectives  12.5 us (13%)
  starting transfers between devices  11.7 us (12%)
  other arithmetic  7.16 us (7%)
  waiting for transfers between devices  4.83 us (5%)
    gather x1, local copies, waits for them, and re-layouts, per_device(): remote = item_table[jnp.stack(by_offset[1:], axis=0)]  16.6 us
    all_to_all x1, blocking collectives, per_device(): lax.all_to_all(payload, ('table', 'batch', 'ctx'), split_axis=0, concat_a...  12.5 us
    gather x1, local copies, waits for them, and re-layouts, per_device(): context_table[context_flat].astype(jnp.float32)  9 us
    gather x1, local copies, waits for them, and re-layouts, per_device(): got = [item_table[by_offset[0]]]  7.92 us
    dot_general x1, matrix products, per_device(): jnp.dot(placing, fetched.reshape(n_table * capacity, rank_width), preferr...  6.04 us
    dot_general x2, matrix products, gram_of(): lax.dot_general(table_rows, table_rows, (((0,), (0,)), ((), ())), preferr...  5.49 us
    ppermute x3, waiting for transfers between devices, per_device(): got.append(lax.ppermute(remote[k - 1], 'table', pairs))  4.81 us
    ppermute x3, starting transfers between devices, per_device(): by_offset.append(lax.ppermute(outgoing, 'table', pairs))  4.6 us
  transfers between devices with their start and end apart: 10, of which 1 were waited for; matrix products, arithmetic and copies ran while one was open for 43% of the time, Pallas kernels for 0%

profile of v11, /device:TPU:0, one launch (start us, length us, event | category | flops | bytes accessed | tf_op | source)
XLA Modules:
  0.0 96.5 jit_solution(15777108985510596573)
XLA Ops:
  0.0 0.9 eq.114
  0.9 1.1 %reduce-window.6 = s32[4,16,128]{2,1,0:T(8,128)S(1)} reduce-window(s32[4,16,128]{2,1,0:T(8,128)S(1)} %fusion.32, s32[]{:T(128)} %constant.153.clone.1), window={size=1x1x128 pad=0_0x0_0x127_0}, to_apply=%region_2.3 | reduce-window | flops 1040384 | bytes 65540 | tf_op jit(solution)/shard_map/reduce-window
  2.1 0.2 slice_reduce_fusion
  2.3 0.2 reduce-window.9
  2.5 0.1 select_reduce_fusion
  2.6 0.5 broadcast.442
  3.1 1.4 %reduce.18 = s32[32,64]{1,0:T(8,128)S(1)} reduce(s32[32,64,1]{1,2,0:T(1,128)} %param.13, s32[]{:T(128)} %broadcast.442), dimensions={2}, to_apply=%param.13.reduce_sub_computation.5 | reduce | bytes 16388 | tf_op args[3]
  4.5 0.1 reshape.517
  4.6 0.8 reshape.519
  5.5 1.7 %fusion.3 = f32[4,2,1024]{2,0,1:T(4,128)S(1)} fusion(s32[2048]{0:T(1024)S(1)} %get-tuple-element.38, s32[2,2048]{1,0:T(2,128)S(1)} %pad_add_fusion, pred[4,2048]{1,0:T(4,128)(4,1)S(1)} %iota_compare_fusion.10), kind=kOutput, calls=%fused_computation.8 | convolution fusion | flops 35684352 | bytes 65536 | tf_op jit(solution)/shard_map/dot_general | solution.py:119
  7.3 4.0 %collective-permute-start.2 = (s32[1024]{0:T(1024)S(1)}, s32[1024]{0:T(1024)S(1)}, u32[]{:S(2)}, u32[]{:S(2)}) collective-permute-start(s32[1024]{0:T(1024)S(1)} %bitcast.155), channel_id=1, source_target_pairs={{0,24},{8,16},{16,8},{24,0},{1,25},{9,17},{17,9},{25,1},{2,26},{10... | collective-permute-start | bytes 12296 | tf_op jit(solution)/shard_map/ppermute | solution.py:130
  11.2 0.5 collective-permute-start
  11.8 0.1 collective-permute-start.1
  11.9 4.7 %fusion.5 = f32[256,256]{1,0:T(8,128)S(1)} fusion(bf16[16384,256]{1,0:T(8,128)(2,1)} %param.10, s32[]{:T(128)S(6)} %select_n.137), kind=kOutput, calls=%fused_computation.9 | convolution fusion | flops 1073741824 | bytes 4456452 | tf_op jit(solution)/shard_map/dot_general | solution.py:15
  16.6 0.1 collective-permute-start.3
  16.7 0.0 copy-start.4
  16.7 0.0 copy-start.5
  16.8 0.7 fusion.60
  17.5 0.1 reshape.521
  17.7 0.2 reduce_window_sum.24
  17.9 0.2 fusion.42
  18.2 0.1 convert_reduce_fusion.1
  18.2 0.0 collective-permute-done.2
  18.2 0.0 collective-permute-done
  18.3 2.0 %collective-permute-start.4 = (bf16[256,256]{1,0:T(8,128)(2,1)S(1)}, bf16[256,256]{1,0:T(8,128)(2,1)S(1)}, u32[]{:S(2)}, u32[]{:S(2)}) collective-permute-start(bf16[256,256]{1,0:T(8,128)(2,1)S(1)} %get-tuple-element.27), channel_id=1, source_target_pairs={{0,8},{8,0},{16,24},{24,16},{1,9},{9,1},{17,25},{25,17},{2,10},{10... | collective-permute-start | bytes 393224 | tf_op jit(solution)/shard_map/ppermute | solution.py:36
  20.3 1.5 %collective-permute-start.5 = (bf16[256,256]{1,0:T(8,128)(2,1)S(1)}, bf16[256,256]{1,0:T(8,128)(2,1)S(1)}, u32[]{:S(2)}, u32[]{:S(2)}) collective-permute-start(bf16[256,256]{1,0:T(8,128)(2,1)S(1)} %get-tuple-element.27), channel_id=1, source_target_pairs={{0,16},{8,24},{16,0},{24,8},{1,17},{9,25},{17,1},{25,9},{2,18},{10... | collective-permute-start | bytes 393224 | tf_op jit(solution)/shard_map/ppermute | solution.py:36
  21.8 0.1 collective-permute-start.6
  21.9 16.6 %gather_fusion.1 = bf16[3072,256]{1,0:T(8,128)(2,1)} fusion(bf16[16384,256]{1,0:T(8,128)(2,1)} %param.10, s32[3072]{0:T(1024)S(1)} %broadcast_clamp_fusion), kind=kCustom, calls=%fused_computation.1 | custom fusion | bytes 3158016 | tf_op jit(solution)/shard_map/gather | solution.py:139
  38.5 0.1 multiply_multiply_fusion
  38.6 2.4 %slice_bitcast_fusion.2 = (bf16[1024,256]{1,0:T(8,128)(2,1)}, bf16[1024,256]{1,0:T(8,128)(2,1)S(1)}, bf16[1024,256]{1,0:T(8,128)(2,1)}) fusion(bf16[3,1024,256]{2,1,0:T(8,128)(2,1)} %bitcast.135), kind=kLoop, calls=%fused_computation.29 | loop fusion | bytes 3145728 | tf_op jit(solution)/shard_map/squeeze | solution.py:144
  41.0 1.9 %collective-permute-start.7 = (bf16[1024,256]{1,0:T(8,128)(2,1)}, bf16[1024,256]{1,0:T(8,128)(2,1)}, u32[]{:S(2)}, u32[]{:S(2)}) collective-permute-start(bf16[1024,256]{1,0:T(8,128)(2,1)} %get-tuple-element.34), channel_id=1, source_target_pairs={{0,8},{8,0},{16,24},{24,16},{1,9},{9,1},{17,25},{25,17},{2,10},{10... | collective-permute-start | bytes 1572872 | tf_op jit(solution)/shard_map/ppermute | solution.py:144
  42.9 1.5 %collective-permute-start.8 = (bf16[1024,256]{1,0:T(8,128)(2,1)}, bf16[1024,256]{1,0:T(8,128)(2,1)}, u32[]{:S(2)}, u32[]{:S(2)}) collective-permute-start(bf16[1024,256]{1,0:T(8,128)(2,1)} %get-tuple-element.36), channel_id=1, source_target_pairs={{0,16},{8,24},{16,0},{24,8},{1,17},{9,25},{17,1},{25,9},{2,18},{10... | collective-permute-start | bytes 1572872 | tf_op jit(solution)/shard_map/ppermute | solution.py:144
  44.4 0.1 collective-permute-start.9
  44.5 7.9 %gather_fusion = bf16[1024,256]{1,0:T(8,128)(2,1)S(1)} fusion(bf16[16384,256]{1,0:T(8,128)(2,1)} %param.10, s32[1024]{0:T(1024)S(1)} %broadcast_clamp_fusion.2), kind=kCustom, calls=%fused_computation | custom fusion | bytes 1052672 | tf_op jit(solution)/shard_map/gather | solution.py:141
  52.5 0.0 copy-start.3
  52.5 9.0 %gather_fusion.2 = bf16[2048,256]{1,0:T(8,128)(2,1)} fusion(bf16[4096,256]{1,0:T(8,128)(2,1)S(1)} %copy-done, s32[2048]{0:T(1024)S(1)} %broadcast_clamp_fusion.1), kind=kCustom, calls=%fused_computation.2 | custom fusion | bytes 2105344 | tf_op jit(solution)/shard_map/gather | solution.py:153
  61.5 0.1 copy.17
  61.6 0.1 copy.16
  61.7 0.6 compare_reduce_fusion
  62.3 0.5 convert_select_fusion
  62.8 0.0 collective-permute-done.7
  62.9 4.8 %collective-permute-done.8 = bf16[1024,256]{1,0:T(8,128)(2,1)} collective-permute-done((bf16[1024,256]{1,0:T(8,128)(2,1)}, bf16[1024,256]{1,0:T(8,128)(2,1)}, u32[]{:S(2)}, u32[]{:S(2)}) %collective-permute-start.8) | collective-permute-done | bytes 524320 | tf_op jit(solution)/shard_map/ppermute | solution.py:144
  67.7 1.7 %pad_maximum_fusion = bf16[4,1024,256]{2,1,0:T(8,128)(2,1)S(1)} fusion(bf16[1,1024,256]{2,1,0:T(8,128)(2,1)} %bitcast.18, bf16[1,1024,256]{2,1,0:T(8,128)(2,1)} %bitcast.16, bf16[1,1024,256]{2,1,0:T(8,128)(2,1)} %bitcast.14, bf16[1,1024,256]{2,1,0:T(8,128)(2,1)S(1)} %bitcast.137), kind=kLoop, calls=%fused_computation.14 | loop fusion | flops 3145728 | bytes 4194304 | tf_op jit(solution)/shard_map/stack | solution.py:145
  69.4 6.0 %fusion.9 = bf16[2048,256]{1,0:T(8,128)(2,1)S(1)} fusion(bf16[4096,256]{1,0:T(8,128)(2,1)S(1)} %bitcast.136, s32[2048]{0:T(1024)S(1)} %get-tuple-element.37, bf16[2048,256]{1,0:T(8,128)(2,1)S(1)} %copy-done.1), kind=kOutput, calls=%fused_computation.13 | convolution fusion | flops 4304928768 | bytes 4202496 | tf_op jit(solution)/shard_map/dot_general | solution.py:150
  75.4 0.5 fusion.61
  76.0 0.9 fusion.28
  76.9 0.5 fusion.62
  77.4 0.3 multiply_reduce_fusion.3
  77.8 0.2 multiply_reduce_fusion.2
  78.0 0.1 fusion.23
  78.1 0.9 fusion.26
  79.0 0.5 fusion.63
  79.6 0.3 multiply_reduce_fusion.1
  79.9 0.2 multiply_reduce_fusion
  80.1 0.1 multiply_add_fusion
  80.2 0.9 fusion.24
  81.1 0.5 fusion.64
  81.7 0.3 fusion.16
  82.0 0.3 fusion.15
  82.4 12.5 %all_to_all.5 = f32[32,2,384]{2,1,0:T(2,128)S(1)} all-to-all(f32[32,2,384]{2,1,0:T(2,128)S(1)} %bitcast.138), channel_id=1, replica_groups=mesh['table'=4,'batch'=4,'ctx'=2] {'table','batch','ctx'}, dimensions={0} | all-to-all | bytes 196608 | tf_op jit(solution)/shard_map/all_to_all | solution.py:180
  94.9 0.1 reshape.524
  95.0 0.1 fusion.19
  95.1 0.1 convert_reduce_fusion
  95.2 1.3 %fusion.10 = bf16[1024,256]{1,0:T(8,128)(2,1)} fusion(bf16[1024,256]{1,0:T(8,128)(2,1)S(1)} %copy-done.2, pred[1024]{0:T(1024)(128)(4,1)S(1)} %broadcast_compare_fusion, s32[64]{0:T(128)S(1)} %fusion.19, f32[64,384]{1,0:T(8,128)S(1)} %reshape.524), kind=kOutput, calls=%fused_computation.16 | convolution fusion | flops 34144256 | bytes 1082880 | tf_op jit(solution)/shard_map/dot_general | solution.py:187
  (52 shorter events, 0.5 us)
Async XLA Ops:
  0.0 16.7 %copy-start = (bf16[4096,256]{1,0:T(8,128)(2,1)S(1)}, bf16[4096,256]{1,0:T(8,128)(2,1)}, u32[]{:S(2)}) copy-start(bf16[4096,256]{1,0:T(8,128)(2,1)} %param.11) | copy-start | bytes 6291460
  7.3 11.0 %collective-permute-start.2 = (s32[1024]{0:T(1024)S(1)}, s32[1024]{0:T(1024)S(1)}, u32[]{:S(2)}, u32[]{:S(2)}) collective-permute-start(s32[1024]{0:T(1024)S(1)} %bitcast.155), channel_id=1, source_target_pairs={{0,24},{8,16},{16,8},{24,0},{1,25},{9,17},{17,9},{25,1},{2,26},{10... | collective-permute-start | bytes 12296 | tf_op jit(solution)/shard_map/ppermute | solution.py:130
  11.2 7.0 %collective-permute-start = (s32[1024]{0:T(1024)S(1)}, s32[1024]{0:T(1024)S(1)}, u32[]{:S(2)}, u32[]{:S(2)}) collective-permute-start(s32[1024]{0:T(1024)S(1)} %bitcast.154), channel_id=1, source_target_pairs={{0,8},{8,0},{16,24},{24,16},{1,9},{9,1},{17,25},{25,17},{2,10},{10... | collective-permute-start | bytes 12296 | tf_op jit(solution)/shard_map/ppermute | solution.py:130
  11.8 6.5 %collective-permute-start.1 = (s32[1024]{0:T(1024)S(1)}, s32[1024]{0:T(1024)S(1)}, u32[]{:S(2)}, u32[]{:S(2)}) collective-permute-start(s32[1024]{0:T(1024)S(1)} %bitcast.153), channel_id=1, source_target_pairs={{0,16},{8,24},{16,0},{24,8},{1,17},{9,25},{17,1},{25,9},{2,18},{10... | collective-permute-start | bytes 12296 | tf_op jit(solution)/shard_map/ppermute | solution.py:130
  16.6 1.7 %collective-permute-start.3 = (f32[256,256]{1,0:T(8,128)S(1)}, f32[256,256]{1,0:T(8,128)S(1)}, u32[]{:S(2)}, u32[]{:S(2)}) collective-permute-start(f32[256,256]{1,0:T(8,128)S(1)} %fusion.5), channel_id=1, source_target_pairs={{0,1},{1,0},{2,3},{3,2},{4,5},{5,4},{6,7},{7,6},{8,9},{9,8},{10,11... | collective-permute-start | bytes 786440 | tf_op jit(solution)/shard_map/ppermute | solution.py:26
  16.7 0.8 copy-start.4
  16.7 0.9 copy-start.5
  18.3 20.2 %collective-permute-start.4 = (bf16[256,256]{1,0:T(8,128)(2,1)S(1)}, bf16[256,256]{1,0:T(8,128)(2,1)S(1)}, u32[]{:S(2)}, u32[]{:S(2)}) collective-permute-start(bf16[256,256]{1,0:T(8,128)(2,1)S(1)} %get-tuple-element.27), channel_id=1, source_target_pairs={{0,8},{8,0},{16,24},{24,16},{1,9},{9,1},{17,25},{25,17},{2,10},{10... | collective-permute-start | bytes 393224 | tf_op jit(solution)/shard_map/ppermute | solution.py:36
  20.3 18.2 %collective-permute-start.5 = (bf16[256,256]{1,0:T(8,128)(2,1)S(1)}, bf16[256,256]{1,0:T(8,128)(2,1)S(1)}, u32[]{:S(2)}, u32[]{:S(2)}) collective-permute-start(bf16[256,256]{1,0:T(8,128)(2,1)S(1)} %get-tuple-element.27), channel_id=1, source_target_pairs={{0,16},{8,24},{16,0},{24,8},{1,17},{9,25},{17,1},{25,9},{2,18},{10... | collective-permute-start | bytes 393224 | tf_op jit(solution)/shard_map/ppermute | solution.py:36
  21.8 16.7 %collective-permute-start.6 = (bf16[256,256]{1,0:T(8,128)(2,1)S(1)}, bf16[256,256]{1,0:T(8,128)(2,1)S(1)}, u32[]{:S(2)}, u32[]{:S(2)}) collective-permute-start(bf16[256,256]{1,0:T(8,128)(2,1)S(1)} %get-tuple-element.27), channel_id=1, source_target_pairs={{0,24},{8,16},{16,8},{24,0},{1,25},{9,17},{17,9},{25,1},{2,26},{10... | collective-permute-start | bytes 393224 | tf_op jit(solution)/shard_map/ppermute | solution.py:36
  41.0 21.8 %collective-permute-start.7 = (bf16[1024,256]{1,0:T(8,128)(2,1)}, bf16[1024,256]{1,0:T(8,128)(2,1)}, u32[]{:S(2)}, u32[]{:S(2)}) collective-permute-start(bf16[1024,256]{1,0:T(8,128)(2,1)} %get-tuple-element.34), channel_id=1, source_target_pairs={{0,8},{8,0},{16,24},{24,16},{1,9},{9,1},{17,25},{25,17},{2,10},{10... | collective-permute-start | bytes 1572872 | tf_op jit(solution)/shard_map/ppermute | solution.py:144
  42.9 24.7 %collective-permute-start.8 = (bf16[1024,256]{1,0:T(8,128)(2,1)}, bf16[1024,256]{1,0:T(8,128)(2,1)}, u32[]{:S(2)}, u32[]{:S(2)}) collective-permute-start(bf16[1024,256]{1,0:T(8,128)(2,1)} %get-tuple-element.36), channel_id=1, source_target_pairs={{0,16},{8,24},{16,0},{24,8},{1,17},{9,25},{17,1},{25,9},{2,18},{10... | collective-permute-start | bytes 1572872 | tf_op jit(solution)/shard_map/ppermute | solution.py:144
  44.4 23.2 %collective-permute-start.9 = (bf16[1024,256]{1,0:T(8,128)(2,1)S(1)}, bf16[1024,256]{1,0:T(8,128)(2,1)}, u32[]{:S(2)}, u32[]{:S(2)}) collective-permute-start(bf16[1024,256]{1,0:T(8,128)(2,1)S(1)} %get-tuple-element.35), channel_id=1, source_target_pairs={{0,24},{8,16},{16,8},{24,0},{1,25},{9,17},{17,9},{25,1},{2,26},{10... | collective-permute-start | bytes 1572872 | tf_op jit(solution)/shard_map/ppermute | solution.py:144
  52.5 9.8 %copy-start.3 = (s32[32,64]{1,0:T(8,128)S(1)}, s32[32,64]{1,0:T(8,128)}, u32[]{:S(2)}) copy-start(s32[32,64]{1,0:T(8,128)} %param.16) | copy-start | bytes 24580
  67.7 1.7 %copy-start.1 = (bf16[2048,256]{1,0:T(8,128)(2,1)S(1)}, bf16[2048,256]{1,0:T(8,128)(2,1)}, u32[]{:S(2)}) copy-start(bf16[2048,256]{1,0:T(8,128)(2,1)} %gather_fusion.2) | copy-start | bytes 3145732
  79.6 15.7 %copy-start.2 = (bf16[1024,256]{1,0:T(8,128)(2,1)S(1)}, bf16[1024,256]{1,0:T(8,128)(2,1)}, u32[]{:S(2)}) copy-start(bf16[1024,256]{1,0:T(8,128)(2,1)} %param.12) | copy-start | bytes 1572868

commit v12 on v11

--- a/solution.py
+++ b/solution.py
@@ -138,19 +138,26 @@
     gram_matrix = item_gram * context_gram / pair_count
     remote = item_table[jnp.stack(by_offset[1:], axis=0)]
     remote, gram_matrix = lax.optimization_barrier((remote, gram_matrix))
-    got = [item_table[by_offset[0]]]
+    remote, late_items, late_contexts, local_requests = lax.optimization_barrier(
+        (remote, item_table, context_table, by_offset[0])
+    )
+    got = [late_items[local_requests]]
     for k in range(1, n_table):
         pairs = [(i, i ^ k) for i in range(n_table)]
         got.append(lax.ppermute(remote[k - 1], "table", pairs))
-    fetched = jnp.stack(got, axis=0)
     relative = (owners ^ table_index) * capacity + target % capacity
-    placing = (relative[:, None] == jnp.arange(n_table * capacity, dtype=jnp.int32)[None, :]).astype(
-        jnp.bfloat16
-    )
-    picked = jnp.dot(
-        placing, fetched.reshape(n_table * capacity, rank_width), preferred_element_type=jnp.float32
-    )
-    slot_rows = (picked * context_table[context_flat].astype(jnp.float32)).astype(jnp.bfloat16)
+    placing_local = (relative[:, None] == jnp.arange(capacity, dtype=jnp.int32)[None, :]).astype(
+        jnp.bfloat16
+    )
+    picked_local = jnp.dot(placing_local, got[0], preferred_element_type=jnp.float32)
+    placing = (
+        relative[:, None] == jnp.arange(capacity, n_table * capacity, dtype=jnp.int32)[None, :]
+    ).astype(jnp.bfloat16)
+    fetched = jnp.stack(got[1:], axis=0)
+    picked = picked_local + jnp.dot(
+        placing, fetched.reshape((n_table - 1) * capacity, rank_width), preferred_element_type=jnp.float32
+    )
+    slot_rows = (picked * late_contexts[context_flat].astype(jnp.float32)).astype(jnp.bfloat16)
     slot_rows = slot_rows.reshape(user_count, slot_count, rank_width)
     confidence = CONF_SCALE * bucket.astype(jnp.float32)
     weights = jnp.where(bucket > 0, 1.0 + confidence, 0.0)

time: 97 us -> 96.6 us (level)
  waiting for transfers between devices: 4.83 us -> 3.78 us
    ppermute x3, waiting for transfers between devices: 4.81 us -> 3.76 us  [per_device(): got.append(lax.ppermute(remote[k - 1], 'table', pairs))]
    dot_general x1 -> x2, matrix products: 6.04 us -> 6.92 us  [the longest x1 4.23 us: per_device(): jnp.dot(placing, fetched.reshape((n_table - 1) * capacity, rank_width), p...]
  transfers between devices with their start and end apart: 10 -> 10, of which waited for: 1 -> 1; matrix products, arithmetic and copies ran while one was open for 43% -> 45% of each run, Pallas kernels for 0% -> 0%
where the time goes in v12:
time: 96.6 us; the launch traced here: 96.1 us
  local copies, waits for them, and re-layouts  38.9 us (40%)
  matrix products  21.8 us (23%)
  blocking collectives  12.5 us (13%)
  starting transfers between devices  11.7 us (12%)
  other arithmetic  7.12 us (7%)
  waiting for transfers between devices  3.78 us (4%)
    gather x1, local copies, waits for them, and re-layouts, per_device(): remote = item_table[jnp.stack(by_offset[1:], axis=0)]  16.6 us
    all_to_all x1, blocking collectives, per_device(): lax.all_to_all(payload, ('table', 'batch', 'ctx'), split_axis=0, concat_a...  12.5 us
    gather x1, local copies, waits for them, and re-layouts, per_device(): got = [late_items[local_requests]]  9.07 us
    gather x1, local copies, waits for them, and re-layouts, per_device(): late_contexts[context_flat].astype(jnp.float32)  7.67 us
    dot_general x2, matrix products, gram_of(): lax.dot_general(table_rows, table_rows, (((0,), (0,)), ((), ())), preferr...  5.48 us
    ppermute x3, starting transfers between devices, per_device(): by_offset.append(lax.ppermute(outgoing, 'table', pairs))  4.54 us
    dot_general x1, matrix products, per_device(): jnp.dot(placing, fetched.reshape((n_table - 1) * capacity, rank_width), p...  4.23 us
    ppermute x3, waiting for transfers between devices, per_device(): got.append(lax.ppermute(remote[k - 1], 'table', pairs))  3.76 us
  transfers between devices with their start and end apart: 10, of which 1 were waited for; matrix products, arithmetic and copies ran while one was open for 45% of the time, Pallas kernels for 0%

profile of v12, /device:TPU:0, one launch (start us, length us, event | category | flops | bytes accessed | tf_op | source)
XLA Modules:
  0.0 96.1 jit_solution(10300359162294921980)
XLA Ops:
  0.0 0.9 eq.127
  0.9 1.1 %reduce-window.6 = s32[4,16,128]{2,1,0:T(8,128)S(1)} reduce-window(s32[4,16,128]{2,1,0:T(8,128)S(1)} %fusion.43, s32[]{:T(128)} %constant.154.clone.1), window={size=1x1x128 pad=0_0x0_0x127_0}, to_apply=%region_2.3 | reduce-window | flops 1040384 | bytes 65540 | tf_op jit(solution)/shard_map/reduce-window
  2.1 0.2 slice_reduce_fusion
  2.3 0.2 reduce-window.9
  2.5 0.1 select_reduce_fusion
  2.6 0.5 broadcast.432
  3.1 1.4 %reduce.18 = s32[32,64]{1,0:T(8,128)S(1)} reduce(s32[32,64,1]{1,2,0:T(1,128)} %param.13, s32[]{:T(128)} %broadcast.432), dimensions={2}, to_apply=%param.13.reduce_sub_computation.5 | reduce | bytes 16388 | tf_op args[3]
  4.5 0.1 reshape.493
  4.6 0.8 reshape.495
  5.5 1.7 %fusion.6 = f32[4,2,1024]{2,0,1:T(4,128)S(1)} fusion(s32[2048]{0:T(1024)S(1)} %get-tuple-element.46, s32[2,2048]{1,0:T(2,128)S(1)} %pad_add_fusion, pred[4,2048]{1,0:T(4,128)(4,1)S(1)} %iota_compare_fusion.6), kind=kOutput, calls=%fused_computation.11 | convolution fusion | flops 35684352 | bytes 65536 | tf_op jit(solution)/shard_map/dot_general | solution.py:119
  7.3 3.0 %collective-permute-start = (s32[1024]{0:T(1024)S(1)}, s32[1024]{0:T(1024)S(1)}, u32[]{:S(2)}, u32[]{:S(2)}) collective-permute-start(s32[1024]{0:T(1024)S(1)} %bitcast.152), channel_id=1, source_target_pairs={{0,8},{8,0},{16,24},{24,16},{1,9},{9,1},{17,25},{25,17},{2,10},{10... | collective-permute-start | bytes 12296 | tf_op jit(solution)/shard_map/ppermute | solution.py:130
  10.3 1.5 %collective-permute-start.1 = (s32[1024]{0:T(1024)S(1)}, s32[1024]{0:T(1024)S(1)}, u32[]{:S(2)}, u32[]{:S(2)}) collective-permute-start(s32[1024]{0:T(1024)S(1)} %bitcast.151), channel_id=1, source_target_pairs={{0,16},{8,24},{16,0},{24,8},{1,17},{9,25},{17,1},{25,9},{2,18},{10... | collective-permute-start | bytes 12296 | tf_op jit(solution)/shard_map/ppermute | solution.py:130
  11.8 0.0 collective-permute-start.2
  11.8 4.7 %fusion.8 = f32[256,256]{1,0:T(8,128)S(1)} fusion(bf16[16384,256]{1,0:T(8,128)(2,1)} %param.10, s32[]{:T(128)S(6)} %select_n.128), kind=kOutput, calls=%fused_computation.12 | convolution fusion | flops 1073741824 | bytes 4456452 | tf_op jit(solution)/shard_map/dot_general | solution.py:15
  16.6 0.1 collective-permute-start.3
  16.7 0.6 compare_reduce_fusion
  17.3 0.7 fusion.72
  18.1 0.1 reshape.497
  18.3 0.2 reduce_window_sum.24
  18.5 0.1 convert_reduce_fusion.1
  18.6 0.2 fusion.53
  18.8 0.1 copy.17
  18.9 0.1 copy.16
  19.0 0.7 convert_select_fusion
  19.7 0.0 collective-permute-done
  19.7 0.0 collective-permute-done.1
  19.7 0.0 collective-permute-done.2
  19.7 0.0 collective-permute-done.3
  19.8 2.0 %collective-permute-start.4 = (bf16[256,256]{1,0:T(8,128)(2,1)S(1)}, bf16[256,256]{1,0:T(8,128)(2,1)S(1)}, u32[]{:S(2)}, u32[]{:S(2)}) collective-permute-start(bf16[256,256]{1,0:T(8,128)(2,1)S(1)} %get-tuple-element.35), channel_id=1, source_target_pairs={{0,8},{8,0},{16,24},{24,16},{1,9},{9,1},{17,25},{25,17},{2,10},{10... | collective-permute-start | bytes 393224 | tf_op jit(solution)/shard_map/ppermute | solution.py:36
  21.8 1.5 %collective-permute-start.5 = (bf16[256,256]{1,0:T(8,128)(2,1)S(1)}, bf16[256,256]{1,0:T(8,128)(2,1)S(1)}, u32[]{:S(2)}, u32[]{:S(2)}) collective-permute-start(bf16[256,256]{1,0:T(8,128)(2,1)S(1)} %get-tuple-element.35), channel_id=1, source_target_pairs={{0,16},{8,24},{16,0},{24,8},{1,17},{9,25},{17,1},{25,9},{2,18},{10... | collective-permute-start | bytes 393224 | tf_op jit(solution)/shard_map/ppermute | solution.py:36
  23.3 0.0 collective-permute-start.6
  23.3 16.6 %gather_fusion = bf16[3072,256]{1,0:T(8,128)(2,1)} fusion(bf16[16384,256]{1,0:T(8,128)(2,1)} %param.10, s32[3072]{0:T(1024)S(1)} %broadcast_clamp_fusion), kind=kCustom, calls=%fused_computation | custom fusion | bytes 3158016 | tf_op jit(solution)/shard_map/gather | solution.py:139
  39.9 0.1 multiply_multiply_fusion
  40.0 2.6 %slice_bitcast_fusion.2 = (bf16[1024,256]{1,0:T(8,128)(2,1)}, bf16[1024,256]{1,0:T(8,128)(2,1)}, bf16[1024,256]{1,0:T(8,128)(2,1)}) fusion(bf16[3,1024,256]{2,1,0:T(8,128)(2,1)} %bitcast.133), kind=kLoop, calls=%fused_computation.34 | loop fusion | bytes 3145728 | tf_op jit(solution)/shard_map/squeeze | solution.py:147
  42.6 1.9 %collective-permute-start.7 = (bf16[1024,256]{1,0:T(8,128)(2,1)}, bf16[1024,256]{1,0:T(8,128)(2,1)}, u32[]{:S(2)}, u32[]{:S(2)}) collective-permute-start(bf16[1024,256]{1,0:T(8,128)(2,1)} %get-tuple-element.42), channel_id=1, source_target_pairs={{0,8},{8,0},{16,24},{24,16},{1,9},{9,1},{17,25},{25,17},{2,10},{10... | collective-permute-start | bytes 1572872 | tf_op jit(solution)/shard_map/ppermute | solution.py:147
  44.6 1.5 %collective-permute-start.8 = (bf16[1024,256]{1,0:T(8,128)(2,1)}, bf16[1024,256]{1,0:T(8,128)(2,1)}, u32[]{:S(2)}, u32[]{:S(2)}) collective-permute-start(bf16[1024,256]{1,0:T(8,128)(2,1)} %get-tuple-element.44), channel_id=1, source_target_pairs={{0,16},{8,24},{16,0},{24,8},{1,17},{9,25},{17,1},{25,9},{2,18},{10... | collective-permute-start | bytes 1572872 | tf_op jit(solution)/shard_map/ppermute | solution.py:147
  46.1 0.0 collective-permute-start.9
  46.1 9.1 %gather_fusion.1 = bf16[1024,256]{1,0:T(8,128)(2,1)} fusion(bf16[16384,256]{1,0:T(8,128)(2,1)} %param.10, s32[1024]{0:T(1024)S(1)} %fusion.62), kind=kCustom, calls=%fused_computation.1 | custom fusion | bytes 1052672 | tf_op jit(solution)/shard_map/gather | solution.py:144
  55.2 7.7 %gather_fusion.2 = bf16[2048,256]{1,0:T(8,128)(2,1)S(1)} fusion(bf16[4096,256]{1,0:T(8,128)(2,1)S(1)} %copy-done, s32[2048]{0:T(1024)S(1)} %broadcast_clamp_fusion.1), kind=kCustom, calls=%fused_computation.2 | custom fusion | bytes 2105344 | tf_op jit(solution)/shard_map/gather | solution.py:160
  62.9 2.7 %fusion.4 = f32[2048,256]{1,0:T(8,128)S(1)} fusion(bf16[1024,256]{1,0:T(8,128)(2,1)} %gather_fusion.1, s32[2048]{0:T(1024)S(1)} %get-tuple-element.45), kind=kOutput, calls=%fused_computation.9 | convolution fusion | flops 1075838976 | bytes 2629632 | tf_op jit(solution)/shard_map/dot_general | solution.py:152
  65.6 0.0 collective-permute-done.7
  65.6 3.8 %collective-permute-done.8 = bf16[1024,256]{1,0:T(8,128)(2,1)} collective-permute-done((bf16[1024,256]{1,0:T(8,128)(2,1)}, bf16[1024,256]{1,0:T(8,128)(2,1)}, u32[]{:S(2)}, u32[]{:S(2)}) %collective-permute-start.8) | collective-permute-done | bytes 524320 | tf_op jit(solution)/shard_map/ppermute | solution.py:147
  69.3 1.5 %pad_maximum_fusion = bf16[3,1024,256]{2,1,0:T(8,128)(2,1)S(1)} fusion(bf16[1,1024,256]{2,1,0:T(8,128)(2,1)} %bitcast.16, bf16[1,1024,256]{2,1,0:T(8,128)(2,1)} %bitcast.14, bf16[1,1024,256]{2,1,0:T(8,128)(2,1)} %bitcast.12), kind=kLoop, calls=%fused_computation.19 | loop fusion | flops 1572864 | bytes 3145728 | tf_op jit(solution)/shard_map/stack | solution.py:156
  70.9 4.2 %fusion.18 = bf16[2048,256]{1,0:T(8,128)(2,1)S(1)} fusion(f32[2048,256]{1,0:T(8,128)S(1)} %fusion.4, bf16[3072,256]{1,0:T(8,128)(2,1)S(1)} %bitcast.134, s32[3072]{0:T(1024)S(1)} %iota_add_fusion, s32[2048]{0:T(1024)S(1)} %get-tuple-element.45, bf16[2048,256]{1,0:T(8,128)(2,1)S(1)} %gather_fusion.2), kind=kOutput, calls=%fused_computation.18 | convolution fusion | flops 3229614080 | bytes 5787648 | tf_op jit(solution)/shard_map/dot_general | solution.py:157
  75.1 0.5 fusion.73
  75.6 0.9 fusion.39
  76.6 0.5 fusion.74
  77.1 0.3 multiply_reduce_fusion.3
  77.5 0.2 multiply_reduce_fusion.2
  77.7 0.1 fusion.34
  77.7 0.9 fusion.37
  78.7 0.5 fusion.75
  79.2 0.3 multiply_reduce_fusion.1
  79.6 0.2 multiply_reduce_fusion
  79.8 0.1 multiply_add_fusion
  79.9 0.9 fusion.35
  80.8 0.5 fusion.76
  81.3 0.3 fusion.27
  81.7 0.3 fusion.26
  82.0 12.5 %all_to_all.5 = f32[32,2,384]{2,1,0:T(2,128)S(1)} all-to-all(f32[32,2,384]{2,1,0:T(2,128)S(1)} %bitcast.135), channel_id=1, replica_groups=mesh['table'=4,'batch'=4,'ctx'=2] {'table','batch','ctx'}, dimensions={0} | all-to-all | bytes 196608 | tf_op jit(solution)/shard_map/all_to_all | solution.py:187
  94.6 0.1 reshape.500
  94.6 0.1 fusion.30
  94.7 0.1 convert_reduce_fusion
  94.9 1.3 %fusion.21 = bf16[1024,256]{1,0:T(8,128)(2,1)} fusion(bf16[1024,256]{1,0:T(8,128)(2,1)S(1)} %copy-done.1, pred[1024]{0:T(1024)(128)(4,1)S(1)} %broadcast_compare_fusion, s32[64]{0:T(128)S(1)} %fusion.30, f32[64,384]{1,0:T(8,128)S(1)} %reshape.500), kind=kOutput, calls=%fused_computation.21 | convolution fusion | flops 34144256 | bytes 1082880 | tf_op jit(solution)/shard_map/dot_general | solution.py:194
  (51 shorter events, 0.5 us)
Async XLA Ops:
  0.0 17.3 %copy-start = (bf16[4096,256]{1,0:T(8,128)(2,1)S(1)}, bf16[4096,256]{1,0:T(8,128)(2,1)}, u32[]{:S(2)}) copy-start(bf16[4096,256]{1,0:T(8,128)(2,1)} %param.11) | copy-start | bytes 6291460
  7.3 12.4 %collective-permute-start = (s32[1024]{0:T(1024)S(1)}, s32[1024]{0:T(1024)S(1)}, u32[]{:S(2)}, u32[]{:S(2)}) collective-permute-start(s32[1024]{0:T(1024)S(1)} %bitcast.152), channel_id=1, source_target_pairs={{0,8},{8,0},{16,24},{24,16},{1,9},{9,1},{17,25},{25,17},{2,10},{10... | collective-permute-start | bytes 12296 | tf_op jit(solution)/shard_map/ppermute | solution.py:130
  10.3 9.4 %collective-permute-start.1 = (s32[1024]{0:T(1024)S(1)}, s32[1024]{0:T(1024)S(1)}, u32[]{:S(2)}, u32[]{:S(2)}) collective-permute-start(s32[1024]{0:T(1024)S(1)} %bitcast.151), channel_id=1, source_target_pairs={{0,16},{8,24},{16,0},{24,8},{1,17},{9,25},{17,1},{25,9},{2,18},{10... | collective-permute-start | bytes 12296 | tf_op jit(solution)/shard_map/ppermute | solution.py:130
  11.8 7.9 %collective-permute-start.2 = (s32[1024]{0:T(1024)S(1)}, s32[1024]{0:T(1024)S(1)}, u32[]{:S(2)}, u32[]{:S(2)}) collective-permute-start(s32[1024]{0:T(1024)S(1)} %bitcast.150), channel_id=1, source_target_pairs={{0,24},{8,16},{16,8},{24,0},{1,25},{9,17},{17,9},{25,1},{2,26},{10... | collective-permute-start | bytes 12296 | tf_op jit(solution)/shard_map/ppermute | solution.py:130
  16.6 3.1 %collective-permute-start.3 = (f32[256,256]{1,0:T(8,128)S(1)}, f32[256,256]{1,0:T(8,128)S(1)}, u32[]{:S(2)}, u32[]{:S(2)}) collective-permute-start(f32[256,256]{1,0:T(8,128)S(1)} %fusion.8), channel_id=1, source_target_pairs={{0,1},{1,0},{2,3},{3,2},{4,5},{5,4},{6,7},{7,6},{8,9},{9,8},{10,11... | collective-permute-start | bytes 786440 | tf_op jit(solution)/shard_map/ppermute | solution.py:26
  17.3 0.8 copy-start.3
  17.3 0.9 copy-start.2
  17.3 0.9 copy-start.4
  19.8 20.2 %collective-permute-start.4 = (bf16[256,256]{1,0:T(8,128)(2,1)S(1)}, bf16[256,256]{1,0:T(8,128)(2,1)S(1)}, u32[]{:S(2)}, u32[]{:S(2)}) collective-permute-start(bf16[256,256]{1,0:T(8,128)(2,1)S(1)} %get-tuple-element.35), channel_id=1, source_target_pairs={{0,8},{8,0},{16,24},{24,16},{1,9},{9,1},{17,25},{25,17},{2,10},{10... | collective-permute-start | bytes 393224 | tf_op jit(solution)/shard_map/ppermute | solution.py:36
  21.8 18.1 %collective-permute-start.5 = (bf16[256,256]{1,0:T(8,128)(2,1)S(1)}, bf16[256,256]{1,0:T(8,128)(2,1)S(1)}, u32[]{:S(2)}, u32[]{:S(2)}) collective-permute-start(bf16[256,256]{1,0:T(8,128)(2,1)S(1)} %get-tuple-element.35), channel_id=1, source_target_pairs={{0,16},{8,24},{16,0},{24,8},{1,17},{9,25},{17,1},{25,9},{2,18},{10... | collective-permute-start | bytes 393224 | tf_op jit(solution)/shard_map/ppermute | solution.py:36
  23.3 16.6 %collective-permute-start.6 = (bf16[256,256]{1,0:T(8,128)(2,1)S(1)}, bf16[256,256]{1,0:T(8,128)(2,1)S(1)}, u32[]{:S(2)}, u32[]{:S(2)}) collective-permute-start(bf16[256,256]{1,0:T(8,128)(2,1)S(1)} %get-tuple-element.35), channel_id=1, source_target_pairs={{0,24},{8,16},{16,8},{24,0},{1,25},{9,17},{17,9},{25,1},{2,26},{10... | collective-permute-start | bytes 393224 | tf_op jit(solution)/shard_map/ppermute | solution.py:36
  42.6 22.9 %collective-permute-start.7 = (bf16[1024,256]{1,0:T(8,128)(2,1)}, bf16[1024,256]{1,0:T(8,128)(2,1)}, u32[]{:S(2)}, u32[]{:S(2)}) collective-permute-start(bf16[1024,256]{1,0:T(8,128)(2,1)} %get-tuple-element.42), channel_id=1, source_target_pairs={{0,8},{8,0},{16,24},{24,16},{1,9},{9,1},{17,25},{25,17},{2,10},{10... | collective-permute-start | bytes 1572872 | tf_op jit(solution)/shard_map/ppermute | solution.py:147
  44.6 24.8 %collective-permute-start.8 = (bf16[1024,256]{1,0:T(8,128)(2,1)}, bf16[1024,256]{1,0:T(8,128)(2,1)}, u32[]{:S(2)}, u32[]{:S(2)}) collective-permute-start(bf16[1024,256]{1,0:T(8,128)(2,1)} %get-tuple-element.44), channel_id=1, source_target_pairs={{0,16},{8,24},{16,0},{24,8},{1,17},{9,25},{17,1},{25,9},{2,18},{10... | collective-permute-start | bytes 1572872 | tf_op jit(solution)/shard_map/ppermute | solution.py:147
  46.1 23.2 %collective-permute-start.9 = (bf16[1024,256]{1,0:T(8,128)(2,1)}, bf16[1024,256]{1,0:T(8,128)(2,1)}, u32[]{:S(2)}, u32[]{:S(2)}) collective-permute-start(bf16[1024,256]{1,0:T(8,128)(2,1)} %get-tuple-element.43), channel_id=1, source_target_pairs={{0,24},{8,16},{16,8},{24,0},{1,25},{9,17},{17,9},{25,1},{2,26},{10... | collective-permute-start | bytes 1572872 | tf_op jit(solution)/shard_map/ppermute | solution.py:147
  79.2 15.7 %copy-start.1 = (bf16[1024,256]{1,0:T(8,128)(2,1)S(1)}, bf16[1024,256]{1,0:T(8,128)(2,1)}, u32[]{:S(2)}) copy-start(bf16[1024,256]{1,0:T(8,128)(2,1)} %param.12) | copy-start | bytes 1572868

commit v13 on v12

--- a/solution.py
+++ b/solution.py
@@ -52,6 +52,14 @@
         stacked, placing, (((1,), (0,)), ((), ())), preferred_element_type=jnp.float32
     )
     return placed[0].astype(jnp.int32) * 128 + placed[1].astype(jnp.int32)
+
+
+def split_three(values):
+    high = values.astype(jnp.bfloat16)
+    rest = values - high.astype(jnp.float32)
+    middle = rest.astype(jnp.bfloat16)
+    low = (rest - middle.astype(jnp.float32)).astype(jnp.bfloat16)
+    return jnp.stack([high, middle, low], axis=1)
 
 
 def conjugate_solve(slot_rows, confidence, weights, gram_matrix):
@@ -65,22 +73,23 @@
     direction = right_side
     norm_now = jnp.sum(residual * residual, axis=1, keepdims=True)
     for iteration in range(CG_STEPS):
-        projected = jnp.einsum(
-            "usk,uk->us",
-            slot_rows,
-            direction,
-            precision=highest,
-            preferred_element_type=jnp.float32,
+        projected = jnp.sum(
+            jnp.einsum(
+                "usk,uvk->usv", slot_rows, split_three(direction), preferred_element_type=jnp.float32
+            ),
+            axis=2,
         )
         image_vec = (
             jnp.dot(direction, gram_matrix, precision=highest)
             + REG_LAMBDA * direction
-            + jnp.einsum(
-                "us,usk->uk",
-                confidence * projected,
-                slot_rows,
-                precision=highest,
-                preferred_element_type=jnp.float32,
+            + jnp.sum(
+                jnp.einsum(
+                    "uvs,usk->uvk",
+                    split_three(confidence * projected),
+                    slot_rows,
+                    preferred_element_type=jnp.float32,
+                ),
+                axis=1,
             )
             / rank_width
         )

time: 96.6 us -> 94.6 us (0.979)
  matrix products: 21.8 us -> 19.4 us
    dot_general x6, matrix products: 4.39 us -> 2.03 us  [the longest x3 1.18 us: conjugate_solve(): jnp.einsum('usk,uvk->usv', slot_rows, split_three(direction), preferred_e...]
    another operation x4 -> x15, other arithmetic: 2.62 us -> 2.88 us
  transfers between devices with their start and end apart: 10 -> 10, of which waited for: 1 -> 1; matrix products, arithmetic and copies ran while one was open for 45% -> 46% of each run, Pallas kernels for 0% -> 0%
where the time goes in v13:
time: 94.6 us; the launch traced here: 94.1 us
  local copies, waits for them, and re-layouts  39.1 us (41%)
  matrix products  19.4 us (21%)
  blocking collectives  12.5 us (13%)
  starting transfers between devices  11.7 us (12%)
  other arithmetic  7.18 us (8%)
  waiting for transfers between devices  3.78 us (4%)
    gather x1, local copies, waits for them, and re-layouts, per_device(): remote = item_table[jnp.stack(by_offset[1:], axis=0)]  16.6 us
    all_to_all x1, blocking collectives, per_device(): lax.all_to_all(payload, ('table', 'batch', 'ctx'), split_axis=0, concat_a...  12.5 us
    gather x1, local copies, waits for them, and re-layouts, per_device(): got = [late_items[local_requests]]  9.07 us
    gather x1, local copies, waits for them, and re-layouts, per_device(): late_contexts[context_flat].astype(jnp.float32)  7.67 us
    dot_general x2, matrix products, gram_of(): lax.dot_general(table_rows, table_rows, (((0,), (0,)), ((), ())), preferr...  5.48 us
    ppermute x3, starting transfers between devices, per_device(): by_offset.append(lax.ppermute(outgoing, 'table', pairs))  4.54 us
    dot_general x1, matrix products, per_device(): jnp.dot(placing, fetched.reshape((n_table - 1) * capacity, rank_width), p...  4.23 us
    ppermute x3, waiting for transfers between devices, per_device(): got.append(lax.ppermute(remote[k - 1], 'table', pairs))  3.76 us
  transfers between devices with their start and end apart: 10, of which 1 were waited for; matrix products, arithmetic and copies ran while one was open for 46% of the time, Pallas kernels for 0%

profile of v13, /device:TPU:0, one launch (start us, length us, event | category | flops | bytes accessed | tf_op | source)
XLA Modules:
  0.0 94.1 jit_solution(8926793483547376093)
XLA Ops:
  0.0 0.9 eq.127
  0.9 1.1 %reduce-window.6 = s32[4,16,128]{2,1,0:T(8,128)S(1)} reduce-window(s32[4,16,128]{2,1,0:T(8,128)S(1)} %fusion.55, s32[]{:T(128)} %constant.154.clone.1), window={size=1x1x128 pad=0_0x0_0x127_0}, to_apply=%region_2.3 | reduce-window | flops 1040384 | bytes 65540 | tf_op jit(solution)/shard_map/reduce-window
  2.1 0.2 slice_reduce_fusion
  2.3 0.2 reduce-window.9
  2.5 0.1 select_reduce_fusion
  2.6 0.5 broadcast.432
  3.1 1.4 %reduce.18 = s32[32,64]{1,0:T(8,128)S(1)} reduce(s32[32,64,1]{1,2,0:T(1,128)} %param.13, s32[]{:T(128)} %broadcast.432), dimensions={2}, to_apply=%param.13.reduce_sub_computation.5 | reduce | bytes 16388 | tf_op args[3]
  4.5 0.1 reshape.493
  4.6 0.8 reshape.495
  5.5 1.7 %fusion.6 = f32[4,2,1024]{2,0,1:T(4,128)S(1)} fusion(s32[2048]{0:T(1024)S(1)} %get-tuple-element.66, s32[2,2048]{1,0:T(2,128)S(1)} %pad_add_fusion, pred[4,2048]{1,0:T(4,128)(4,1)S(1)} %iota_compare_fusion.6), kind=kOutput, calls=%fused_computation.11 | convolution fusion | flops 35684352 | bytes 65536 | tf_op jit(solution)/shard_map/dot_general | solution.py:128
  7.3 3.0 %collective-permute-start = (s32[1024]{0:T(1024)S(1)}, s32[1024]{0:T(1024)S(1)}, u32[]{:S(2)}, u32[]{:S(2)}) collective-permute-start(s32[1024]{0:T(1024)S(1)} %bitcast.163), channel_id=1, source_target_pairs={{0,8},{8,0},{16,24},{24,16},{1,9},{9,1},{17,25},{25,17},{2,10},{10... | collective-permute-start | bytes 12296 | tf_op jit(solution)/shard_map/ppermute | solution.py:139
  10.3 1.5 %collective-permute-start.1 = (s32[1024]{0:T(1024)S(1)}, s32[1024]{0:T(1024)S(1)}, u32[]{:S(2)}, u32[]{:S(2)}) collective-permute-start(s32[1024]{0:T(1024)S(1)} %bitcast.162), channel_id=1, source_target_pairs={{0,16},{8,24},{16,0},{24,8},{1,17},{9,25},{17,1},{25,9},{2,18},{10... | collective-permute-start | bytes 12296 | tf_op jit(solution)/shard_map/ppermute | solution.py:139
  11.8 0.0 collective-permute-start.2
  11.8 4.7 %fusion.8 = f32[256,256]{1,0:T(8,128)S(1)} fusion(bf16[16384,256]{1,0:T(8,128)(2,1)} %param.10, s32[]{:T(128)S(6)} %select_n.128), kind=kOutput, calls=%fused_computation.12 | convolution fusion | flops 1073741824 | bytes 4456452 | tf_op jit(solution)/shard_map/dot_general | solution.py:15
  16.6 0.1 collective-permute-start.3
  16.7 0.6 compare_reduce_fusion
  17.3 0.7 fusion.107
  18.1 0.1 reshape.497
  18.3 0.2 reduce_window_sum.24
  18.5 0.1 convert_reduce_fusion.1
  18.6 0.2 fusion.74
  18.8 0.1 copy.134
  18.9 0.1 copy.133
  19.0 0.7 convert_select_fusion
  19.7 0.0 collective-permute-done
  19.7 0.0 collective-permute-done.1
  19.7 0.0 collective-permute-done.2
  19.7 0.0 collective-permute-done.3
  19.8 2.0 %collective-permute-start.4 = (bf16[256,256]{1,0:T(8,128)(2,1)S(1)}, bf16[256,256]{1,0:T(8,128)(2,1)S(1)}, u32[]{:S(2)}, u32[]{:S(2)}) collective-permute-start(bf16[256,256]{1,0:T(8,128)(2,1)S(1)} %get-tuple-element.39), channel_id=1, source_target_pairs={{0,8},{8,0},{16,24},{24,16},{1,9},{9,1},{17,25},{25,17},{2,10},{10... | collective-permute-start | bytes 393224 | tf_op jit(solution)/shard_map/ppermute | solution.py:36
  21.8 1.5 %collective-permute-start.5 = (bf16[256,256]{1,0:T(8,128)(2,1)S(1)}, bf16[256,256]{1,0:T(8,128)(2,1)S(1)}, u32[]{:S(2)}, u32[]{:S(2)}) collective-permute-start(bf16[256,256]{1,0:T(8,128)(2,1)S(1)} %get-tuple-element.39), channel_id=1, source_target_pairs={{0,16},{8,24},{16,0},{24,8},{1,17},{9,25},{17,1},{25,9},{2,18},{10... | collective-permute-start | bytes 393224 | tf_op jit(solution)/shard_map/ppermute | solution.py:36
  23.3 0.0 collective-permute-start.6
  23.3 16.6 %gather_fusion = bf16[3072,256]{1,0:T(8,128)(2,1)} fusion(bf16[16384,256]{1,0:T(8,128)(2,1)} %param.10, s32[3072]{0:T(1024)S(1)} %broadcast_clamp_fusion), kind=kCustom, calls=%fused_computation | custom fusion | bytes 3158016 | tf_op jit(solution)/shard_map/gather | solution.py:148
  39.9 0.1 multiply_multiply_fusion
  40.0 2.6 %slice_bitcast_fusion.2 = (bf16[1024,256]{1,0:T(8,128)(2,1)}, bf16[1024,256]{1,0:T(8,128)(2,1)}, bf16[1024,256]{1,0:T(8,128)(2,1)}) fusion(bf16[3,1024,256]{2,1,0:T(8,128)(2,1)} %bitcast.152), kind=kLoop, calls=%fused_computation.40 | loop fusion | bytes 3145728 | tf_op jit(solution)/shard_map/squeeze | solution.py:156
  42.6 1.9 %collective-permute-start.7 = (bf16[1024,256]{1,0:T(8,128)(2,1)}, bf16[1024,256]{1,0:T(8,128)(2,1)}, u32[]{:S(2)}, u32[]{:S(2)}) collective-permute-start(bf16[1024,256]{1,0:T(8,128)(2,1)} %get-tuple-element.46), channel_id=1, source_target_pairs={{0,8},{8,0},{16,24},{24,16},{1,9},{9,1},{17,25},{25,17},{2,10},{10... | collective-permute-start | bytes 1572872 | tf_op jit(solution)/shard_map/ppermute | solution.py:156
  44.6 1.5 %collective-permute-start.8 = (bf16[1024,256]{1,0:T(8,128)(2,1)}, bf16[1024,256]{1,0:T(8,128)(2,1)}, u32[]{:S(2)}, u32[]{:S(2)}) collective-permute-start(bf16[1024,256]{1,0:T(8,128)(2,1)} %get-tuple-element.48), channel_id=1, source_target_pairs={{0,16},{8,24},{16,0},{24,8},{1,17},{9,25},{17,1},{25,9},{2,18},{10... | collective-permute-start | bytes 1572872 | tf_op jit(solution)/shard_map/ppermute | solution.py:156
  46.1 0.0 collective-permute-start.9
  46.1 9.1 %gather_fusion.1 = bf16[1024,256]{1,0:T(8,128)(2,1)} fusion(bf16[16384,256]{1,0:T(8,128)(2,1)} %param.10, s32[1024]{0:T(1024)S(1)} %fusion.93), kind=kCustom, calls=%fused_computation.1 | custom fusion | bytes 1052672 | tf_op jit(solution)/shard_map/gather | solution.py:153
  55.2 7.7 %gather_fusion.2 = bf16[2048,256]{1,0:T(8,128)(2,1)S(1)} fusion(bf16[4096,256]{1,0:T(8,128)(2,1)S(1)} %copy-done, s32[2048]{0:T(1024)S(1)} %broadcast_clamp_fusion.1), kind=kCustom, calls=%fused_computation.2 | custom fusion | bytes 2105344 | tf_op jit(solution)/shard_map/gather | solution.py:169
  62.9 2.7 %fusion.4 = f32[2048,256]{1,0:T(8,128)S(1)} fusion(bf16[1024,256]{1,0:T(8,128)(2,1)} %gather_fusion.1, s32[2048]{0:T(1024)S(1)} %get-tuple-element.65), kind=kOutput, calls=%fused_computation.9 | convolution fusion | flops 1075838976 | bytes 2629632 | tf_op jit(solution)/shard_map/dot_general | solution.py:161
  65.6 0.0 collective-permute-done.7
  65.6 3.8 %collective-permute-done.8 = bf16[1024,256]{1,0:T(8,128)(2,1)} collective-permute-done((bf16[1024,256]{1,0:T(8,128)(2,1)}, bf16[1024,256]{1,0:T(8,128)(2,1)}, u32[]{:S(2)}, u32[]{:S(2)}) %collective-permute-start.8) | collective-permute-done | bytes 524320 | tf_op jit(solution)/shard_map/ppermute | solution.py:156
  69.3 1.5 %pad_maximum_fusion = bf16[3,1024,256]{2,1,0:T(8,128)(2,1)S(1)} fusion(bf16[1,1024,256]{2,1,0:T(8,128)(2,1)} %bitcast.16, bf16[1,1024,256]{2,1,0:T(8,128)(2,1)} %bitcast.14, bf16[1,1024,256]{2,1,0:T(8,128)(2,1)} %bitcast.12), kind=kLoop, calls=%fused_computation.19 | loop fusion | flops 1572864 | bytes 3145728 | tf_op jit(solution)/shard_map/stack | solution.py:165
  70.9 4.2 %fusion.18 = bf16[2048,256]{1,0:T(8,128)(2,1)S(1)} fusion(f32[2048,256]{1,0:T(8,128)S(1)} %fusion.4, bf16[3072,256]{1,0:T(8,128)(2,1)S(1)} %bitcast.153, s32[3072]{0:T(1024)S(1)} %iota_add_fusion, s32[2048]{0:T(1024)S(1)} %get-tuple-element.65, bf16[2048,256]{1,0:T(8,128)(2,1)S(1)} %gather_fusion.2), kind=kOutput, calls=%fused_computation.18 | convolution fusion | flops 3229614080 | bytes 5787648 | tf_op jit(solution)/shard_map/dot_general | solution.py:166
  75.1 0.5 fusion.108
  75.7 0.4 convolution_reduce_fusion.5
  76.2 0.3 convolution_reduce_fusion.2
  76.4 0.3 multiply_reduce_fusion.3
  76.8 0.2 multiply_reduce_fusion.2
  77.0 0.1 convert_bitcast_fusion
  77.1 0.4 convolution_reduce_fusion.4
  77.6 0.3 convolution_reduce_fusion.1
  77.9 0.3 multiply_reduce_fusion.1
  78.3 0.2 multiply_reduce_fusion
  78.5 0.1 convert_bitcast_fusion.1
  78.6 0.4 convolution_reduce_fusion.3
  79.1 0.3 convolution_reduce_fusion
  79.3 0.3 fusion.27
  79.7 0.3 fusion.26
  80.0 12.5 %all_to_all.5 = f32[32,2,384]{2,1,0:T(2,128)S(1)} all-to-all(f32[32,2,384]{2,1,0:T(2,128)S(1)} %bitcast.154), channel_id=1, replica_groups=mesh['table'=4,'batch'=4,'ctx'=2] {'table','batch','ctx'}, dimensions={0} | all-to-all | bytes 196608 | tf_op jit(solution)/shard_map/all_to_all | solution.py:196
  92.6 0.1 reshape.500
  92.6 0.1 fusion.33
  92.7 0.1 convert_reduce_fusion
  92.9 1.3 %fusion.21 = bf16[1024,256]{1,0:T(8,128)(2,1)} fusion(bf16[1024,256]{1,0:T(8,128)(2,1)S(1)} %copy-done.1, pred[1024]{0:T(1024)(128)(4,1)S(1)} %broadcast_compare_fusion, s32[64]{0:T(128)S(1)} %fusion.33, f32[64,384]{1,0:T(8,128)S(1)} %reshape.500), kind=kOutput, calls=%fused_computation.21 | convolution fusion | flops 34144256 | bytes 1082880 | tf_op jit(solution)/shard_map/dot_general | solution.py:203
  (65 shorter events, 0.7 us)
Async XLA Ops:
  0.0 17.3 %copy-start = (bf16[4096,256]{1,0:T(8,128)(2,1)S(1)}, bf16[4096,256]{1,0:T(8,128)(2,1)}, u32[]{:S(2)}) copy-start(bf16[4096,256]{1,0:T(8,128)(2,1)} %param.11) | copy-start | bytes 6291460
  7.3 12.4 %collective-permute-start = (s32[1024]{0:T(1024)S(1)}, s32[1024]{0:T(1024)S(1)}, u32[]{:S(2)}, u32[]{:S(2)}) collective-permute-start(s32[1024]{0:T(1024)S(1)} %bitcast.163), channel_id=1, source_target_pairs={{0,8},{8,0},{16,24},{24,16},{1,9},{9,1},{17,25},{25,17},{2,10},{10... | collective-permute-start | bytes 12296 | tf_op jit(solution)/shard_map/ppermute | solution.py:139
  10.3 9.4 %collective-permute-start.1 = (s32[1024]{0:T(1024)S(1)}, s32[1024]{0:T(1024)S(1)}, u32[]{:S(2)}, u32[]{:S(2)}) collective-permute-start(s32[1024]{0:T(1024)S(1)} %bitcast.162), channel_id=1, source_target_pairs={{0,16},{8,24},{16,0},{24,8},{1,17},{9,25},{17,1},{25,9},{2,18},{10... | collective-permute-start | bytes 12296 | tf_op jit(solution)/shard_map/ppermute | solution.py:139
  11.8 7.9 %collective-permute-start.2 = (s32[1024]{0:T(1024)S(1)}, s32[1024]{0:T(1024)S(1)}, u32[]{:S(2)}, u32[]{:S(2)}) collective-permute-start(s32[1024]{0:T(1024)S(1)} %bitcast.161), channel_id=1, source_target_pairs={{0,24},{8,16},{16,8},{24,0},{1,25},{9,17},{17,9},{25,1},{2,26},{10... | collective-permute-start | bytes 12296 | tf_op jit(solution)/shard_map/ppermute | solution.py:139
  16.6 3.1 %collective-permute-start.3 = (f32[256,256]{1,0:T(8,128)S(1)}, f32[256,256]{1,0:T(8,128)S(1)}, u32[]{:S(2)}, u32[]{:S(2)}) collective-permute-start(f32[256,256]{1,0:T(8,128)S(1)} %fusion.8), channel_id=1, source_target_pairs={{0,1},{1,0},{2,3},{3,2},{4,5},{5,4},{6,7},{7,6},{8,9},{9,8},{10,11... | collective-permute-start | bytes 786440 | tf_op jit(solution)/shard_map/ppermute | solution.py:26
  17.3 0.8 copy-start.3
  17.3 0.9 copy-start.2
  17.3 0.9 copy-start.4
  19.8 20.2 %collective-permute-start.4 = (bf16[256,256]{1,0:T(8,128)(2,1)S(1)}, bf16[256,256]{1,0:T(8,128)(2,1)S(1)}, u32[]{:S(2)}, u32[]{:S(2)}) collective-permute-start(bf16[256,256]{1,0:T(8,128)(2,1)S(1)} %get-tuple-element.39), channel_id=1, source_target_pairs={{0,8},{8,0},{16,24},{24,16},{1,9},{9,1},{17,25},{25,17},{2,10},{10... | collective-permute-start | bytes 393224 | tf_op jit(solution)/shard_map/ppermute | solution.py:36
  21.8 18.1 %collective-permute-start.5 = (bf16[256,256]{1,0:T(8,128)(2,1)S(1)}, bf16[256,256]{1,0:T(8,128)(2,1)S(1)}, u32[]{:S(2)}, u32[]{:S(2)}) collective-permute-start(bf16[256,256]{1,0:T(8,128)(2,1)S(1)} %get-tuple-element.39), channel_id=1, source_target_pairs={{0,16},{8,24},{16,0},{24,8},{1,17},{9,25},{17,1},{25,9},{2,18},{10... | collective-permute-start | bytes 393224 | tf_op jit(solution)/shard_map/ppermute | solution.py:36
  23.3 16.6 %collective-permute-start.6 = (bf16[256,256]{1,0:T(8,128)(2,1)S(1)}, bf16[256,256]{1,0:T(8,128)(2,1)S(1)}, u32[]{:S(2)}, u32[]{:S(2)}) collective-permute-start(bf16[256,256]{1,0:T(8,128)(2,1)S(1)} %get-tuple-element.39), channel_id=1, source_target_pairs={{0,24},{8,16},{16,8},{24,0},{1,25},{9,17},{17,9},{25,1},{2,26},{10... | collective-permute-start | bytes 393224 | tf_op jit(solution)/shard_map/ppermute | solution.py:36
  42.6 22.9 %collective-permute-start.7 = (bf16[1024,256]{1,0:T(8,128)(2,1)}, bf16[1024,256]{1,0:T(8,128)(2,1)}, u32[]{:S(2)}, u32[]{:S(2)}) collective-permute-start(bf16[1024,256]{1,0:T(8,128)(2,1)} %get-tuple-element.46), channel_id=1, source_target_pairs={{0,8},{8,0},{16,24},{24,16},{1,9},{9,1},{17,25},{25,17},{2,10},{10... | collective-permute-start | bytes 1572872 | tf_op jit(solution)/shard_map/ppermute | solution.py:156
  44.6 24.8 %collective-permute-start.8 = (bf16[1024,256]{1,0:T(8,128)(2,1)}, bf16[1024,256]{1,0:T(8,128)(2,1)}, u32[]{:S(2)}, u32[]{:S(2)}) collective-permute-start(bf16[1024,256]{1,0:T(8,128)(2,1)} %get-tuple-element.48), channel_id=1, source_target_pairs={{0,16},{8,24},{16,0},{24,8},{1,17},{9,25},{17,1},{25,9},{2,18},{10... | collective-permute-start | bytes 1572872 | tf_op jit(solution)/shard_map/ppermute | solution.py:156
  46.1 23.2 %collective-permute-start.9 = (bf16[1024,256]{1,0:T(8,128)(2,1)}, bf16[1024,256]{1,0:T(8,128)(2,1)}, u32[]{:S(2)}, u32[]{:S(2)}) collective-permute-start(bf16[1024,256]{1,0:T(8,128)(2,1)} %get-tuple-element.47), channel_id=1, source_target_pairs={{0,24},{8,16},{16,8},{24,0},{1,25},{9,17},{17,9},{25,1},{2,26},{10... | collective-permute-start | bytes 1572872 | tf_op jit(solution)/shard_map/ppermute | solution.py:156
  78.2 14.6 %copy-start.1 = (bf16[1024,256]{1,0:T(8,128)(2,1)S(1)}, bf16[1024,256]{1,0:T(8,128)(2,1)}, u32[]{:S(2)}) copy-start(bf16[1024,256]{1,0:T(8,128)(2,1)} %param.12) | copy-start | bytes 1572868

commit v14 on v13

--- a/solution.py
+++ b/solution.py
@@ -55,11 +55,11 @@
 
 
 def split_three(values):
-    high = values.astype(jnp.bfloat16)
-    rest = values - high.astype(jnp.float32)
-    middle = rest.astype(jnp.bfloat16)
-    low = (rest - middle.astype(jnp.float32)).astype(jnp.bfloat16)
-    return jnp.stack([high, middle, low], axis=1)
+    high = lax.reduce_precision(values, exponent_bits=8, mantissa_bits=7)
+    rest = values - high
+    middle = lax.reduce_precision(rest, exponent_bits=8, mantissa_bits=7)
+    low = rest - middle
+    return jnp.stack([high, middle, low], axis=1).astype(jnp.bfloat16)
 
 
 def conjugate_solve(slot_rows, confidence, weights, gram_matrix):

time: 94.6 us -> 94.7 us (level)
  no operation moved by 1% of the time
where the time goes in v14:
time: 94.7 us; the launch traced here: 94.2 us
  local copies, waits for them, and re-layouts  39.1 us (41%)
  matrix products  19.4 us (20%)
  blocking collectives  12.5 us (13%)
  starting transfers between devices  11.7 us (12%)
  other arithmetic  7.19 us (8%)
  waiting for transfers between devices  3.78 us (4%)
    gather x1, local copies, waits for them, and re-layouts, per_device(): remote = item_table[jnp.stack(by_offset[1:], axis=0)]  16.6 us
    all_to_all x1, blocking collectives, per_device(): lax.all_to_all(payload, ('table', 'batch', 'ctx'), split_axis=0, concat_a...  12.5 us
    gather x1, local copies, waits for them, and re-layouts, per_device(): got = [late_items[local_requests]]  9.07 us
    gather x1, local copies, waits for them, and re-layouts, per_device(): late_contexts[context_flat].astype(jnp.float32)  7.67 us
    dot_general x2, matrix products, gram_of(): lax.dot_general(table_rows, table_rows, (((0,), (0,)), ((), ())), preferr...  5.48 us
    ppermute x3, starting transfers between devices, per_device(): by_offset.append(lax.ppermute(outgoing, 'table', pairs))  4.54 us
    dot_general x1, matrix products, per_device(): jnp.dot(placing, fetched.reshape((n_table - 1) * capacity, rank_width), p...  4.23 us
    ppermute x3, waiting for transfers between devices, per_device(): got.append(lax.ppermute(remote[k - 1], 'table', pairs))  3.76 us
  transfers between devices with their start and end apart: 10, of which 1 were waited for; matrix products, arithmetic and copies ran while one was open for 46% of the time, Pallas kernels for 0%

profile of v14, /device:TPU:0, one launch (start us, length us, event | category | flops | bytes accessed | tf_op | source)
XLA Modules:
  0.0 94.2 jit_solution(12472892274330218698)
XLA Ops:
  0.0 0.9 eq.127
  0.9 1.1 %reduce-window.6 = s32[4,16,128]{2,1,0:T(8,128)S(1)} reduce-window(s32[4,16,128]{2,1,0:T(8,128)S(1)} %fusion.58, s32[]{:T(128)} %constant.154.clone.1), window={size=1x1x128 pad=0_0x0_0x127_0}, to_apply=%region_2.3 | reduce-window | flops 1040384 | bytes 65540 | tf_op jit(solution)/shard_map/reduce-window
  2.1 0.2 slice_reduce_fusion
  2.3 0.2 reduce-window.9
  2.5 0.1 select_reduce_fusion
  2.6 0.5 broadcast.432
  3.1 1.4 %reduce.18 = s32[32,64]{1,0:T(8,128)S(1)} reduce(s32[32,64,1]{1,2,0:T(1,128)} %param.13, s32[]{:T(128)} %broadcast.432), dimensions={2}, to_apply=%param.13.reduce_sub_computation.5 | reduce | bytes 16388 | tf_op args[3]
  4.5 0.1 reshape.493
  4.6 0.8 reshape.495
  5.5 1.7 %fusion.6 = f32[4,2,1024]{2,0,1:T(4,128)S(1)} fusion(s32[2048]{0:T(1024)S(1)} %get-tuple-element.66, s32[2,2048]{1,0:T(2,128)S(1)} %pad_add_fusion, pred[4,2048]{1,0:T(4,128)(4,1)S(1)} %iota_compare_fusion.6), kind=kOutput, calls=%fused_computation.11 | convolution fusion | flops 35684352 | bytes 65536 | tf_op jit(solution)/shard_map/dot_general | solution.py:128
  7.3 3.0 %collective-permute-start = (s32[1024]{0:T(1024)S(1)}, s32[1024]{0:T(1024)S(1)}, u32[]{:S(2)}, u32[]{:S(2)}) collective-permute-start(s32[1024]{0:T(1024)S(1)} %bitcast.157), channel_id=1, source_target_pairs={{0,8},{8,0},{16,24},{24,16},{1,9},{9,1},{17,25},{25,17},{2,10},{10... | collective-permute-start | bytes 12296 | tf_op jit(solution)/shard_map/ppermute | solution.py:139
  10.3 1.5 %collective-permute-start.1 = (s32[1024]{0:T(1024)S(1)}, s32[1024]{0:T(1024)S(1)}, u32[]{:S(2)}, u32[]{:S(2)}) collective-permute-start(s32[1024]{0:T(1024)S(1)} %bitcast.156), channel_id=1, source_target_pairs={{0,16},{8,24},{16,0},{24,8},{1,17},{9,25},{17,1},{25,9},{2,18},{10... | collective-permute-start | bytes 12296 | tf_op jit(solution)/shard_map/ppermute | solution.py:139
  11.8 0.0 collective-permute-start.2
  11.8 4.7 %fusion.8 = f32[256,256]{1,0:T(8,128)S(1)} fusion(bf16[16384,256]{1,0:T(8,128)(2,1)} %param.10, s32[]{:T(128)S(6)} %select_n.128), kind=kOutput, calls=%fused_computation.12 | convolution fusion | flops 1073741824 | bytes 4456452 | tf_op jit(solution)/shard_map/dot_general | solution.py:15
  16.6 0.1 collective-permute-start.3
  16.7 0.6 compare_reduce_fusion
  17.3 0.7 fusion.112
  18.1 0.1 reshape.497
  18.3 0.2 reduce_window_sum.24
  18.5 0.1 convert_reduce_fusion.1
  18.6 0.2 fusion.80
  18.8 0.1 copy.134
  18.9 0.1 copy.133
  19.0 0.7 convert_select_fusion
  19.7 0.0 collective-permute-done
  19.7 0.0 collective-permute-done.1
  19.7 0.0 collective-permute-done.2
  19.7 0.0 collective-permute-done.3
  19.8 2.0 %collective-permute-start.4 = (bf16[256,256]{1,0:T(8,128)(2,1)S(1)}, bf16[256,256]{1,0:T(8,128)(2,1)S(1)}, u32[]{:S(2)}, u32[]{:S(2)}) collective-permute-start(bf16[256,256]{1,0:T(8,128)(2,1)S(1)} %get-tuple-element.39), channel_id=1, source_target_pairs={{0,8},{8,0},{16,24},{24,16},{1,9},{9,1},{17,25},{25,17},{2,10},{10... | collective-permute-start | bytes 393224 | tf_op jit(solution)/shard_map/ppermute | solution.py:36
  21.8 1.5 %collective-permute-start.5 = (bf16[256,256]{1,0:T(8,128)(2,1)S(1)}, bf16[256,256]{1,0:T(8,128)(2,1)S(1)}, u32[]{:S(2)}, u32[]{:S(2)}) collective-permute-start(bf16[256,256]{1,0:T(8,128)(2,1)S(1)} %get-tuple-element.39), channel_id=1, source_target_pairs={{0,16},{8,24},{16,0},{24,8},{1,17},{9,25},{17,1},{25,9},{2,18},{10... | collective-permute-start | bytes 393224 | tf_op jit(solution)/shard_map/ppermute | solution.py:36
  23.3 0.0 collective-permute-start.6
  23.3 16.6 %gather_fusion = bf16[3072,256]{1,0:T(8,128)(2,1)} fusion(bf16[16384,256]{1,0:T(8,128)(2,1)} %param.10, s32[3072]{0:T(1024)S(1)} %broadcast_clamp_fusion), kind=kCustom, calls=%fused_computation | custom fusion | bytes 3158016 | tf_op jit(solution)/shard_map/gather | solution.py:148
  39.9 0.1 multiply_multiply_fusion
  40.0 2.6 %slice_bitcast_fusion.2 = (bf16[1024,256]{1,0:T(8,128)(2,1)}, bf16[1024,256]{1,0:T(8,128)(2,1)}, bf16[1024,256]{1,0:T(8,128)(2,1)}) fusion(bf16[3,1024,256]{2,1,0:T(8,128)(2,1)} %bitcast.146), kind=kLoop, calls=%fused_computation.40 | loop fusion | bytes 3145728 | tf_op jit(solution)/shard_map/squeeze | solution.py:156
  42.6 1.9 %collective-permute-start.7 = (bf16[1024,256]{1,0:T(8,128)(2,1)}, bf16[1024,256]{1,0:T(8,128)(2,1)}, u32[]{:S(2)}, u32[]{:S(2)}) collective-permute-start(bf16[1024,256]{1,0:T(8,128)(2,1)} %get-tuple-element.46), channel_id=1, source_target_pairs={{0,8},{8,0},{16,24},{24,16},{1,9},{9,1},{17,25},{25,17},{2,10},{10... | collective-permute-start | bytes 1572872 | tf_op jit(solution)/shard_map/ppermute | solution.py:156
  44.6 1.5 %collective-permute-start.8 = (bf16[1024,256]{1,0:T(8,128)(2,1)}, bf16[1024,256]{1,0:T(8,128)(2,1)}, u32[]{:S(2)}, u32[]{:S(2)}) collective-permute-start(bf16[1024,256]{1,0:T(8,128)(2,1)} %get-tuple-element.48), channel_id=1, source_target_pairs={{0,16},{8,24},{16,0},{24,8},{1,17},{9,25},{17,1},{25,9},{2,18},{10... | collective-permute-start | bytes 1572872 | tf_op jit(solution)/shard_map/ppermute | solution.py:156
  46.1 0.0 collective-permute-start.9
  46.1 9.1 %gather_fusion.1 = bf16[1024,256]{1,0:T(8,128)(2,1)} fusion(bf16[16384,256]{1,0:T(8,128)(2,1)} %param.10, s32[1024]{0:T(1024)S(1)} %fusion.98), kind=kCustom, calls=%fused_computation.1 | custom fusion | bytes 1052672 | tf_op jit(solution)/shard_map/gather | solution.py:153
  55.2 7.7 %gather_fusion.2 = bf16[2048,256]{1,0:T(8,128)(2,1)S(1)} fusion(bf16[4096,256]{1,0:T(8,128)(2,1)S(1)} %copy-done, s32[2048]{0:T(1024)S(1)} %broadcast_clamp_fusion.1), kind=kCustom, calls=%fused_computation.2 | custom fusion | bytes 2105344 | tf_op jit(solution)/shard_map/gather | solution.py:169
  62.9 2.7 %fusion.4 = f32[2048,256]{1,0:T(8,128)S(1)} fusion(bf16[1024,256]{1,0:T(8,128)(2,1)} %gather_fusion.1, s32[2048]{0:T(1024)S(1)} %get-tuple-element.65), kind=kOutput, calls=%fused_computation.9 | convolution fusion | flops 1075838976 | bytes 2629632 | tf_op jit(solution)/shard_map/dot_general | solution.py:161
  65.6 0.0 collective-permute-done.7
  65.6 3.8 %collective-permute-done.8 = bf16[1024,256]{1,0:T(8,128)(2,1)} collective-permute-done((bf16[1024,256]{1,0:T(8,128)(2,1)}, bf16[1024,256]{1,0:T(8,128)(2,1)}, u32[]{:S(2)}, u32[]{:S(2)}) %collective-permute-start.8) | collective-permute-done | bytes 524320 | tf_op jit(solution)/shard_map/ppermute | solution.py:156
  69.3 1.5 %pad_maximum_fusion = bf16[3,1024,256]{2,1,0:T(8,128)(2,1)S(1)} fusion(bf16[1,1024,256]{2,1,0:T(8,128)(2,1)} %bitcast.16, bf16[1,1024,256]{2,1,0:T(8,128)(2,1)} %bitcast.14, bf16[1,1024,256]{2,1,0:T(8,128)(2,1)} %bitcast.12), kind=kLoop, calls=%fused_computation.19 | loop fusion | flops 1572864 | bytes 3145728 | tf_op jit(solution)/shard_map/stack | solution.py:165
  70.9 4.2 %fusion.18 = bf16[2048,256]{1,0:T(8,128)(2,1)S(1)} fusion(f32[2048,256]{1,0:T(8,128)S(1)} %fusion.4, bf16[3072,256]{1,0:T(8,128)(2,1)S(1)} %bitcast.147, s32[3072]{0:T(1024)S(1)} %iota_add_fusion, s32[2048]{0:T(1024)S(1)} %get-tuple-element.65, bf16[2048,256]{1,0:T(8,128)(2,1)S(1)} %gather_fusion.2), kind=kOutput, calls=%fused_computation.18 | convolution fusion | flops 3229614080 | bytes 5787648 | tf_op jit(solution)/shard_map/dot_general | solution.py:166
  75.1 0.5 fusion.113
  75.7 0.4 convolution_reduce_fusion.5
  76.2 0.3 convolution_reduce_fusion.2
  76.5 0.3 multiply_reduce_fusion.3
  76.8 0.2 multiply_reduce_fusion.2
  77.0 0.1 fusion.70
  77.1 0.4 convolution_reduce_fusion.4
  77.6 0.3 convolution_reduce_fusion.1
  77.9 0.3 multiply_reduce_fusion.1
  78.3 0.2 multiply_reduce_fusion
  78.5 0.1 fusion.72
  78.6 0.4 convolution_reduce_fusion.3
  79.1 0.3 convolution_reduce_fusion
  79.4 0.3 fusion.27
  79.7 0.3 fusion.26
  80.1 12.5 %all_to_all.5 = f32[32,2,384]{2,1,0:T(2,128)S(1)} all-to-all(f32[32,2,384]{2,1,0:T(2,128)S(1)} %bitcast.148), channel_id=1, replica_groups=mesh['table'=4,'batch'=4,'ctx'=2] {'table','batch','ctx'}, dimensions={0} | all-to-all | bytes 196608 | tf_op jit(solution)/shard_map/all_to_all | solution.py:196
  92.6 0.1 reshape.500
  92.7 0.1 fusion.36
  92.8 0.1 convert_reduce_fusion
  92.9 1.3 %fusion.21 = bf16[1024,256]{1,0:T(8,128)(2,1)} fusion(bf16[1024,256]{1,0:T(8,128)(2,1)S(1)} %copy-done.1, pred[1024]{0:T(1024)(128)(4,1)S(1)} %broadcast_compare_fusion, s32[64]{0:T(128)S(1)} %fusion.36, f32[64,384]{1,0:T(8,128)S(1)} %reshape.500), kind=kOutput, calls=%fused_computation.21 | convolution fusion | flops 34144256 | bytes 1082880 | tf_op jit(solution)/shard_map/dot_general | solution.py:203
  (65 shorter events, 0.7 us)
Async XLA Ops:
  0.0 17.3 %copy-start = (bf16[4096,256]{1,0:T(8,128)(2,1)S(1)}, bf16[4096,256]{1,0:T(8,128)(2,1)}, u32[]{:S(2)}) copy-start(bf16[4096,256]{1,0:T(8,128)(2,1)} %param.11) | copy-start | bytes 6291460
  7.3 12.4 %collective-permute-start = (s32[1024]{0:T(1024)S(1)}, s32[1024]{0:T(1024)S(1)}, u32[]{:S(2)}, u32[]{:S(2)}) collective-permute-start(s32[1024]{0:T(1024)S(1)} %bitcast.157), channel_id=1, source_target_pairs={{0,8},{8,0},{16,24},{24,16},{1,9},{9,1},{17,25},{25,17},{2,10},{10... | collective-permute-start | bytes 12296 | tf_op jit(solution)/shard_map/ppermute | solution.py:139
  10.3 9.4 %collective-permute-start.1 = (s32[1024]{0:T(1024)S(1)}, s32[1024]{0:T(1024)S(1)}, u32[]{:S(2)}, u32[]{:S(2)}) collective-permute-start(s32[1024]{0:T(1024)S(1)} %bitcast.156), channel_id=1, source_target_pairs={{0,16},{8,24},{16,0},{24,8},{1,17},{9,25},{17,1},{25,9},{2,18},{10... | collective-permute-start | bytes 12296 | tf_op jit(solution)/shard_map/ppermute | solution.py:139
  11.8 7.9 %collective-permute-start.2 = (s32[1024]{0:T(1024)S(1)}, s32[1024]{0:T(1024)S(1)}, u32[]{:S(2)}, u32[]{:S(2)}) collective-permute-start(s32[1024]{0:T(1024)S(1)} %bitcast.155), channel_id=1, source_target_pairs={{0,24},{8,16},{16,8},{24,0},{1,25},{9,17},{17,9},{25,1},{2,26},{10... | collective-permute-start | bytes 12296 | tf_op jit(solution)/shard_map/ppermute | solution.py:139
  16.6 3.1 %collective-permute-start.3 = (f32[256,256]{1,0:T(8,128)S(1)}, f32[256,256]{1,0:T(8,128)S(1)}, u32[]{:S(2)}, u32[]{:S(2)}) collective-permute-start(f32[256,256]{1,0:T(8,128)S(1)} %fusion.8), channel_id=1, source_target_pairs={{0,1},{1,0},{2,3},{3,2},{4,5},{5,4},{6,7},{7,6},{8,9},{9,8},{10,11... | collective-permute-start | bytes 786440 | tf_op jit(solution)/shard_map/ppermute | solution.py:26
  17.3 0.8 copy-start.3
  17.3 0.9 copy-start.2
  17.3 0.9 copy-start.4
  19.8 20.2 %collective-permute-start.4 = (bf16[256,256]{1,0:T(8,128)(2,1)S(1)}, bf16[256,256]{1,0:T(8,128)(2,1)S(1)}, u32[]{:S(2)}, u32[]{:S(2)}) collective-permute-start(bf16[256,256]{1,0:T(8,128)(2,1)S(1)} %get-tuple-element.39), channel_id=1, source_target_pairs={{0,8},{8,0},{16,24},{24,16},{1,9},{9,1},{17,25},{25,17},{2,10},{10... | collective-permute-start | bytes 393224 | tf_op jit(solution)/shard_map/ppermute | solution.py:36
  21.8 18.1 %collective-permute-start.5 = (bf16[256,256]{1,0:T(8,128)(2,1)S(1)}, bf16[256,256]{1,0:T(8,128)(2,1)S(1)}, u32[]{:S(2)}, u32[]{:S(2)}) collective-permute-start(bf16[256,256]{1,0:T(8,128)(2,1)S(1)} %get-tuple-element.39), channel_id=1, source_target_pairs={{0,16},{8,24},{16,0},{24,8},{1,17},{9,25},{17,1},{25,9},{2,18},{10... | collective-permute-start | bytes 393224 | tf_op jit(solution)/shard_map/ppermute | solution.py:36
  23.3 16.6 %collective-permute-start.6 = (bf16[256,256]{1,0:T(8,128)(2,1)S(1)}, bf16[256,256]{1,0:T(8,128)(2,1)S(1)}, u32[]{:S(2)}, u32[]{:S(2)}) collective-permute-start(bf16[256,256]{1,0:T(8,128)(2,1)S(1)} %get-tuple-element.39), channel_id=1, source_target_pairs={{0,24},{8,16},{16,8},{24,0},{1,25},{9,17},{17,9},{25,1},{2,26},{10... | collective-permute-start | bytes 393224 | tf_op jit(solution)/shard_map/ppermute | solution.py:36
  42.6 22.9 %collective-permute-start.7 = (bf16[1024,256]{1,0:T(8,128)(2,1)}, bf16[1024,256]{1,0:T(8,128)(2,1)}, u32[]{:S(2)}, u32[]{:S(2)}) collective-permute-start(bf16[1024,256]{1,0:T(8,128)(2,1)} %get-tuple-element.46), channel_id=1, source_target_pairs={{0,8},{8,0},{16,24},{24,16},{1,9},{9,1},{17,25},{25,17},{2,10},{10... | collective-permute-start | bytes 1572872 | tf_op jit(solution)/shard_map/ppermute | solution.py:156
  44.6 24.8 %collective-permute-start.8 = (bf16[1024,256]{1,0:T(8,128)(2,1)}, bf16[1024,256]{1,0:T(8,128)(2,1)}, u32[]{:S(2)}, u32[]{:S(2)}) collective-permute-start(bf16[1024,256]{1,0:T(8,128)(2,1)} %get-tuple-element.48), channel_id=1, source_target_pairs={{0,16},{8,24},{16,0},{24,8},{1,17},{9,25},{17,1},{25,9},{2,18},{10... | collective-permute-start | bytes 1572872 | tf_op jit(solution)/shard_map/ppermute | solution.py:156
  46.1 23.2 %collective-permute-start.9 = (bf16[1024,256]{1,0:T(8,128)(2,1)}, bf16[1024,256]{1,0:T(8,128)(2,1)}, u32[]{:S(2)}, u32[]{:S(2)}) collective-permute-start(bf16[1024,256]{1,0:T(8,128)(2,1)} %get-tuple-element.47), channel_id=1, source_target_pairs={{0,24},{8,16},{16,8},{24,0},{1,25},{9,17},{17,9},{25,1},{2,26},{10... | collective-permute-start | bytes 1572872 | tf_op jit(solution)/shard_map/ppermute | solution.py:156
  78.2 14.6 %copy-start.1 = (bf16[1024,256]{1,0:T(8,128)(2,1)S(1)}, bf16[1024,256]{1,0:T(8,128)(2,1)}, u32[]{:S(2)}) copy-start(bf16[1024,256]{1,0:T(8,128)(2,1)} %param.12) | copy-start | bytes 1572868

commit v15 on v14

--- a/solution.py
+++ b/solution.py
@@ -185,9 +185,13 @@
     ).astype(jnp.bfloat16)
     filled = jnp.sum(user_placing.astype(jnp.float32), axis=0)
     placed_ids = place_integers(local_rows, user_placing)
-    send_ids = jnp.where(filled > 0.5, placed_ids, user_rows).astype(jnp.float32)
-    id_column = jnp.zeros((owner_count * user_capacity, 128), jnp.float32).at[:, 0].set(send_ids)
-    payload = jnp.concatenate([send_rows.astype(jnp.float32), id_column], axis=1)
+    send_ids = jnp.where(filled > 0.5, placed_ids, user_rows)
+    id_column = (
+        jnp.zeros((owner_count * user_capacity, 128), jnp.bfloat16)
+        .at[:, 0].set((send_ids // 128).astype(jnp.bfloat16))
+        .at[:, 1].set((send_ids % 128).astype(jnp.bfloat16))
+    )
+    payload = jnp.concatenate([send_rows, id_column], axis=1)
     payload = payload.reshape(owner_count, 1, user_capacity, rank_width + 128)
     n_ctx = lax.axis_size("ctx")
     payload = jnp.broadcast_to(
@@ -195,8 +199,8 @@
     ).reshape(owner_count * n_ctx, user_capacity, rank_width + 128)
     got = lax.all_to_all(payload, ("table", "batch", "ctx"), split_axis=0, concat_axis=0, tiled=True)
     got = got.reshape(owner_count * n_ctx * user_capacity, rank_width + 128)
-    all_rows = got[:, :rank_width].astype(jnp.bfloat16)
-    all_ids = got[:, rank_width].astype(jnp.int32)
+    all_rows = got[:, :rank_width]
+    all_ids = got[:, rank_width].astype(jnp.int32) * 128 + got[:, rank_width + 1].astype(jnp.int32)
     hitting = (jnp.arange(user_rows, dtype=jnp.int32)[:, None] == all_ids[None, :]).astype(
         jnp.bfloat16
     )

time: 94.7 us -> 96 us (1.014)
  other arithmetic: 7.19 us -> 8.69 us
    another operation x4 -> x5, other arithmetic: 2.62 us -> 4.05 us
  transfers between devices with their start and end apart: 10 -> 10, of which waited for: 1 -> 1; matrix products, arithmetic and copies ran while one was open for 46% -> 47% of each run, Pallas kernels for 0% -> 0%
where the time goes in v15:
time: 96 us; the launch traced here: 95.5 us
  local copies, waits for them, and re-layouts  39.1 us (41%)
  matrix products  19.4 us (20%)
  blocking collectives  12.1 us (13%)
  starting transfers between devices  11.7 us (12%)
  other arithmetic  8.69 us (9%)
  waiting for transfers between devices  3.96 us (4%)
    gather x1, local copies, waits for them, and re-layouts, per_device(): remote = item_table[jnp.stack(by_offset[1:], axis=0)]  16.8 us
    all_to_all x1, blocking collectives, per_device(): lax.all_to_all(payload, ('table', 'batch', 'ctx'), split_axis=0, concat_a...  12.1 us
    gather x1, local copies, waits for them, and re-layouts, per_device(): got = [late_items[local_requests]]  9.07 us
    gather x1, local copies, waits for them, and re-layouts, per_device(): late_contexts[context_flat].astype(jnp.float32)  7.49 us
    dot_general x2, matrix products, gram_of(): lax.dot_general(table_rows, table_rows, (((0,), (0,)), ((), ())), preferr...  5.48 us
    ppermute x3, starting transfers between devices, per_device(): by_offset.append(lax.ppermute(outgoing, 'table', pairs))  4.54 us
    dot_general x1, matrix products, per_device(): jnp.dot(placing, fetched.reshape((n_table - 1) * capacity, rank_width), p...  4.23 us
    another operation x5, other arithmetic  4.05 us
  transfers between devices with their start and end apart: 10, of which 1 were waited for; matrix products, arithmetic and copies ran while one was open for 47% of the time, Pallas kernels for 0%

profile of v15, /device:TPU:0, one launch (start us, length us, event | category | flops | bytes accessed | tf_op | source)
XLA Modules:
  0.0 95.5 jit_solution(1935653729595179224)
XLA Ops:
  0.0 0.9 eq.128
  0.9 1.1 %reduce-window.6 = s32[4,16,128]{2,1,0:T(8,128)S(1)} reduce-window(s32[4,16,128]{2,1,0:T(8,128)S(1)} %fusion.57, s32[]{:T(128)} %constant.191.clone.1), window={size=1x1x128 pad=0_0x0_0x127_0}, to_apply=%region_2.3 | reduce-window | flops 1040384 | bytes 65540 | tf_op jit(solution)/shard_map/reduce-window
  2.1 0.2 slice_reduce_fusion
  2.3 0.2 reduce-window.9
  2.5 0.1 select_reduce_fusion
  2.6 0.5 broadcast.549
  3.1 1.4 %reduce.26 = s32[32,64]{1,0:T(8,128)S(1)} reduce(s32[32,64,1]{1,2,0:T(1,128)} %param.15, s32[]{:T(128)} %broadcast.549), dimensions={2}, to_apply=%param.15.reduce_sub_computation.5 | reduce | bytes 16388 | tf_op args[3]
  4.5 0.1 reshape.577
  4.6 0.8 reshape.579
  5.5 1.7 %fusion.6 = f32[4,2,1024]{2,0,1:T(4,128)S(1)} fusion(s32[2048]{0:T(1024)S(1)} %get-tuple-element.80, s32[2,2048]{1,0:T(2,128)S(1)} %pad_add_fusion, pred[4,2048]{1,0:T(4,128)(4,1)S(1)} %iota_compare_fusion.5), kind=kOutput, calls=%fused_computation.11 | convolution fusion | flops 35684352 | bytes 65536 | tf_op jit(solution)/shard_map/dot_general | solution.py:128
  7.3 3.0 %collective-permute-start = (s32[1024]{0:T(1024)S(1)}, s32[1024]{0:T(1024)S(1)}, u32[]{:S(2)}, u32[]{:S(2)}) collective-permute-start(s32[1024]{0:T(1024)S(1)} %bitcast.157), channel_id=1, source_target_pairs={{0,8},{8,0},{16,24},{24,16},{1,9},{9,1},{17,25},{25,17},{2,10},{10... | collective-permute-start | bytes 12296 | tf_op jit(solution)/shard_map/ppermute | solution.py:139
  10.3 1.5 %collective-permute-start.1 = (s32[1024]{0:T(1024)S(1)}, s32[1024]{0:T(1024)S(1)}, u32[]{:S(2)}, u32[]{:S(2)}) collective-permute-start(s32[1024]{0:T(1024)S(1)} %bitcast.156), channel_id=1, source_target_pairs={{0,16},{8,24},{16,0},{24,8},{1,17},{9,25},{17,1},{25,9},{2,18},{10... | collective-permute-start | bytes 12296 | tf_op jit(solution)/shard_map/ppermute | solution.py:139
  11.8 0.0 collective-permute-start.2
  11.8 4.7 %fusion.8 = f32[256,256]{1,0:T(8,128)S(1)} fusion(bf16[16384,256]{1,0:T(8,128)(2,1)} %param.12, s32[]{:T(128)S(6)} %select_n.148), kind=kOutput, calls=%fused_computation.12 | convolution fusion | flops 1073741824 | bytes 4456452 | tf_op jit(solution)/shard_map/dot_general | solution.py:15
  16.6 0.1 collective-permute-start.3
  16.7 0.6 compare_reduce_fusion
  17.3 0.7 compare_reduce_fusion.1
  18.0 0.7 fusion.116
  18.8 0.1 reshape.581
  19.0 0.2 reduce_window_sum.24
  19.2 0.1 convert_reduce_fusion.1
  19.3 0.2 fusion.81
  19.5 0.1 copy.134
  19.6 0.1 copy.133
  19.7 1.4 %fusion.88 = (bf16[32,1]{1,0:T(8,128)(2,1)S(1)}, bf16[32,1]{1,0:T(8,128)(2,1)S(1)}) fusion(pred[32,1]{1,0:T(8,128)(4,1)S(1)} %copy.133, s32[32,1]{1,0:T(8,128)S(1)} %copy.134, pred[]{:T(512)} %compare_reduce_fusion, pred[]{:T(512)} %compare_reduce_fusion.1), kind=kLoop, calls=%fused_computation.174 | loop fusion | flops 768 | bytes 290 | tf_op jit(solution)/shard_map/select.103
  21.1 0.1 scatter.9
  21.2 0.0 collective-permute-done
  21.3 0.0 collective-permute-done.1
  21.3 0.0 collective-permute-done.3
  21.4 2.0 %collective-permute-start.4 = (bf16[256,256]{1,0:T(8,128)(2,1)S(1)}, bf16[256,256]{1,0:T(8,128)(2,1)S(1)}, u32[]{:S(2)}, u32[]{:S(2)}) collective-permute-start(bf16[256,256]{1,0:T(8,128)(2,1)S(1)} %get-tuple-element.51), channel_id=1, source_target_pairs={{0,8},{8,0},{16,24},{24,16},{1,9},{9,1},{17,25},{25,17},{2,10},{10... | collective-permute-start | bytes 393224 | tf_op jit(solution)/shard_map/ppermute | solution.py:36
  23.4 1.5 %collective-permute-start.5 = (bf16[256,256]{1,0:T(8,128)(2,1)S(1)}, bf16[256,256]{1,0:T(8,128)(2,1)S(1)}, u32[]{:S(2)}, u32[]{:S(2)}) collective-permute-start(bf16[256,256]{1,0:T(8,128)(2,1)S(1)} %get-tuple-element.51), channel_id=1, source_target_pairs={{0,16},{8,24},{16,0},{24,8},{1,17},{9,25},{17,1},{25,9},{2,18},{10... | collective-permute-start | bytes 393224 | tf_op jit(solution)/shard_map/ppermute | solution.py:36
  24.9 0.0 collective-permute-start.6
  24.9 16.8 %gather_fusion = bf16[3072,256]{1,0:T(8,128)(2,1)} fusion(bf16[16384,256]{1,0:T(8,128)(2,1)} %param.12, s32[3072]{0:T(1024)S(1)} %broadcast_clamp_fusion), kind=kCustom, calls=%fused_computation | custom fusion | bytes 3158016 | tf_op jit(solution)/shard_map/gather | solution.py:148
  41.7 0.1 multiply_multiply_fusion
  41.8 2.6 %slice_bitcast_fusion.2 = (bf16[1024,256]{1,0:T(8,128)(2,1)}, bf16[1024,256]{1,0:T(8,128)(2,1)}, bf16[1024,256]{1,0:T(8,128)(2,1)}) fusion(bf16[3,1024,256]{2,1,0:T(8,128)(2,1)} %bitcast.146), kind=kLoop, calls=%fused_computation.39 | loop fusion | bytes 3145728 | tf_op jit(solution)/shard_map/squeeze | solution.py:156
  44.4 1.9 %collective-permute-start.7 = (bf16[1024,256]{1,0:T(8,128)(2,1)}, bf16[1024,256]{1,0:T(8,128)(2,1)}, u32[]{:S(2)}, u32[]{:S(2)}) collective-permute-start(bf16[1024,256]{1,0:T(8,128)(2,1)} %get-tuple-element.58), channel_id=1, source_target_pairs={{0,8},{8,0},{16,24},{24,16},{1,9},{9,1},{17,25},{25,17},{2,10},{10... | collective-permute-start | bytes 1572872 | tf_op jit(solution)/shard_map/ppermute | solution.py:156
  46.3 1.5 %collective-permute-start.8 = (bf16[1024,256]{1,0:T(8,128)(2,1)}, bf16[1024,256]{1,0:T(8,128)(2,1)}, u32[]{:S(2)}, u32[]{:S(2)}) collective-permute-start(bf16[1024,256]{1,0:T(8,128)(2,1)} %get-tuple-element.60), channel_id=1, source_target_pairs={{0,16},{8,24},{16,0},{24,8},{1,17},{9,25},{17,1},{25,9},{2,18},{10... | collective-permute-start | bytes 1572872 | tf_op jit(solution)/shard_map/ppermute | solution.py:156
  47.9 0.0 collective-permute-start.9
  47.9 9.1 %gather_fusion.1 = bf16[1024,256]{1,0:T(8,128)(2,1)} fusion(bf16[16384,256]{1,0:T(8,128)(2,1)} %param.12, s32[1024]{0:T(1024)S(1)} %fusion.102), kind=kCustom, calls=%fused_computation.1 | custom fusion | bytes 1052672 | tf_op jit(solution)/shard_map/gather | solution.py:153
  57.0 7.5 %gather_fusion.2 = bf16[2048,256]{1,0:T(8,128)(2,1)S(1)} fusion(bf16[4096,256]{1,0:T(8,128)(2,1)S(1)} %copy-done, s32[2048]{0:T(1024)S(1)} %broadcast_clamp_fusion.1), kind=kCustom, calls=%fused_computation.2 | custom fusion | bytes 2105344 | tf_op jit(solution)/shard_map/gather | solution.py:169
  64.5 2.7 %fusion.4 = f32[2048,256]{1,0:T(8,128)S(1)} fusion(bf16[1024,256]{1,0:T(8,128)(2,1)} %gather_fusion.1, s32[2048]{0:T(1024)S(1)} %get-tuple-element.79), kind=kOutput, calls=%fused_computation.9 | convolution fusion | flops 1075838976 | bytes 2629632 | tf_op jit(solution)/shard_map/dot_general | solution.py:161
  67.2 3.9 %collective-permute-done.8 = bf16[1024,256]{1,0:T(8,128)(2,1)} collective-permute-done((bf16[1024,256]{1,0:T(8,128)(2,1)}, bf16[1024,256]{1,0:T(8,128)(2,1)}, u32[]{:S(2)}, u32[]{:S(2)}) %collective-permute-start.8) | collective-permute-done | bytes 524320 | tf_op jit(solution)/shard_map/ppermute | solution.py:156
  71.1 1.5 %pad_maximum_fusion = bf16[3,1024,256]{2,1,0:T(8,128)(2,1)S(1)} fusion(bf16[1,1024,256]{2,1,0:T(8,128)(2,1)} %bitcast.16, bf16[1,1024,256]{2,1,0:T(8,128)(2,1)} %bitcast.14, bf16[1,1024,256]{2,1,0:T(8,128)(2,1)} %bitcast.12), kind=kLoop, calls=%fused_computation.19 | loop fusion | flops 1572864 | bytes 3145728 | tf_op jit(solution)/shard_map/stack | solution.py:165
  72.6 4.2 %fusion.18 = bf16[2048,256]{1,0:T(8,128)(2,1)S(1)} fusion(f32[2048,256]{1,0:T(8,128)S(1)} %fusion.4, bf16[3072,256]{1,0:T(8,128)(2,1)S(1)} %bitcast.147, s32[3072]{0:T(1024)S(1)} %iota_add_fusion, s32[2048]{0:T(1024)S(1)} %get-tuple-element.79, bf16[2048,256]{1,0:T(8,128)(2,1)S(1)} %gather_fusion.2), kind=kOutput, calls=%fused_computation.18 | convolution fusion | flops 3229614080 | bytes 5787648 | tf_op jit(solution)/shard_map/dot_general | solution.py:166
  76.9 0.5 fusion.117
  77.4 0.4 convolution_reduce_fusion.5
  77.9 0.3 convolution_reduce_fusion.2
  78.2 0.3 multiply_reduce_fusion.3
  78.6 0.2 multiply_reduce_fusion.2
  78.8 0.1 fusion.71
  78.9 0.4 convolution_reduce_fusion.4
  79.4 0.3 convolution_reduce_fusion.1
  79.7 0.0 copy-start.1
  79.7 0.3 multiply_reduce_fusion.1
  80.0 0.2 multiply_reduce_fusion
  80.2 0.1 fusion.73
  80.3 0.4 convolution_reduce_fusion.3
  80.8 0.3 convolution_reduce_fusion
  81.1 0.3 fusion.26
  81.5 0.3 convolution_convert_fusion.1
  81.8 12.1 %all_to_all.5 = bf16[32,2,384]{2,1,0:T(2,128)(2,1)S(1)} all-to-all(bf16[32,2,384]{2,1,0:T(2,128)(2,1)S(1)} %bitcast.148), channel_id=1, replica_groups=mesh['table'=4,'batch'=4,'ctx'=2] {'table','batch','ctx'}, dimensions={0} | all-to-all | bytes 98304 | tf_op jit(solution)/shard_map/all_to_all | solution.py:200
  93.9 0.2 add_reduce_fusion
  94.1 0.1 convert_reduce_fusion
  94.2 1.3 %fusion.21 = bf16[1024,256]{1,0:T(8,128)(2,1)} fusion(bf16[1024,256]{1,0:T(8,128)(2,1)S(1)} %copy-done.1, pred[1024]{0:T(1024)(128)(4,1)S(1)} %broadcast_compare_fusion.1, s32[64]{0:T(128)S(1)} %add_reduce_fusion, bf16[64,384]{1,0:T(8,128)(2,1)S(1)} %reshape.584), kind=kOutput, calls=%fused_computation.21 | convolution fusion | flops 34144256 | bytes 1082880 | tf_op jit(solution)/shard_map/dot_general | solution.py:207
  (68 shorter events, 0.7 us)
Async XLA Ops:
  0.0 18.0 %copy-start = (bf16[4096,256]{1,0:T(8,128)(2,1)S(1)}, bf16[4096,256]{1,0:T(8,128)(2,1)}, u32[]{:S(2)}) copy-start(bf16[4096,256]{1,0:T(8,128)(2,1)} %param.13) | copy-start | bytes 6291460
  7.3 14.0 %collective-permute-start = (s32[1024]{0:T(1024)S(1)}, s32[1024]{0:T(1024)S(1)}, u32[]{:S(2)}, u32[]{:S(2)}) collective-permute-start(s32[1024]{0:T(1024)S(1)} %bitcast.157), channel_id=1, source_target_pairs={{0,8},{8,0},{16,24},{24,16},{1,9},{9,1},{17,25},{25,17},{2,10},{10... | collective-permute-start | bytes 12296 | tf_op jit(solution)/shard_map/ppermute | solution.py:139
  10.3 11.0 %collective-permute-start.1 = (s32[1024]{0:T(1024)S(1)}, s32[1024]{0:T(1024)S(1)}, u32[]{:S(2)}, u32[]{:S(2)}) collective-permute-start(s32[1024]{0:T(1024)S(1)} %bitcast.156), channel_id=1, source_target_pairs={{0,16},{8,24},{16,0},{24,8},{1,17},{9,25},{17,1},{25,9},{2,18},{10... | collective-permute-start | bytes 12296 | tf_op jit(solution)/shard_map/ppermute | solution.py:139
  11.8 9.4 %collective-permute-start.2 = (s32[1024]{0:T(1024)S(1)}, s32[1024]{0:T(1024)S(1)}, u32[]{:S(2)}, u32[]{:S(2)}) collective-permute-start(s32[1024]{0:T(1024)S(1)} %bitcast.155), channel_id=1, source_target_pairs={{0,24},{8,16},{16,8},{24,0},{1,25},{9,17},{17,9},{25,1},{2,26},{10... | collective-permute-start | bytes 12296 | tf_op jit(solution)/shard_map/ppermute | solution.py:139
  16.6 4.7 %collective-permute-start.3 = (f32[256,256]{1,0:T(8,128)S(1)}, f32[256,256]{1,0:T(8,128)S(1)}, u32[]{:S(2)}, u32[]{:S(2)}) collective-permute-start(f32[256,256]{1,0:T(8,128)S(1)} %fusion.8), channel_id=1, source_target_pairs={{0,1},{1,0},{2,3},{3,2},{4,5},{5,4},{6,7},{7,6},{8,9},{9,8},{10,11... | collective-permute-start | bytes 786440 | tf_op jit(solution)/shard_map/ppermute | solution.py:26
  18.0 0.8 copy-start.3
  18.0 0.9 copy-start.2
  18.0 0.9 copy-start.4
  21.4 20.3 %collective-permute-start.4 = (bf16[256,256]{1,0:T(8,128)(2,1)S(1)}, bf16[256,256]{1,0:T(8,128)(2,1)S(1)}, u32[]{:S(2)}, u32[]{:S(2)}) collective-permute-start(bf16[256,256]{1,0:T(8,128)(2,1)S(1)} %get-tuple-element.51), channel_id=1, source_target_pairs={{0,8},{8,0},{16,24},{24,16},{1,9},{9,1},{17,25},{25,17},{2,10},{10... | collective-permute-start | bytes 393224 | tf_op jit(solution)/shard_map/ppermute | solution.py:36
  23.4 18.3 %collective-permute-start.5 = (bf16[256,256]{1,0:T(8,128)(2,1)S(1)}, bf16[256,256]{1,0:T(8,128)(2,1)S(1)}, u32[]{:S(2)}, u32[]{:S(2)}) collective-permute-start(bf16[256,256]{1,0:T(8,128)(2,1)S(1)} %get-tuple-element.51), channel_id=1, source_target_pairs={{0,16},{8,24},{16,0},{24,8},{1,17},{9,25},{17,1},{25,9},{2,18},{10... | collective-permute-start | bytes 393224 | tf_op jit(solution)/shard_map/ppermute | solution.py:36
  24.9 16.8 %collective-permute-start.6 = (bf16[256,256]{1,0:T(8,128)(2,1)S(1)}, bf16[256,256]{1,0:T(8,128)(2,1)S(1)}, u32[]{:S(2)}, u32[]{:S(2)}) collective-permute-start(bf16[256,256]{1,0:T(8,128)(2,1)S(1)} %get-tuple-element.51), channel_id=1, source_target_pairs={{0,24},{8,16},{16,8},{24,0},{1,25},{9,17},{17,9},{25,1},{2,26},{10... | collective-permute-start | bytes 393224 | tf_op jit(solution)/shard_map/ppermute | solution.py:36
  44.4 22.8 %collective-permute-start.7 = (bf16[1024,256]{1,0:T(8,128)(2,1)}, bf16[1024,256]{1,0:T(8,128)(2,1)}, u32[]{:S(2)}, u32[]{:S(2)}) collective-permute-start(bf16[1024,256]{1,0:T(8,128)(2,1)} %get-tuple-element.58), channel_id=1, source_target_pairs={{0,8},{8,0},{16,24},{24,16},{1,9},{9,1},{17,25},{25,17},{2,10},{10... | collective-permute-start | bytes 1572872 | tf_op jit(solution)/shard_map/ppermute | solution.py:156
  46.3 24.8 %collective-permute-start.8 = (bf16[1024,256]{1,0:T(8,128)(2,1)}, bf16[1024,256]{1,0:T(8,128)(2,1)}, u32[]{:S(2)}, u32[]{:S(2)}) collective-permute-start(bf16[1024,256]{1,0:T(8,128)(2,1)} %get-tuple-element.60), channel_id=1, source_target_pairs={{0,16},{8,24},{16,0},{24,8},{1,17},{9,25},{17,1},{25,9},{2,18},{10... | collective-permute-start | bytes 1572872 | tf_op jit(solution)/shard_map/ppermute | solution.py:156
  47.9 23.2 %collective-permute-start.9 = (bf16[1024,256]{1,0:T(8,128)(2,1)}, bf16[1024,256]{1,0:T(8,128)(2,1)}, u32[]{:S(2)}, u32[]{:S(2)}) collective-permute-start(bf16[1024,256]{1,0:T(8,128)(2,1)} %get-tuple-element.59), channel_id=1, source_target_pairs={{0,24},{8,16},{16,8},{24,0},{1,25},{9,17},{17,9},{25,1},{2,26},{10... | collective-permute-start | bytes 1572872 | tf_op jit(solution)/shard_map/ppermute | solution.py:156
  79.7 14.5 %copy-start.1 = (bf16[1024,256]{1,0:T(8,128)(2,1)S(1)}, bf16[1024,256]{1,0:T(8,128)(2,1)}, u32[]{:S(2)}) copy-start(bf16[1024,256]{1,0:T(8,128)(2,1)} %param.14) | copy-start | bytes 1572868

commit v16 on v14

--- a/solution.py
+++ b/solution.py
@@ -140,13 +140,11 @@
     gram_source = item_table
     share = gram_source.shape[0] // n_ctx
     own_rows = lax.dynamic_slice_in_dim(gram_source, lax.axis_index("ctx") * share, share, axis=0)
-    item_gram = butterfly_sum(gram_of(own_rows), (("ctx", n_ctx),))
-    item_gram = exchange_sum(item_gram, "table", n_table, jnp.bfloat16)
+    item_gram = lax.psum(gram_of(own_rows), ("ctx", "table"))
     context_gram = gram_of(context_table)
     pair_count = item_table.shape[0] * n_table * context_table.shape[0]
     gram_matrix = item_gram * context_gram / pair_count
     remote = item_table[jnp.stack(by_offset[1:], axis=0)]
-    remote, gram_matrix = lax.optimization_barrier((remote, gram_matrix))
     remote, late_items, late_contexts, local_requests = lax.optimization_barrier(
         (remote, item_table, context_table, by_offset[0])
     )

time: 94.7 us -> 113 us (1.19)
  between operations: 0.55 us -> 13.9 us
  waiting for transfers between devices: 3.78 us -> 12.3 us
  starting transfers between devices: 11.7 us -> 8.03 us
  matrix products: 19.4 us -> 21.2 us
    psum x0 -> x1, waiting for transfers between devices: none -> 12.3 us  [per_device(): item_gram = lax.psum(gram_of(own_rows), ('ctx', 'table'))]
    ppermute x3, waiting for transfers between devices: 3.76 us -> 0.01 us  [per_device(): got.append(lax.ppermute(remote[k - 1], 'table', pairs))]
    ppermute x4 -> x0, starting transfers between devices: 3.63 us -> none  [the longest x3 3.55 us: exchange_sum(): total = total + lax.ppermute(sent, name, pairs).astype(value.dtype)]
    dot_general x2, matrix products: 5.48 us -> 7.19 us  [gram_of(): lax.dot_general(table_rows, table_rows, (((0,), (0,)), ((), ())), preferr...]
    gather x1, local copies, waits for them, and re-layouts: 9.07 us -> 7.94 us  [per_device(): got = [late_items[local_requests]]]
  transfers between devices with their start and end apart: 10 -> 7, of which waited for: 1 -> 1; matrix products, arithmetic and copies ran while one was open for 46% -> 42% of each run, Pallas kernels for 0% -> 0%
where the time goes in v16:
time: 113 us; the launch traced here: 112 us
  local copies, waits for them, and re-layouts  38.2 us (34%)
  matrix products  21.2 us (19%)
  between operations  13.9 us (12%)
  waiting for transfers between devices  12.3 us (11%)
  blocking collectives  11.5 us (10%)
  starting transfers between devices  8.03 us (7%)
  other arithmetic  7.23 us (6%)
    gather x1, local copies, waits for them, and re-layouts, per_device(): remote = item_table[jnp.stack(by_offset[1:], axis=0)]  16.6 us
    psum x1, waiting for transfers between devices, per_device(): item_gram = lax.psum(gram_of(own_rows), ('ctx', 'table'))  12.3 us
    all_to_all x1, blocking collectives, per_device(): lax.all_to_all(payload, ('table', 'batch', 'ctx'), split_axis=0, concat_a...  11.5 us
    gather x1, local copies, waits for them, and re-layouts, per_device(): got = [late_items[local_requests]]  7.94 us
    gather x1, local copies, waits for them, and re-layouts, per_device(): late_contexts[context_flat].astype(jnp.float32)  7.67 us
    dot_general x2, matrix products, gram_of(): lax.dot_general(table_rows, table_rows, (((0,), (0,)), ((), ())), preferr...  7.19 us
    ppermute x3, starting transfers between devices, per_device(): by_offset.append(lax.ppermute(outgoing, 'table', pairs))  4.54 us
    dot_general x1, matrix products, per_device(): jnp.dot(placing, fetched.reshape((n_table - 1) * capacity, rank_width), p...  4.31 us
  transfers between devices with their start and end apart: 7, of which 1 were waited for; matrix products, arithmetic and copies ran while one was open for 42% of the time, Pallas kernels for 0%

profile of v16, /device:TPU:0, one launch (start us, length us, event | category | flops | bytes accessed | tf_op | source)
XLA Modules:
  0.0 112.5 jit_solution(16177533366850618991)
XLA Ops:
  6.5 0.0 copy-start
  6.5 0.0 all-reduce.3.cloned.1.call-start
  6.5 0.9 eq.127
  7.5 1.1 %reduce-window.6 = s32[4,16,128]{2,1,0:T(8,128)S(1)} reduce-window(s32[4,16,128]{2,1,0:T(8,128)S(1)} %fusion.59, s32[]{:T(128)} %constant.154.clone.1), window={size=1x1x128 pad=0_0x0_0x127_0}, to_apply=%region_2.3 | reduce-window | flops 1040384 | bytes 65540 | tf_op jit(solution)/shard_map/reduce-window
  8.6 0.2 slice_reduce_fusion
  8.8 0.2 reduce-window.9
  9.0 0.1 select_reduce_fusion
  9.1 0.5 broadcast.432
  9.6 1.4 %reduce.18 = s32[32,64]{1,0:T(8,128)S(1)} reduce(s32[32,64,1]{1,2,0:T(1,128)} %param.13, s32[]{:T(128)} %broadcast.432), dimensions={2}, to_apply=%param.13.reduce_sub_computation.5 | reduce | bytes 16388 | tf_op args[3]
  11.0 0.1 reshape.493
  11.2 0.8 reshape.495
  12.0 1.7 %fusion.6 = f32[4,2,1024]{2,0,1:T(4,128)S(1)} fusion(s32[2048]{0:T(1024)S(1)} %get-tuple-element.60, s32[2,2048]{1,0:T(2,128)S(1)} %pad_add_fusion, pred[4,2048]{1,0:T(4,128)(4,1)S(1)} %iota_compare_fusion.6), kind=kOutput, calls=%fused_computation.11 | convolution fusion | flops 35684352 | bytes 65536 | tf_op jit(solution)/shard_map/dot_general | solution.py:128
  13.8 3.0 %collective-permute-start = (s32[1024]{0:T(1024)S(1)}, s32[1024]{0:T(1024)S(1)}, u32[]{:S(2)}, u32[]{:S(2)}) collective-permute-start(s32[1024]{0:T(1024)S(1)} %bitcast.157), channel_id=1, source_target_pairs={{0,8},{8,0},{16,24},{24,16},{1,9},{9,1},{17,25},{25,17},{2,10},{10... | collective-permute-start | bytes 12296 | tf_op jit(solution)/shard_map/ppermute | solution.py:139
  16.8 1.5 %collective-permute-start.1 = (s32[1024]{0:T(1024)S(1)}, s32[1024]{0:T(1024)S(1)}, u32[]{:S(2)}, u32[]{:S(2)}) collective-permute-start(s32[1024]{0:T(1024)S(1)} %bitcast.156), channel_id=1, source_target_pairs={{0,16},{8,24},{16,0},{24,8},{1,17},{9,25},{17,1},{25,9},{2,18},{10... | collective-permute-start | bytes 12296 | tf_op jit(solution)/shard_map/ppermute | solution.py:139
  18.4 0.0 collective-permute-start.2
  18.4 5.5 %fusion.8 = f32[256,256]{1,0:T(8,128)} fusion(bf16[16384,256]{1,0:T(8,128)(2,1)} %param.10, s32[]{:T(128)S(6)} %select_n.132), kind=kOutput, calls=%fused_computation.12 | convolution fusion | flops 1073741824 | bytes 4456452 | tf_op jit(solution)/shard_map/dot_general | solution.py:15
  23.9 0.0 all-reduce.3.cloned.1.call-update
  23.9 0.6 compare_reduce_fusion
  24.6 0.1 reshape.497
  24.7 0.2 reduce_window_sum.24
  25.0 0.1 convert_reduce_fusion.1
  25.1 0.2 fusion.81
  25.3 0.1 copy.134
  25.4 0.1 copy.133
  25.5 0.7 convert_select_fusion
  26.1 0.0 collective-permute-done
  26.2 0.0 collective-permute-done.1
  26.2 0.0 collective-permute-done.2
  26.2 16.6 %gather_fusion = bf16[3072,256]{1,0:T(8,128)(2,1)} fusion(bf16[16384,256]{1,0:T(8,128)(2,1)} %param.10, s32[3072]{0:T(1024)S(1)} %broadcast_clamp_fusion), kind=kCustom, calls=%fused_computation | custom fusion | bytes 3158016 | tf_op jit(solution)/shard_map/gather | solution.py:147
  42.8 2.5 %slice_bitcast_fusion.2 = (bf16[1024,256]{1,0:T(8,128)(2,1)}, bf16[1024,256]{1,0:T(8,128)(2,1)}, bf16[1024,256]{1,0:T(8,128)(2,1)}) fusion(bf16[3,1024,256]{2,1,0:T(8,128)(2,1)} %bitcast.146), kind=kLoop, calls=%fused_computation.42 | loop fusion | bytes 3145728 | tf_op jit(solution)/shard_map/squeeze | solution.py:154
  45.4 1.9 %collective-permute-start.3 = (bf16[1024,256]{1,0:T(8,128)(2,1)}, bf16[1024,256]{1,0:T(8,128)(2,1)}, u32[]{:S(2)}, u32[]{:S(2)}) collective-permute-start(bf16[1024,256]{1,0:T(8,128)(2,1)} %get-tuple-element.40), channel_id=1, source_target_pairs={{0,8},{8,0},{16,24},{24,16},{1,9},{9,1},{17,25},{25,17},{2,10},{10... | collective-permute-start | bytes 1572872 | tf_op jit(solution)/shard_map/ppermute | solution.py:154
  47.3 1.5 %collective-permute-start.4 = (bf16[1024,256]{1,0:T(8,128)(2,1)}, bf16[1024,256]{1,0:T(8,128)(2,1)}, u32[]{:S(2)}, u32[]{:S(2)}) collective-permute-start(bf16[1024,256]{1,0:T(8,128)(2,1)} %get-tuple-element.42), channel_id=1, source_target_pairs={{0,16},{8,24},{16,0},{24,8},{1,17},{9,25},{17,1},{25,9},{2,18},{10... | collective-permute-start | bytes 1572872 | tf_op jit(solution)/shard_map/ppermute | solution.py:154
  48.8 0.0 collective-permute-start.5
  48.9 7.9 %gather_fusion.1 = bf16[1024,256]{1,0:T(8,128)(2,1)S(1)} fusion(bf16[16384,256]{1,0:T(8,128)(2,1)} %param.10, s32[1024]{0:T(1024)S(1)} %fusion.99), kind=kCustom, calls=%fused_computation.1 | custom fusion | bytes 1052672 | tf_op jit(solution)/shard_map/gather | solution.py:151
  56.8 2.7 %fusion.4 = f32[2048,256]{1,0:T(8,128)} fusion(bf16[1024,256]{1,0:T(8,128)(2,1)S(1)} %gather_fusion.1, s32[2048]{0:T(1024)S(1)} %get-tuple-element.59), kind=kOutput, calls=%fused_computation.9 | convolution fusion | flops 1075838976 | bytes 2629632 | tf_op jit(solution)/shard_map/dot_general | solution.py:159
  59.5 7.7 %gather_fusion.2 = bf16[2048,256]{1,0:T(8,128)(2,1)S(1)} fusion(bf16[4096,256]{1,0:T(8,128)(2,1)S(1)} %copy-done, s32[2048]{0:T(1024)S(1)} %broadcast_clamp_fusion.1), kind=kCustom, calls=%fused_computation.2 | custom fusion | bytes 2105344 | tf_op jit(solution)/shard_map/gather | solution.py:167
  67.2 12.3 %all-reduce.3.cloned.1.call-done = f32[256,256]{1,0:T(8,128)} async-done(((f32[256,256]{1,0:T(8,128)}), f32[256,256]{1,0:T(8,128)}) %all-reduce.3.cloned.1.call-update) | async-done | bytes 262160 | tf_op jit(solution)/shard_map/psum | solution.py:143
  79.5 1.7 %fusion.22 = f32[256,256]{1,0:T(8,128)S(1)} fusion(f32[256,256]{1,0:T(8,128)} %all-reduce.3.cloned.1.call-done, bf16[4096,256]{1,0:T(8,128)(2,1)S(1)} %copy-done), kind=kOutput, calls=%fused_computation.23 | convolution fusion | flops 537001984 | bytes 2621440 | tf_op jit(solution)/shard_map/dot_general | solution.py:15
  81.2 0.0 collective-permute-done.3
  81.2 0.0 collective-permute-done.4
  81.2 0.0 collective-permute-done.5
  81.2 1.7 %pad_maximum_fusion = bf16[3,1024,256]{2,1,0:T(8,128)(2,1)S(1)} fusion(bf16[1,1024,256]{2,1,0:T(8,128)(2,1)} %bitcast.16, bf16[1,1024,256]{2,1,0:T(8,128)(2,1)} %bitcast.14, bf16[1,1024,256]{2,1,0:T(8,128)(2,1)} %bitcast.12), kind=kLoop, calls=%fused_computation.19 | loop fusion | flops 1572864 | bytes 3145728 | tf_op jit(solution)/shard_map/stack | solution.py:163
  82.9 0.3 copy-done.5
  83.3 4.3 %fusion.18 = bf16[2048,256]{1,0:T(8,128)(2,1)S(1)} fusion(f32[2048,256]{1,0:T(8,128)S(1)} %copy-done.5, bf16[3072,256]{1,0:T(8,128)(2,1)S(1)} %bitcast.147, s32[3072]{0:T(1024)S(1)} %iota_add_fusion, s32[2048]{0:T(1024)S(1)} %get-tuple-element.59, bf16[2048,256]{1,0:T(8,128)(2,1)S(1)} %gather_fusion.2), kind=kOutput, calls=%fused_computation.18 | convolution fusion | flops 3229614080 | bytes 5787648 | tf_op jit(solution)/shard_map/dot_general | solution.py:164
  87.6 0.5 fusion.112
  88.1 0.4 convolution_reduce_fusion.5
  88.6 0.3 convolution_reduce_fusion.2
  88.9 0.3 multiply_reduce_fusion.3
  89.3 0.2 multiply_reduce_fusion.2
  89.5 0.1 fusion.71
  89.6 0.4 convolution_reduce_fusion.4
  90.1 0.3 convolution_reduce_fusion.1
  90.4 0.3 multiply_reduce_fusion.1
  90.7 0.2 multiply_reduce_fusion
  90.9 0.1 fusion.73
  91.0 0.4 convolution_reduce_fusion.3
  91.5 0.3 convolution_reduce_fusion
  91.8 0.3 fusion.28
  92.2 0.3 fusion.27
  92.5 11.5 %all_to_all.5 = f32[32,2,384]{2,1,0:T(2,128)S(1)} all-to-all(f32[32,2,384]{2,1,0:T(2,128)S(1)} %bitcast.148), channel_id=1, replica_groups=mesh['table'=4,'batch'=4,'ctx'=2] {'table','batch','ctx'}, dimensions={0} | all-to-all | bytes 196608 | tf_op jit(solution)/shard_map/all_to_all | solution.py:194
  104.1 0.1 reshape.500
  104.1 0.1 fusion.37
  104.2 0.1 convert_reduce_fusion
  104.4 1.3 %fusion.21 = bf16[1024,256]{1,0:T(8,128)(2,1)} fusion(bf16[1024,256]{1,0:T(8,128)(2,1)S(1)} %copy-done.1, pred[1024]{0:T(1024)(128)(4,1)S(1)} %broadcast_compare_fusion, s32[64]{0:T(128)S(1)} %fusion.37, f32[64,384]{1,0:T(8,128)S(1)} %reshape.500), kind=kOutput, calls=%fused_computation.21 | convolution fusion | flops 34144256 | bytes 1082880 | tf_op jit(solution)/shard_map/dot_general | solution.py:201
  (60 shorter events, 0.7 us)
Async XLA Ops:
  6.5 53.0 %copy-start = (bf16[4096,256]{1,0:T(8,128)(2,1)S(1)}, bf16[4096,256]{1,0:T(8,128)(2,1)}, u32[]{:S(2)}) copy-start(bf16[4096,256]{1,0:T(8,128)(2,1)} %param.11) | copy-start | bytes 6291460
  6.5 73.0 %all-reduce.3.cloned.1.call-start = ((), (), s32[]{:S(2)}) async-start(), calls=%async_computation.1 | async-start | bytes 524288 | tf_op jit(solution)/shard_map/psum | solution.py:143
  13.8 12.3 %collective-permute-start = (s32[1024]{0:T(1024)S(1)}, s32[1024]{0:T(1024)S(1)}, u32[]{:S(2)}, u32[]{:S(2)}) collective-permute-start(s32[1024]{0:T(1024)S(1)} %bitcast.157), channel_id=1, source_target_pairs={{0,8},{8,0},{16,24},{24,16},{1,9},{9,1},{17,25},{25,17},{2,10},{10... | collective-permute-start | bytes 12296 | tf_op jit(solution)/shard_map/ppermute | solution.py:139
  16.8 9.3 %collective-permute-start.1 = (s32[1024]{0:T(1024)S(1)}, s32[1024]{0:T(1024)S(1)}, u32[]{:S(2)}, u32[]{:S(2)}) collective-permute-start(s32[1024]{0:T(1024)S(1)} %bitcast.156), channel_id=1, source_target_pairs={{0,16},{8,24},{16,0},{24,8},{1,17},{9,25},{17,1},{25,9},{2,18},{10... | collective-permute-start | bytes 12296 | tf_op jit(solution)/shard_map/ppermute | solution.py:139
  18.4 7.8 %collective-permute-start.2 = (s32[1024]{0:T(1024)S(1)}, s32[1024]{0:T(1024)S(1)}, u32[]{:S(2)}, u32[]{:S(2)}) collective-permute-start(s32[1024]{0:T(1024)S(1)} %bitcast.155), channel_id=1, source_target_pairs={{0,24},{8,16},{16,8},{24,0},{1,25},{9,17},{17,9},{25,1},{2,26},{10... | collective-permute-start | bytes 12296 | tf_op jit(solution)/shard_map/ppermute | solution.py:139
  18.4 6.2 %copy-start.3 = (s32[32,64]{1,0:T(8,128)S(1)}, s32[32,64]{1,0:T(8,128)}, u32[]{:S(2)}) copy-start(s32[32,64]{1,0:T(8,128)} %param.15) | copy-start | bytes 24580
  18.4 6.3 %copy-start.2 = (s32[32,64]{1,0:T(8,128)S(1)}, s32[32,64]{1,0:T(8,128)}, u32[]{:S(2)}) copy-start(s32[32,64]{1,0:T(8,128)} %param.16) | copy-start | bytes 24580
  18.4 6.3 %copy-start.4 = (s32[32]{0:T(128)S(1)}, s32[32]{0:T(128)}, u32[]{:S(2)}) copy-start(s32[32]{0:T(128)} %param.17) | copy-start | bytes 388
  45.4 35.8 %collective-permute-start.3 = (bf16[1024,256]{1,0:T(8,128)(2,1)}, bf16[1024,256]{1,0:T(8,128)(2,1)}, u32[]{:S(2)}, u32[]{:S(2)}) collective-permute-start(bf16[1024,256]{1,0:T(8,128)(2,1)} %get-tuple-element.40), channel_id=1, source_target_pairs={{0,8},{8,0},{16,24},{24,16},{1,9},{9,1},{17,25},{25,17},{2,10},{10... | collective-permute-start | bytes 1572872 | tf_op jit(solution)/shard_map/ppermute | solution.py:154
  47.3 33.9 %collective-permute-start.4 = (bf16[1024,256]{1,0:T(8,128)(2,1)}, bf16[1024,256]{1,0:T(8,128)(2,1)}, u32[]{:S(2)}, u32[]{:S(2)}) collective-permute-start(bf16[1024,256]{1,0:T(8,128)(2,1)} %get-tuple-element.42), channel_id=1, source_target_pairs={{0,16},{8,24},{16,0},{24,8},{1,17},{9,25},{17,1},{25,9},{2,18},{10... | collective-permute-start | bytes 1572872 | tf_op jit(solution)/shard_map/ppermute | solution.py:154
  48.8 32.4 %collective-permute-start.5 = (bf16[1024,256]{1,0:T(8,128)(2,1)}, bf16[1024,256]{1,0:T(8,128)(2,1)}, u32[]{:S(2)}, u32[]{:S(2)}) collective-permute-start(bf16[1024,256]{1,0:T(8,128)(2,1)} %get-tuple-element.41), channel_id=1, source_target_pairs={{0,24},{8,16},{16,8},{24,0},{1,25},{9,17},{17,9},{25,1},{2,26},{10... | collective-permute-start | bytes 1572872 | tf_op jit(solution)/shard_map/ppermute | solution.py:154
  81.2 2.1 %copy-start.5 = (f32[2048,256]{1,0:T(8,128)S(1)}, f32[2048,256]{1,0:T(8,128)}, u32[]{:S(2)}) copy-start(f32[2048,256]{1,0:T(8,128)} %fusion.4) | copy-start | bytes 6291460
  90.7 13.7 %copy-start.1 = (bf16[1024,256]{1,0:T(8,128)(2,1)S(1)}, bf16[1024,256]{1,0:T(8,128)(2,1)}, u32[]{:S(2)}) copy-start(bf16[1024,256]{1,0:T(8,128)(2,1)} %param.12) | copy-start | bytes 1572868
Sparse Core Ops, SparseCore 0:
  24.0 55.4 all-reduce.2

commit v17 on v14

--- a/solution.py
+++ b/solution.py
@@ -159,13 +159,13 @@
         jnp.bfloat16
     )
     picked_local = jnp.dot(placing_local, got[0], preferred_element_type=jnp.float32)
-    placing = (
-        relative[:, None] == jnp.arange(capacity, n_table * capacity, dtype=jnp.int32)[None, :]
-    ).astype(jnp.bfloat16)
-    fetched = jnp.stack(got[1:], axis=0)
-    picked = picked_local + jnp.dot(
-        placing, fetched.reshape((n_table - 1) * capacity, rank_width), preferred_element_type=jnp.float32
-    )
+    picked = picked_local
+    for k in range(1, n_table):
+        placing = (
+            relative[:, None]
+            == jnp.arange(k * capacity, (k + 1) * capacity, dtype=jnp.int32)[None, :]
+        ).astype(jnp.bfloat16)
+        picked = picked + jnp.dot(placing, got[k], preferred_element_type=jnp.float32)
     slot_rows = (picked * late_contexts[context_flat].astype(jnp.float32)).astype(jnp.bfloat16)
     slot_rows = slot_rows.reshape(user_count, slot_count, rank_width)
     confidence = CONF_SCALE * bucket.astype(jnp.float32)

time: 94.7 us -> 96.6 us (1.020)
  matrix products: 19.4 us -> 23.1 us
  other arithmetic: 7.19 us -> 5.67 us
  waiting for transfers between devices: 3.78 us -> 2.43 us
  blocking collectives: 12.5 us -> 13.6 us
    dot_general x1 -> x3, matrix products: 4.23 us -> 7.94 us  [per_device(): jnp.dot(placing, got[k], preferred_element_type=jnp.float32)]
    another operation x5 -> x4, other arithmetic: 4.15 us -> 2.62 us
    ppermute x3, waiting for transfers between devices: 3.76 us -> 2.41 us  [per_device(): got.append(lax.ppermute(remote[k - 1], 'table', pairs))]
    all_to_all x1, blocking collectives: 12.5 us -> 13.6 us  [per_device(): lax.all_to_all(payload, ('table', 'batch', 'ctx'), split_axis=0, concat_a...]
  transfers between devices with their start and end apart: 10 -> 10, of which waited for: 1 -> 1; matrix products, arithmetic and copies ran while one was open for 46% -> 51% of each run, Pallas kernels for 0% -> 0%
where the time goes in v17:
time: 96.6 us; the launch traced here: 96 us
  local copies, waits for them, and re-layouts  39 us (40%)
  matrix products  23.1 us (24%)
  blocking collectives  13.6 us (14%)
  starting transfers between devices  11.7 us (12%)
  other arithmetic  5.67 us (6%)
  waiting for transfers between devices  2.43 us (3%)
    gather x1, local copies, waits for them, and re-layouts, per_device(): remote = item_table[jnp.stack(by_offset[1:], axis=0)]  16.6 us
    all_to_all x1, blocking collectives, per_device(): lax.all_to_all(payload, ('table', 'batch', 'ctx'), split_axis=0, concat_a...  13.6 us
    gather x1, local copies, waits for them, and re-layouts, per_device(): got = [late_items[local_requests]]  9.03 us
    dot_general x3, matrix products, per_device(): jnp.dot(placing, got[k], preferred_element_type=jnp.float32)  7.94 us
    gather x1, local copies, waits for them, and re-layouts, per_device(): late_contexts[context_flat].astype(jnp.float32)  7.67 us
    dot_general x2, matrix products, gram_of(): lax.dot_general(table_rows, table_rows, (((0,), (0,)), ((), ())), preferr...  5.48 us
    ppermute x3, starting transfers between devices, per_device(): by_offset.append(lax.ppermute(outgoing, 'table', pairs))  4.54 us
    ppermute x3, starting transfers between devices, exchange_sum(): total = total + lax.ppermute(sent, name, pairs).astype(value.dtype)  3.56 us
  transfers between devices with their start and end apart: 10, of which 1 were waited for; matrix products, arithmetic and copies ran while one was open for 51% of the time, Pallas kernels for 0%

profile of v17, /device:TPU:0, one launch (start us, length us, event | category | flops | bytes accessed | tf_op | source)
XLA Modules:
  0.0 96.0 jit_solution(16663503887956540032)
XLA Ops:
  0.0 0.9 eq.147
  0.9 1.1 %reduce-window.6 = s32[4,16,128]{2,1,0:T(8,128)S(1)} reduce-window(s32[4,16,128]{2,1,0:T(8,128)S(1)} %fusion.72, s32[]{:T(128)} %constant.156.clone.1), window={size=1x1x128 pad=0_0x0_0x127_0}, to_apply=%region_2.3 | reduce-window | flops 1040384 | bytes 65540 | tf_op jit(solution)/shard_map/reduce-window
  2.1 0.2 slice_reduce_fusion
  2.3 0.2 reduce-window.9
  2.5 0.1 select_reduce_fusion
  2.6 0.5 broadcast.440
  3.1 1.4 %reduce.18 = s32[32,64]{1,0:T(8,128)S(1)} reduce(s32[32,64,1]{1,2,0:T(1,128)} %param.13, s32[]{:T(128)} %broadcast.440), dimensions={2}, to_apply=%param.13.reduce_sub_computation.5 | reduce | bytes 16388 | tf_op args[3]
  4.5 0.1 reshape.498
  4.6 0.8 reshape.500
  5.5 1.7 %fusion.8 = f32[4,2,1024]{2,0,1:T(4,128)S(1)} fusion(s32[2048]{0:T(1024)S(1)} %get-tuple-element.66, s32[2,2048]{1,0:T(2,128)S(1)} %pad_add_fusion, pred[4,2048]{1,0:T(4,128)(4,1)S(1)} %iota_compare_fusion.6), kind=kOutput, calls=%fused_computation.13 | convolution fusion | flops 35684352 | bytes 65536 | tf_op jit(solution)/shard_map/dot_general | solution.py:128
  7.3 3.0 %collective-permute-start = (s32[1024]{0:T(1024)S(1)}, s32[1024]{0:T(1024)S(1)}, u32[]{:S(2)}, u32[]{:S(2)}) collective-permute-start(s32[1024]{0:T(1024)S(1)} %bitcast.154), channel_id=1, source_target_pairs={{0,8},{8,0},{16,24},{24,16},{1,9},{9,1},{17,25},{25,17},{2,10},{10... | collective-permute-start | bytes 12296 | tf_op jit(solution)/shard_map/ppermute | solution.py:139
  10.3 1.5 %collective-permute-start.1 = (s32[1024]{0:T(1024)S(1)}, s32[1024]{0:T(1024)S(1)}, u32[]{:S(2)}, u32[]{:S(2)}) collective-permute-start(s32[1024]{0:T(1024)S(1)} %bitcast.153), channel_id=1, source_target_pairs={{0,16},{8,24},{16,0},{24,8},{1,17},{9,25},{17,1},{25,9},{2,18},{10... | collective-permute-start | bytes 12296 | tf_op jit(solution)/shard_map/ppermute | solution.py:139
  11.8 0.0 collective-permute-start.2
  11.8 4.7 %fusion.13 = f32[256,256]{1,0:T(8,128)S(1)} fusion(bf16[16384,256]{1,0:T(8,128)(2,1)} %param.10, s32[]{:T(128)S(6)} %select_n.128), kind=kOutput, calls=%fused_computation.17 | convolution fusion | flops 1073741824 | bytes 4456452 | tf_op jit(solution)/shard_map/dot_general | solution.py:15
  16.6 0.1 collective-permute-start.3
  16.7 0.6 compare_reduce_fusion
  17.3 0.7 fusion.126
  18.1 0.1 reshape.501
  18.3 0.2 reduce_window_sum.24
  18.5 0.1 convert_reduce_fusion.1
  18.6 0.2 fusion.94
  18.8 0.1 copy.134
  18.9 0.1 copy.133
  19.0 0.7 convert_select_fusion
  19.7 0.0 collective-permute-done
  19.7 0.0 collective-permute-done.2
  19.7 0.0 collective-permute-done.3
  19.8 2.0 %collective-permute-start.4 = (bf16[256,256]{1,0:T(8,128)(2,1)S(1)}, bf16[256,256]{1,0:T(8,128)(2,1)S(1)}, u32[]{:S(2)}, u32[]{:S(2)}) collective-permute-start(bf16[256,256]{1,0:T(8,128)(2,1)S(1)} %get-tuple-element.39), channel_id=1, source_target_pairs={{0,8},{8,0},{16,24},{24,16},{1,9},{9,1},{17,25},{25,17},{2,10},{10... | collective-permute-start | bytes 393224 | tf_op jit(solution)/shard_map/ppermute | solution.py:36
  21.8 1.5 %collective-permute-start.5 = (bf16[256,256]{1,0:T(8,128)(2,1)S(1)}, bf16[256,256]{1,0:T(8,128)(2,1)S(1)}, u32[]{:S(2)}, u32[]{:S(2)}) collective-permute-start(bf16[256,256]{1,0:T(8,128)(2,1)S(1)} %get-tuple-element.39), channel_id=1, source_target_pairs={{0,16},{8,24},{16,0},{24,8},{1,17},{9,25},{17,1},{25,9},{2,18},{10... | collective-permute-start | bytes 393224 | tf_op jit(solution)/shard_map/ppermute | solution.py:36
  23.3 0.0 collective-permute-start.6
  23.4 16.6 %gather_fusion = bf16[3072,256]{1,0:T(8,128)(2,1)} fusion(bf16[16384,256]{1,0:T(8,128)(2,1)} %param.10, s32[3072]{0:T(1024)S(1)} %broadcast_clamp_fusion), kind=kCustom, calls=%fused_computation | custom fusion | bytes 3158016 | tf_op jit(solution)/shard_map/gather | solution.py:148
  40.0 0.0 collective-permute-done.6
  40.0 0.1 multiply_multiply_fusion
  40.0 2.5 %slice_bitcast_fusion.2 = (bf16[1024,256]{1,0:T(8,128)(2,1)}, bf16[1024,256]{1,0:T(8,128)(2,1)}, bf16[1024,256]{1,0:T(8,128)(2,1)}) fusion(bf16[3,1024,256]{2,1,0:T(8,128)(2,1)} %bitcast.144), kind=kLoop, calls=%fused_computation.49 | loop fusion | bytes 3145728 | tf_op jit(solution)/shard_map/squeeze | solution.py:156
  42.6 2.0 %collective-permute-start.8 = (bf16[1024,256]{1,0:T(8,128)(2,1)}, bf16[1024,256]{1,0:T(8,128)(2,1)}, u32[]{:S(2)}, u32[]{:S(2)}) collective-permute-start(bf16[1024,256]{1,0:T(8,128)(2,1)} %get-tuple-element.48), channel_id=1, source_target_pairs={{0,16},{8,24},{16,0},{24,8},{1,17},{9,25},{17,1},{25,9},{2,18},{10... | collective-permute-start | bytes 1572872 | tf_op jit(solution)/shard_map/ppermute | solution.py:156
  44.6 1.4 %collective-permute-start.9 = (bf16[1024,256]{1,0:T(8,128)(2,1)}, bf16[1024,256]{1,0:T(8,128)(2,1)}, u32[]{:S(2)}, u32[]{:S(2)}) collective-permute-start(bf16[1024,256]{1,0:T(8,128)(2,1)} %get-tuple-element.47), channel_id=1, source_target_pairs={{0,24},{8,16},{16,8},{24,0},{1,25},{9,17},{17,9},{25,1},{2,26},{10... | collective-permute-start | bytes 1572872 | tf_op jit(solution)/shard_map/ppermute | solution.py:156
  46.0 0.1 collective-permute-start.7
  46.1 9.0 %gather_fusion.1 = bf16[1024,256]{1,0:T(8,128)(2,1)} fusion(bf16[16384,256]{1,0:T(8,128)(2,1)} %param.10, s32[1024]{0:T(1024)S(1)} %fusion.112), kind=kCustom, calls=%fused_computation.1 | custom fusion | bytes 1052672 | tf_op jit(solution)/shard_map/gather | solution.py:153
  55.1 7.7 %gather_fusion.2 = bf16[2048,256]{1,0:T(8,128)(2,1)S(1)} fusion(bf16[4096,256]{1,0:T(8,128)(2,1)S(1)} %copy-done, s32[2048]{0:T(1024)S(1)} %broadcast_clamp_fusion.1), kind=kCustom, calls=%fused_computation.2 | custom fusion | bytes 2105344 | tf_op jit(solution)/shard_map/gather | solution.py:169
  62.8 2.7 %fusion = f32[2048,256]{1,0:T(8,128)S(1)} fusion(bf16[1024,256]{1,0:T(8,128)(2,1)} %gather_fusion.1, s32[2048]{0:T(1024)S(1)} %get-tuple-element.65), kind=kOutput, calls=%fused_computation.5 | convolution fusion | flops 1075838976 | bytes 2629632 | tf_op jit(solution)/shard_map/dot_general | solution.py:161
  65.5 2.4 %collective-permute-done.8 = bf16[1024,256]{1,0:T(8,128)(2,1)} collective-permute-done((bf16[1024,256]{1,0:T(8,128)(2,1)}, bf16[1024,256]{1,0:T(8,128)(2,1)}, u32[]{:S(2)}, u32[]{:S(2)}) %collective-permute-start.8) | collective-permute-done | bytes 524320 | tf_op jit(solution)/shard_map/ppermute | solution.py:156
  67.9 2.5 %fusion.4 = f32[2048,256]{1,0:T(8,128)S(1)} fusion(bf16[1024,256]{1,0:T(8,128)(2,1)} %collective-permute-done.8, s32[1024]{0:T(1024)S(1)} %iota_add_fusion.1, s32[2048]{0:T(1024)S(1)} %get-tuple-element.65), kind=kOutput, calls=%fused_computation.9 | convolution fusion | flops 1075838976 | bytes 2633728 | tf_op jit(solution)/shard_map/dot_general | solution.py:168
  70.4 2.5 %fusion.2 = f32[2048,256]{1,0:T(8,128)S(1)} fusion(bf16[1024,256]{1,0:T(8,128)(2,1)} %collective-permute-done.9, s32[1024]{0:T(1024)S(1)} %iota_add_fusion, s32[2048]{0:T(1024)S(1)} %get-tuple-element.65), kind=kOutput, calls=%fused_computation.7 | convolution fusion | flops 1075838976 | bytes 2633728 | tf_op jit(solution)/shard_map/dot_general | solution.py:168
  72.9 3.0 %fusion.32 = bf16[2048,256]{1,0:T(8,128)(2,1)S(1)} fusion(f32[2048,256]{1,0:T(8,128)S(1)} %fusion.2, f32[2048,256]{1,0:T(8,128)S(1)} %fusion.4, f32[2048,256]{1,0:T(8,128)S(1)} %fusion, bf16[1024,256]{1,0:T(8,128)(2,1)} %collective-permute-done.7, s32[1024]{0:T(1024)S(1)} %iota_add_fusion.2, s32[2048]{0:T(1024)S(1)} %get-tuple-element.65, ...), kind=kOutput, calls=%fused_computation.28 | convolution fusion | flops 1078984704 | bytes 8925184 | tf_op jit(solution)/shard_map/dot_general | solution.py:168
  75.9 0.5 fusion.127
  76.4 0.4 convolution_reduce_fusion.5
  76.9 0.3 convolution_reduce_fusion.2
  77.2 0.3 multiply_reduce_fusion.3
  77.6 0.2 multiply_reduce_fusion.2
  77.8 0.1 fusion.84
  77.9 0.4 convolution_reduce_fusion.4
  78.4 0.3 convolution_reduce_fusion.1
  78.7 0.3 multiply_reduce_fusion.1
  79.0 0.2 multiply_reduce_fusion
  79.2 0.1 fusion.86
  79.3 0.4 convolution_reduce_fusion.3
  79.8 0.3 convolution_reduce_fusion
  80.1 0.3 fusion.41
  80.5 0.3 fusion.40
  80.8 13.6 %all_to_all.5 = f32[32,2,384]{2,1,0:T(2,128)S(1)} all-to-all(f32[32,2,384]{2,1,0:T(2,128)S(1)} %bitcast.145), channel_id=1, replica_groups=mesh['table'=4,'batch'=4,'ctx'=2] {'table','batch','ctx'}, dimensions={0} | all-to-all | bytes 196608 | tf_op jit(solution)/shard_map/all_to_all | solution.py:196
  94.5 0.1 reshape.504
  94.5 0.1 fusion.50
  94.6 0.1 convert_reduce_fusion
  94.8 1.3 %fusion.35 = bf16[1024,256]{1,0:T(8,128)(2,1)} fusion(bf16[1024,256]{1,0:T(8,128)(2,1)S(1)} %copy-done.1, pred[1024]{0:T(1024)(128)(4,1)S(1)} %broadcast_compare_fusion, s32[64]{0:T(128)S(1)} %fusion.50, f32[64,384]{1,0:T(8,128)S(1)} %reshape.504), kind=kOutput, calls=%fused_computation.30 | convolution fusion | flops 34144256 | bytes 1082880 | tf_op jit(solution)/shard_map/dot_general | solution.py:203
  (68 shorter events, 0.7 us)
Async XLA Ops:
  0.0 17.3 %copy-start = (bf16[4096,256]{1,0:T(8,128)(2,1)S(1)}, bf16[4096,256]{1,0:T(8,128)(2,1)}, u32[]{:S(2)}) copy-start(bf16[4096,256]{1,0:T(8,128)(2,1)} %param.11) | copy-start | bytes 6291460
  7.3 12.4 %collective-permute-start = (s32[1024]{0:T(1024)S(1)}, s32[1024]{0:T(1024)S(1)}, u32[]{:S(2)}, u32[]{:S(2)}) collective-permute-start(s32[1024]{0:T(1024)S(1)} %bitcast.154), channel_id=1, source_target_pairs={{0,8},{8,0},{16,24},{24,16},{1,9},{9,1},{17,25},{25,17},{2,10},{10... | collective-permute-start | bytes 12296 | tf_op jit(solution)/shard_map/ppermute | solution.py:139
  10.3 9.4 %collective-permute-start.1 = (s32[1024]{0:T(1024)S(1)}, s32[1024]{0:T(1024)S(1)}, u32[]{:S(2)}, u32[]{:S(2)}) collective-permute-start(s32[1024]{0:T(1024)S(1)} %bitcast.153), channel_id=1, source_target_pairs={{0,16},{8,24},{16,0},{24,8},{1,17},{9,25},{17,1},{25,9},{2,18},{10... | collective-permute-start | bytes 12296 | tf_op jit(solution)/shard_map/ppermute | solution.py:139
  11.8 7.9 %collective-permute-start.2 = (s32[1024]{0:T(1024)S(1)}, s32[1024]{0:T(1024)S(1)}, u32[]{:S(2)}, u32[]{:S(2)}) collective-permute-start(s32[1024]{0:T(1024)S(1)} %bitcast.152), channel_id=1, source_target_pairs={{0,24},{8,16},{16,8},{24,0},{1,25},{9,17},{17,9},{25,1},{2,26},{10... | collective-permute-start | bytes 12296 | tf_op jit(solution)/shard_map/ppermute | solution.py:139
  16.6 3.2 %collective-permute-start.3 = (f32[256,256]{1,0:T(8,128)S(1)}, f32[256,256]{1,0:T(8,128)S(1)}, u32[]{:S(2)}, u32[]{:S(2)}) collective-permute-start(f32[256,256]{1,0:T(8,128)S(1)} %fusion.13), channel_id=1, source_target_pairs={{0,1},{1,0},{2,3},{3,2},{4,5},{5,4},{6,7},{7,6},{8,9},{9,8},{10,11... | collective-permute-start | bytes 786440 | tf_op jit(solution)/shard_map/ppermute | solution.py:26
  17.3 0.8 copy-start.3
  17.3 0.9 copy-start.2
  17.3 0.9 copy-start.4
  19.8 20.2 %collective-permute-start.4 = (bf16[256,256]{1,0:T(8,128)(2,1)S(1)}, bf16[256,256]{1,0:T(8,128)(2,1)S(1)}, u32[]{:S(2)}, u32[]{:S(2)}) collective-permute-start(bf16[256,256]{1,0:T(8,128)(2,1)S(1)} %get-tuple-element.39), channel_id=1, source_target_pairs={{0,8},{8,0},{16,24},{24,16},{1,9},{9,1},{17,25},{25,17},{2,10},{10... | collective-permute-start | bytes 393224 | tf_op jit(solution)/shard_map/ppermute | solution.py:36
  21.8 18.1 %collective-permute-start.5 = (bf16[256,256]{1,0:T(8,128)(2,1)S(1)}, bf16[256,256]{1,0:T(8,128)(2,1)S(1)}, u32[]{:S(2)}, u32[]{:S(2)}) collective-permute-start(bf16[256,256]{1,0:T(8,128)(2,1)S(1)} %get-tuple-element.39), channel_id=1, source_target_pairs={{0,16},{8,24},{16,0},{24,8},{1,17},{9,25},{17,1},{25,9},{2,18},{10... | collective-permute-start | bytes 393224 | tf_op jit(solution)/shard_map/ppermute | solution.py:36
  23.3 16.6 %collective-permute-start.6 = (bf16[256,256]{1,0:T(8,128)(2,1)S(1)}, bf16[256,256]{1,0:T(8,128)(2,1)S(1)}, u32[]{:S(2)}, u32[]{:S(2)}) collective-permute-start(bf16[256,256]{1,0:T(8,128)(2,1)S(1)} %get-tuple-element.39), channel_id=1, source_target_pairs={{0,24},{8,16},{16,8},{24,0},{1,25},{9,17},{17,9},{25,1},{2,26},{10... | collective-permute-start | bytes 393224 | tf_op jit(solution)/shard_map/ppermute | solution.py:36
  42.6 25.3 %collective-permute-start.8 = (bf16[1024,256]{1,0:T(8,128)(2,1)}, bf16[1024,256]{1,0:T(8,128)(2,1)}, u32[]{:S(2)}, u32[]{:S(2)}) collective-permute-start(bf16[1024,256]{1,0:T(8,128)(2,1)} %get-tuple-element.48), channel_id=1, source_target_pairs={{0,16},{8,24},{16,0},{24,8},{1,17},{9,25},{17,1},{25,9},{2,18},{10... | collective-permute-start | bytes 1572872 | tf_op jit(solution)/shard_map/ppermute | solution.py:156
  44.6 25.8 %collective-permute-start.9 = (bf16[1024,256]{1,0:T(8,128)(2,1)}, bf16[1024,256]{1,0:T(8,128)(2,1)}, u32[]{:S(2)}, u32[]{:S(2)}) collective-permute-start(bf16[1024,256]{1,0:T(8,128)(2,1)} %get-tuple-element.47), channel_id=1, source_target_pairs={{0,24},{8,16},{16,8},{24,0},{1,25},{9,17},{17,9},{25,1},{2,26},{10... | collective-permute-start | bytes 1572872 | tf_op jit(solution)/shard_map/ppermute | solution.py:156
  46.0 26.9 %collective-permute-start.7 = (bf16[1024,256]{1,0:T(8,128)(2,1)}, bf16[1024,256]{1,0:T(8,128)(2,1)}, u32[]{:S(2)}, u32[]{:S(2)}) collective-permute-start(bf16[1024,256]{1,0:T(8,128)(2,1)} %get-tuple-element.46), channel_id=1, source_target_pairs={{0,8},{8,0},{16,24},{24,16},{1,9},{9,1},{17,25},{25,17},{2,10},{10... | collective-permute-start | bytes 1572872 | tf_op jit(solution)/shard_map/ppermute | solution.py:156
  79.0 15.8 %copy-start.1 = (bf16[1024,256]{1,0:T(8,128)(2,1)S(1)}, bf16[1024,256]{1,0:T(8,128)(2,1)}, u32[]{:S(2)}) copy-start(bf16[1024,256]{1,0:T(8,128)(2,1)} %param.12) | copy-start | bytes 1572868

commit v18 on v14

--- a/solution.py
+++ b/solution.py
@@ -147,8 +147,8 @@
     gram_matrix = item_gram * context_gram / pair_count
     remote = item_table[jnp.stack(by_offset[1:], axis=0)]
     remote, gram_matrix = lax.optimization_barrier((remote, gram_matrix))
-    remote, late_items, late_contexts, local_requests = lax.optimization_barrier(
-        (remote, item_table, context_table, by_offset[0])
+    remote, late_items, late_contexts, local_requests, bucket, user_ids = lax.optimization_barrier(
+        (remote, item_table, context_table, by_offset[0], bucket, user_ids)
     )
     got = [late_items[local_requests]]
     for k in range(1, n_table):

time: 94.7 us -> 93.1 us (0.983)
  waiting for transfers between devices: 3.78 us -> 2.41 us
    ppermute x3, waiting for transfers between devices: 3.76 us -> 2.39 us  [per_device(): got.append(lax.ppermute(remote[k - 1], 'table', pairs))]
  transfers between devices with their start and end apart: 10 -> 10, of which waited for: 1 -> 1; matrix products, arithmetic and copies ran while one was open for 46% -> 47% of each run, Pallas kernels for 0% -> 0%
where the time goes in v18:
time: 93.1 us; the launch traced here: 92.6 us
  local copies, waits for them, and re-layouts  39.1 us (42%)
  matrix products  19.4 us (21%)
  blocking collectives  12.5 us (13%)
  starting transfers between devices  11.7 us (13%)
  other arithmetic  7.05 us (8%)
  waiting for transfers between devices  2.41 us (3%)
    gather x1, local copies, waits for them, and re-layouts, per_device(): remote = item_table[jnp.stack(by_offset[1:], axis=0)]  16.6 us
    all_to_all x1, blocking collectives, per_device(): lax.all_to_all(payload, ('table', 'batch', 'ctx'), split_axis=0, concat_a...  12.5 us
    gather x1, local copies, waits for them, and re-layouts, per_device(): got = [late_items[local_requests]]  9.07 us
    gather x1, local copies, waits for them, and re-layouts, per_device(): late_contexts[context_flat].astype(jnp.float32)  7.67 us
    dot_general x2, matrix products, gram_of(): lax.dot_general(table_rows, table_rows, (((0,), (0,)), ((), ())), preferr...  5.48 us
    ppermute x3, starting transfers between devices, per_device(): by_offset.append(lax.ppermute(outgoing, 'table', pairs))  4.54 us
    dot_general x1, matrix products, per_device(): jnp.dot(placing, fetched.reshape((n_table - 1) * capacity, rank_width), p...  4.23 us
    ppermute x3, starting transfers between devices, exchange_sum(): total = total + lax.ppermute(sent, name, pairs).astype(value.dtype)  3.56 us
  transfers between devices with their start and end apart: 10, of which 1 were waited for; matrix products, arithmetic and copies ran while one was open for 47% of the time, Pallas kernels for 0%

profile of v18, /device:TPU:0, one launch (start us, length us, event | category | flops | bytes accessed | tf_op | source)
XLA Modules:
  0.0 92.6 jit_solution(5767433461116557036)
XLA Ops:
  0.0 0.9 %eq.127 = s32[16,128]{1,0:T(8,128)S(1)} reshape(s32[32,64]{1,0:T(8,128)} %bitcast.150) | data formatting | bytes 16384 | tf_op jit(solution)/shard_map/eq | solution.py:124
  0.9 1.1 %reduce-window.6 = s32[4,16,128]{2,1,0:T(8,128)S(1)} reduce-window(s32[4,16,128]{2,1,0:T(8,128)S(1)} %fusion.56, s32[]{:T(128)} %constant.154.clone.1), window={size=1x1x128 pad=0_0x0_0x127_0}, to_apply=%region_0.0 | reduce-window | flops 1040384 | bytes 65540 | tf_op jit(solution)/shard_map/reduce-window
  2.1 0.2 slice_reduce_fusion
  2.3 0.2 reduce-window.9
  2.5 0.1 select_reduce_fusion
  2.6 0.5 broadcast.432
  3.1 1.4 %reduce.18 = s32[32,64]{1,0:T(8,128)S(1)} reduce(s32[32,64,1]{1,2,0:T(1,128)} %param.13, s32[]{:T(128)} %broadcast.432), dimensions={2}, to_apply=%param.13.reduce_sub_computation.5 | reduce | bytes 16388 | tf_op args[3]
  4.5 0.1 eq.123
  4.6 0.8 reshape.491
  5.5 1.7 %fusion.6 = f32[4,2,1024]{2,0,1:T(4,128)S(1)} fusion(s32[2048]{0:T(1024)S(1)} %get-tuple-element.70, s32[2,2048]{1,0:T(2,128)S(1)} %pad_add_fusion, pred[4,2048]{1,0:T(4,128)(4,1)S(1)} %iota_compare_fusion.7), kind=kOutput, calls=%fused_computation.11 | convolution fusion | flops 35684352 | bytes 65536 | tf_op jit(solution)/shard_map/dot_general | solution.py:128
  7.3 3.0 %collective-permute-start = (s32[1024]{0:T(1024)S(1)}, s32[1024]{0:T(1024)S(1)}, u32[]{:S(2)}, u32[]{:S(2)}) collective-permute-start(s32[1024]{0:T(1024)S(1)} %bitcast.157), channel_id=1, source_target_pairs={{0,8},{8,0},{16,24},{24,16},{1,9},{9,1},{17,25},{25,17},{2,10},{10... | collective-permute-start | bytes 12296 | tf_op jit(solution)/shard_map/ppermute | solution.py:139
  10.3 1.5 %collective-permute-start.1 = (s32[1024]{0:T(1024)S(1)}, s32[1024]{0:T(1024)S(1)}, u32[]{:S(2)}, u32[]{:S(2)}) collective-permute-start(s32[1024]{0:T(1024)S(1)} %bitcast.156), channel_id=1, source_target_pairs={{0,16},{8,24},{16,0},{24,8},{1,17},{9,25},{17,1},{25,9},{2,18},{10... | collective-permute-start | bytes 12296 | tf_op jit(solution)/shard_map/ppermute | solution.py:139
  11.8 0.0 collective-permute-start.2
  11.8 4.7 %fusion.9 = f32[256,256]{1,0:T(8,128)S(1)} fusion(bf16[16384,256]{1,0:T(8,128)(2,1)} %param.10, s32[]{:T(128)S(6)} %select_n.127), kind=kOutput, calls=%fused_computation.13 | convolution fusion | flops 1073741824 | bytes 4456452 | tf_op jit(solution)/shard_map/dot_general | solution.py:15
  16.6 0.0 copy-start.3
  16.6 0.1 collective-permute-start.3
  16.7 0.7 fusion.112
  17.4 0.1 reshape.494
  17.6 0.6 compare_reduce_fusion
  18.2 0.0 collective-permute-done
  18.2 0.0 collective-permute-done.1
  18.2 0.0 collective-permute-done.2
  18.3 2.0 %collective-permute-start.4 = (bf16[256,256]{1,0:T(8,128)(2,1)S(1)}, bf16[256,256]{1,0:T(8,128)(2,1)S(1)}, u32[]{:S(2)}, u32[]{:S(2)}) collective-permute-start(bf16[256,256]{1,0:T(8,128)(2,1)S(1)} %get-tuple-element.46), channel_id=1, source_target_pairs={{0,8},{8,0},{16,24},{24,16},{1,9},{9,1},{17,25},{25,17},{2,10},{10... | collective-permute-start | bytes 393224 | tf_op jit(solution)/shard_map/ppermute | solution.py:36
  20.3 1.5 %collective-permute-start.5 = (bf16[256,256]{1,0:T(8,128)(2,1)S(1)}, bf16[256,256]{1,0:T(8,128)(2,1)S(1)}, u32[]{:S(2)}, u32[]{:S(2)}) collective-permute-start(bf16[256,256]{1,0:T(8,128)(2,1)S(1)} %get-tuple-element.46), channel_id=1, source_target_pairs={{0,16},{8,24},{16,0},{24,8},{1,17},{9,25},{17,1},{25,9},{2,18},{10... | collective-permute-start | bytes 393224 | tf_op jit(solution)/shard_map/ppermute | solution.py:36
  21.8 0.0 collective-permute-start.6
  21.8 16.6 %gather_fusion = bf16[3072,256]{1,0:T(8,128)(2,1)} fusion(bf16[16384,256]{1,0:T(8,128)(2,1)} %param.10, s32[3072]{0:T(1024)S(1)} %broadcast_clamp_fusion), kind=kCustom, calls=%fused_computation | custom fusion | bytes 3158016 | tf_op jit(solution)/shard_map/gather | solution.py:148
  38.4 0.0 copy-start.4
  38.4 0.1 multiply_multiply_fusion
  38.5 2.6 %slice_bitcast_fusion.2 = (bf16[1024,256]{1,0:T(8,128)(2,1)}, bf16[1024,256]{1,0:T(8,128)(2,1)}, bf16[1024,256]{1,0:T(8,128)(2,1)}) fusion(bf16[3,1024,256]{2,1,0:T(8,128)(2,1)} %bitcast.146), kind=kLoop, calls=%fused_computation.40 | loop fusion | bytes 3145728 | tf_op jit(solution)/shard_map/squeeze | solution.py:156
  41.1 1.9 %collective-permute-start.7 = (bf16[1024,256]{1,0:T(8,128)(2,1)}, bf16[1024,256]{1,0:T(8,128)(2,1)}, u32[]{:S(2)}, u32[]{:S(2)}) collective-permute-start(bf16[1024,256]{1,0:T(8,128)(2,1)} %get-tuple-element.50), channel_id=1, source_target_pairs={{0,8},{8,0},{16,24},{24,16},{1,9},{9,1},{17,25},{25,17},{2,10},{10... | collective-permute-start | bytes 1572872 | tf_op jit(solution)/shard_map/ppermute | solution.py:156
  43.1 1.5 %collective-permute-start.8 = (bf16[1024,256]{1,0:T(8,128)(2,1)}, bf16[1024,256]{1,0:T(8,128)(2,1)}, u32[]{:S(2)}, u32[]{:S(2)}) collective-permute-start(bf16[1024,256]{1,0:T(8,128)(2,1)} %get-tuple-element.52), channel_id=1, source_target_pairs={{0,16},{8,24},{16,0},{24,8},{1,17},{9,25},{17,1},{25,9},{2,18},{10... | collective-permute-start | bytes 1572872 | tf_op jit(solution)/shard_map/ppermute | solution.py:156
  44.6 0.0 collective-permute-start.9
  44.7 0.2 reduce_window_sum.25
  44.9 0.1 convert_reduce_fusion.1
  45.0 0.2 fusion.80
  45.2 0.1 copy.134
  45.3 0.1 copy.133
  45.4 9.1 %gather_fusion.1 = bf16[1024,256]{1,0:T(8,128)(2,1)} fusion(bf16[16384,256]{1,0:T(8,128)(2,1)} %param.10, s32[1024]{0:T(1024)S(1)} %fusion.98), kind=kCustom, calls=%fused_computation.1 | custom fusion | bytes 1052672 | tf_op jit(solution)/shard_map/gather | solution.py:153
  54.5 7.7 %gather_fusion.2 = bf16[2048,256]{1,0:T(8,128)(2,1)S(1)} fusion(bf16[4096,256]{1,0:T(8,128)(2,1)S(1)} %copy-done, s32[2048]{0:T(1024)S(1)} %broadcast_clamp_fusion.1), kind=kCustom, calls=%fused_computation.2 | custom fusion | bytes 2105344 | tf_op jit(solution)/shard_map/gather | solution.py:169
  62.2 0.5 convert_select_fusion
  62.7 2.7 %fusion.5 = f32[2048,256]{1,0:T(8,128)S(1)} fusion(bf16[1024,256]{1,0:T(8,128)(2,1)} %gather_fusion.1, s32[2048]{0:T(1024)S(1)} %get-tuple-element.69), kind=kOutput, calls=%fused_computation.10 | convolution fusion | flops 1075838976 | bytes 2629632 | tf_op jit(solution)/shard_map/dot_general | solution.py:161
  65.4 2.4 %collective-permute-done.8 = bf16[1024,256]{1,0:T(8,128)(2,1)} collective-permute-done((bf16[1024,256]{1,0:T(8,128)(2,1)}, bf16[1024,256]{1,0:T(8,128)(2,1)}, u32[]{:S(2)}, u32[]{:S(2)}) %collective-permute-start.8) | collective-permute-done | bytes 524320 | tf_op jit(solution)/shard_map/ppermute | solution.py:156
  67.8 1.5 %pad_maximum_fusion = bf16[3,1024,256]{2,1,0:T(8,128)(2,1)S(1)} fusion(bf16[1,1024,256]{2,1,0:T(8,128)(2,1)} %bitcast.16, bf16[1,1024,256]{2,1,0:T(8,128)(2,1)} %bitcast.14, bf16[1,1024,256]{2,1,0:T(8,128)(2,1)} %bitcast.12), kind=kLoop, calls=%fused_computation.19 | loop fusion | flops 1572864 | bytes 3145728 | tf_op jit(solution)/shard_map/stack | solution.py:165
  69.4 4.2 %fusion.18 = bf16[2048,256]{1,0:T(8,128)(2,1)S(1)} fusion(f32[2048,256]{1,0:T(8,128)S(1)} %fusion.5, bf16[3072,256]{1,0:T(8,128)(2,1)S(1)} %bitcast.147, s32[3072]{0:T(1024)S(1)} %iota_add_fusion, s32[2048]{0:T(1024)S(1)} %get-tuple-element.69, bf16[2048,256]{1,0:T(8,128)(2,1)S(1)} %gather_fusion.2), kind=kOutput, calls=%fused_computation.18 | convolution fusion | flops 3229614080 | bytes 5787648 | tf_op jit(solution)/shard_map/dot_general | solution.py:166
  73.6 0.5 fusion.113
  74.2 0.4 convolution_reduce_fusion.5
  74.7 0.3 convolution_reduce_fusion.2
  74.9 0.3 multiply_reduce_fusion.3
  75.3 0.2 multiply_reduce_fusion.2
  75.5 0.1 fusion.70
  75.6 0.4 convolution_reduce_fusion.4
  76.1 0.3 convolution_reduce_fusion.1
  76.4 0.3 multiply_reduce_fusion.1
  76.8 0.2 multiply_reduce_fusion
  76.9 0.1 fusion.72
  77.1 0.4 convolution_reduce_fusion.3
  77.6 0.3 convolution_reduce_fusion
  77.8 0.3 fusion.27
  78.2 0.3 fusion.26
  78.6 12.5 %all_to_all.5 = f32[32,2,384]{2,1,0:T(2,128)S(1)} all-to-all(f32[32,2,384]{2,1,0:T(2,128)S(1)} %bitcast.148), channel_id=1, replica_groups=mesh['table'=4,'batch'=4,'ctx'=2] {'table','batch','ctx'}, dimensions={0} | all-to-all | bytes 196608 | tf_op jit(solution)/shard_map/all_to_all | solution.py:196
  91.1 0.1 reshape.497
  91.1 0.1 fusion.36
  91.2 0.1 convert_reduce_fusion
  91.4 1.3 %fusion.21 = bf16[1024,256]{1,0:T(8,128)(2,1)} fusion(bf16[1024,256]{1,0:T(8,128)(2,1)S(1)} %copy-done.1, pred[1024]{0:T(1024)(128)(4,1)S(1)} %broadcast_compare_fusion, s32[64]{0:T(128)S(1)} %fusion.36, f32[64,384]{1,0:T(8,128)S(1)} %reshape.497), kind=kOutput, calls=%fused_computation.21 | convolution fusion | flops 34144256 | bytes 1082880 | tf_op jit(solution)/shard_map/dot_general | solution.py:203
  (65 shorter events, 0.7 us)
Async XLA Ops:
  0.0 16.7 %copy-start = (bf16[4096,256]{1,0:T(8,128)(2,1)S(1)}, bf16[4096,256]{1,0:T(8,128)(2,1)}, u32[]{:S(2)}) copy-start(bf16[4096,256]{1,0:T(8,128)(2,1)} %param.11) | copy-start | bytes 6291460
  7.3 10.9 %collective-permute-start = (s32[1024]{0:T(1024)S(1)}, s32[1024]{0:T(1024)S(1)}, u32[]{:S(2)}, u32[]{:S(2)}) collective-permute-start(s32[1024]{0:T(1024)S(1)} %bitcast.157), channel_id=1, source_target_pairs={{0,8},{8,0},{16,24},{24,16},{1,9},{9,1},{17,25},{25,17},{2,10},{10... | collective-permute-start | bytes 12296 | tf_op jit(solution)/shard_map/ppermute | solution.py:139
  10.3 7.9 %collective-permute-start.1 = (s32[1024]{0:T(1024)S(1)}, s32[1024]{0:T(1024)S(1)}, u32[]{:S(2)}, u32[]{:S(2)}) collective-permute-start(s32[1024]{0:T(1024)S(1)} %bitcast.156), channel_id=1, source_target_pairs={{0,16},{8,24},{16,0},{24,8},{1,17},{9,25},{17,1},{25,9},{2,18},{10... | collective-permute-start | bytes 12296 | tf_op jit(solution)/shard_map/ppermute | solution.py:139
  11.8 6.4 %collective-permute-start.2 = (s32[1024]{0:T(1024)S(1)}, s32[1024]{0:T(1024)S(1)}, u32[]{:S(2)}, u32[]{:S(2)}) collective-permute-start(s32[1024]{0:T(1024)S(1)} %bitcast.155), channel_id=1, source_target_pairs={{0,24},{8,16},{16,8},{24,0},{1,25},{9,17},{17,9},{25,1},{2,26},{10... | collective-permute-start | bytes 12296 | tf_op jit(solution)/shard_map/ppermute | solution.py:139
  16.6 0.9 copy-start.3
  16.6 1.6 %collective-permute-start.3 = (f32[256,256]{1,0:T(8,128)S(1)}, f32[256,256]{1,0:T(8,128)S(1)}, u32[]{:S(2)}, u32[]{:S(2)}) collective-permute-start(f32[256,256]{1,0:T(8,128)S(1)} %fusion.9), channel_id=1, source_target_pairs={{0,1},{1,0},{2,3},{3,2},{4,5},{5,4},{6,7},{7,6},{8,9},{9,8},{10,11... | collective-permute-start | bytes 786440 | tf_op jit(solution)/shard_map/ppermute | solution.py:26
  18.3 20.2 %collective-permute-start.4 = (bf16[256,256]{1,0:T(8,128)(2,1)S(1)}, bf16[256,256]{1,0:T(8,128)(2,1)S(1)}, u32[]{:S(2)}, u32[]{:S(2)}) collective-permute-start(bf16[256,256]{1,0:T(8,128)(2,1)S(1)} %get-tuple-element.46), channel_id=1, source_target_pairs={{0,8},{8,0},{16,24},{24,16},{1,9},{9,1},{17,25},{25,17},{2,10},{10... | collective-permute-start | bytes 393224 | tf_op jit(solution)/shard_map/ppermute | solution.py:36
  20.3 18.1 %collective-permute-start.5 = (bf16[256,256]{1,0:T(8,128)(2,1)S(1)}, bf16[256,256]{1,0:T(8,128)(2,1)S(1)}, u32[]{:S(2)}, u32[]{:S(2)}) collective-permute-start(bf16[256,256]{1,0:T(8,128)(2,1)S(1)} %get-tuple-element.46), channel_id=1, source_target_pairs={{0,16},{8,24},{16,0},{24,8},{1,17},{9,25},{17,1},{25,9},{2,18},{10... | collective-permute-start | bytes 393224 | tf_op jit(solution)/shard_map/ppermute | solution.py:36
  21.8 16.6 %collective-permute-start.6 = (bf16[256,256]{1,0:T(8,128)(2,1)S(1)}, bf16[256,256]{1,0:T(8,128)(2,1)S(1)}, u32[]{:S(2)}, u32[]{:S(2)}) collective-permute-start(bf16[256,256]{1,0:T(8,128)(2,1)S(1)} %get-tuple-element.46), channel_id=1, source_target_pairs={{0,24},{8,16},{16,8},{24,0},{1,25},{9,17},{17,9},{25,1},{2,26},{10... | collective-permute-start | bytes 393224 | tf_op jit(solution)/shard_map/ppermute | solution.py:36
  38.4 6.2 %copy-start.4 = (s32[32]{0:T(128)S(1)}, s32[32]{0:T(128)}, u32[]{:S(2)}) copy-start(s32[32]{0:T(128)} %param.17) | copy-start | bytes 388
  41.1 24.3 %collective-permute-start.7 = (bf16[1024,256]{1,0:T(8,128)(2,1)}, bf16[1024,256]{1,0:T(8,128)(2,1)}, u32[]{:S(2)}, u32[]{:S(2)}) collective-permute-start(bf16[1024,256]{1,0:T(8,128)(2,1)} %get-tuple-element.50), channel_id=1, source_target_pairs={{0,8},{8,0},{16,24},{24,16},{1,9},{9,1},{17,25},{25,17},{2,10},{10... | collective-permute-start | bytes 1572872 | tf_op jit(solution)/shard_map/ppermute | solution.py:156
  43.1 24.7 %collective-permute-start.8 = (bf16[1024,256]{1,0:T(8,128)(2,1)}, bf16[1024,256]{1,0:T(8,128)(2,1)}, u32[]{:S(2)}, u32[]{:S(2)}) collective-permute-start(bf16[1024,256]{1,0:T(8,128)(2,1)} %get-tuple-element.52), channel_id=1, source_target_pairs={{0,16},{8,24},{16,0},{24,8},{1,17},{9,25},{17,1},{25,9},{2,18},{10... | collective-permute-start | bytes 1572872 | tf_op jit(solution)/shard_map/ppermute | solution.py:156
  44.6 23.2 %collective-permute-start.9 = (bf16[1024,256]{1,0:T(8,128)(2,1)}, bf16[1024,256]{1,0:T(8,128)(2,1)}, u32[]{:S(2)}, u32[]{:S(2)}) collective-permute-start(bf16[1024,256]{1,0:T(8,128)(2,1)} %get-tuple-element.51), channel_id=1, source_target_pairs={{0,24},{8,16},{16,8},{24,0},{1,25},{9,17},{17,9},{25,1},{2,26},{10... | collective-permute-start | bytes 1572872 | tf_op jit(solution)/shard_map/ppermute | solution.py:156
  54.5 8.2 %copy-start.2 = (s32[32,64]{1,0:T(8,128)S(1)}, s32[32,64]{1,0:T(8,128)}, u32[]{:S(2)}) copy-start(s32[32,64]{1,0:T(8,128)} %param.16) | copy-start | bytes 24580
  76.7 14.6 %copy-start.1 = (bf16[1024,256]{1,0:T(8,128)(2,1)S(1)}, bf16[1024,256]{1,0:T(8,128)(2,1)}, u32[]{:S(2)}) copy-start(bf16[1024,256]{1,0:T(8,128)(2,1)} %param.12) | copy-start | bytes 1572868

commit v19 on v18

--- a/solution.py
+++ b/solution.py
@@ -142,15 +142,14 @@
     own_rows = lax.dynamic_slice_in_dim(gram_source, lax.axis_index("ctx") * share, share, axis=0)
     item_gram = butterfly_sum(gram_of(own_rows), (("ctx", n_ctx),))
     item_gram = exchange_sum(item_gram, "table", n_table, jnp.bfloat16)
-    context_gram = gram_of(context_table)
-    pair_count = item_table.shape[0] * n_table * context_table.shape[0]
-    gram_matrix = item_gram * context_gram / pair_count
     remote = item_table[jnp.stack(by_offset[1:], axis=0)]
-    remote, gram_matrix = lax.optimization_barrier((remote, gram_matrix))
+    remote, item_gram = lax.optimization_barrier((remote, item_gram))
     remote, late_items, late_contexts, local_requests, bucket, user_ids = lax.optimization_barrier(
         (remote, item_table, context_table, by_offset[0], bucket, user_ids)
     )
     got = [late_items[local_requests]]
+    pair_count = item_table.shape[0] * n_table * context_table.shape[0]
+    gram_matrix = item_gram * gram_of(late_contexts) / pair_count
     for k in range(1, n_table):
         pairs = [(i, i ^ k) for i in range(n_table)]
         got.append(lax.ppermute(remote[k - 1], "table", pairs))

time: 93.1 us -> 92.7 us (level)
  local copies, waits for them, and re-layouts: 39.1 us -> 37.9 us
    gather x1, local copies, waits for them, and re-layouts: 9.07 us -> 7.92 us  [per_device(): got = [late_items[local_requests]]]
  transfers between devices with their start and end apart: 10 -> 10, of which waited for: 1 -> 2; matrix products, arithmetic and copies ran while one was open for 47% -> 46% of each run, Pallas kernels for 0% -> 0%
where the time goes in v19:
time: 92.7 us; the launch traced here: 92.3 us
  local copies, waits for them, and re-layouts  37.9 us (41%)
  matrix products  19.5 us (21%)
  blocking collectives  12.5 us (13%)
  starting transfers between devices  11.7 us (13%)
  other arithmetic  7.04 us (8%)
  waiting for transfers between devices  3.15 us (3%)
    gather x1, local copies, waits for them, and re-layouts, per_device(): remote = item_table[jnp.stack(by_offset[1:], axis=0)]  16.6 us
    all_to_all x1, blocking collectives, per_device(): lax.all_to_all(payload, ('table', 'batch', 'ctx'), split_axis=0, concat_a...  12.5 us
    gather x1, local copies, waits for them, and re-layouts, per_device(): got = [late_items[local_requests]]  7.92 us
    gather x1, local copies, waits for them, and re-layouts, per_device(): late_contexts[context_flat].astype(jnp.float32)  7.67 us
    dot_general x2, matrix products, gram_of(): lax.dot_general(table_rows, table_rows, (((0,), (0,)), ((), ())), preferr...  5.49 us
    ppermute x3, starting transfers between devices, per_device(): by_offset.append(lax.ppermute(outgoing, 'table', pairs))  4.54 us
    dot_general x1, matrix products, per_device(): jnp.dot(placing, fetched.reshape((n_table - 1) * capacity, rank_width), p...  4.23 us
    ppermute x3, starting transfers between devices, exchange_sum(): total = total + lax.ppermute(sent, name, pairs).astype(value.dtype)  3.55 us
  transfers between devices with their start and end apart: 10, of which 2 were waited for; matrix products, arithmetic and copies ran while one was open for 46% of the time, Pallas kernels for 0%

profile of v19, /device:TPU:0, one launch (start us, length us, event | category | flops | bytes accessed | tf_op | source)
XLA Modules:
  0.0 92.3 jit_solution(16214227201524409875)
XLA Ops:
  0.0 0.9 %eq.127 = s32[16,128]{1,0:T(8,128)S(1)} reshape(s32[32,64]{1,0:T(8,128)} %bitcast.147) | data formatting | bytes 16384 | tf_op jit(solution)/shard_map/eq | solution.py:124
  0.9 1.1 %reduce-window.6 = s32[4,16,128]{2,1,0:T(8,128)S(1)} reduce-window(s32[4,16,128]{2,1,0:T(8,128)S(1)} %fusion.56, s32[]{:T(128)} %constant.154.clone.1), window={size=1x1x128 pad=0_0x0_0x127_0}, to_apply=%region_0.0 | reduce-window | flops 1040384 | bytes 65540 | tf_op jit(solution)/shard_map/reduce-window
  2.1 0.2 slice_reduce_fusion
  2.3 0.2 reduce-window.9
  2.5 0.1 select_reduce_fusion
  2.6 0.5 broadcast.432
  3.1 1.4 %reduce.18 = s32[32,64]{1,0:T(8,128)S(1)} reduce(s32[32,64,1]{1,2,0:T(1,128)} %param.13, s32[]{:T(128)} %broadcast.432), dimensions={2}, to_apply=%param.13.reduce_sub_computation.5 | reduce | bytes 16388 | tf_op args[3]
  4.5 0.1 eq.123
  4.6 0.8 reshape.491
  5.5 1.7 %fusion.6 = f32[4,2,1024]{2,0,1:T(4,128)S(1)} fusion(s32[2048]{0:T(1024)S(1)} %get-tuple-element.70, s32[2,2048]{1,0:T(2,128)S(1)} %pad_add_fusion, pred[4,2048]{1,0:T(4,128)(4,1)S(1)} %iota_compare_fusion.7), kind=kOutput, calls=%fused_computation.11 | convolution fusion | flops 35684352 | bytes 65536 | tf_op jit(solution)/shard_map/dot_general | solution.py:128
  7.3 3.0 %collective-permute-start = (s32[1024]{0:T(1024)S(1)}, s32[1024]{0:T(1024)S(1)}, u32[]{:S(2)}, u32[]{:S(2)}) collective-permute-start(s32[1024]{0:T(1024)S(1)} %bitcast.154), channel_id=1, source_target_pairs={{0,8},{8,0},{16,24},{24,16},{1,9},{9,1},{17,25},{25,17},{2,10},{10... | collective-permute-start | bytes 12296 | tf_op jit(solution)/shard_map/ppermute | solution.py:139
  10.3 1.5 %collective-permute-start.1 = (s32[1024]{0:T(1024)S(1)}, s32[1024]{0:T(1024)S(1)}, u32[]{:S(2)}, u32[]{:S(2)}) collective-permute-start(s32[1024]{0:T(1024)S(1)} %bitcast.153), channel_id=1, source_target_pairs={{0,16},{8,24},{16,0},{24,8},{1,17},{9,25},{17,1},{25,9},{2,18},{10... | collective-permute-start | bytes 12296 | tf_op jit(solution)/shard_map/ppermute | solution.py:139
  11.8 0.0 collective-permute-start.2
  11.8 4.8 %fusion.9 = f32[256,256]{1,0:T(8,128)S(1)} fusion(bf16[16384,256]{1,0:T(8,128)(2,1)} %param.10, s32[]{:T(128)S(6)} %select_n.127), kind=kOutput, calls=%fused_computation.13 | convolution fusion | flops 1073741824 | bytes 4456452 | tf_op jit(solution)/shard_map/dot_general | solution.py:15
  16.6 0.1 collective-permute-start.3
  16.7 0.1 reshape.494
  16.8 0.6 compare_reduce_fusion
  17.4 0.0 collective-permute-done
  17.4 0.0 collective-permute-done.1
  17.4 0.0 collective-permute-done.2
  17.5 0.7 collective-permute-done.3
  18.2 2.0 %collective-permute-start.4 = (bf16[256,256]{1,0:T(8,128)(2,1)S(1)}, bf16[256,256]{1,0:T(8,128)(2,1)S(1)}, u32[]{:S(2)}, u32[]{:S(2)}) collective-permute-start(bf16[256,256]{1,0:T(8,128)(2,1)S(1)} %get-tuple-element.46), channel_id=1, source_target_pairs={{0,8},{8,0},{16,24},{24,16},{1,9},{9,1},{17,25},{25,17},{2,10},{10... | collective-permute-start | bytes 393224 | tf_op jit(solution)/shard_map/ppermute | solution.py:36
  20.3 1.5 %collective-permute-start.5 = (bf16[256,256]{1,0:T(8,128)(2,1)S(1)}, bf16[256,256]{1,0:T(8,128)(2,1)S(1)}, u32[]{:S(2)}, u32[]{:S(2)}) collective-permute-start(bf16[256,256]{1,0:T(8,128)(2,1)S(1)} %get-tuple-element.46), channel_id=1, source_target_pairs={{0,16},{8,24},{16,0},{24,8},{1,17},{9,25},{17,1},{25,9},{2,18},{10... | collective-permute-start | bytes 393224 | tf_op jit(solution)/shard_map/ppermute | solution.py:36
  21.8 0.0 collective-permute-start.6
  21.8 16.6 %gather_fusion = bf16[3072,256]{1,0:T(8,128)(2,1)} fusion(bf16[16384,256]{1,0:T(8,128)(2,1)} %param.10, s32[3072]{0:T(1024)S(1)} %broadcast_clamp_fusion), kind=kCustom, calls=%fused_computation | custom fusion | bytes 3158016 | tf_op jit(solution)/shard_map/gather | solution.py:145
  38.4 0.1 convert_add_fusion
  38.5 2.5 %slice_bitcast_fusion.2 = (bf16[1024,256]{1,0:T(8,128)(2,1)}, bf16[1024,256]{1,0:T(8,128)(2,1)}, bf16[1024,256]{1,0:T(8,128)(2,1)}) fusion(bf16[3,1024,256]{2,1,0:T(8,128)(2,1)} %bitcast.143), kind=kLoop, calls=%fused_computation.40 | loop fusion | bytes 3145728 | tf_op jit(solution)/shard_map/squeeze | solution.py:155
  41.0 1.9 %collective-permute-start.7 = (bf16[1024,256]{1,0:T(8,128)(2,1)}, bf16[1024,256]{1,0:T(8,128)(2,1)}, u32[]{:S(2)}, u32[]{:S(2)}) collective-permute-start(bf16[1024,256]{1,0:T(8,128)(2,1)} %get-tuple-element.50), channel_id=1, source_target_pairs={{0,8},{8,0},{16,24},{24,16},{1,9},{9,1},{17,25},{25,17},{2,10},{10... | collective-permute-start | bytes 1572872 | tf_op jit(solution)/shard_map/ppermute | solution.py:155
  43.0 1.5 %collective-permute-start.8 = (bf16[1024,256]{1,0:T(8,128)(2,1)}, bf16[1024,256]{1,0:T(8,128)(2,1)}, u32[]{:S(2)}, u32[]{:S(2)}) collective-permute-start(bf16[1024,256]{1,0:T(8,128)(2,1)} %get-tuple-element.52), channel_id=1, source_target_pairs={{0,16},{8,24},{16,0},{24,8},{1,17},{9,25},{17,1},{25,9},{2,18},{10... | collective-permute-start | bytes 1572872 | tf_op jit(solution)/shard_map/ppermute | solution.py:155
  44.5 0.0 collective-permute-start.9
  44.6 0.2 reduce_window_sum.25
  44.8 0.1 convert_reduce_fusion.1
  44.9 0.2 fusion.80
  45.1 0.1 copy.134
  45.2 0.1 copy.133
  45.3 7.9 %gather_fusion.1 = bf16[1024,256]{1,0:T(8,128)(2,1)S(1)} fusion(bf16[16384,256]{1,0:T(8,128)(2,1)} %param.10, s32[1024]{0:T(1024)S(1)} %fusion.98), kind=kCustom, calls=%fused_computation.1 | custom fusion | bytes 1052672 | tf_op jit(solution)/shard_map/gather | solution.py:150
  53.2 2.7 %fusion.5 = f32[2048,256]{1,0:T(8,128)} fusion(bf16[1024,256]{1,0:T(8,128)(2,1)S(1)} %gather_fusion.1, s32[2048]{0:T(1024)S(1)} %get-tuple-element.69), kind=kOutput, calls=%fused_computation.10 | convolution fusion | flops 1075838976 | bytes 2629632 | tf_op jit(solution)/shard_map/dot_general | solution.py:160
  56.0 7.7 %gather_fusion.2 = bf16[2048,256]{1,0:T(8,128)(2,1)S(1)} fusion(bf16[4096,256]{1,0:T(8,128)(2,1)S(1)} %copy-done, s32[2048]{0:T(1024)S(1)} %broadcast_clamp_fusion.1), kind=kCustom, calls=%fused_computation.2 | custom fusion | bytes 2105344 | tf_op jit(solution)/shard_map/gather | solution.py:168
  63.6 0.6 convert_select_fusion
  64.2 0.7 fusion.113
  65.0 2.4 %collective-permute-done.8 = bf16[1024,256]{1,0:T(8,128)(2,1)} collective-permute-done((bf16[1024,256]{1,0:T(8,128)(2,1)}, bf16[1024,256]{1,0:T(8,128)(2,1)}, u32[]{:S(2)}, u32[]{:S(2)}) %collective-permute-start.8) | collective-permute-done | bytes 524320 | tf_op jit(solution)/shard_map/ppermute | solution.py:155
  67.4 1.5 %pad_maximum_fusion = bf16[3,1024,256]{2,1,0:T(8,128)(2,1)S(1)} fusion(bf16[1,1024,256]{2,1,0:T(8,128)(2,1)} %bitcast.16, bf16[1,1024,256]{2,1,0:T(8,128)(2,1)} %bitcast.14, bf16[1,1024,256]{2,1,0:T(8,128)(2,1)} %bitcast.12), kind=kLoop, calls=%fused_computation.19 | loop fusion | flops 1572864 | bytes 3145728 | tf_op jit(solution)/shard_map/stack | solution.py:164
  68.9 4.2 %fusion.18 = bf16[2048,256]{1,0:T(8,128)(2,1)S(1)} fusion(f32[2048,256]{1,0:T(8,128)S(1)} %copy-done.5, bf16[3072,256]{1,0:T(8,128)(2,1)S(1)} %bitcast.144, s32[3072]{0:T(1024)S(1)} %iota_add_fusion, s32[2048]{0:T(1024)S(1)} %get-tuple-element.69, bf16[2048,256]{1,0:T(8,128)(2,1)S(1)} %gather_fusion.2), kind=kOutput, calls=%fused_computation.18 | convolution fusion | flops 3229614080 | bytes 5787648 | tf_op jit(solution)/shard_map/dot_general | solution.py:165
  73.2 0.5 fusion.112
  73.7 0.4 convolution_reduce_fusion.5
  74.2 0.3 convolution_reduce_fusion.2
  74.5 0.4 multiply_reduce_fusion.3
  74.9 0.2 multiply_reduce_fusion.2
  75.1 0.1 fusion.70
  75.2 0.4 convolution_reduce_fusion.4
  75.7 0.3 convolution_reduce_fusion.1
  76.0 0.4 multiply_reduce_fusion.1
  76.3 0.2 multiply_reduce_fusion
  76.5 0.1 fusion.72
  76.6 0.0 copy-start.1
  76.7 0.4 convolution_reduce_fusion.3
  77.2 0.3 convolution_reduce_fusion
  77.4 0.4 fusion.27
  77.8 0.3 fusion.26
  78.2 12.5 %all_to_all.5 = f32[32,2,384]{2,1,0:T(2,128)S(1)} all-to-all(f32[32,2,384]{2,1,0:T(2,128)S(1)} %bitcast.145), channel_id=1, replica_groups=mesh['table'=4,'batch'=4,'ctx'=2] {'table','batch','ctx'}, dimensions={0} | all-to-all | bytes 196608 | tf_op jit(solution)/shard_map/all_to_all | solution.py:195
  90.7 0.1 reshape.497
  90.8 0.1 fusion.36
  90.9 0.1 convert_reduce_fusion
  91.0 1.3 %fusion.21 = bf16[1024,256]{1,0:T(8,128)(2,1)} fusion(bf16[1024,256]{1,0:T(8,128)(2,1)S(1)} %copy-done.1, pred[1024]{0:T(1024)(128)(4,1)S(1)} %broadcast_compare_fusion, s32[64]{0:T(128)S(1)} %fusion.36, f32[64,384]{1,0:T(8,128)S(1)} %reshape.497), kind=kOutput, calls=%fused_computation.21 | convolution fusion | flops 34144256 | bytes 1082880 | tf_op jit(solution)/shard_map/dot_general | solution.py:202
  (67 shorter events, 0.7 us)
Async XLA Ops:
  0.0 56.0 %copy-start = (bf16[4096,256]{1,0:T(8,128)(2,1)S(1)}, bf16[4096,256]{1,0:T(8,128)(2,1)}, u32[]{:S(2)}) copy-start(bf16[4096,256]{1,0:T(8,128)(2,1)} %param.11) | copy-start | bytes 6291460
  7.3 10.1 %collective-permute-start = (s32[1024]{0:T(1024)S(1)}, s32[1024]{0:T(1024)S(1)}, u32[]{:S(2)}, u32[]{:S(2)}) collective-permute-start(s32[1024]{0:T(1024)S(1)} %bitcast.154), channel_id=1, source_target_pairs={{0,8},{8,0},{16,24},{24,16},{1,9},{9,1},{17,25},{25,17},{2,10},{10... | collective-permute-start | bytes 12296 | tf_op jit(solution)/shard_map/ppermute | solution.py:139
  10.3 7.1 %collective-permute-start.1 = (s32[1024]{0:T(1024)S(1)}, s32[1024]{0:T(1024)S(1)}, u32[]{:S(2)}, u32[]{:S(2)}) collective-permute-start(s32[1024]{0:T(1024)S(1)} %bitcast.153), channel_id=1, source_target_pairs={{0,16},{8,24},{16,0},{24,8},{1,17},{9,25},{17,1},{25,9},{2,18},{10... | collective-permute-start | bytes 12296 | tf_op jit(solution)/shard_map/ppermute | solution.py:139
  11.8 5.6 %collective-permute-start.2 = (s32[1024]{0:T(1024)S(1)}, s32[1024]{0:T(1024)S(1)}, u32[]{:S(2)}, u32[]{:S(2)}) collective-permute-start(s32[1024]{0:T(1024)S(1)} %bitcast.152), channel_id=1, source_target_pairs={{0,24},{8,16},{16,8},{24,0},{1,25},{9,17},{17,9},{25,1},{2,26},{10... | collective-permute-start | bytes 12296 | tf_op jit(solution)/shard_map/ppermute | solution.py:139
  11.8 4.8 %copy-start.3 = (s32[32,64]{1,0:T(8,128)S(1)}, s32[32,64]{1,0:T(8,128)}, u32[]{:S(2)}) copy-start(s32[32,64]{1,0:T(8,128)} %param.15) | copy-start | bytes 24580
  16.6 1.6 %collective-permute-start.3 = (f32[256,256]{1,0:T(8,128)S(1)}, f32[256,256]{1,0:T(8,128)S(1)}, u32[]{:S(2)}, u32[]{:S(2)}) collective-permute-start(f32[256,256]{1,0:T(8,128)S(1)} %fusion.9), channel_id=1, source_target_pairs={{0,1},{1,0},{2,3},{3,2},{4,5},{5,4},{6,7},{7,6},{8,9},{9,8},{10,11... | collective-permute-start | bytes 786440 | tf_op jit(solution)/shard_map/ppermute | solution.py:26
  18.2 20.2 %collective-permute-start.4 = (bf16[256,256]{1,0:T(8,128)(2,1)S(1)}, bf16[256,256]{1,0:T(8,128)(2,1)S(1)}, u32[]{:S(2)}, u32[]{:S(2)}) collective-permute-start(bf16[256,256]{1,0:T(8,128)(2,1)S(1)} %get-tuple-element.46), channel_id=1, source_target_pairs={{0,8},{8,0},{16,24},{24,16},{1,9},{9,1},{17,25},{25,17},{2,10},{10... | collective-permute-start | bytes 393224 | tf_op jit(solution)/shard_map/ppermute | solution.py:36
  20.3 18.1 %collective-permute-start.5 = (bf16[256,256]{1,0:T(8,128)(2,1)S(1)}, bf16[256,256]{1,0:T(8,128)(2,1)S(1)}, u32[]{:S(2)}, u32[]{:S(2)}) collective-permute-start(bf16[256,256]{1,0:T(8,128)(2,1)S(1)} %get-tuple-element.46), channel_id=1, source_target_pairs={{0,16},{8,24},{16,0},{24,8},{1,17},{9,25},{17,1},{25,9},{2,18},{10... | collective-permute-start | bytes 393224 | tf_op jit(solution)/shard_map/ppermute | solution.py:36
  21.8 16.6 %collective-permute-start.6 = (bf16[256,256]{1,0:T(8,128)(2,1)S(1)}, bf16[256,256]{1,0:T(8,128)(2,1)S(1)}, u32[]{:S(2)}, u32[]{:S(2)}) collective-permute-start(bf16[256,256]{1,0:T(8,128)(2,1)S(1)} %get-tuple-element.46), channel_id=1, source_target_pairs={{0,24},{8,16},{16,8},{24,0},{1,25},{9,17},{17,9},{25,1},{2,26},{10... | collective-permute-start | bytes 393224 | tf_op jit(solution)/shard_map/ppermute | solution.py:36
  38.4 6.1 %copy-start.4 = (s32[32]{0:T(128)S(1)}, s32[32]{0:T(128)}, u32[]{:S(2)}) copy-start(s32[32]{0:T(128)} %param.17) | copy-start | bytes 388
  41.0 24.0 %collective-permute-start.7 = (bf16[1024,256]{1,0:T(8,128)(2,1)}, bf16[1024,256]{1,0:T(8,128)(2,1)}, u32[]{:S(2)}, u32[]{:S(2)}) collective-permute-start(bf16[1024,256]{1,0:T(8,128)(2,1)} %get-tuple-element.50), channel_id=1, source_target_pairs={{0,8},{8,0},{16,24},{24,16},{1,9},{9,1},{17,25},{25,17},{2,10},{10... | collective-permute-start | bytes 1572872 | tf_op jit(solution)/shard_map/ppermute | solution.py:155
  43.0 24.4 %collective-permute-start.8 = (bf16[1024,256]{1,0:T(8,128)(2,1)}, bf16[1024,256]{1,0:T(8,128)(2,1)}, u32[]{:S(2)}, u32[]{:S(2)}) collective-permute-start(bf16[1024,256]{1,0:T(8,128)(2,1)} %get-tuple-element.52), channel_id=1, source_target_pairs={{0,16},{8,24},{16,0},{24,8},{1,17},{9,25},{17,1},{25,9},{2,18},{10... | collective-permute-start | bytes 1572872 | tf_op jit(solution)/shard_map/ppermute | solution.py:155
  44.5 22.9 %collective-permute-start.9 = (bf16[1024,256]{1,0:T(8,128)(2,1)}, bf16[1024,256]{1,0:T(8,128)(2,1)}, u32[]{:S(2)}, u32[]{:S(2)}) collective-permute-start(bf16[1024,256]{1,0:T(8,128)(2,1)} %get-tuple-element.51), channel_id=1, source_target_pairs={{0,24},{8,16},{16,8},{24,0},{1,25},{9,17},{17,9},{25,1},{2,26},{10... | collective-permute-start | bytes 1572872 | tf_op jit(solution)/shard_map/ppermute | solution.py:155
  56.0 8.2 %copy-start.2 = (s32[32,64]{1,0:T(8,128)S(1)}, s32[32,64]{1,0:T(8,128)}, u32[]{:S(2)}) copy-start(s32[32,64]{1,0:T(8,128)} %param.16) | copy-start | bytes 24580
  65.0 3.9 %copy-start.5 = (f32[2048,256]{1,0:T(8,128)S(1)}, f32[2048,256]{1,0:T(8,128)}, u32[]{:S(2)}) copy-start(f32[2048,256]{1,0:T(8,128)} %fusion.5) | copy-start | bytes 6291460
  76.6 14.4 %copy-start.1 = (bf16[1024,256]{1,0:T(8,128)(2,1)S(1)}, bf16[1024,256]{1,0:T(8,128)(2,1)}, u32[]{:S(2)}) copy-start(bf16[1024,256]{1,0:T(8,128)(2,1)} %param.12) | copy-start | bytes 1572868

commit v20 on v19

--- a/solution.py
+++ b/solution.py
@@ -65,8 +65,11 @@
 def conjugate_solve(slot_rows, confidence, weights, gram_matrix):
     highest = lax.Precision.HIGHEST
     rank_width = slot_rows.shape[-1]
-    right_side = jnp.einsum(
-        "usk,us->uk", slot_rows, weights, precision=highest, preferred_element_type=jnp.float32
+    right_side = jnp.sum(
+        jnp.einsum(
+            "usk,uvs->uvk", slot_rows, split_three(weights), preferred_element_type=jnp.float32
+        ),
+        axis=1,
     ) * rank_width ** (-0.5)
     solution = jnp.zeros_like(right_side)
     residual = right_side

time: 92.7 us -> 92.5 us (level)
    another operation x4 -> x5, other arithmetic: 2.49 us -> 2.51 us
where the time goes in v20:
time: 92.5 us; the launch traced here: 92 us
  local copies, waits for them, and re-layouts  37.9 us (41%)
  matrix products  19.3 us (21%)
  blocking collectives  12.5 us (14%)
  starting transfers between devices  11.7 us (13%)
  other arithmetic  7.05 us (8%)
  waiting for transfers between devices  3.08 us (3%)
    gather x1, local copies, waits for them, and re-layouts, per_device(): remote = item_table[jnp.stack(by_offset[1:], axis=0)]  16.6 us
    all_to_all x1, blocking collectives, per_device(): lax.all_to_all(payload, ('table', 'batch', 'ctx'), split_axis=0, concat_a...  12.5 us
    gather x1, local copies, waits for them, and re-layouts, per_device(): got = [late_items[local_requests]]  7.92 us
    gather x1, local copies, waits for them, and re-layouts, per_device(): late_contexts[context_flat].astype(jnp.float32)  7.67 us
    dot_general x2, matrix products, gram_of(): lax.dot_general(table_rows, table_rows, (((0,), (0,)), ((), ())), preferr...  5.49 us
    ppermute x3, starting transfers between devices, per_device(): by_offset.append(lax.ppermute(outgoing, 'table', pairs))  4.54 us
    dot_general x1, matrix products, per_device(): jnp.dot(placing, fetched.reshape((n_table - 1) * capacity, rank_width), p...  4.23 us
    ppermute x3, starting transfers between devices, exchange_sum(): total = total + lax.ppermute(sent, name, pairs).astype(value.dtype)  3.55 us
  transfers between devices with their start and end apart: 10, of which 2 were waited for; matrix products, arithmetic and copies ran while one was open for 46% of the time, Pallas kernels for 0%

profile of v20, /device:TPU:0, one launch (start us, length us, event | category | flops | bytes accessed | tf_op | source)
XLA Modules:
  0.0 92.0 jit_solution(15761397600824479732)
XLA Ops:
  0.0 0.9 %eq.127 = s32[16,128]{1,0:T(8,128)S(1)} reshape(s32[32,64]{1,0:T(8,128)} %bitcast.110) | data formatting | bytes 16384 | tf_op jit(solution)/shard_map/eq | solution.py:127
  0.9 1.1 %reduce-window.6 = s32[4,16,128]{2,1,0:T(8,128)S(1)} reduce-window(s32[4,16,128]{2,1,0:T(8,128)S(1)} %fusion.57, s32[]{:T(128)} %constant.154.clone.1), window={size=1x1x128 pad=0_0x0_0x127_0}, to_apply=%region_0.0 | reduce-window | flops 1040384 | bytes 65540 | tf_op jit(solution)/shard_map/reduce-window
  2.1 0.2 slice_reduce_fusion
  2.3 0.2 reduce-window.9
  2.5 0.1 select_reduce_fusion
  2.6 0.5 broadcast.449
  3.1 1.4 %reduce.18 = s32[32,64]{1,0:T(8,128)S(1)} reduce(s32[32,64,1]{1,2,0:T(1,128)} %param.13, s32[]{:T(128)} %broadcast.449), dimensions={2}, to_apply=%param.13.reduce_sub_computation.5 | reduce | bytes 16388 | tf_op args[3]
  4.5 0.1 eq.123
  4.6 0.8 reshape.520
  5.5 1.7 %fusion.6 = f32[4,2,1024]{2,0,1:T(4,128)S(1)} fusion(s32[2048]{0:T(1024)S(1)} %get-tuple-element.73, s32[2,2048]{1,0:T(2,128)S(1)} %pad_add_fusion, pred[4,2048]{1,0:T(4,128)(4,1)S(1)} %iota_compare_fusion.7), kind=kOutput, calls=%fused_computation.11 | convolution fusion | flops 35684352 | bytes 65536 | tf_op jit(solution)/shard_map/dot_general | solution.py:131
  7.3 3.0 %collective-permute-start = (s32[1024]{0:T(1024)S(1)}, s32[1024]{0:T(1024)S(1)}, u32[]{:S(2)}, u32[]{:S(2)}) collective-permute-start(s32[1024]{0:T(1024)S(1)} %bitcast.117), channel_id=1, source_target_pairs={{0,8},{8,0},{16,24},{24,16},{1,9},{9,1},{17,25},{25,17},{2,10},{10... | collective-permute-start | bytes 12296 | tf_op jit(solution)/shard_map/ppermute | solution.py:142
  10.3 1.5 %collective-permute-start.1 = (s32[1024]{0:T(1024)S(1)}, s32[1024]{0:T(1024)S(1)}, u32[]{:S(2)}, u32[]{:S(2)}) collective-permute-start(s32[1024]{0:T(1024)S(1)} %bitcast.116), channel_id=1, source_target_pairs={{0,16},{8,24},{16,0},{24,8},{1,17},{9,25},{17,1},{25,9},{2,18},{10... | collective-permute-start | bytes 12296 | tf_op jit(solution)/shard_map/ppermute | solution.py:142
  11.8 0.0 collective-permute-start.2
  11.8 4.8 %fusion.9 = f32[256,256]{1,0:T(8,128)S(1)} fusion(bf16[16384,256]{1,0:T(8,128)(2,1)} %param.10, s32[]{:T(128)S(6)} %select_n.127), kind=kOutput, calls=%fused_computation.13 | convolution fusion | flops 1073741824 | bytes 4456452 | tf_op jit(solution)/shard_map/dot_general | solution.py:15
  16.6 0.1 collective-permute-start.3
  16.7 0.1 reshape.523
  16.8 0.6 compare_reduce_fusion
  17.4 0.0 collective-permute-done
  17.4 0.0 collective-permute-done.1
  17.5 0.7 collective-permute-done.3
  18.2 2.0 %collective-permute-start.4 = (bf16[256,256]{1,0:T(8,128)(2,1)S(1)}, bf16[256,256]{1,0:T(8,128)(2,1)S(1)}, u32[]{:S(2)}, u32[]{:S(2)}) collective-permute-start(bf16[256,256]{1,0:T(8,128)(2,1)S(1)} %get-tuple-element.46), channel_id=1, source_target_pairs={{0,8},{8,0},{16,24},{24,16},{1,9},{9,1},{17,25},{25,17},{2,10},{10... | collective-permute-start | bytes 393224 | tf_op jit(solution)/shard_map/ppermute | solution.py:36
  20.3 1.5 %collective-permute-start.5 = (bf16[256,256]{1,0:T(8,128)(2,1)S(1)}, bf16[256,256]{1,0:T(8,128)(2,1)S(1)}, u32[]{:S(2)}, u32[]{:S(2)}) collective-permute-start(bf16[256,256]{1,0:T(8,128)(2,1)S(1)} %get-tuple-element.46), channel_id=1, source_target_pairs={{0,16},{8,24},{16,0},{24,8},{1,17},{9,25},{17,1},{25,9},{2,18},{10... | collective-permute-start | bytes 393224 | tf_op jit(solution)/shard_map/ppermute | solution.py:36
  21.8 0.0 collective-permute-start.6
  21.8 16.6 %gather_fusion = bf16[3072,256]{1,0:T(8,128)(2,1)} fusion(bf16[16384,256]{1,0:T(8,128)(2,1)} %param.10, s32[3072]{0:T(1024)S(1)} %broadcast_clamp_fusion), kind=kCustom, calls=%fused_computation | custom fusion | bytes 3158016 | tf_op jit(solution)/shard_map/gather | solution.py:148
  38.4 0.0 copy-start.4
  38.4 0.1 convert_add_fusion
  38.5 2.5 %slice_bitcast_fusion.2 = (bf16[1024,256]{1,0:T(8,128)(2,1)}, bf16[1024,256]{1,0:T(8,128)(2,1)}, bf16[1024,256]{1,0:T(8,128)(2,1)}) fusion(bf16[3,1024,256]{2,1,0:T(8,128)(2,1)} %bitcast.107), kind=kLoop, calls=%fused_computation.41 | loop fusion | bytes 3145728 | tf_op jit(solution)/shard_map/squeeze | solution.py:158
  41.0 1.9 %collective-permute-start.7 = (bf16[1024,256]{1,0:T(8,128)(2,1)}, bf16[1024,256]{1,0:T(8,128)(2,1)}, u32[]{:S(2)}, u32[]{:S(2)}) collective-permute-start(bf16[1024,256]{1,0:T(8,128)(2,1)} %get-tuple-element.50), channel_id=1, source_target_pairs={{0,8},{8,0},{16,24},{24,16},{1,9},{9,1},{17,25},{25,17},{2,10},{10... | collective-permute-start | bytes 1572872 | tf_op jit(solution)/shard_map/ppermute | solution.py:158
  43.0 1.5 %collective-permute-start.8 = (bf16[1024,256]{1,0:T(8,128)(2,1)}, bf16[1024,256]{1,0:T(8,128)(2,1)}, u32[]{:S(2)}, u32[]{:S(2)}) collective-permute-start(bf16[1024,256]{1,0:T(8,128)(2,1)} %get-tuple-element.52), channel_id=1, source_target_pairs={{0,16},{8,24},{16,0},{24,8},{1,17},{9,25},{17,1},{25,9},{2,18},{10... | collective-permute-start | bytes 1572872 | tf_op jit(solution)/shard_map/ppermute | solution.py:158
  44.5 0.0 collective-permute-start.9
  44.7 0.2 reduce_window_sum.25
  44.9 0.1 convert_reduce_fusion.1
  45.0 0.2 fusion.78
  45.2 0.1 copy.197
  45.3 0.1 copy.196
  45.4 7.9 %gather_fusion.1 = bf16[1024,256]{1,0:T(8,128)(2,1)S(1)} fusion(bf16[16384,256]{1,0:T(8,128)(2,1)} %param.10, s32[1024]{0:T(1024)S(1)} %fusion.99), kind=kCustom, calls=%fused_computation.1 | custom fusion | bytes 1052672 | tf_op jit(solution)/shard_map/gather | solution.py:153
  53.3 2.7 %fusion.5 = f32[2048,256]{1,0:T(8,128)} fusion(bf16[1024,256]{1,0:T(8,128)(2,1)S(1)} %gather_fusion.1, s32[2048]{0:T(1024)S(1)} %get-tuple-element.72), kind=kOutput, calls=%fused_computation.10 | convolution fusion | flops 1075838976 | bytes 2629632 | tf_op jit(solution)/shard_map/dot_general | solution.py:163
  56.1 7.7 %gather_fusion.2 = bf16[2048,256]{1,0:T(8,128)(2,1)S(1)} fusion(bf16[4096,256]{1,0:T(8,128)(2,1)S(1)} %copy-done, s32[2048]{0:T(1024)S(1)} %broadcast_clamp_fusion.1), kind=kCustom, calls=%fused_computation.2 | custom fusion | bytes 2105344 | tf_op jit(solution)/shard_map/gather | solution.py:171
  63.7 0.6 convert_select_fusion
  64.3 0.7 fusion.113
  65.1 2.3 %collective-permute-done.8 = bf16[1024,256]{1,0:T(8,128)(2,1)} collective-permute-done((bf16[1024,256]{1,0:T(8,128)(2,1)}, bf16[1024,256]{1,0:T(8,128)(2,1)}, u32[]{:S(2)}, u32[]{:S(2)}) %collective-permute-start.8) | collective-permute-done | bytes 524320 | tf_op jit(solution)/shard_map/ppermute | solution.py:158
  67.4 1.5 %pad_maximum_fusion = bf16[3,1024,256]{2,1,0:T(8,128)(2,1)S(1)} fusion(bf16[1,1024,256]{2,1,0:T(8,128)(2,1)} %bitcast.19, bf16[1,1024,256]{2,1,0:T(8,128)(2,1)} %bitcast.17, bf16[1,1024,256]{2,1,0:T(8,128)(2,1)} %bitcast.15), kind=kLoop, calls=%fused_computation.19 | loop fusion | flops 1572864 | bytes 3145728 | tf_op jit(solution)/shard_map/stack | solution.py:167
  68.9 4.2 %fusion.18 = bf16[2048,256]{1,0:T(8,128)(2,1)S(1)} fusion(f32[2048,256]{1,0:T(8,128)S(1)} %copy-done.5, bf16[3072,256]{1,0:T(8,128)(2,1)S(1)} %bitcast.108, s32[3072]{0:T(1024)S(1)} %iota_add_fusion, s32[2048]{0:T(1024)S(1)} %get-tuple-element.72, bf16[2048,256]{1,0:T(8,128)(2,1)S(1)} %gather_fusion.2), kind=kOutput, calls=%fused_computation.18 | convolution fusion | flops 3229614080 | bytes 5787648 | tf_op jit(solution)/shard_map/dot_general | solution.py:168
  73.2 0.3 convolution_reduce_fusion.3
  73.5 0.4 convolution_reduce_fusion.6
  74.0 0.3 convolution_reduce_fusion.2
  74.3 0.4 multiply_reduce_fusion.3
  74.6 0.2 multiply_reduce_fusion.2
  74.8 0.1 fusion.68
  75.0 0.4 convolution_reduce_fusion.5
  75.5 0.3 convolution_reduce_fusion.1
  75.7 0.4 multiply_reduce_fusion.1
  76.1 0.2 multiply_reduce_fusion
  76.3 0.1 fusion.70
  76.4 0.0 copy-start.1
  76.4 0.4 convolution_reduce_fusion.4
  76.9 0.3 convolution_reduce_fusion
  77.2 0.4 fusion.27
  77.6 0.3 fusion.26
  77.9 12.5 %all_to_all.5 = f32[32,2,384]{2,1,0:T(2,128)S(1)} all-to-all(f32[32,2,384]{2,1,0:T(2,128)S(1)} %bitcast.109), channel_id=1, replica_groups=mesh['table'=4,'batch'=4,'ctx'=2] {'table','batch','ctx'}, dimensions={0} | all-to-all | bytes 196608 | tf_op jit(solution)/shard_map/all_to_all | solution.py:198
  90.5 0.1 reshape.526
  90.5 0.1 fusion.36
  90.6 0.1 convert_reduce_fusion
  90.8 1.3 %fusion.21 = bf16[1024,256]{1,0:T(8,128)(2,1)} fusion(bf16[1024,256]{1,0:T(8,128)(2,1)S(1)} %copy-done.1, pred[1024]{0:T(1024)(128)(4,1)S(1)} %broadcast_compare_fusion, s32[64]{0:T(128)S(1)} %fusion.36, f32[64,384]{1,0:T(8,128)S(1)} %reshape.526), kind=kOutput, calls=%fused_computation.21 | convolution fusion | flops 34144256 | bytes 1082880 | tf_op jit(solution)/shard_map/dot_general | solution.py:205
  (70 shorter events, 0.7 us)
Async XLA Ops:
  0.0 56.1 %copy-start = (bf16[4096,256]{1,0:T(8,128)(2,1)S(1)}, bf16[4096,256]{1,0:T(8,128)(2,1)}, u32[]{:S(2)}) copy-start(bf16[4096,256]{1,0:T(8,128)(2,1)} %param.11) | copy-start | bytes 6291460
  7.3 10.1 %collective-permute-start = (s32[1024]{0:T(1024)S(1)}, s32[1024]{0:T(1024)S(1)}, u32[]{:S(2)}, u32[]{:S(2)}) collective-permute-start(s32[1024]{0:T(1024)S(1)} %bitcast.117), channel_id=1, source_target_pairs={{0,8},{8,0},{16,24},{24,16},{1,9},{9,1},{17,25},{25,17},{2,10},{10... | collective-permute-start | bytes 12296 | tf_op jit(solution)/shard_map/ppermute | solution.py:142
  10.3 7.1 %collective-permute-start.1 = (s32[1024]{0:T(1024)S(1)}, s32[1024]{0:T(1024)S(1)}, u32[]{:S(2)}, u32[]{:S(2)}) collective-permute-start(s32[1024]{0:T(1024)S(1)} %bitcast.116), channel_id=1, source_target_pairs={{0,16},{8,24},{16,0},{24,8},{1,17},{9,25},{17,1},{25,9},{2,18},{10... | collective-permute-start | bytes 12296 | tf_op jit(solution)/shard_map/ppermute | solution.py:142
  11.8 5.6 %collective-permute-start.2 = (s32[1024]{0:T(1024)S(1)}, s32[1024]{0:T(1024)S(1)}, u32[]{:S(2)}, u32[]{:S(2)}) collective-permute-start(s32[1024]{0:T(1024)S(1)} %bitcast.115), channel_id=1, source_target_pairs={{0,24},{8,16},{16,8},{24,0},{1,25},{9,17},{17,9},{25,1},{2,26},{10... | collective-permute-start | bytes 12296 | tf_op jit(solution)/shard_map/ppermute | solution.py:142
  11.8 4.8 %copy-start.3 = (s32[32,64]{1,0:T(8,128)S(1)}, s32[32,64]{1,0:T(8,128)}, u32[]{:S(2)}) copy-start(s32[32,64]{1,0:T(8,128)} %param.15) | copy-start | bytes 24580
  16.6 1.6 %collective-permute-start.3 = (f32[256,256]{1,0:T(8,128)S(1)}, f32[256,256]{1,0:T(8,128)S(1)}, u32[]{:S(2)}, u32[]{:S(2)}) collective-permute-start(f32[256,256]{1,0:T(8,128)S(1)} %fusion.9), channel_id=1, source_target_pairs={{0,1},{1,0},{2,3},{3,2},{4,5},{5,4},{6,7},{7,6},{8,9},{9,8},{10,11... | collective-permute-start | bytes 786440 | tf_op jit(solution)/shard_map/ppermute | solution.py:26
  18.2 20.2 %collective-permute-start.4 = (bf16[256,256]{1,0:T(8,128)(2,1)S(1)}, bf16[256,256]{1,0:T(8,128)(2,1)S(1)}, u32[]{:S(2)}, u32[]{:S(2)}) collective-permute-start(bf16[256,256]{1,0:T(8,128)(2,1)S(1)} %get-tuple-element.46), channel_id=1, source_target_pairs={{0,8},{8,0},{16,24},{24,16},{1,9},{9,1},{17,25},{25,17},{2,10},{10... | collective-permute-start | bytes 393224 | tf_op jit(solution)/shard_map/ppermute | solution.py:36
  20.3 18.1 %collective-permute-start.5 = (bf16[256,256]{1,0:T(8,128)(2,1)S(1)}, bf16[256,256]{1,0:T(8,128)(2,1)S(1)}, u32[]{:S(2)}, u32[]{:S(2)}) collective-permute-start(bf16[256,256]{1,0:T(8,128)(2,1)S(1)} %get-tuple-element.46), channel_id=1, source_target_pairs={{0,16},{8,24},{16,0},{24,8},{1,17},{9,25},{17,1},{25,9},{2,18},{10... | collective-permute-start | bytes 393224 | tf_op jit(solution)/shard_map/ppermute | solution.py:36
  21.8 16.6 %collective-permute-start.6 = (bf16[256,256]{1,0:T(8,128)(2,1)S(1)}, bf16[256,256]{1,0:T(8,128)(2,1)S(1)}, u32[]{:S(2)}, u32[]{:S(2)}) collective-permute-start(bf16[256,256]{1,0:T(8,128)(2,1)S(1)} %get-tuple-element.46), channel_id=1, source_target_pairs={{0,24},{8,16},{16,8},{24,0},{1,25},{9,17},{17,9},{25,1},{2,26},{10... | collective-permute-start | bytes 393224 | tf_op jit(solution)/shard_map/ppermute | solution.py:36
  38.4 6.1 %copy-start.2 = (s32[32,64]{1,0:T(8,128)S(1)}, s32[32,64]{1,0:T(8,128)}, u32[]{:S(2)}) copy-start(s32[32,64]{1,0:T(8,128)} %param.16) | copy-start | bytes 24580
  38.4 6.2 %copy-start.4 = (s32[32]{0:T(128)S(1)}, s32[32]{0:T(128)}, u32[]{:S(2)}) copy-start(s32[32]{0:T(128)} %param.17) | copy-start | bytes 388
  41.0 24.0 %collective-permute-start.7 = (bf16[1024,256]{1,0:T(8,128)(2,1)}, bf16[1024,256]{1,0:T(8,128)(2,1)}, u32[]{:S(2)}, u32[]{:S(2)}) collective-permute-start(bf16[1024,256]{1,0:T(8,128)(2,1)} %get-tuple-element.50), channel_id=1, source_target_pairs={{0,8},{8,0},{16,24},{24,16},{1,9},{9,1},{17,25},{25,17},{2,10},{10... | collective-permute-start | bytes 1572872 | tf_op jit(solution)/shard_map/ppermute | solution.py:158
  43.0 24.4 %collective-permute-start.8 = (bf16[1024,256]{1,0:T(8,128)(2,1)}, bf16[1024,256]{1,0:T(8,128)(2,1)}, u32[]{:S(2)}, u32[]{:S(2)}) collective-permute-start(bf16[1024,256]{1,0:T(8,128)(2,1)} %get-tuple-element.52), channel_id=1, source_target_pairs={{0,16},{8,24},{16,0},{24,8},{1,17},{9,25},{17,1},{25,9},{2,18},{10... | collective-permute-start | bytes 1572872 | tf_op jit(solution)/shard_map/ppermute | solution.py:158
  44.5 22.9 %collective-permute-start.9 = (bf16[1024,256]{1,0:T(8,128)(2,1)}, bf16[1024,256]{1,0:T(8,128)(2,1)}, u32[]{:S(2)}, u32[]{:S(2)}) collective-permute-start(bf16[1024,256]{1,0:T(8,128)(2,1)} %get-tuple-element.51), channel_id=1, source_target_pairs={{0,24},{8,16},{16,8},{24,0},{1,25},{9,17},{17,9},{25,1},{2,26},{10... | collective-permute-start | bytes 1572872 | tf_op jit(solution)/shard_map/ppermute | solution.py:158
  65.1 3.9 %copy-start.5 = (f32[2048,256]{1,0:T(8,128)S(1)}, f32[2048,256]{1,0:T(8,128)}, u32[]{:S(2)}) copy-start(f32[2048,256]{1,0:T(8,128)} %fusion.5) | copy-start | bytes 6291460
  76.4 14.4 %copy-start.1 = (bf16[1024,256]{1,0:T(8,128)(2,1)S(1)}, bf16[1024,256]{1,0:T(8,128)(2,1)}, u32[]{:S(2)}) copy-start(bf16[1024,256]{1,0:T(8,128)(2,1)} %param.12) | copy-start | bytes 1572868
